TPU v7x, 32 devices: a whole 2x2x4 slice. The times are simulated.
32 devices in a mesh: group: 16 (over z, x, core), loop: 2 (over y).
Axes of the slice: x: 2, y: 2, z: 4, core: 2. Of those that a mesh axis runs over, the one named last changes fastest.
Arguments:
- user_factors: bfloat16 [32768, 256], P('group'), may hold values from -1.5 to 1.5
- item_factors: bfloat16 [2048, 256], P('loop'), may hold values from -1.5 to 1.5
- tag_factors: bfloat16 [2048, 256], P('group'), may hold values from -1.5 to 1.5
- ratings: bfloat16 [32768, 2048], P('group', 'loop'), may hold values from -6 to 6
- rating_tiles: int32 [256, 16], P('group', 'loop'), may hold values 0 or 1
- tag_links: bfloat16 [2048, 2048], P('loop', 'group'), may hold values from -6 to 6
- link_tiles: int32 [16, 16], P('loop', 'group'), may hold values 0 or 1
Outputs:
- new_users: bfloat16 [32768, 256], P('group')
- new_items: bfloat16 [2048, 256], P('loop')
- new_tags: bfloat16 [2048, 256], P('group')
Inputs may be any that keep to these rules, and one draw needn't show every extreme that they name: `rating_tiles`: 1 marks a tile of observed entries, 0 an empty tile. `link_tiles`: 1 marks a tile of observed entries, 0 an empty tile.
All inputs are finite; a program needn't handle non-finite values. No bound on the sum of `rating_tiles` or of `link_tiles` on one device may be relied on, other than what follows from the above.
Results may differ from a plain program's by a relative error of at most 0.0034.
Values may be sent and summed in bfloat16 or wider, within the bound.
No kernel may reach another device: no remote copies, remote signals or barrier semaphores. Data moves between devices by JAX's collectives and lax.ppermute only.
A program may use at most 64 MiB of HBM per device.

v0:
```python
import jax
import jax.numpy as jnp
from jax import lax
from jax.sharding import PartitionSpec as P

step_users = 0.015
step_items = 0.004
step_tags = 0.015


def tile_masked(values, tile_flags):
    height, breadth = values.shape
    blocks = values.reshape(height // 128, 128, breadth // 128, 128)
    masked = blocks * tile_flags.astype(jnp.float32)[:, None, :, None]
    return masked.reshape(height, breadth)


def residual_of(observed, row_factors, column_factors, tile_flags):
    predicted = lax.dot_general(
        row_factors, column_factors, (((1,), (1,)), ((), ())), preferred_element_type=jnp.float32
    )
    return tile_masked(observed.astype(jnp.float32) - predicted, tile_flags).astype(jnp.bfloat16)


def transposed_product(first_operand, second_operand):
    return lax.dot_general(
        first_operand, second_operand, (((0,), (0,)), ((), ())), preferred_element_type=jnp.float32
    )


def advance(factors, gradient, rate):
    return (factors.astype(jnp.float32) + rate * gradient).astype(jnp.bfloat16)


def own_share(factors, axis_count, position):
    share_rows = factors.shape[0] // axis_count
    return lax.dynamic_slice_in_dim(factors, position * share_rows, share_rows, 0)


def shards(user_factors, item_factors, tag_factors, ratings, rating_tiles, tag_links, link_tiles):
    link_errors = residual_of(tag_links, item_factors, tag_factors, link_tiles)
    rating_errors = residual_of(ratings, user_factors, item_factors, rating_tiles)
    item_part = transposed_product(rating_errors, user_factors) + jnp.dot(
        link_errors, tag_factors, preferred_element_type=jnp.float32
    )
    user_part = jnp.dot(rating_errors, item_factors, preferred_element_type=jnp.float32)
    tag_part = transposed_product(link_errors, item_factors)
    item_share = lax.psum_scatter(item_part, "group", scatter_dimension=0, tiled=True)
    group_count = lax.axis_size("group")
    group_position = lax.axis_index("group")
    fresh_share = advance(
        own_share(item_factors, group_count, group_position), item_share, step_items
    )
    new_items = lax.all_gather(fresh_share, "group", axis=0, tiled=True)
    user_grad, tag_grad = lax.psum((user_part, tag_part), "loop")
    new_users = advance(user_factors, user_grad, step_users)
    new_tags = advance(tag_factors, tag_grad, step_tags)
    return (new_users, new_items, new_tags)


def solution(mesh):
    in_specs = (
        P("group", None),
        P("loop", None),
        P("group", None),
        P("group", "loop"),
        P("group", "loop"),
        P("loop", "group"),
        P("loop", "group"),
    )
    out_specs = (P("group", None), P("loop", None), P("group", None))
    return jax.shard_map(shards, mesh=mesh, in_specs=in_specs, out_specs=out_specs, check_vma=False)
```

profile of v0, /device:TPU:0, one launch (start us, length us, event | category | flops | bytes accessed | tf_op | source)
XLA Modules:
  0.0 111.5 jit_solution(9205640242450746977)
XLA Ops:
  8.0 0.0 reduce-scatter.2.cloned.1.call-start
  8.0 0.7 convert_element_type.38
  8.7 0.1 copy.10
  8.8 0.7 convert_bitcast_fusion
  9.5 0.1 broadcast_bitcast_fusion
  9.5 0.6 mul.49
  10.2 0.4 copy-done
  10.6 0.3 copy-done.1
  10.9 1.3 %copy-done.2 = bf16[2048,1024]{1,0:T(8,128)(2,1)S(1)} copy-done((bf16[2048,1024]{1,0:T(8,128)(2,1)S(1)}, bf16[2048,1024]{1,0:T(8,128)(2,1)}, u32[]{:S(2)}) %copy-start.2) | copy-done | bytes 4194328
  12.2 2.0 %fusion = bf16[2048,1024]{1,0:T(8,128)(2,1)S(1)} fusion(f32[256,8,8,128]{3,2,1,0:T(8,128)S(1)} %bitcast.22, bf16[2048,1024]{1,0:T(8,128)(2,1)S(1)} %copy-done.2, bf16[2048,256]{1,0:T(8,128)(2,1)S(1)} %copy-done.1, bf16[1024,256]{1,0:T(8,128)(2,1)S(1)} %copy-done), kind=kOutput, calls=%fused_computation.1 | convolution fusion | flops 1082130432 | bytes 18350080 | tf_op jit(solution)/shard_map/dot_general | solution.py:19
  14.3 1.3 %fusion.4 = f32[1024,256]{1,0:T(8,128)S(1)} fusion(bf16[2048,1024]{1,0:T(8,128)(2,1)S(1)} %fusion, bf16[2048,256]{1,0:T(8,128)(2,1)S(1)} %copy-done.1), kind=kOutput, calls=%fused_computation.12 | convolution fusion | flops 1073741824 | bytes 6291456 | tf_op jit(solution)/shard_map/dot_general | solution.py:26
  15.6 0.6 copy-done.3
  16.2 0.3 fusion.2
  16.5 1.2 %convolution_add_fusion = f32[1024,256]{1,0:T(8,128)} fusion(f32[1024,256]{1,0:T(8,128)S(1)} %fusion.4, bf16[1024,128]{1,0:T(8,128)(2,1)S(1)} %fusion.2, bf16[128,256]{1,0:T(8,128)(2,1)S(1)} %copy-done.4), kind=kOutput, calls=%fused_computation.3 | convolution fusion | flops 67371008 | bytes 2424832 | tf_op jit(solution)/shard_map/dot_general | solution.py:43
  17.8 0.0 all-reduce.3.cloned.1.call-start
  17.9 0.9 fusion.5
  18.8 4.8 %fusion.3 = f32[2048,256]{1,0:T(8,128)} fusion(bf16[2048,1024]{1,0:T(8,128)(2,1)} %copy-done.3, bf16[1024,256]{1,0:T(8,128)(2,1)S(1)} %copy-done), kind=kOutput, calls=%fused_computation.11 | convolution fusion | flops 1073741824 | bytes 6815744 | tf_op jit(solution)/shard_map/dot_general | solution.py:46
  23.5 0.0 all-reduce.3.cloned.1.call-update
  23.6 54.4 %reduce-scatter.2.cloned.1.call-done = f32[64,256]{1,0:T(8,128)} async-done(((f32[1024,256]{1,0:T(8,128)}), f32[64,256]{1,0:T(8,128)}) %reduce-scatter.2.cloned.1.call-update) | async-done | bytes 65552 | tf_op jit(solution)/shard_map/reduce_scatter | solution.py:48
  78.0 0.9 add_convert_fusion.2
  78.8 20.9 %all_gather.3 = bf16[1024,256]{1,0:T(8,128)(2,1)S(1)} all-gather(bf16[64,256]{1,0:T(8,128)(2,1)S(1)} %add_convert_fusion.2), channel_id=1, replica_groups=mesh['group'=16,'loop'=2] {'group'}, dimensions={0}, use_global_device_ids=true | all-gather | bytes 557056 | tf_op jit(solution)/shard_map/all_gather | solution.py:54
  99.7 2.9 %add_convert_fusion = bf16[2048,256]{1,0:T(8,128)(2,1)} fusion(f32[2048,256]{1,0:T(8,128)} %get-tuple-element.3, bf16[2048,256]{1,0:T(8,128)(2,1)S(1)} %copy-done.1), kind=kLoop, calls=%fused_computation.2 | loop fusion | flops 2097152 | bytes 4194304 | tf_op jit(solution)/shard_map/convert_element_type | solution.py:32
  102.6 0.7 add_convert_fusion.1
  103.3 0.8 copy.16
  (12 shorter events, 0.0 us)
Async XLA Ops:
  8.0 70.0 %reduce-scatter.2.cloned.1.call-start = ((), (), s32[]{:S(2)}) async-start(), calls=%async_computation.1 | async-start | bytes 1114112 | tf_op jit(solution)/shard_map/reduce_scatter | solution.py:48
  9.5 1.0 copy-start
  9.5 1.4 %copy-start.1 = (bf16[2048,256]{1,0:T(8,128)(2,1)S(1)}, bf16[2048,256]{1,0:T(8,128)(2,1)}, u32[]{:S(2)}) copy-start(bf16[2048,256]{1,0:T(8,128)(2,1)} %param.7) | copy-start | bytes 3145732
  9.5 2.7 %copy-start.2 = (bf16[2048,1024]{1,0:T(8,128)(2,1)S(1)}, bf16[2048,1024]{1,0:T(8,128)(2,1)}, u32[]{:S(2)}) copy-start(bf16[2048,1024]{1,0:T(8,128)(2,1)} %param.10) | copy-start | bytes 12582916
  14.3 1.9 %copy-start.3 = (bf16[2048,1024]{1,0:T(8,128)(2,1)}, bf16[2048,1024]{1,0:T(8,128)(2,1)S(1)}, u32[]{:S(2)}) copy-start(bf16[2048,1024]{1,0:T(8,128)(2,1)S(1)} %fusion) | copy-start | bytes 12582916
  14.3 1.9 %copy-start.4 = (bf16[128,256]{1,0:T(8,128)(2,1)S(1)}, bf16[128,256]{1,0:T(8,128)(2,1)}, u32[]{:S(2)}) copy-start(bf16[128,256]{1,0:T(8,128)(2,1)} %param.9) | copy-start | bytes 196612
  14.3 1.9 %copy-start.5 = (bf16[1024,128]{1,0:T(8,128)(2,1)S(1)}, bf16[1024,128]{1,0:T(8,128)(2,1)}, u32[]{:S(2)}) copy-start(bf16[1024,128]{1,0:T(8,128)(2,1)} %param.12) | copy-start | bytes 786436
  17.8 81.9 %all-reduce.3.cloned.1.call-start = ((), (), s32[]{:S(2)}) async-start(), calls=%async_computation.2 | async-start | bytes 4456448 | tf_op jit(solution)/shard_map/psum | solution.py:55
  99.7 2.9 %copy-start.6 = (f32[128,256]{1,0:T(8,128)S(1)}, f32[128,256]{1,0:T(8,128)}, u32[]{:S(2)}) copy-start(f32[128,256]{1,0:T(8,128)} %get-tuple-element.4) | copy-start | bytes 393220
Sparse Core Ops, SparseCore 0:
  17.9 60.0 reduce-scatter.1
Sparse Core Ops, SparseCore 1:
  23.6 68.5 all-reduce.2
where the time goes:
time: 112 us
  waiting for transfers between devices  54.4 us (49%)
  blocking collectives  20.9 us (19%)
  between operations  15.5 us (14%)
  matrix products  10.6 us (9%)
  other arithmetic  5.74 us (5%)
  local copies, waits for them, and re-layouts  4.24 us (4%)
    reduce_scatter x1, waiting for transfers between devices, shards(): lax.psum_scatter(item_part, 'group', scatter_dimension=0, tiled=True)  54.4 us
    all_gather x1, blocking collectives, shards(): new_items = lax.all_gather(fresh_share, 'group', axis=0, tiled=True)  20.9 us
    dot_general x1, matrix products, shards(): jnp.dot(rating_errors, item_factors, preferred_element_type=jnp.float32)  4.76 us
    convert_element_type x3, other arithmetic, advance(): return (factors.astype(jnp.float32) + rate * gradient).astype(jnp.bfloat16)  4.4 us
    unnamed x15, local copies, waits for them, and re-layouts  3.49 us
    dot_general x2, matrix products, residual_of(): lax.dot_general(row_factors, column_factors, (((1,), (1,)), ((), ())), pr...  2.34 us
  transfers between devices with their start and end apart: 2, of which 1 were waited for; matrix products, arithmetic and copies ran while one was open for 6% of the time, Pallas kernels for 0%

commit v1 on v0

--- a/solution.py
+++ b/solution.py
@@ -32,29 +32,74 @@
     return (factors.astype(jnp.float32) + rate * gradient).astype(jnp.bfloat16)
 
 
-def own_share(factors, axis_count, position):
-    share_rows = factors.shape[0] // axis_count
-    return lax.dynamic_slice_in_dim(factors, position * share_rows, share_rows, 0)
+def xor_pairs(count, bit):
+    return [(i, i ^ (1 << bit)) for i in range(count)]
+
+
+def halving_scatter(parts, axis, count, position):
+    steps = count.bit_length() - 1
+    offsets = [0 for _ in parts]
+    for bit in range(steps):
+        side = (position >> bit) & 1
+        halves = [p.shape[0] // 2 for p in parts]
+        kept = [lax.dynamic_slice_in_dim(p, side * h, h, 0) for p, h in zip(parts, halves)]
+        sent = [lax.dynamic_slice_in_dim(p, (1 - side) * h, h, 0) for p, h in zip(parts, halves)]
+        got = lax.ppermute(tuple(sent), axis, xor_pairs(count, bit))
+        parts = [k + g for k, g in zip(kept, got)]
+        offsets = [o + side * h for o, h in zip(offsets, halves)]
+    return parts, offsets
+
+
+def doubling_gather(parts, axis, count, position):
+    steps = count.bit_length() - 1
+    for bit in reversed(range(steps)):
+        side = (position >> bit) & 1
+        got = lax.ppermute(tuple(parts), axis, xor_pairs(count, bit))
+        parts = [
+            jnp.where(side == 0, jnp.concatenate([m, g], 0), jnp.concatenate([g, m], 0))
+            for m, g in zip(parts, got)
+        ]
+    return parts
 
 
 def shards(user_factors, item_factors, tag_factors, ratings, rating_tiles, tag_links, link_tiles):
+    group_count = lax.axis_size("group")
+    loop_count = lax.axis_size("loop")
+    group_position = lax.axis_index("group")
+    loop_position = lax.axis_index("loop")
+
     link_errors = residual_of(tag_links, item_factors, tag_factors, link_tiles)
     rating_errors = residual_of(ratings, user_factors, item_factors, rating_tiles)
+    user_part = jnp.dot(rating_errors, item_factors, preferred_element_type=jnp.float32)
+    tag_part = transposed_product(link_errors, item_factors)
     item_part = transposed_product(rating_errors, user_factors) + jnp.dot(
         link_errors, tag_factors, preferred_element_type=jnp.float32
     )
-    user_part = jnp.dot(rating_errors, item_factors, preferred_element_type=jnp.float32)
-    tag_part = transposed_product(link_errors, item_factors)
-    item_share = lax.psum_scatter(item_part, "group", scatter_dimension=0, tiled=True)
-    group_count = lax.axis_size("group")
-    group_position = lax.axis_index("group")
-    fresh_share = advance(
-        own_share(item_factors, group_count, group_position), item_share, step_items
+
+    (user_share, tag_share), (user_offset, tag_offset) = halving_scatter(
+        [user_part, tag_part], "loop", loop_count, loop_position
     )
-    new_items = lax.all_gather(fresh_share, "group", axis=0, tiled=True)
-    user_grad, tag_grad = lax.psum((user_part, tag_part), "loop")
-    new_users = advance(user_factors, user_grad, step_users)
-    new_tags = advance(tag_factors, tag_grad, step_tags)
+    fresh_users = advance(
+        lax.dynamic_slice_in_dim(user_factors, user_offset, user_share.shape[0], 0),
+        user_share,
+        step_users,
+    )
+    fresh_tags = advance(
+        lax.dynamic_slice_in_dim(tag_factors, tag_offset, tag_share.shape[0], 0),
+        tag_share,
+        step_tags,
+    )
+    new_users, new_tags = doubling_gather(
+        [fresh_users, fresh_tags], "loop", loop_count, loop_position
+    )
+
+    (item_share,), (item_offset,) = halving_scatter([item_part], "group", group_count, group_position)
+    fresh_items = advance(
+        lax.dynamic_slice_in_dim(item_factors, item_offset, item_share.shape[0], 0),
+        item_share,
+        step_items,
+    )
+    (new_items,) = doubling_gather([fresh_items], "group", group_count, group_position)
     return (new_users, new_items, new_tags)
 
 

time: 112 us -> 66.9 us (0.60)
  waiting for transfers between devices: 54.4 us -> 26.4 us
  blocking collectives: 20.9 us -> 0 us
  starting transfers between devices: 0.08 us -> 20.2 us
  between operations: 15.5 us -> 0.83 us
    reduce_scatter x1 -> x0, waiting for transfers between devices: 54.4 us -> none  [shards(): lax.psum_scatter(item_part, 'group', scatter_dimension=0, tiled=True)]
    ppermute x0 -> x12, waiting for transfers between devices: none -> 26.4 us  [the longest x6 14.2 us: halving_scatter(): got = lax.ppermute(tuple(sent), axis, xor_pairs(count, bit))]
    all_gather x1 -> x0, blocking collectives: 20.9 us -> none  [shards(): new_items = lax.all_gather(fresh_share, 'group', axis=0, tiled=True)]
    ppermute x0 -> x12, starting transfers between devices: none -> 20.2 us  [the longest x6 11.2 us: halving_scatter(): got = lax.ppermute(tuple(sent), axis, xor_pairs(count, bit))]
    select_n x0 -> x6, other arithmetic: none -> 3.03 us  [doubling_gather(): jnp.where(side == 0, jnp.concatenate([m, g], 0), jnp.concatenate([g, m], 0))]
    convert_element_type x3, other arithmetic: 4.4 us -> 1.76 us  [advance(): return (factors.astype(jnp.float32) + rate * gradient).astype(jnp.bfloat16)]
    unnamed x15 -> x16, local copies, waits for them, and re-layouts: 3.49 us -> 2.07 us
    dot_general x1, matrix products: 4.76 us -> 3.46 us  [shards(): jnp.dot(rating_errors, item_factors, preferred_element_type=jnp.float32)]
  transfers between devices with their start and end apart: 2 -> 12, of which waited for: 1 -> 8; matrix products, arithmetic and copies ran while one was open for 6% -> 11% of each run, Pallas kernels for 0% -> 0%
where the time goes in v1:
time: 66.9 us; the launch traced here: 66.6 us
  waiting for transfers between devices  26.4 us (39%)
  starting transfers between devices  20.2 us (30%)
  matrix products  9.87 us (15%)
  other arithmetic  5.6 us (8%)
  local copies, waits for them, and re-layouts  3.79 us (6%)
  between operations  0.83 us (1%)
    ppermute x6, waiting for transfers between devices, halving_scatter(): got = lax.ppermute(tuple(sent), axis, xor_pairs(count, bit))  14.2 us
    ppermute x6, waiting for transfers between devices, doubling_gather(): got = lax.ppermute(tuple(parts), axis, xor_pairs(count, bit))  12.1 us
    ppermute x6, starting transfers between devices, halving_scatter(): got = lax.ppermute(tuple(sent), axis, xor_pairs(count, bit))  11.2 us
    ppermute x6, starting transfers between devices, doubling_gather(): got = lax.ppermute(tuple(parts), axis, xor_pairs(count, bit))  8.97 us
    dot_general x1, matrix products, shards(): jnp.dot(rating_errors, item_factors, preferred_element_type=jnp.float32)  3.46 us
    select_n x6, other arithmetic, doubling_gather(): jnp.where(side == 0, jnp.concatenate([m, g], 0), jnp.concatenate([g, m], 0))  3.03 us
    dot_general x2, matrix products, transposed_product(): lax.dot_general(first_operand, second_operand, (((0,), (0,)), ((), ())),...  2.57 us
    dot_general x2, matrix products, residual_of(): lax.dot_general(row_factors, column_factors, (((1,), (1,)), ((), ())), pr...  2.34 us
  transfers between devices with their start and end apart: 12, of which 8 were waited for; matrix products, arithmetic and copies ran while one was open for 11% of the time, Pallas kernels for 0%

profile of v1, /device:TPU:0, one launch (start us, length us, event | category | flops | bytes accessed | tf_op | source)
XLA Modules:
  0.0 66.6 jit_solution(8756958896858589658)
XLA Ops:
  2.4 1.3 %copy-done.1 = bf16[2048,1024]{1,0:T(8,128)(2,1)S(1)} copy-done((bf16[2048,1024]{1,0:T(8,128)(2,1)S(1)}, bf16[2048,1024]{1,0:T(8,128)(2,1)}, u32[]{:S(2)}) %copy-start.1) | copy-done | bytes 4194328
  4.1 2.0 %fusion = bf16[2048,1024]{1,0:T(8,128)(2,1)S(1)} fusion(f32[256,8,8,128]{3,2,1,0:T(8,128)S(1)} %bitcast.22, bf16[2048,1024]{1,0:T(8,128)(2,1)S(1)} %copy-done.1, bf16[2048,256]{1,0:T(8,128)(2,1)S(1)} %copy-done.3, bf16[1024,256]{1,0:T(8,128)(2,1)S(1)} %copy-done), kind=kOutput, calls=%fused_computation.1 | convolution fusion | flops 1082130432 | bytes 18350080 | tf_op jit(solution)/shard_map/dot_general | solution.py:19
  6.1 2.3 %fusion.4 = f32[1024,256]{1,0:T(8,128)} fusion(bf16[2048,1024]{1,0:T(8,128)(2,1)S(1)} %fusion, bf16[2048,256]{1,0:T(8,128)(2,1)S(1)} %copy-done.3), kind=kOutput, calls=%fused_computation.27 | convolution fusion | flops 1073741824 | bytes 6291456 | tf_op jit(solution)/shard_map/dot_general | solution.py:26
  8.8 1.5 %convolution_add_fusion = f32[1024,256]{1,0:T(8,128)S(1)} fusion(f32[1024,256]{1,0:T(8,128)} %fusion.4, bf16[1024,128]{1,0:T(8,128)(2,1)S(1)} %fusion.2, bf16[128,256]{1,0:T(8,128)(2,1)S(1)} %copy-done.5), kind=kOutput, calls=%fused_computation.2 | convolution fusion | flops 67371008 | bytes 2424832 | tf_op jit(solution)/shard_map/dot_general | solution.py:75
  11.7 1.7 %collective-permute-done.2 = f32[512,256]{1,0:T(8,128)S(1)} collective-permute-done((f32[512,256]{1,0:T(8,128)}, f32[512,256]{1,0:T(8,128)S(1)}, u32[]{:S(2)}, u32[]{:S(2)}) %collective-permute-start.2) | collective-permute-done | bytes 524320 | tf_op jit(solution)/shard_map/ppermute | solution.py:47
  13.5 2.9 %collective-permute-start.3 = (f32[256,256]{1,0:T(8,128)S(1)}, f32[256,256]{1,0:T(8,128)S(1)}, u32[]{:S(2)}, u32[]{:S(2)}) collective-permute-start(f32[256,256]{1,0:T(8,128)S(1)} %constant_dynamic-slice_fusion.2), channel_id=1, source_target_pairs={{0,4},{2,6},{4,0},{6,2},{8,12},{10,14},{12,8},{14,10},{16,20},{18,... | collective-permute-start | bytes 786440 | tf_op jit(solution)/shard_map/ppermute | solution.py:47
  16.4 3.5 %fusion.3 = f32[2048,256]{1,0:T(8,128)S(1)} fusion(bf16[2048,1024]{1,0:T(8,128)(2,1)} %copy-done.2, bf16[1024,256]{1,0:T(8,128)(2,1)S(1)} %copy-done), kind=kOutput, calls=%fused_computation.26 | convolution fusion | flops 1073741824 | bytes 6815744 | tf_op jit(solution)/shard_map/dot_general | solution.py:73
  19.9 3.1 %collective-permute-done.3 = f32[256,256]{1,0:T(8,128)S(1)} collective-permute-done((f32[256,256]{1,0:T(8,128)S(1)}, f32[256,256]{1,0:T(8,128)S(1)}, u32[]{:S(2)}, u32[]{:S(2)}) %collective-permute-start.3) | collective-permute-done | bytes 262176 | tf_op jit(solution)/shard_map/ppermute | solution.py:47
  23.1 1.9 %collective-permute-start.4 = (f32[128,256]{1,0:T(8,128)S(1)}, f32[128,256]{1,0:T(8,128)S(1)}, u32[]{:S(2)}, u32[]{:S(2)}) collective-permute-start(f32[128,256]{1,0:T(8,128)S(1)} %constant_dynamic-slice_fusion.1), channel_id=1, source_target_pairs={{0,8},{2,10},{4,12},{6,14},{8,0},{10,2},{12,4},{14,6},{16,24},{18,... | collective-permute-start | bytes 393224 | tf_op jit(solution)/shard_map/ppermute | solution.py:47
  25.1 1.6 %collective-permute-start = (f32[1024,256]{1,0:T(8,128)S(1)}, f32[1024,256]{1,0:T(8,128)}, u32[]{:S(2)}, u32[]{:S(2)}) collective-permute-start(f32[1024,256]{1,0:T(8,128)S(1)} %constant_dynamic-slice_fusion.4), channel_id=1, source_target_pairs={{0,1},{1,0},{2,3},{3,2},{4,5},{5,4},{6,7},{7,6},{8,9},{9,8},{10,11... | collective-permute-start | bytes 3145736 | tf_op jit(solution)/shard_map/ppermute | solution.py:47
  26.6 1.5 %collective-permute-done.4 = f32[128,256]{1,0:T(8,128)S(1)} collective-permute-done((f32[128,256]{1,0:T(8,128)S(1)}, f32[128,256]{1,0:T(8,128)S(1)}, u32[]{:S(2)}, u32[]{:S(2)}) %collective-permute-start.4) | collective-permute-done | bytes 131104 | tf_op jit(solution)/shard_map/ppermute | solution.py:47
  28.2 2.8 %collective-permute-start.5 = (f32[64,256]{1,0:T(8,128)S(1)}, f32[64,256]{1,0:T(8,128)S(1)}, u32[]{:S(2)}, u32[]{:S(2)}) collective-permute-start(f32[64,256]{1,0:T(8,128)S(1)} %constant_dynamic-slice_fusion), channel_id=1, source_target_pairs={{0,16},{2,18},{4,20},{6,22},{8,24},{10,26},{12,28},{14,30},{16,0},... | collective-permute-start | bytes 196616 | tf_op jit(solution)/shard_map/ppermute | solution.py:47
  31.1 2.4 %collective-permute-done.5 = f32[64,256]{1,0:T(8,128)S(1)} collective-permute-done((f32[64,256]{1,0:T(8,128)S(1)}, f32[64,256]{1,0:T(8,128)S(1)}, u32[]{:S(2)}, u32[]{:S(2)}) %collective-permute-start.5) | collective-permute-done | bytes 65568 | tf_op jit(solution)/shard_map/ppermute | solution.py:47
  33.5 2.9 %collective-permute-start.6 = (bf16[64,256]{1,0:T(8,128)(2,1)S(1)}, bf16[64,256]{1,0:T(8,128)(2,1)S(1)}, u32[]{:S(2)}, u32[]{:S(2)}) collective-permute-start(bf16[64,256]{1,0:T(8,128)(2,1)S(1)} %add_convert_fusion.2), channel_id=1, source_target_pairs={{0,16},{2,18},{4,20},{6,22},{8,24},{10,26},{12,28},{14,30},{16,0},... | collective-permute-start | bytes 98312 | tf_op jit(solution)/shard_map/ppermute | solution.py:57
  36.7 1.8 %collective-permute-done.6 = bf16[64,256]{1,0:T(8,128)(2,1)S(1)} collective-permute-done((bf16[64,256]{1,0:T(8,128)(2,1)S(1)}, bf16[64,256]{1,0:T(8,128)(2,1)S(1)}, u32[]{:S(2)}, u32[]{:S(2)}) %collective-permute-start.6) | collective-permute-done | bytes 32800 | tf_op jit(solution)/shard_map/ppermute | solution.py:57
  38.5 2.3 %collective-permute-start.7 = (bf16[128,256]{1,0:T(8,128)(2,1)S(1)}, bf16[128,256]{1,0:T(8,128)(2,1)S(1)}, u32[]{:S(2)}, u32[]{:S(2)}) collective-permute-start(bf16[128,256]{1,0:T(8,128)(2,1)S(1)} %maximum_select_fusion.4), channel_id=1, source_target_pairs={{0,8},{2,10},{4,12},{6,14},{8,0},{10,2},{12,4},{14,6},{16,24},{18,... | collective-permute-start | bytes 196616 | tf_op jit(solution)/shard_map/ppermute | solution.py:57
  40.8 1.5 %collective-permute-start.10 = (f32[64,256]{1,0:T(8,128)S(1)}, f32[64,256]{1,0:T(8,128)S(1)}, u32[]{:S(2)}, u32[]{:S(2)}) collective-permute-start(f32[64,256]{1,0:T(8,128)S(1)} %constant_dynamic-slice_fusion.5), channel_id=1, source_target_pairs={{0,1},{1,0},{2,3},{3,2},{4,5},{5,4},{6,7},{7,6},{8,9},{9,8},{10,11... | collective-permute-start | bytes 196616 | tf_op jit(solution)/shard_map/ppermute | solution.py:47
  43.0 1.6 %collective-permute-start.8 = (bf16[256,256]{1,0:T(8,128)(2,1)S(1)}, bf16[256,256]{1,0:T(8,128)(2,1)S(1)}, u32[]{:S(2)}, u32[]{:S(2)}) collective-permute-start(bf16[256,256]{1,0:T(8,128)(2,1)S(1)} %maximum_select_fusion.3), channel_id=1, source_target_pairs={{0,4},{2,6},{4,0},{6,2},{8,12},{10,14},{12,8},{14,10},{16,20},{18,... | collective-permute-start | bytes 393224 | tf_op jit(solution)/shard_map/ppermute | solution.py:57
  44.6 5.4 %collective-permute-done = f32[1024,256]{1,0:T(8,128)} collective-permute-done((f32[1024,256]{1,0:T(8,128)S(1)}, f32[1024,256]{1,0:T(8,128)}, u32[]{:S(2)}, u32[]{:S(2)}) %collective-permute-start) | collective-permute-done | bytes 1048608 | tf_op jit(solution)/shard_map/ppermute | solution.py:47
  50.0 1.7 %add_convert_fusion = bf16[1024,256]{1,0:T(8,128)(2,1)S(1)} fusion(f32[1024,256]{1,0:T(8,128)} %collective-permute-done, f32[2048,256]{1,0:T(8,128)} %copy-done.4, s32[]{:T(128)S(6)} %select_n.88, bf16[2048,256]{1,0:T(8,128)(2,1)S(1)} %copy-done.3), kind=kLoop, calls=%fused_computation.7 | loop fusion | flops 1310720 | bytes 3145732 | tf_op jit(solution)/shard_map/convert_element_type | solution.py:32
  51.7 1.6 %collective-permute-start.1 = (bf16[1024,256]{1,0:T(8,128)(2,1)S(1)}, bf16[1024,256]{1,0:T(8,128)(2,1)S(1)}, u32[]{:S(2)}, u32[]{:S(2)}) collective-permute-start(bf16[1024,256]{1,0:T(8,128)(2,1)S(1)} %add_convert_fusion), channel_id=1, source_target_pairs={{0,1},{1,0},{2,3},{3,2},{4,5},{5,4},{6,7},{7,6},{8,9},{9,8},{10,11... | collective-permute-start | bytes 1572872 | tf_op jit(solution)/shard_map/ppermute | solution.py:57
  54.1 9.6 %collective-permute-done.11 = bf16[64,256]{1,0:T(8,128)(2,1)S(1)} collective-permute-done((bf16[64,256]{1,0:T(8,128)(2,1)S(1)}, bf16[64,256]{1,0:T(8,128)(2,1)S(1)}, u32[]{:S(2)}, u32[]{:S(2)}) %collective-permute-start.11) | collective-permute-done | bytes 32800 | tf_op jit(solution)/shard_map/ppermute | solution.py:57
  64.4 1.0 %maximum_select_fusion.1 = bf16[1024,256]{1,0:T(8,128)(2,1)} fusion(bf16[512,256]{1,0:T(8,128)(2,1)S(1)} %collective-permute-done.9, bf16[512,256]{1,0:T(8,128)(2,1)S(1)} %maximum_select_fusion.2, pred[]{:T(512)S(6)} %eq.17), kind=kLoop, calls=%fused_computation.8 | loop fusion | flops 2359296 | bytes 1048577 | tf_op jit(solution)/shard_map/jit(_where)/select_n | solution.py:59
  65.4 1.2 %maximum_select_fusion = bf16[2048,256]{1,0:T(8,128)(2,1)} fusion(bf16[1024,256]{1,0:T(8,128)(2,1)S(1)} %collective-permute-done.1, bf16[1024,256]{1,0:T(8,128)(2,1)S(1)} %add_convert_fusion, pred[]{:T(512)S(6)} %eq.16), kind=kLoop, calls=%fused_computation.6 | loop fusion | flops 4718592 | bytes 2097153 | tf_op jit(solution)/shard_map/jit(_where)/select_n | solution.py:59
  (45 shorter events, 6.5 us)
Async XLA Ops:
  1.4 1.0 %copy-start = (bf16[1024,256]{1,0:T(8,128)(2,1)S(1)}, bf16[1024,256]{1,0:T(8,128)(2,1)}, u32[]{:S(2)}) copy-start(bf16[1024,256]{1,0:T(8,128)(2,1)} %param.8) | copy-start | bytes 1572868
  1.4 2.4 %copy-start.1 = (bf16[2048,1024]{1,0:T(8,128)(2,1)S(1)}, bf16[2048,1024]{1,0:T(8,128)(2,1)}, u32[]{:S(2)}) copy-start(bf16[2048,1024]{1,0:T(8,128)(2,1)} %param.10) | copy-start | bytes 12582916
  1.4 2.6 %copy-start.3 = (bf16[2048,256]{1,0:T(8,128)(2,1)S(1)}, bf16[2048,256]{1,0:T(8,128)(2,1)}, u32[]{:S(2)}) copy-start(bf16[2048,256]{1,0:T(8,128)(2,1)} %param.7) | copy-start | bytes 3145732
  6.1 2.4 %copy-start.2 = (bf16[2048,1024]{1,0:T(8,128)(2,1)}, bf16[2048,1024]{1,0:T(8,128)(2,1)S(1)}, u32[]{:S(2)}) copy-start(bf16[2048,1024]{1,0:T(8,128)(2,1)S(1)} %fusion) | copy-start | bytes 12582916
  6.1 2.3 %copy-start.7 = (s32[8,1]{0,1:T(1,128)S(1)}, s32[8,1]{0,1:T(1,128)}, u32[]{:S(2)}) copy-start(s32[8,1]{0,1:T(1,128)} %param.13) | copy-start | bytes 100
  6.1 2.4 %copy-start.5 = (bf16[128,256]{1,0:T(8,128)(2,1)S(1)}, bf16[128,256]{1,0:T(8,128)(2,1)}, u32[]{:S(2)}) copy-start(bf16[128,256]{1,0:T(8,128)(2,1)} %param.9) | copy-start | bytes 196612
  6.1 2.4 %copy-start.6 = (bf16[1024,128]{1,0:T(8,128)(2,1)S(1)}, bf16[1024,128]{1,0:T(8,128)(2,1)}, u32[]{:S(2)}) copy-start(bf16[1024,128]{1,0:T(8,128)(2,1)} %param.12) | copy-start | bytes 786436
  11.2 2.2 %collective-permute-start.2 = (f32[512,256]{1,0:T(8,128)}, f32[512,256]{1,0:T(8,128)S(1)}, u32[]{:S(2)}, u32[]{:S(2)}) collective-permute-start(f32[512,256]{1,0:T(8,128)} %constant_dynamic-slice_fusion.3), channel_id=1, source_target_pairs={{0,2},{2,0},{4,6},{6,4},{8,10},{10,8},{12,14},{14,12},{16,18},{18,... | collective-permute-start | bytes 1572872 | tf_op jit(solution)/shard_map/ppermute | solution.py:47
  13.5 9.5 %collective-permute-start.3 = (f32[256,256]{1,0:T(8,128)S(1)}, f32[256,256]{1,0:T(8,128)S(1)}, u32[]{:S(2)}, u32[]{:S(2)}) collective-permute-start(f32[256,256]{1,0:T(8,128)S(1)} %constant_dynamic-slice_fusion.2), channel_id=1, source_target_pairs={{0,4},{2,6},{4,0},{6,2},{8,12},{10,14},{12,8},{14,10},{16,20},{18,... | collective-permute-start | bytes 786440 | tf_op jit(solution)/shard_map/ppermute | solution.py:47
  19.9 5.1 %copy-start.4 = (f32[2048,256]{1,0:T(8,128)}, f32[2048,256]{1,0:T(8,128)S(1)}, u32[]{:S(2)}) copy-start(f32[2048,256]{1,0:T(8,128)S(1)} %fusion.3) | copy-start | bytes 6291460
  23.1 5.1 %collective-permute-start.4 = (f32[128,256]{1,0:T(8,128)S(1)}, f32[128,256]{1,0:T(8,128)S(1)}, u32[]{:S(2)}, u32[]{:S(2)}) collective-permute-start(f32[128,256]{1,0:T(8,128)S(1)} %constant_dynamic-slice_fusion.1), channel_id=1, source_target_pairs={{0,8},{2,10},{4,12},{6,14},{8,0},{10,2},{12,4},{14,6},{16,24},{18,... | collective-permute-start | bytes 393224 | tf_op jit(solution)/shard_map/ppermute | solution.py:47
  25.1 25.0 %collective-permute-start = (f32[1024,256]{1,0:T(8,128)S(1)}, f32[1024,256]{1,0:T(8,128)}, u32[]{:S(2)}, u32[]{:S(2)}) collective-permute-start(f32[1024,256]{1,0:T(8,128)S(1)} %constant_dynamic-slice_fusion.4), channel_id=1, source_target_pairs={{0,1},{1,0},{2,3},{3,2},{4,5},{5,4},{6,7},{7,6},{8,9},{9,8},{10,11... | collective-permute-start | bytes 3145736 | tf_op jit(solution)/shard_map/ppermute | solution.py:47
  28.2 5.2 %collective-permute-start.5 = (f32[64,256]{1,0:T(8,128)S(1)}, f32[64,256]{1,0:T(8,128)S(1)}, u32[]{:S(2)}, u32[]{:S(2)}) collective-permute-start(f32[64,256]{1,0:T(8,128)S(1)} %constant_dynamic-slice_fusion), channel_id=1, source_target_pairs={{0,16},{2,18},{4,20},{6,22},{8,24},{10,26},{12,28},{14,30},{16,0},... | collective-permute-start | bytes 196616 | tf_op jit(solution)/shard_map/ppermute | solution.py:47
  33.5 5.0 %collective-permute-start.6 = (bf16[64,256]{1,0:T(8,128)(2,1)S(1)}, bf16[64,256]{1,0:T(8,128)(2,1)S(1)}, u32[]{:S(2)}, u32[]{:S(2)}) collective-permute-start(bf16[64,256]{1,0:T(8,128)(2,1)S(1)} %add_convert_fusion.2), channel_id=1, source_target_pairs={{0,16},{2,18},{4,20},{6,22},{8,24},{10,26},{12,28},{14,30},{16,0},... | collective-permute-start | bytes 98312 | tf_op jit(solution)/shard_map/ppermute | solution.py:57
  38.5 4.5 %collective-permute-start.7 = (bf16[128,256]{1,0:T(8,128)(2,1)S(1)}, bf16[128,256]{1,0:T(8,128)(2,1)S(1)}, u32[]{:S(2)}, u32[]{:S(2)}) collective-permute-start(bf16[128,256]{1,0:T(8,128)(2,1)S(1)} %maximum_select_fusion.4), channel_id=1, source_target_pairs={{0,8},{2,10},{4,12},{6,14},{8,0},{10,2},{12,4},{14,6},{16,24},{18,... | collective-permute-start | bytes 196616 | tf_op jit(solution)/shard_map/ppermute | solution.py:57
  40.8 12.8 %collective-permute-start.10 = (f32[64,256]{1,0:T(8,128)S(1)}, f32[64,256]{1,0:T(8,128)S(1)}, u32[]{:S(2)}, u32[]{:S(2)}) collective-permute-start(f32[64,256]{1,0:T(8,128)S(1)} %constant_dynamic-slice_fusion.5), channel_id=1, source_target_pairs={{0,1},{1,0},{2,3},{3,2},{4,5},{5,4},{6,7},{7,6},{8,9},{9,8},{10,11... | collective-permute-start | bytes 196616 | tf_op jit(solution)/shard_map/ppermute | solution.py:47
  43.0 10.3 %collective-permute-start.8 = (bf16[256,256]{1,0:T(8,128)(2,1)S(1)}, bf16[256,256]{1,0:T(8,128)(2,1)S(1)}, u32[]{:S(2)}, u32[]{:S(2)}) collective-permute-start(bf16[256,256]{1,0:T(8,128)(2,1)S(1)} %maximum_select_fusion.3), channel_id=1, source_target_pairs={{0,4},{2,6},{4,0},{6,2},{8,12},{10,14},{12,8},{14,10},{16,20},{18,... | collective-permute-start | bytes 393224 | tf_op jit(solution)/shard_map/ppermute | solution.py:57
  51.7 13.7 %collective-permute-start.1 = (bf16[1024,256]{1,0:T(8,128)(2,1)S(1)}, bf16[1024,256]{1,0:T(8,128)(2,1)S(1)}, u32[]{:S(2)}, u32[]{:S(2)}) collective-permute-start(bf16[1024,256]{1,0:T(8,128)(2,1)S(1)} %add_convert_fusion), channel_id=1, source_target_pairs={{0,1},{1,0},{2,3},{3,2},{4,5},{5,4},{6,7},{7,6},{8,9},{9,8},{10,11... | collective-permute-start | bytes 1572872 | tf_op jit(solution)/shard_map/ppermute | solution.py:57
  53.5 10.9 %collective-permute-start.9 = (bf16[512,256]{1,0:T(8,128)(2,1)S(1)}, bf16[512,256]{1,0:T(8,128)(2,1)S(1)}, u32[]{:S(2)}, u32[]{:S(2)}) collective-permute-start(bf16[512,256]{1,0:T(8,128)(2,1)S(1)} %maximum_select_fusion.2), channel_id=1, source_target_pairs={{0,2},{2,0},{4,6},{6,4},{8,10},{10,8},{12,14},{14,12},{16,18},{18,... | collective-permute-start | bytes 786440 | tf_op jit(solution)/shard_map/ppermute | solution.py:57
  53.6 10.2 %collective-permute-start.11 = (bf16[64,256]{1,0:T(8,128)(2,1)S(1)}, bf16[64,256]{1,0:T(8,128)(2,1)S(1)}, u32[]{:S(2)}, u32[]{:S(2)}) collective-permute-start(bf16[64,256]{1,0:T(8,128)(2,1)S(1)} %add_convert_fusion.1), channel_id=1, source_target_pairs={{0,1},{1,0},{2,3},{3,2},{4,5},{5,4},{6,7},{7,6},{8,9},{9,8},{10,11... | collective-permute-start | bytes 98312 | tf_op jit(solution)/shard_map/ppermute | solution.py:57

commit v2 on v1

--- a/solution.py
+++ b/solution.py
@@ -62,6 +62,19 @@
     return parts
 
 
+def spread_scatter(part, axis, count):
+    rows = part.shape[0] // count
+    pieces = part.reshape(count, rows, part.shape[1])
+    pieces = lax.all_to_all(pieces, axis, 0, 0, tiled=False)
+    return jnp.sum(pieces, axis=0)
+
+
+def spread_gather(share, axis, count):
+    pieces = jnp.broadcast_to(share[None], (count,) + share.shape)
+    pieces = lax.all_to_all(pieces, axis, 0, 0, tiled=False)
+    return pieces.reshape(count * share.shape[0], share.shape[1])
+
+
 def shards(user_factors, item_factors, tag_factors, ratings, rating_tiles, tag_links, link_tiles):
     group_count = lax.axis_size("group")
     loop_count = lax.axis_size("loop")
@@ -72,8 +85,8 @@
     rating_errors = residual_of(ratings, user_factors, item_factors, rating_tiles)
     user_part = jnp.dot(rating_errors, item_factors, preferred_element_type=jnp.float32)
     tag_part = transposed_product(link_errors, item_factors)
-    item_part = transposed_product(rating_errors, user_factors) + jnp.dot(
-        link_errors, tag_factors, preferred_element_type=jnp.float32
+    user_part, tag_part, rating_errors, link_errors = lax.optimization_barrier(
+        (user_part, tag_part, rating_errors, link_errors)
     )
 
     (user_share, tag_share), (user_offset, tag_offset) = halving_scatter(
@@ -93,13 +106,17 @@
         [fresh_users, fresh_tags], "loop", loop_count, loop_position
     )
 
-    (item_share,), (item_offset,) = halving_scatter([item_part], "group", group_count, group_position)
+    item_part = transposed_product(rating_errors, user_factors) + jnp.dot(
+        link_errors, tag_factors, preferred_element_type=jnp.float32
+    )
+    item_share = spread_scatter(item_part, "group", group_count)
+    share_rows = item_share.shape[0]
     fresh_items = advance(
-        lax.dynamic_slice_in_dim(item_factors, item_offset, item_share.shape[0], 0),
+        lax.dynamic_slice_in_dim(item_factors, group_position * share_rows, share_rows, 0),
         item_share,
         step_items,
     )
-    (new_items,) = doubling_gather([fresh_items], "group", group_count, group_position)
+    new_items = spread_gather(fresh_items, "group", group_count)
     return (new_users, new_items, new_tags)
 
 

time: 66.9 us -> 74.7 us (1.12)
  waiting for transfers between devices: 26.4 us -> 35.2 us
  local copies, waits for them, and re-layouts: 3.79 us -> 6.72 us
  matrix products: 9.87 us -> 7.81 us
  other arithmetic: 5.6 us -> 4.38 us
  starting transfers between devices: 20.2 us -> 19.4 us
    all_to_all x0 -> x2, waiting for transfers between devices: none -> 19.2 us  [the longest x1 19.2 us: spread_scatter(): pieces = lax.all_to_all(pieces, axis, 0, 0, tiled=False)]
    all_to_all x0 -> x2, starting transfers between devices: none -> 14.2 us  [the longest x1 7.36 us: spread_scatter(): pieces = lax.all_to_all(pieces, axis, 0, 0, tiled=False)]
    ppermute x6 -> x2, waiting for transfers between devices: 12.1 us -> 2.4 us  [doubling_gather(): got = lax.ppermute(tuple(parts), axis, xor_pairs(count, bit))]
    ppermute x6 -> x2, starting transfers between devices: 11.2 us -> 2.03 us  [halving_scatter(): got = lax.ppermute(tuple(sent), axis, xor_pairs(count, bit))]
    ppermute x6 -> x2, starting transfers between devices: 8.97 us -> 3.17 us  [doubling_gather(): got = lax.ppermute(tuple(parts), axis, xor_pairs(count, bit))]
    dynamic_slice x6 -> x2, local copies, waits for them, and re-layouts: 0.97 us -> 2.27 us  [halving_scatter(): lax.dynamic_slice_in_dim(p, (1 - side) * h, h, 0)]
    select_n x6 -> x2, other arithmetic: 3.03 us -> 1.85 us  [doubling_gather(): jnp.where(side == 0, jnp.concatenate([m, g], 0), jnp.concatenate([g, m], 0))]
    dot_general x2, matrix products: 2.57 us -> 1.57 us  [transposed_product(): lax.dot_general(first_operand, second_operand, (((0,), (0,)), ((), ())),...]
  transfers between devices with their start and end apart: 12 -> 6, of which waited for: 8 -> 3; matrix products, arithmetic and copies ran while one was open for 11% -> 9% of each run, Pallas kernels for 0% -> 0%
where the time goes in v2:
time: 74.7 us; the launch traced here: 74.3 us
  waiting for transfers between devices  35.2 us (47%)
  starting transfers between devices  19.4 us (26%)
  matrix products  7.81 us (10%)
  local copies, waits for them, and re-layouts  6.72 us (9%)
  other arithmetic  4.38 us (6%)
  between operations  0.75 us (1%)
    all_to_all x1, waiting for transfers between devices, spread_scatter(): pieces = lax.all_to_all(pieces, axis, 0, 0, tiled=False)  19.2 us
    ppermute x2, waiting for transfers between devices, halving_scatter(): got = lax.ppermute(tuple(sent), axis, xor_pairs(count, bit))  13.6 us
    all_to_all x1, starting transfers between devices, spread_scatter(): pieces = lax.all_to_all(pieces, axis, 0, 0, tiled=False)  7.36 us
    all_to_all x1, starting transfers between devices, spread_gather(): pieces = lax.all_to_all(pieces, axis, 0, 0, tiled=False)  6.86 us
    ppermute x2, starting transfers between devices, doubling_gather(): got = lax.ppermute(tuple(parts), axis, xor_pairs(count, bit))  3.17 us
    unnamed x13, local copies, waits for them, and re-layouts  2.85 us
    dot_general x1, matrix products, shards(): jnp.dot(rating_errors, item_factors, preferred_element_type=jnp.float32)  2.61 us
    ppermute x2, waiting for transfers between devices, doubling_gather(): got = lax.ppermute(tuple(parts), axis, xor_pairs(count, bit))  2.4 us
  transfers between devices with their start and end apart: 6, of which 3 were waited for; matrix products, arithmetic and copies ran while one was open for 9% of the time, Pallas kernels for 0%

profile of v2, /device:TPU:0, one launch (start us, length us, event | category | flops | bytes accessed | tf_op | source)
XLA Modules:
  0.0 74.3 jit_solution(15578925380956724546)
XLA Ops:
  0.6 0.7 convert_element_type.38
  1.4 0.6 mul.64
  2.0 0.4 copy-done
  2.4 1.3 %copy-done.1 = bf16[2048,1024]{1,0:T(8,128)(2,1)S(1)} copy-done((bf16[2048,1024]{1,0:T(8,128)(2,1)S(1)}, bf16[2048,1024]{1,0:T(8,128)(2,1)}, u32[]{:S(2)}) %copy-start.1) | copy-done | bytes 4194328
  4.0 2.0 %fusion = bf16[2048,1024]{1,0:T(8,128)(2,1)S(1)} fusion(f32[256,8,8,128]{3,2,1,0:T(8,128)S(1)} %bitcast.24, bf16[2048,1024]{1,0:T(8,128)(2,1)S(1)} %copy-done.1, bf16[2048,256]{1,0:T(8,128)(2,1)S(1)} %copy-done.2, bf16[1024,256]{1,0:T(8,128)(2,1)S(1)} %copy-done), kind=kOutput, calls=%fused_computation.1 | convolution fusion | flops 1082130432 | bytes 18350080 | tf_op jit(solution)/shard_map/dot_general | solution.py:19
  6.1 2.6 %fusion.3 = f32[2048,256]{1,0:T(8,128)} fusion(bf16[2048,1024]{1,0:T(8,128)(2,1)S(1)} %fusion, bf16[1024,256]{1,0:T(8,128)(2,1)S(1)} %copy-done), kind=kOutput, calls=%fused_computation.15 | convolution fusion | flops 1073741824 | bytes 6815744 | tf_op jit(solution)/shard_map/dot_general | solution.py:86
  8.8 0.3 fusion.2
  9.4 1.3 %fusion.5 = f32[1024,256]{1,0:T(8,128)S(1)} fusion(bf16[2048,1024]{1,0:T(8,128)(2,1)S(1)} %fusion, bf16[2048,256]{1,0:T(8,128)(2,1)S(1)} %copy-done.2), kind=kOutput, calls=%fused_computation.17 | convolution fusion | flops 1073741824 | bytes 6291456 | tf_op jit(solution)/shard_map/dot_general | solution.py:26
  10.7 1.3 %convolution_add_fusion = f32[1024,256]{1,0:T(8,128)} fusion(f32[1024,256]{1,0:T(8,128)S(1)} %fusion.5, bf16[1024,128]{1,0:T(8,128)(2,1)S(1)} %fusion.2, bf16[128,256]{1,0:T(8,128)(2,1)S(1)} %copy-done.3), kind=kOutput, calls=%fused_computation.2 | convolution fusion | flops 67371008 | bytes 2424832 | tf_op jit(solution)/shard_map/dot_general | solution.py:109
  12.0 7.4 %all-to-all-start = ((f32[16,64,256]{2,1,0:T(8,128)}), f32[16,64,256]{2,1,0:T(8,128)S(1)}, u32[]{:S(2)}, u32[]{:S(2)}) async-start(f32[16,64,256]{2,1,0:T(8,128)} %bitcast.2), calls=%async_computation | async-start | bytes 2097152 | tf_op jit(solution)/shard_map/all_to_all | solution.py:68
  19.4 2.3 %constant_dynamic-slice_fusion = f32[1024,256]{1,0:T(8,128)} fusion(f32[2048,256]{1,0:T(8,128)} %fusion.3, s32[]{:T(128)S(6)} %select_n.35), kind=kLoop, calls=%fused_computation.12 | loop fusion | bytes 2097156 | tf_op jit(solution)/shard_map/dynamic_slice | solution.py:46
  21.7 1.5 %collective-permute-start = (f32[1024,256]{1,0:T(8,128)}, f32[1024,256]{1,0:T(8,128)}, u32[]{:S(2)}, u32[]{:S(2)}) collective-permute-start(f32[1024,256]{1,0:T(8,128)} %constant_dynamic-slice_fusion), channel_id=1, source_target_pairs={{0,1},{1,0},{2,3},{3,2},{4,5},{5,4},{6,7},{7,6},{8,9},{9,8},{10,11... | collective-permute-start | bytes 3145736 | tf_op jit(solution)/shard_map/ppermute | solution.py:47
  23.2 19.2 %all-to-all-done = f32[16,64,256]{2,1,0:T(8,128)S(1)} async-done(((f32[16,64,256]{2,1,0:T(8,128)}), f32[16,64,256]{2,1,0:T(8,128)S(1)}, u32[]{:S(2)}, u32[]{:S(2)}) %all-to-all-start) | async-done | bytes 1048608 | tf_op jit(solution)/shard_map/all_to_all | solution.py:68
  42.4 0.8 %broadcast_in_dim.2 = bf16[16,64,256]{2,1,0:T(8,128)(2,1)} broadcast(bf16[64,256]{1,0:T(8,128)(2,1)S(1)} %add_convert_fusion.2), dimensions={1,2} | broadcast | bytes 557056 | tf_op jit(solution)/shard_map/broadcast_in_dim | solution.py:73
  43.3 6.9 %all-to-all-start.1 = ((bf16[16,64,256]{2,1,0:T(8,128)(2,1)}), bf16[16,64,256]{2,1,0:T(8,128)(2,1)S(1)}, u32[]{:S(2)}, u32[]{:S(2)}) async-start(bf16[16,64,256]{2,1,0:T(8,128)(2,1)} %broadcast_in_dim.2), calls=%async_computation.1 | async-start | bytes 1048576 | tf_op jit(solution)/shard_map/all_to_all | solution.py:74
  50.1 1.7 %add_convert_fusion = bf16[1024,256]{1,0:T(8,128)(2,1)S(1)} fusion(f32[1024,256]{1,0:T(8,128)} %collective-permute-done, f32[2048,256]{1,0:T(8,128)} %fusion.3, s32[]{:T(128)S(6)} %select_n.34, bf16[2048,256]{1,0:T(8,128)(2,1)S(1)} %copy-done.2), kind=kLoop, calls=%fused_computation.7 | loop fusion | flops 1310720 | bytes 3145732 | tf_op jit(solution)/shard_map/convert_element_type | solution.py:32
  51.9 1.6 %collective-permute-start.1 = (bf16[1024,256]{1,0:T(8,128)(2,1)S(1)}, bf16[1024,256]{1,0:T(8,128)(2,1)S(1)}, u32[]{:S(2)}, u32[]{:S(2)}) collective-permute-start(bf16[1024,256]{1,0:T(8,128)(2,1)S(1)} %add_convert_fusion), channel_id=1, source_target_pairs={{0,1},{1,0},{2,3},{3,2},{4,5},{5,4},{6,7},{7,6},{8,9},{9,8},{10,11... | collective-permute-start | bytes 1572872 | tf_op jit(solution)/shard_map/ppermute | solution.py:57
  53.5 0.5 collective-permute-start.2
  54.0 13.6 %collective-permute-done.2 = f32[64,256]{1,0:T(8,128)S(1)} collective-permute-done((f32[64,256]{1,0:T(8,128)S(1)}, f32[64,256]{1,0:T(8,128)S(1)}, u32[]{:S(2)}, u32[]{:S(2)}) %collective-permute-start.2) | collective-permute-done | bytes 65568 | tf_op jit(solution)/shard_map/ppermute | solution.py:47
  67.6 1.6 %collective-permute-start.3 = (bf16[64,256]{1,0:T(8,128)(2,1)S(1)}, bf16[64,256]{1,0:T(8,128)(2,1)S(1)}, u32[]{:S(2)}, u32[]{:S(2)}) collective-permute-start(bf16[64,256]{1,0:T(8,128)(2,1)S(1)} %add_convert_fusion.1), channel_id=1, source_target_pairs={{0,1},{1,0},{2,3},{3,2},{4,5},{5,4},{6,7},{7,6},{8,9},{9,8},{10,11... | collective-permute-start | bytes 98312 | tf_op jit(solution)/shard_map/ppermute | solution.py:57
  69.2 2.4 %collective-permute-done.3 = bf16[64,256]{1,0:T(8,128)(2,1)S(1)} collective-permute-done((bf16[64,256]{1,0:T(8,128)(2,1)S(1)}, bf16[64,256]{1,0:T(8,128)(2,1)S(1)}, u32[]{:S(2)}, u32[]{:S(2)}) %collective-permute-start.3) | collective-permute-done | bytes 32800 | tf_op jit(solution)/shard_map/ppermute | solution.py:57
  71.6 0.6 maximum_select_fusion.1
  72.3 1.2 %maximum_select_fusion = bf16[2048,256]{1,0:T(8,128)(2,1)} fusion(bf16[1024,256]{1,0:T(8,128)(2,1)S(1)} %collective-permute-done.1, bf16[1024,256]{1,0:T(8,128)(2,1)S(1)} %add_convert_fusion, pred[]{:T(512)S(6)} %eq.4), kind=kLoop, calls=%fused_computation.6 | loop fusion | flops 4718592 | bytes 2097153 | tf_op jit(solution)/shard_map/jit(_where)/select_n | solution.py:59
  73.5 0.8 %copy.14 = bf16[1024,256]{1,0:T(8,128)(2,1)} copy(bf16[1024,256]{1,0:T(8,128)(2,1)S(1)} %bitcast.25) | data formatting | bytes 1048576
  (21 shorter events, 0.9 us)
Async XLA Ops:
  1.4 1.0 %copy-start = (bf16[1024,256]{1,0:T(8,128)(2,1)S(1)}, bf16[1024,256]{1,0:T(8,128)(2,1)}, u32[]{:S(2)}) copy-start(bf16[1024,256]{1,0:T(8,128)(2,1)} %param.8) | copy-start | bytes 1572868
  1.4 2.4 %copy-start.1 = (bf16[2048,1024]{1,0:T(8,128)(2,1)S(1)}, bf16[2048,1024]{1,0:T(8,128)(2,1)}, u32[]{:S(2)}) copy-start(bf16[2048,1024]{1,0:T(8,128)(2,1)} %param.10) | copy-start | bytes 12582916
  1.4 2.6 %copy-start.2 = (bf16[2048,256]{1,0:T(8,128)(2,1)S(1)}, bf16[2048,256]{1,0:T(8,128)(2,1)}, u32[]{:S(2)}) copy-start(bf16[2048,256]{1,0:T(8,128)(2,1)} %param.7) | copy-start | bytes 3145732
  6.1 2.7 %copy-start.5 = (s32[8,1]{0,1:T(1,128)S(1)}, s32[8,1]{0,1:T(1,128)}, u32[]{:S(2)}) copy-start(s32[8,1]{0,1:T(1,128)} %param.13) | copy-start | bytes 100
  6.1 2.7 %copy-start.3 = (bf16[128,256]{1,0:T(8,128)(2,1)S(1)}, bf16[128,256]{1,0:T(8,128)(2,1)}, u32[]{:S(2)}) copy-start(bf16[128,256]{1,0:T(8,128)(2,1)} %param.9) | copy-start | bytes 196612
  6.1 2.7 %copy-start.4 = (bf16[1024,128]{1,0:T(8,128)(2,1)S(1)}, bf16[1024,128]{1,0:T(8,128)(2,1)}, u32[]{:S(2)}) copy-start(bf16[1024,128]{1,0:T(8,128)(2,1)} %param.12) | copy-start | bytes 786436
  12.0 30.3 %all-to-all-start = ((f32[16,64,256]{2,1,0:T(8,128)}), f32[16,64,256]{2,1,0:T(8,128)S(1)}, u32[]{:S(2)}, u32[]{:S(2)}) async-start(f32[16,64,256]{2,1,0:T(8,128)} %bitcast.2), calls=%async_computation | async-start | bytes 2097152 | tf_op jit(solution)/shard_map/all_to_all | solution.py:68
  21.7 28.5 %collective-permute-start = (f32[1024,256]{1,0:T(8,128)}, f32[1024,256]{1,0:T(8,128)}, u32[]{:S(2)}, u32[]{:S(2)}) collective-permute-start(f32[1024,256]{1,0:T(8,128)} %constant_dynamic-slice_fusion), channel_id=1, source_target_pairs={{0,1},{1,0},{2,3},{3,2},{4,5},{5,4},{6,7},{7,6},{8,9},{9,8},{10,11... | collective-permute-start | bytes 3145736 | tf_op jit(solution)/shard_map/ppermute | solution.py:47
  43.3 30.2 %all-to-all-start.1 = ((bf16[16,64,256]{2,1,0:T(8,128)(2,1)}), bf16[16,64,256]{2,1,0:T(8,128)(2,1)S(1)}, u32[]{:S(2)}, u32[]{:S(2)}) async-start(bf16[16,64,256]{2,1,0:T(8,128)(2,1)} %broadcast_in_dim.2), calls=%async_computation.1 | async-start | bytes 1048576 | tf_op jit(solution)/shard_map/all_to_all | solution.py:74
  51.9 20.4 %collective-permute-start.1 = (bf16[1024,256]{1,0:T(8,128)(2,1)S(1)}, bf16[1024,256]{1,0:T(8,128)(2,1)S(1)}, u32[]{:S(2)}, u32[]{:S(2)}) collective-permute-start(bf16[1024,256]{1,0:T(8,128)(2,1)S(1)} %add_convert_fusion), channel_id=1, source_target_pairs={{0,1},{1,0},{2,3},{3,2},{4,5},{5,4},{6,7},{7,6},{8,9},{9,8},{10,11... | collective-permute-start | bytes 1572872 | tf_op jit(solution)/shard_map/ppermute | solution.py:57
  53.5 14.1 %collective-permute-start.2 = (f32[64,256]{1,0:T(8,128)S(1)}, f32[64,256]{1,0:T(8,128)S(1)}, u32[]{:S(2)}, u32[]{:S(2)}) collective-permute-start(f32[64,256]{1,0:T(8,128)S(1)} %constant_dynamic-slice_fusion.1), channel_id=1, source_target_pairs={{0,1},{1,0},{2,3},{3,2},{4,5},{5,4},{6,7},{7,6},{8,9},{9,8},{10,11... | collective-permute-start | bytes 196616 | tf_op jit(solution)/shard_map/ppermute | solution.py:47
  67.6 4.0 %collective-permute-start.3 = (bf16[64,256]{1,0:T(8,128)(2,1)S(1)}, bf16[64,256]{1,0:T(8,128)(2,1)S(1)}, u32[]{:S(2)}, u32[]{:S(2)}) collective-permute-start(bf16[64,256]{1,0:T(8,128)(2,1)S(1)} %add_convert_fusion.1), channel_id=1, source_target_pairs={{0,1},{1,0},{2,3},{3,2},{4,5},{5,4},{6,7},{7,6},{8,9},{9,8},{10,11... | collective-permute-start | bytes 98312 | tf_op jit(solution)/shard_map/ppermute | solution.py:57

commit v3 on v1

--- a/solution.py
+++ b/solution.py
@@ -72,26 +72,30 @@
     rating_errors = residual_of(ratings, user_factors, item_factors, rating_tiles)
     user_part = jnp.dot(rating_errors, item_factors, preferred_element_type=jnp.float32)
     tag_part = transposed_product(link_errors, item_factors)
+    joint_part = jnp.concatenate([user_part, tag_part], 0)
+
+    joint_part, rating_errors, link_errors = lax.optimization_barrier(
+        (joint_part, rating_errors, link_errors)
+    )
+    (joint_share,), (joint_offset,) = halving_scatter(
+        [joint_part], "loop", loop_count, loop_position
+    )
     item_part = transposed_product(rating_errors, user_factors) + jnp.dot(
         link_errors, tag_factors, preferred_element_type=jnp.float32
     )
-
-    (user_share, tag_share), (user_offset, tag_offset) = halving_scatter(
-        [user_part, tag_part], "loop", loop_count, loop_position
+    joint_factors = jnp.concatenate([user_factors, tag_factors], 0)
+    fresh_joint = advance(
+        lax.dynamic_slice_in_dim(joint_factors, joint_offset, joint_share.shape[0], 0),
+        joint_share,
+        jnp.where(
+            joint_offset + jnp.arange(joint_share.shape[0])[:, None] < user_factors.shape[0],
+            step_users,
+            step_tags,
+        ),
     )
-    fresh_users = advance(
-        lax.dynamic_slice_in_dim(user_factors, user_offset, user_share.shape[0], 0),
-        user_share,
-        step_users,
-    )
-    fresh_tags = advance(
-        lax.dynamic_slice_in_dim(tag_factors, tag_offset, tag_share.shape[0], 0),
-        tag_share,
-        step_tags,
-    )
-    new_users, new_tags = doubling_gather(
-        [fresh_users, fresh_tags], "loop", loop_count, loop_position
-    )
+    (new_joint,) = doubling_gather([fresh_joint], "loop", loop_count, loop_position)
+    new_users = new_joint[: user_factors.shape[0]]
+    new_tags = new_joint[user_factors.shape[0] :]
 
     (item_share,), (item_offset,) = halving_scatter([item_part], "group", group_count, group_position)
     fresh_items = advance(

time: 66.9 us -> 64.7 us (0.967)
  local copies, waits for them, and re-layouts: 3.79 us -> 6.65 us
  matrix products: 9.87 us -> 7.55 us
  starting transfers between devices: 20.2 us -> 17.9 us
  waiting for transfers between devices: 26.4 us -> 25.2 us
  other arithmetic: 5.6 us -> 6.3 us
    ppermute x6 -> x5, waiting for transfers between devices: 14.2 us -> 11.4 us  [halving_scatter(): got = lax.ppermute(tuple(sent), axis, xor_pairs(count, bit))]
    dot_general x1, matrix products: 3.46 us -> 1.28 us  [shards(): jnp.dot(rating_errors, item_factors, preferred_element_type=jnp.float32)]
    add x3, other arithmetic: 0.12 us -> 2.27 us  [halving_scatter(): parts = [k + g for k, g in zip(kept, got)]]
    slice x0 -> x2, local copies, waits for them, and re-layouts: none -> 1.67 us  [the longest x1 1.04 us: shards(): new_users = new_joint[:user_factors.shape[0]]]
    ppermute x6 -> x5, waiting for transfers between devices: 12.1 us -> 13.8 us  [doubling_gather(): got = lax.ppermute(tuple(parts), axis, xor_pairs(count, bit))]
    select_n x6 -> x5, other arithmetic: 3.03 us -> 1.42 us  [doubling_gather(): jnp.where(side == 0, jnp.concatenate([m, g], 0), jnp.concatenate([g, m], 0))]
    ppermute x6 -> x5, starting transfers between devices: 11.2 us -> 9.65 us  [halving_scatter(): got = lax.ppermute(tuple(sent), axis, xor_pairs(count, bit))]
    unnamed x16 -> x14, local copies, waits for them, and re-layouts: 2.07 us -> 3.05 us
  transfers between devices with their start and end apart: 12 -> 10, of which waited for: 8 -> 8; matrix products, arithmetic and copies ran while one was open for 11% -> 8% of each run, Pallas kernels for 0% -> 0%
where the time goes in v3:
time: 64.7 us; the launch traced here: 64.4 us
  waiting for transfers between devices  25.2 us (39%)
  starting transfers between devices  17.9 us (28%)
  matrix products  7.55 us (12%)
  local copies, waits for them, and re-layouts  6.65 us (10%)
  other arithmetic  6.3 us (10%)
  between operations  0.83 us (1%)
    ppermute x5, waiting for transfers between devices, doubling_gather(): got = lax.ppermute(tuple(parts), axis, xor_pairs(count, bit))  13.8 us
    ppermute x5, waiting for transfers between devices, halving_scatter(): got = lax.ppermute(tuple(sent), axis, xor_pairs(count, bit))  11.4 us
    ppermute x5, starting transfers between devices, halving_scatter(): got = lax.ppermute(tuple(sent), axis, xor_pairs(count, bit))  9.65 us
    ppermute x5, starting transfers between devices, doubling_gather(): got = lax.ppermute(tuple(parts), axis, xor_pairs(count, bit))  8.21 us
    unnamed x14, local copies, waits for them, and re-layouts  3.05 us
    dot_general x2, matrix products, transposed_product(): lax.dot_general(first_operand, second_operand, (((0,), (0,)), ((), ())),...  2.52 us
    add x3, other arithmetic, halving_scatter(): parts = [k + g for k, g in zip(kept, got)]  2.27 us
    dot_general x2, matrix products, residual_of(): lax.dot_general(row_factors, column_factors, (((1,), (1,)), ((), ())), pr...  2.26 us
  transfers between devices with their start and end apart: 10, of which 8 were waited for; matrix products, arithmetic and copies ran while one was open for 8% of the time, Pallas kernels for 0%

profile of v3, /device:TPU:0, one launch (start us, length us, event | category | flops | bytes accessed | tf_op | source)
XLA Modules:
  0.0 64.4 jit_solution(11957146935831366107)
XLA Ops:
  2.8 1.3 %copy-done.3 = bf16[2048,1024]{1,0:T(8,128)(2,1)S(1)} copy-done((bf16[2048,1024]{1,0:T(8,128)(2,1)S(1)}, bf16[2048,1024]{1,0:T(8,128)(2,1)}, u32[]{:S(2)}) %copy-start.3) | copy-done | bytes 4194328
  4.1 1.9 %fusion = bf16[2048,1024]{1,0:T(8,128)(2,1)S(1)} fusion(f32[256,8,8,128]{3,2,1,0:T(8,128)S(1)} %bitcast.22, bf16[2048,1024]{1,0:T(8,128)(2,1)S(1)} %copy-done.3, bf16[2048,256]{1,0:T(8,128)(2,1)S(1)} %copy-done.1, bf16[1024,256]{1,0:T(8,128)(2,1)S(1)} %copy-done), kind=kOutput, calls=%fused_computation.1 | convolution fusion | flops 1082130432 | bytes 18350080 | tf_op jit(solution)/shard_map/dot_general | solution.py:19
  6.1 1.3 %fusion.4 = f32[2048,256]{1,0:T(8,128)S(1)} fusion(bf16[2048,1024]{1,0:T(8,128)(2,1)S(1)} %fusion, bf16[1024,256]{1,0:T(8,128)(2,1)S(1)} %copy-done), kind=kOutput, calls=%fused_computation.27 | convolution fusion | flops 1073741824 | bytes 6815744 | tf_op jit(solution)/shard_map/dot_general | solution.py:73
  8.2 2.2 %fusion.6 = f32[1024,256]{1,0:T(8,128)} fusion(bf16[2048,1024]{1,0:T(8,128)(2,1)S(1)} %fusion, bf16[2048,256]{1,0:T(8,128)(2,1)S(1)} %copy-done.1), kind=kOutput, calls=%fused_computation.29 | convolution fusion | flops 1073741824 | bytes 6291456 | tf_op jit(solution)/shard_map/dot_general | solution.py:26
  10.5 1.5 %convolution_add_fusion = f32[1024,256]{1,0:T(8,128)S(1)} fusion(f32[1024,256]{1,0:T(8,128)} %fusion.6, bf16[1024,128]{1,0:T(8,128)(2,1)S(1)} %fusion.2, bf16[128,256]{1,0:T(8,128)(2,1)S(1)} %copy-done.4), kind=kOutput, calls=%fused_computation.3 | convolution fusion | flops 67371008 | bytes 2424832 | tf_op jit(solution)/shard_map/dot_general | solution.py:83
  13.5 1.7 %collective-permute-done.2 = f32[512,256]{1,0:T(8,128)} collective-permute-done((f32[512,256]{1,0:T(8,128)S(1)}, f32[512,256]{1,0:T(8,128)}, u32[]{:S(2)}, u32[]{:S(2)}) %collective-permute-start.2) | collective-permute-done | bytes 524320 | tf_op jit(solution)/shard_map/ppermute | solution.py:47
  15.2 1.3 %dynamic-slice_add_fusion = f32[512,256]{1,0:T(8,128)S(1)} fusion(f32[512,256]{1,0:T(8,128)} %collective-permute-done.2, f32[1024,256]{1,0:T(8,128)} %copy-done.2, s32[]{:T(128)S(6)} %select_n.85), kind=kLoop, calls=%fused_computation.13 | loop fusion | flops 131072 | bytes 1572868 | tf_op jit(solution)/shard_map/add | solution.py:48
  16.5 2.9 %collective-permute-start.3 = (f32[256,256]{1,0:T(8,128)S(1)}, f32[256,256]{1,0:T(8,128)}, u32[]{:S(2)}, u32[]{:S(2)}) collective-permute-start(f32[256,256]{1,0:T(8,128)S(1)} %constant_dynamic-slice_fusion.1), channel_id=1, source_target_pairs={{0,4},{2,6},{4,0},{6,2},{8,12},{10,14},{12,8},{14,10},{16,20},{18,... | collective-permute-start | bytes 786440 | tf_op jit(solution)/shard_map/ppermute | solution.py:47
  19.4 1.1 %constant_dynamic-slice_fusion.3 = f32[1088,256]{1,0:T(8,128)} fusion(f32[2176,256]{1,0:T(8,128)S(1)} %pad_maximum_fusion, s32[]{:T(128)S(6)} %select_n.78), kind=kLoop, calls=%fused_computation.23 | loop fusion | bytes 2228228 | tf_op jit(solution)/shard_map/dynamic_slice | solution.py:46
  20.5 1.5 %collective-permute-start = (f32[1088,256]{1,0:T(8,128)}, f32[1088,256]{1,0:T(8,128)}, u32[]{:S(2)}, u32[]{:S(2)}) collective-permute-start(f32[1088,256]{1,0:T(8,128)} %constant_dynamic-slice_fusion.3), channel_id=1, source_target_pairs={{0,1},{1,0},{2,3},{3,2},{4,5},{5,4},{6,7},{7,6},{8,9},{9,8},{10,11... | collective-permute-start | bytes 3342344 | tf_op jit(solution)/shard_map/ppermute | solution.py:47
  22.0 4.1 %collective-permute-done.3 = f32[256,256]{1,0:T(8,128)} collective-permute-done((f32[256,256]{1,0:T(8,128)S(1)}, f32[256,256]{1,0:T(8,128)}, u32[]{:S(2)}, u32[]{:S(2)}) %collective-permute-start.3) | collective-permute-done | bytes 262176 | tf_op jit(solution)/shard_map/ppermute | solution.py:47
  27.1 1.9 %collective-permute-start.4 = (f32[128,256]{1,0:T(8,128)S(1)}, f32[128,256]{1,0:T(8,128)S(1)}, u32[]{:S(2)}, u32[]{:S(2)}) collective-permute-start(f32[128,256]{1,0:T(8,128)S(1)} %constant_dynamic-slice_fusion), channel_id=1, source_target_pairs={{0,8},{2,10},{4,12},{6,14},{8,0},{10,2},{12,4},{14,6},{16,24},{18,... | collective-permute-start | bytes 393224 | tf_op jit(solution)/shard_map/ppermute | solution.py:47
  29.0 3.2 %collective-permute-done.4 = f32[128,256]{1,0:T(8,128)S(1)} collective-permute-done((f32[128,256]{1,0:T(8,128)S(1)}, f32[128,256]{1,0:T(8,128)S(1)}, u32[]{:S(2)}, u32[]{:S(2)}) %collective-permute-start.4) | collective-permute-done | bytes 131104 | tf_op jit(solution)/shard_map/ppermute | solution.py:47
  32.3 2.8 %collective-permute-start.5 = (f32[64,256]{1,0:T(8,128)S(1)}, f32[64,256]{1,0:T(8,128)S(1)}, u32[]{:S(2)}, u32[]{:S(2)}) collective-permute-start(f32[64,256]{1,0:T(8,128)S(1)} %constant_dynamic-slice_fusion.4), channel_id=1, source_target_pairs={{0,16},{2,18},{4,20},{6,22},{8,24},{10,26},{12,28},{14,30},{16,0},... | collective-permute-start | bytes 196616 | tf_op jit(solution)/shard_map/ppermute | solution.py:47
  35.1 2.4 %collective-permute-done.5 = f32[64,256]{1,0:T(8,128)S(1)} collective-permute-done((f32[64,256]{1,0:T(8,128)S(1)}, f32[64,256]{1,0:T(8,128)S(1)}, u32[]{:S(2)}, u32[]{:S(2)}) %collective-permute-start.5) | collective-permute-done | bytes 65568 | tf_op jit(solution)/shard_map/ppermute | solution.py:47
  37.5 2.9 %collective-permute-start.6 = (bf16[64,256]{1,0:T(8,128)(2,1)S(1)}, bf16[64,256]{1,0:T(8,128)(2,1)S(1)}, u32[]{:S(2)}, u32[]{:S(2)}) collective-permute-start(bf16[64,256]{1,0:T(8,128)(2,1)S(1)} %add_convert_fusion.1), channel_id=1, source_target_pairs={{0,16},{2,18},{4,20},{6,22},{8,24},{10,26},{12,28},{14,30},{16,0},... | collective-permute-start | bytes 98312 | tf_op jit(solution)/shard_map/ppermute | solution.py:57
  40.4 2.1 %collective-permute-done.6 = bf16[64,256]{1,0:T(8,128)(2,1)S(1)} collective-permute-done((bf16[64,256]{1,0:T(8,128)(2,1)S(1)}, bf16[64,256]{1,0:T(8,128)(2,1)S(1)}, u32[]{:S(2)}, u32[]{:S(2)}) %collective-permute-start.6) | collective-permute-done | bytes 32800 | tf_op jit(solution)/shard_map/ppermute | solution.py:57
  42.5 2.0 %collective-permute-start.7 = (bf16[128,256]{1,0:T(8,128)(2,1)S(1)}, bf16[128,256]{1,0:T(8,128)(2,1)S(1)}, u32[]{:S(2)}, u32[]{:S(2)}) collective-permute-start(bf16[128,256]{1,0:T(8,128)(2,1)S(1)} %maximum_select_fusion.4), channel_id=1, source_target_pairs={{0,8},{2,10},{4,12},{6,14},{8,0},{10,2},{12,4},{14,6},{16,24},{18,... | collective-permute-start | bytes 196616 | tf_op jit(solution)/shard_map/ppermute | solution.py:57
  44.5 2.4 %collective-permute-done.7 = bf16[128,256]{1,0:T(8,128)(2,1)S(1)} collective-permute-done((bf16[128,256]{1,0:T(8,128)(2,1)S(1)}, bf16[128,256]{1,0:T(8,128)(2,1)S(1)}, u32[]{:S(2)}, u32[]{:S(2)}) %collective-permute-start.7) | collective-permute-done | bytes 65568 | tf_op jit(solution)/shard_map/ppermute | solution.py:57
  46.9 1.7 %collective-permute-start.8 = (bf16[256,256]{1,0:T(8,128)(2,1)S(1)}, bf16[256,256]{1,0:T(8,128)(2,1)S(1)}, u32[]{:S(2)}, u32[]{:S(2)}) collective-permute-start(bf16[256,256]{1,0:T(8,128)(2,1)S(1)} %maximum_select_fusion.3), channel_id=1, source_target_pairs={{0,4},{2,6},{4,0},{6,2},{8,12},{10,14},{12,8},{14,10},{16,20},{18,... | collective-permute-start | bytes 393224 | tf_op jit(solution)/shard_map/ppermute | solution.py:57
  48.6 1.8 %add_convert_fusion = bf16[1088,256]{1,0:T(8,128)(2,1)S(1)} fusion(f32[1088,256]{1,0:T(8,128)} %collective-permute-done, f32[2176,256]{1,0:T(8,128)S(1)} %pad_maximum_fusion, s32[]{:T(128)S(6)} %select_n.77, bf16[2048,256]{1,0:T(8,128)(2,1)} %param.7, bf16[128,256]{1,0:T(8,128)(2,1)} %param.9), kind=kLoop, calls=%fused_computation.10 | loop fusion | flops 2228224 | bytes 3899396 | tf_op jit(solution)/shard_map/convert_element_type | solution.py:32
  50.4 1.6 %collective-permute-start.1 = (bf16[1088,256]{1,0:T(8,128)(2,1)S(1)}, bf16[1088,256]{1,0:T(8,128)(2,1)S(1)}, u32[]{:S(2)}, u32[]{:S(2)}) collective-permute-start(bf16[1088,256]{1,0:T(8,128)(2,1)S(1)} %add_convert_fusion), channel_id=1, source_target_pairs={{0,1},{1,0},{2,3},{3,2},{4,5},{5,4},{6,7},{7,6},{8,9},{9,8},{10,11... | collective-permute-start | bytes 1671176 | tf_op jit(solution)/shard_map/ppermute | solution.py:57
  52.1 1.5 %collective-permute-done.9 = bf16[512,256]{1,0:T(8,128)(2,1)S(1)} collective-permute-done((bf16[512,256]{1,0:T(8,128)(2,1)S(1)}, bf16[512,256]{1,0:T(8,128)(2,1)S(1)}, u32[]{:S(2)}, u32[]{:S(2)}) %collective-permute-start.9) | collective-permute-done | bytes 262176 | tf_op jit(solution)/shard_map/ppermute | solution.py:57
  54.7 7.8 %collective-permute-done.1 = bf16[1088,256]{1,0:T(8,128)(2,1)S(1)} collective-permute-done((bf16[1088,256]{1,0:T(8,128)(2,1)S(1)}, bf16[1088,256]{1,0:T(8,128)(2,1)S(1)}, u32[]{:S(2)}, u32[]{:S(2)}) %collective-permute-start.1) | collective-permute-done | bytes 557088 | tf_op jit(solution)/shard_map/ppermute | solution.py:57
  (39 shorter events, 8.7 us)
Async XLA Ops:
  1.4 1.0 %copy-start = (bf16[1024,256]{1,0:T(8,128)(2,1)S(1)}, bf16[1024,256]{1,0:T(8,128)(2,1)}, u32[]{:S(2)}) copy-start(bf16[1024,256]{1,0:T(8,128)(2,1)} %param.8) | copy-start | bytes 1572868
  1.4 1.4 %copy-start.1 = (bf16[2048,256]{1,0:T(8,128)(2,1)S(1)}, bf16[2048,256]{1,0:T(8,128)(2,1)}, u32[]{:S(2)}) copy-start(bf16[2048,256]{1,0:T(8,128)(2,1)} %param.7) | copy-start | bytes 3145732
  1.4 2.7 %copy-start.3 = (bf16[2048,1024]{1,0:T(8,128)(2,1)S(1)}, bf16[2048,1024]{1,0:T(8,128)(2,1)}, u32[]{:S(2)}) copy-start(bf16[2048,1024]{1,0:T(8,128)(2,1)} %param.10) | copy-start | bytes 12582916
  6.0 1.3 %copy-start.6 = (s32[8,1]{0,1:T(1,128)S(1)}, s32[8,1]{0,1:T(1,128)}, u32[]{:S(2)}) copy-start(s32[8,1]{0,1:T(1,128)} %param.13) | copy-start | bytes 100
  6.1 1.4 %copy-start.4 = (bf16[128,256]{1,0:T(8,128)(2,1)S(1)}, bf16[128,256]{1,0:T(8,128)(2,1)}, u32[]{:S(2)}) copy-start(bf16[128,256]{1,0:T(8,128)(2,1)} %param.9) | copy-start | bytes 196612
  6.1 1.4 %copy-start.5 = (bf16[1024,128]{1,0:T(8,128)(2,1)S(1)}, bf16[1024,128]{1,0:T(8,128)(2,1)}, u32[]{:S(2)}) copy-start(bf16[1024,128]{1,0:T(8,128)(2,1)} %param.12) | copy-start | bytes 786436
  12.0 1.0 %copy-start.2 = (f32[1024,256]{1,0:T(8,128)}, f32[1024,256]{1,0:T(8,128)S(1)}, u32[]{:S(2)}) copy-start(f32[1024,256]{1,0:T(8,128)S(1)} %convolution_add_fusion) | copy-start | bytes 3145732
  13.0 2.2 %collective-permute-start.2 = (f32[512,256]{1,0:T(8,128)S(1)}, f32[512,256]{1,0:T(8,128)}, u32[]{:S(2)}, u32[]{:S(2)}) collective-permute-start(f32[512,256]{1,0:T(8,128)S(1)} %constant_dynamic-slice_fusion.2), channel_id=1, source_target_pairs={{0,2},{2,0},{4,6},{6,4},{8,10},{10,8},{12,14},{14,12},{16,18},{18,... | collective-permute-start | bytes 1572872 | tf_op jit(solution)/shard_map/ppermute | solution.py:47
  16.5 9.6 %collective-permute-start.3 = (f32[256,256]{1,0:T(8,128)S(1)}, f32[256,256]{1,0:T(8,128)}, u32[]{:S(2)}, u32[]{:S(2)}) collective-permute-start(f32[256,256]{1,0:T(8,128)S(1)} %constant_dynamic-slice_fusion.1), channel_id=1, source_target_pairs={{0,4},{2,6},{4,0},{6,2},{8,12},{10,14},{12,8},{14,10},{16,20},{18,... | collective-permute-start | bytes 786440 | tf_op jit(solution)/shard_map/ppermute | solution.py:47
  20.5 28.1 %collective-permute-start = (f32[1088,256]{1,0:T(8,128)}, f32[1088,256]{1,0:T(8,128)}, u32[]{:S(2)}, u32[]{:S(2)}) collective-permute-start(f32[1088,256]{1,0:T(8,128)} %constant_dynamic-slice_fusion.3), channel_id=1, source_target_pairs={{0,1},{1,0},{2,3},{3,2},{4,5},{5,4},{6,7},{7,6},{8,9},{9,8},{10,11... | collective-permute-start | bytes 3342344 | tf_op jit(solution)/shard_map/ppermute | solution.py:47
  27.1 5.1 %collective-permute-start.4 = (f32[128,256]{1,0:T(8,128)S(1)}, f32[128,256]{1,0:T(8,128)S(1)}, u32[]{:S(2)}, u32[]{:S(2)}) collective-permute-start(f32[128,256]{1,0:T(8,128)S(1)} %constant_dynamic-slice_fusion), channel_id=1, source_target_pairs={{0,8},{2,10},{4,12},{6,14},{8,0},{10,2},{12,4},{14,6},{16,24},{18,... | collective-permute-start | bytes 393224 | tf_op jit(solution)/shard_map/ppermute | solution.py:47
  32.3 5.2 %collective-permute-start.5 = (f32[64,256]{1,0:T(8,128)S(1)}, f32[64,256]{1,0:T(8,128)S(1)}, u32[]{:S(2)}, u32[]{:S(2)}) collective-permute-start(f32[64,256]{1,0:T(8,128)S(1)} %constant_dynamic-slice_fusion.4), channel_id=1, source_target_pairs={{0,16},{2,18},{4,20},{6,22},{8,24},{10,26},{12,28},{14,30},{16,0},... | collective-permute-start | bytes 196616 | tf_op jit(solution)/shard_map/ppermute | solution.py:47
  37.5 5.0 %collective-permute-start.6 = (bf16[64,256]{1,0:T(8,128)(2,1)S(1)}, bf16[64,256]{1,0:T(8,128)(2,1)S(1)}, u32[]{:S(2)}, u32[]{:S(2)}) collective-permute-start(bf16[64,256]{1,0:T(8,128)(2,1)S(1)} %add_convert_fusion.1), channel_id=1, source_target_pairs={{0,16},{2,18},{4,20},{6,22},{8,24},{10,26},{12,28},{14,30},{16,0},... | collective-permute-start | bytes 98312 | tf_op jit(solution)/shard_map/ppermute | solution.py:57
  42.5 4.3 %collective-permute-start.7 = (bf16[128,256]{1,0:T(8,128)(2,1)S(1)}, bf16[128,256]{1,0:T(8,128)(2,1)S(1)}, u32[]{:S(2)}, u32[]{:S(2)}) collective-permute-start(bf16[128,256]{1,0:T(8,128)(2,1)S(1)} %maximum_select_fusion.4), channel_id=1, source_target_pairs={{0,8},{2,10},{4,12},{6,14},{8,0},{10,2},{12,4},{14,6},{16,24},{18,... | collective-permute-start | bytes 196616 | tf_op jit(solution)/shard_map/ppermute | solution.py:57
  46.9 5.1 %collective-permute-start.8 = (bf16[256,256]{1,0:T(8,128)(2,1)S(1)}, bf16[256,256]{1,0:T(8,128)(2,1)S(1)}, u32[]{:S(2)}, u32[]{:S(2)}) collective-permute-start(bf16[256,256]{1,0:T(8,128)(2,1)S(1)} %maximum_select_fusion.3), channel_id=1, source_target_pairs={{0,4},{2,6},{4,0},{6,2},{8,12},{10,14},{12,8},{14,10},{16,20},{18,... | collective-permute-start | bytes 393224 | tf_op jit(solution)/shard_map/ppermute | solution.py:57
  50.4 12.1 %collective-permute-start.1 = (bf16[1088,256]{1,0:T(8,128)(2,1)S(1)}, bf16[1088,256]{1,0:T(8,128)(2,1)S(1)}, u32[]{:S(2)}, u32[]{:S(2)}) collective-permute-start(bf16[1088,256]{1,0:T(8,128)(2,1)S(1)} %add_convert_fusion), channel_id=1, source_target_pairs={{0,1},{1,0},{2,3},{3,2},{4,5},{5,4},{6,7},{7,6},{8,9},{9,8},{10,11... | collective-permute-start | bytes 1671176 | tf_op jit(solution)/shard_map/ppermute | solution.py:57
  52.1 1.6 %collective-permute-start.9 = (bf16[512,256]{1,0:T(8,128)(2,1)S(1)}, bf16[512,256]{1,0:T(8,128)(2,1)S(1)}, u32[]{:S(2)}, u32[]{:S(2)}) collective-permute-start(bf16[512,256]{1,0:T(8,128)(2,1)S(1)} %maximum_select_fusion.2), channel_id=1, source_target_pairs={{0,2},{2,0},{4,6},{6,4},{8,10},{10,8},{12,14},{14,12},{16,18},{18,... | collective-permute-start | bytes 786440 | tf_op jit(solution)/shard_map/ppermute | solution.py:57

commit v4 on v1

--- a/solution.py
+++ b/solution.py
@@ -32,8 +32,9 @@
     return (factors.astype(jnp.float32) + rate * gradient).astype(jnp.bfloat16)
 
 
-def xor_pairs(count, bit):
-    return [(i, i ^ (1 << bit)) for i in range(count)]
+def xor_pairs(count, bit, mask=0):
+    mask = mask or (1 << bit)
+    return [(i, i ^ mask) for i in range(count)]
 
 
 def halving_scatter(parts, axis, count, position):
@@ -62,6 +63,92 @@
     return parts
 
 
+def radix_stages(count):
+    bits = count.bit_length() - 1
+    stages = []
+    low = 0
+    while low < bits:
+        width = 1 if low == 0 else min(3, bits - low)
+        stages.append((low, width))
+        low += width
+    return stages
+
+
+def radix_scatter(part, axis, count, position, stages):
+    offset = 0
+    for low, width in stages:
+        radix = 1 << width
+        local = (position >> low) & (radix - 1)
+        rows = part.shape[0] // radix
+        total = lax.dynamic_slice_in_dim(part, local * rows, rows, 0)
+        for shift in range(1, radix):
+            sent = lax.dynamic_slice_in_dim(part, (local ^ shift) * rows, rows, 0)
+            total = total + lax.ppermute(sent, axis, xor_pairs(count, 0, shift << low))
+        part = total
+        offset = offset + local * rows
+    return part, offset
+
+
+def radix_gather(share, axis, count, position, stages):
+    for low, width in reversed(stages):
+        radix = 1 << width
+        local = (position >> low) & (radix - 1)
+        pieces = [share] + [
+            lax.ppermute(share, axis, xor_pairs(count, 0, shift << low))
+            for shift in range(1, radix)
+        ]
+        stacked = jnp.stack(pieces, 0)
+        share = jnp.concatenate(
+            [lax.dynamic_index_in_dim(stacked, local ^ block, 0, False) for block in range(radix)],
+            0,
+        )
+    return share
+
+
+def loop_pair_step(user_factors, item_factors, tag_factors, rating_errors, link_errors, position):
+    user_half = user_factors.shape[0] // 2
+    tag_half = tag_factors.shape[0] // 2
+    side = position & 1
+
+    def partial(rows_side):
+        users = jnp.dot(
+            lax.dynamic_slice_in_dim(rating_errors, rows_side * user_half, user_half, 0),
+            item_factors,
+            preferred_element_type=jnp.float32,
+        )
+        tags = transposed_product(
+            lax.dynamic_slice_in_dim(link_errors, rows_side * tag_half, tag_half, 1),
+            item_factors,
+        )
+        return jnp.concatenate([users, tags], 0)
+
+    sent = partial(1 - side)
+    sent, rating_errors, link_errors = lax.optimization_barrier((sent, rating_errors, link_errors))
+    got = lax.ppermute(sent, "loop", [(0, 1), (1, 0)])
+    total = partial(side) + got
+    fresh = jnp.concatenate(
+        [
+            advance(
+                lax.dynamic_slice_in_dim(user_factors, side * user_half, user_half, 0),
+                total[:user_half],
+                step_users,
+            ),
+            advance(
+                lax.dynamic_slice_in_dim(tag_factors, side * tag_half, tag_half, 0),
+                total[user_half:],
+                step_tags,
+            ),
+        ],
+        0,
+    )
+    other = lax.ppermute(fresh, "loop", [(0, 1), (1, 0)])
+    low = jnp.where(side == 0, fresh, other)
+    high = jnp.where(side == 0, other, fresh)
+    new_users = jnp.concatenate([low[:user_half], high[:user_half]], 0)
+    new_tags = jnp.concatenate([low[user_half:], high[user_half:]], 0)
+    return new_users, new_tags, rating_errors, link_errors, got
+
+
 def shards(user_factors, item_factors, tag_factors, ratings, rating_tiles, tag_links, link_tiles):
     group_count = lax.axis_size("group")
     loop_count = lax.axis_size("loop")
@@ -70,36 +157,45 @@
 
     link_errors = residual_of(tag_links, item_factors, tag_factors, link_tiles)
     rating_errors = residual_of(ratings, user_factors, item_factors, rating_tiles)
-    user_part = jnp.dot(rating_errors, item_factors, preferred_element_type=jnp.float32)
-    tag_part = transposed_product(link_errors, item_factors)
+    if loop_count == 2:
+        new_users, new_tags, rating_errors, link_errors, got = loop_pair_step(
+            user_factors, item_factors, tag_factors, rating_errors, link_errors, loop_position
+        )
+    else:
+        got = None
+        user_part = jnp.dot(rating_errors, item_factors, preferred_element_type=jnp.float32)
+        tag_part = transposed_product(link_errors, item_factors)
+        (user_share, tag_share), (user_offset, tag_offset) = halving_scatter(
+            [user_part, tag_part], "loop", loop_count, loop_position
+        )
+        fresh_users = advance(
+            lax.dynamic_slice_in_dim(user_factors, user_offset, user_share.shape[0], 0),
+            user_share,
+            step_users,
+        )
+        fresh_tags = advance(
+            lax.dynamic_slice_in_dim(tag_factors, tag_offset, tag_share.shape[0], 0),
+            tag_share,
+            step_tags,
+        )
+        new_users, new_tags = doubling_gather(
+            [fresh_users, fresh_tags], "loop", loop_count, loop_position
+        )
     item_part = transposed_product(rating_errors, user_factors) + jnp.dot(
         link_errors, tag_factors, preferred_element_type=jnp.float32
     )
-
-    (user_share, tag_share), (user_offset, tag_offset) = halving_scatter(
-        [user_part, tag_part], "loop", loop_count, loop_position
-    )
-    fresh_users = advance(
-        lax.dynamic_slice_in_dim(user_factors, user_offset, user_share.shape[0], 0),
-        user_share,
-        step_users,
-    )
-    fresh_tags = advance(
-        lax.dynamic_slice_in_dim(tag_factors, tag_offset, tag_share.shape[0], 0),
-        tag_share,
-        step_tags,
-    )
-    new_users, new_tags = doubling_gather(
-        [fresh_users, fresh_tags], "loop", loop_count, loop_position
-    )
-
-    (item_share,), (item_offset,) = halving_scatter([item_part], "group", group_count, group_position)
+    if got is not None:
+        item_part, _ = lax.optimization_barrier((item_part, got))
+    group_stages = radix_stages(group_count)
+    item_share, item_offset = radix_scatter(
+        item_part, "group", group_count, group_position, group_stages
+    )
     fresh_items = advance(
         lax.dynamic_slice_in_dim(item_factors, item_offset, item_share.shape[0], 0),
         item_share,
         step_items,
     )
-    (new_items,) = doubling_gather([fresh_items], "group", group_count, group_position)
+    new_items = radix_gather(fresh_items, "group", group_count, group_position, group_stages)
     return (new_users, new_items, new_tags)
 
 

time: 66.9 us -> 80.1 us (1.20)
  starting transfers between devices: 20.2 us -> 28.1 us
  waiting for transfers between devices: 26.4 us -> 30.9 us
  local copies, waits for them, and re-layouts: 3.79 us -> 6.55 us
  matrix products: 9.87 us -> 7.52 us
    ppermute x12 -> x18, starting transfers between devices: 20.2 us -> 28.1 us  [the longest x8 11.8 us: radix_scatter(): total = total + lax.ppermute(sent, axis, xor_pairs(count, 0, shift << low))]
    ppermute x12 -> x18, waiting for transfers between devices: 26.4 us -> 30.9 us  [the longest x1 20.1 us: loop_pair_step(): got = lax.ppermute(sent, 'loop', [(0, 1), (1, 0)])]
    concatenate x0 -> x5, other arithmetic: none -> 3.65 us  [the longest x1 1.11 us: partial(): return jnp.concatenate([users, tags], 0)]
    unnamed x16 -> x26, local copies, waits for them, and re-layouts: 2.07 us -> 5.62 us
    select_n x6 -> x1, other arithmetic: 3.03 us -> 0.2 us  [loop_pair_step(): low = jnp.where(side == 0, fresh, other)]
    convert_element_type x3 -> x2, other arithmetic: 1.76 us -> 0.18 us  [advance(): return (factors.astype(jnp.float32) + rate * gradient).astype(jnp.bfloat16)]
    dot_general x1, matrix products: 1.5 us -> 0.32 us  [shards(): jnp.dot(link_errors, tag_factors, preferred_element_type=jnp.float32)]
    dynamic_slice x6 -> x2, local copies, waits for them, and re-layouts: 0.97 us -> 0.08 us  [radix_scatter(): sent = lax.dynamic_slice_in_dim(part, (local ^ shift) * rows, rows, 0)]
  transfers between devices with their start and end apart: 12 -> 18, of which waited for: 8 -> 6; matrix products, arithmetic and copies ran while one was open for 11% -> 8% of each run, Pallas kernels for 0% -> 0%
where the time goes in v4:
time: 80.1 us; the launch traced here: 79.8 us
  waiting for transfers between devices  30.9 us (39%)
  starting transfers between devices  28.1 us (35%)
  matrix products  7.52 us (9%)
  local copies, waits for them, and re-layouts  6.55 us (8%)
  other arithmetic  5.82 us (7%)
  between operations  0.98 us (1%)
    ppermute x1, waiting for transfers between devices, loop_pair_step(): got = lax.ppermute(sent, 'loop', [(0, 1), (1, 0)])  20.1 us
    ppermute x8, starting transfers between devices, radix_scatter(): total = total + lax.ppermute(sent, axis, xor_pairs(count, 0, shift << low))  11.8 us
    ppermute x8, starting transfers between devices, radix_gather(): lax.ppermute(share, axis, xor_pairs(count, 0, shift << low))  11.5 us
    ppermute x8, waiting for transfers between devices, radix_scatter(): total = total + lax.ppermute(sent, axis, xor_pairs(count, 0, shift << low))  6.34 us
    unnamed x26, local copies, waits for them, and re-layouts  5.62 us
    ppermute x8, waiting for transfers between devices, radix_gather(): lax.ppermute(share, axis, xor_pairs(count, 0, shift << low))  4.47 us
    dot_general x2, matrix products, partial(): jnp.dot(lax.dynamic_slice_in_dim(rating_errors, rows_side * user_half, us...  3.17 us
    ppermute x1, starting transfers between devices, loop_pair_step(): got = lax.ppermute(sent, 'loop', [(0, 1), (1, 0)])  2.97 us
  transfers between devices with their start and end apart: 18, of which 6 were waited for; matrix products, arithmetic and copies ran while one was open for 8% of the time, Pallas kernels for 0%

profile of v4, /device:TPU:0, one launch (start us, length us, event | category | flops | bytes accessed | tf_op | source)
XLA Modules:
  0.0 79.8 jit_solution(13295374749567460987)
XLA Ops:
  1.4 1.1 %copy.11 = bf16[1024,128]{0,1:T(8,128)(2,1)S(1)} copy(bf16[1024,128]{1,0:T(8,128)(2,1)} %param.12) | data formatting | bytes 524288 | tf_op args[5]
  4.3 1.3 %copy-done.1 = bf16[2048,1024]{1,0:T(8,128)(2,1)S(1)} copy-done((bf16[2048,1024]{1,0:T(8,128)(2,1)S(1)}, bf16[2048,1024]{1,0:T(8,128)(2,1)}, u32[]{:S(2)}) %copy-start.1) | copy-done | bytes 4194328
  5.9 2.0 %fusion = bf16[2048,1024]{1,0:T(8,128)(2,1)S(1)} fusion(f32[256,8,8,128]{3,2,1,0:T(8,128)S(1)} %bitcast.60, bf16[2048,1024]{1,0:T(8,128)(2,1)S(1)} %copy-done.1, bf16[2048,256]{1,0:T(8,128)(2,1)S(1)} %copy-done.4, bf16[1024,256]{1,0:T(8,128)(2,1)S(1)} %copy-done), kind=kOutput, calls=%fused_computation.1 | convolution fusion | flops 1082130432 | bytes 18350080 | tf_op jit(solution)/shard_map/dot_general | solution.py:19
  7.9 1.9 %copy-done.2 = bf16[2048,1024]{1,0:T(8,128)(2,1)} copy-done((bf16[2048,1024]{1,0:T(8,128)(2,1)}, bf16[2048,1024]{1,0:T(8,128)(2,1)S(1)}, u32[]{:S(2)}) %copy-start.2) | copy-done | bytes 4194328
  11.2 1.1 %pad_maximum_fusion = f32[1088,256]{1,0:T(8,128)} fusion(f32[64,256]{1,0:T(8,128)S(1)} %fusion.15, f32[1024,256]{1,0:T(8,128)S(1)} %fusion.3), kind=kLoop, calls=%fused_computation.10 | loop fusion | flops 278528 | bytes 2228224 | tf_op jit(solution)/shard_map/concatenate | solution.py:123
  12.3 3.0 %collective-permute-start = (f32[1088,256]{1,0:T(8,128)}, f32[1088,256]{1,0:T(8,128)S(1)}, u32[]{:S(2)}, u32[]{:S(2)}) collective-permute-start(f32[1088,256]{1,0:T(8,128)} %pad_maximum_fusion), channel_id=1, source_target_pairs={{0,1},{1,0},{2,3},{3,2},{4,5},{5,4},{6,7},{7,6},{8,9},{9,8},{10,11... | collective-permute-start | bytes 3342344 | tf_op jit(solution)/shard_map/ppermute | solution.py:127
  15.6 2.5 %fusion.1 = f32[1024,256]{1,0:T(8,128)S(1)} fusion(bf16[1024,256]{1,0:T(8,128)(2,1)S(1)} %copy-done, bf16[2048,1024]{1,0:T(8,128)(2,1)} %copy-done.2, s32[]{:T(128)S(6)} %select_n.92), kind=kOutput, calls=%fused_computation.2 | convolution fusion | flops 536870912 | bytes 3670020 | tf_op jit(solution)/shard_map/dot_general | solution.py:114
  18.4 1.3 %fusion.23 = f32[1024,256]{1,0:T(8,128)S(1)} fusion(bf16[2048,1024]{1,0:T(8,128)(2,1)S(1)} %copy-done.3, bf16[2048,256]{1,0:T(8,128)(2,1)S(1)} %copy-done.4), kind=kOutput, calls=%fused_computation.68 | convolution fusion | flops 1073741824 | bytes 6291456 | tf_op jit(solution)/shard_map/dot_general | solution.py:26
  20.0 20.1 %collective-permute-done = f32[1088,256]{1,0:T(8,128)S(1)} collective-permute-done((f32[1088,256]{1,0:T(8,128)}, f32[1088,256]{1,0:T(8,128)S(1)}, u32[]{:S(2)}, u32[]{:S(2)}) %collective-permute-start) | collective-permute-done | bytes 1114144 | tf_op jit(solution)/shard_map/ppermute | solution.py:127
  40.6 1.8 %collective-permute-start.1 = (bf16[1088,256]{1,0:T(8,128)(2,1)S(1)}, bf16[1088,256]{1,0:T(8,128)(2,1)S(1)}, u32[]{:S(2)}, u32[]{:S(2)}) collective-permute-start(bf16[1088,256]{1,0:T(8,128)(2,1)S(1)} %pad_maximum_fusion.2), channel_id=1, source_target_pairs={{0,1},{1,0},{2,3},{3,2},{4,5},{5,4},{6,7},{7,6},{8,9},{9,8},{10,11... | collective-permute-start | bytes 1671176 | tf_op jit(solution)/shard_map/ppermute | solution.py:144
  42.5 1.6 %collective-permute-start.3 = (f32[64,256]{1,0:T(8,128)S(1)}, f32[64,256]{1,0:T(8,128)S(1)}, u32[]{:S(2)}, u32[]{:S(2)}) collective-permute-start(f32[64,256]{1,0:T(8,128)S(1)} %get-tuple-element.17), channel_id=1, source_target_pairs={{0,4},{2,6},{4,0},{6,2},{8,12},{10,14},{12,8},{14,10},{16,20},{18,... | collective-permute-start | bytes 196616 | tf_op jit(solution)/shard_map/ppermute | solution.py:86
  44.1 1.6 %collective-permute-start.4 = (f32[64,256]{1,0:T(8,128)S(1)}, f32[64,256]{1,0:T(8,128)S(1)}, u32[]{:S(2)}, u32[]{:S(2)}) collective-permute-start(f32[64,256]{1,0:T(8,128)S(1)} %get-tuple-element.23), channel_id=1, source_target_pairs={{0,8},{2,10},{4,12},{6,14},{8,0},{10,2},{12,4},{14,6},{16,24},{18,... | collective-permute-start | bytes 196616 | tf_op jit(solution)/shard_map/ppermute | solution.py:86
  46.1 2.6 %collective-permute-start.6 = (f32[64,256]{1,0:T(8,128)S(1)}, f32[64,256]{1,0:T(8,128)S(1)}, u32[]{:S(2)}, u32[]{:S(2)}) collective-permute-start(f32[64,256]{1,0:T(8,128)S(1)} %get-tuple-element.21), channel_id=1, source_target_pairs={{0,16},{2,18},{4,20},{6,22},{8,24},{10,26},{12,28},{14,30},{16,0},... | collective-permute-start | bytes 196616 | tf_op jit(solution)/shard_map/ppermute | solution.py:86
  48.7 1.7 %collective-permute-start.7 = (f32[64,256]{1,0:T(8,128)S(1)}, f32[64,256]{1,0:T(8,128)S(1)}, u32[]{:S(2)}, u32[]{:S(2)}) collective-permute-start(f32[64,256]{1,0:T(8,128)S(1)} %get-tuple-element.20), channel_id=1, source_target_pairs={{0,20},{2,22},{4,16},{6,18},{8,28},{10,30},{12,24},{14,26},{16,4},... | collective-permute-start | bytes 196616 | tf_op jit(solution)/shard_map/ppermute | solution.py:86
  50.4 3.2 %collective-permute-start.8 = (f32[64,256]{1,0:T(8,128)S(1)}, f32[64,256]{1,0:T(8,128)S(1)}, u32[]{:S(2)}, u32[]{:S(2)}) collective-permute-start(f32[64,256]{1,0:T(8,128)S(1)} %get-tuple-element.19), channel_id=1, source_target_pairs={{0,24},{2,26},{4,28},{6,30},{8,16},{10,18},{12,20},{14,22},{16,8},... | collective-permute-start | bytes 196616 | tf_op jit(solution)/shard_map/ppermute | solution.py:86
  54.3 4.7 %collective-permute-done.7 = f32[64,256]{1,0:T(8,128)S(1)} collective-permute-done((f32[64,256]{1,0:T(8,128)S(1)}, f32[64,256]{1,0:T(8,128)S(1)}, u32[]{:S(2)}, u32[]{:S(2)}) %collective-permute-start.7) | collective-permute-done | bytes 65568 | tf_op jit(solution)/shard_map/ppermute | solution.py:86
  59.0 1.6 %collective-permute-done.9 = f32[64,256]{1,0:T(8,128)S(1)} collective-permute-done((f32[64,256]{1,0:T(8,128)S(1)}, f32[64,256]{1,0:T(8,128)S(1)}, u32[]{:S(2)}, u32[]{:S(2)}) %collective-permute-start.9) | collective-permute-done | bytes 65568 | tf_op jit(solution)/shard_map/ppermute | solution.py:86
  61.5 2.3 %collective-permute-start.11 = (bf16[64,256]{1,0:T(8,128)(2,1)S(1)}, bf16[64,256]{1,0:T(8,128)(2,1)S(1)}, u32[]{:S(2)}, u32[]{:S(2)}) collective-permute-start(bf16[64,256]{1,0:T(8,128)(2,1)S(1)} %get-tuple-element.12), channel_id=1, source_target_pairs={{0,8},{2,10},{4,12},{6,14},{8,0},{10,2},{12,4},{14,6},{16,24},{18,... | collective-permute-start | bytes 98312 | tf_op jit(solution)/shard_map/ppermute | solution.py:97
  64.5 3.1 %collective-permute-start.13 = (bf16[64,256]{1,0:T(8,128)(2,1)S(1)}, bf16[64,256]{1,0:T(8,128)(2,1)S(1)}, u32[]{:S(2)}, u32[]{:S(2)}) collective-permute-start(bf16[64,256]{1,0:T(8,128)(2,1)S(1)} %get-tuple-element.12), channel_id=1, source_target_pairs={{0,16},{2,18},{4,20},{6,22},{8,24},{10,26},{12,28},{14,30},{16,0},... | collective-permute-start | bytes 98312 | tf_op jit(solution)/shard_map/ppermute | solution.py:97
  67.8 2.4 %collective-permute-start.15 = (bf16[64,256]{1,0:T(8,128)(2,1)S(1)}, bf16[64,256]{1,0:T(8,128)(2,1)S(1)}, u32[]{:S(2)}, u32[]{:S(2)}) collective-permute-start(bf16[64,256]{1,0:T(8,128)(2,1)S(1)} %get-tuple-element.12), channel_id=1, source_target_pairs={{0,24},{2,26},{4,28},{6,30},{8,16},{10,18},{12,20},{14,22},{16,8},... | collective-permute-start | bytes 98312 | tf_op jit(solution)/shard_map/ppermute | solution.py:97
  70.2 2.1 %collective-permute-start.16 = (bf16[64,256]{1,0:T(8,128)(2,1)S(1)}, bf16[64,256]{1,0:T(8,128)(2,1)S(1)}, u32[]{:S(2)}, u32[]{:S(2)}) collective-permute-start(bf16[64,256]{1,0:T(8,128)(2,1)S(1)} %get-tuple-element.12), channel_id=1, source_target_pairs={{0,28},{2,30},{4,24},{6,26},{8,20},{10,22},{12,16},{14,18},{16,12}... | collective-permute-start | bytes 98312 | tf_op jit(solution)/shard_map/ppermute | solution.py:97
  72.4 1.0 %collective-permute-done.14 = bf16[64,256]{1,0:T(8,128)(2,1)S(1)} collective-permute-done((bf16[64,256]{1,0:T(8,128)(2,1)S(1)}, bf16[64,256]{1,0:T(8,128)(2,1)S(1)}, u32[]{:S(2)}, u32[]{:S(2)}) %collective-permute-start.14) | collective-permute-done | bytes 32800 | tf_op jit(solution)/shard_map/ppermute | solution.py:97
  73.6 3.2 %collective-permute-done.16 = bf16[64,256]{1,0:T(8,128)(2,1)S(1)} collective-permute-done((bf16[64,256]{1,0:T(8,128)(2,1)S(1)}, bf16[64,256]{1,0:T(8,128)(2,1)S(1)}, u32[]{:S(2)}, u32[]{:S(2)}) %collective-permute-start.16) | collective-permute-done | bytes 32800 | tf_op jit(solution)/shard_map/ppermute | solution.py:97
  77.8 1.0 %pad_maximum_fusion.1 = bf16[2048,256]{1,0:T(8,128)(2,1)} fusion(bf16[1024,256]{1,0:T(8,128)(2,1)S(1)} %slice.27, bf16[1024,256]{1,0:T(8,128)(2,1)S(1)} %slice.26), kind=kLoop, calls=%fused_computation.15 | loop fusion | flops 2097152 | bytes 2097152 | tf_op jit(solution)/shard_map/concatenate | solution.py:147
  (71 shorter events, 10.7 us)
Async XLA Ops:
  3.2 1.0 %copy-start = (bf16[1024,256]{1,0:T(8,128)(2,1)S(1)}, bf16[1024,256]{1,0:T(8,128)(2,1)}, u32[]{:S(2)}) copy-start(bf16[1024,256]{1,0:T(8,128)(2,1)} %param.8) | copy-start | bytes 1572868
  3.2 2.4 %copy-start.1 = (bf16[2048,1024]{1,0:T(8,128)(2,1)S(1)}, bf16[2048,1024]{1,0:T(8,128)(2,1)}, u32[]{:S(2)}) copy-start(bf16[2048,1024]{1,0:T(8,128)(2,1)} %param.10) | copy-start | bytes 12582916
  3.2 2.6 %copy-start.4 = (bf16[2048,256]{1,0:T(8,128)(2,1)S(1)}, bf16[2048,256]{1,0:T(8,128)(2,1)}, u32[]{:S(2)}) copy-start(bf16[2048,256]{1,0:T(8,128)(2,1)} %param.7) | copy-start | bytes 3145732
  7.9 2.0 %copy-start.2 = (bf16[2048,1024]{1,0:T(8,128)(2,1)}, bf16[2048,1024]{1,0:T(8,128)(2,1)S(1)}, u32[]{:S(2)}) copy-start(bf16[2048,1024]{1,0:T(8,128)(2,1)S(1)} %fusion) | copy-start | bytes 12582916
  9.9 0.8 %copy-start.5 = (bf16[128,256]{1,0:T(8,128)(2,1)S(1)}, bf16[128,256]{1,0:T(8,128)(2,1)}, u32[]{:S(2)}) copy-start(bf16[128,256]{1,0:T(8,128)(2,1)} %param.9) | copy-start | bytes 196612
  12.3 27.7 %collective-permute-start = (f32[1088,256]{1,0:T(8,128)}, f32[1088,256]{1,0:T(8,128)S(1)}, u32[]{:S(2)}, u32[]{:S(2)}) collective-permute-start(f32[1088,256]{1,0:T(8,128)} %pad_maximum_fusion), channel_id=1, source_target_pairs={{0,1},{1,0},{2,3},{3,2},{4,5},{5,4},{6,7},{7,6},{8,9},{9,8},{10,11... | collective-permute-start | bytes 3342344 | tf_op jit(solution)/shard_map/ppermute | solution.py:127
  15.6 2.8 %copy-start.3 = (bf16[2048,1024]{1,0:T(8,128)(2,1)S(1)}, bf16[2048,1024]{1,0:T(8,128)(2,1)}, u32[]{:S(2)}) copy-start(bf16[2048,1024]{1,0:T(8,128)(2,1)} %copy-done.2) | copy-start | bytes 12582916
  40.1 2.3 %collective-permute-start.2 = (f32[512,256]{1,0:T(8,128)S(1)}, f32[512,256]{1,0:T(8,128)S(1)}, u32[]{:S(2)}, u32[]{:S(2)}) collective-permute-start(f32[512,256]{1,0:T(8,128)S(1)} %constant_dynamic-slice_fusion.7), channel_id=1, source_target_pairs={{0,2},{2,0},{4,6},{6,4},{8,10},{10,8},{12,14},{14,12},{16,18},{18,... | collective-permute-start | bytes 1572872 | tf_op jit(solution)/shard_map/ppermute | solution.py:86
  40.6 20.7 %collective-permute-start.1 = (bf16[1088,256]{1,0:T(8,128)(2,1)S(1)}, bf16[1088,256]{1,0:T(8,128)(2,1)S(1)}, u32[]{:S(2)}, u32[]{:S(2)}) collective-permute-start(bf16[1088,256]{1,0:T(8,128)(2,1)S(1)} %pad_maximum_fusion.2), channel_id=1, source_target_pairs={{0,1},{1,0},{2,3},{3,2},{4,5},{5,4},{6,7},{7,6},{8,9},{9,8},{10,11... | collective-permute-start | bytes 1671176 | tf_op jit(solution)/shard_map/ppermute | solution.py:144
  42.5 6.2 %collective-permute-start.3 = (f32[64,256]{1,0:T(8,128)S(1)}, f32[64,256]{1,0:T(8,128)S(1)}, u32[]{:S(2)}, u32[]{:S(2)}) collective-permute-start(f32[64,256]{1,0:T(8,128)S(1)} %get-tuple-element.17), channel_id=1, source_target_pairs={{0,4},{2,6},{4,0},{6,2},{8,12},{10,14},{12,8},{14,10},{16,20},{18,... | collective-permute-start | bytes 196616 | tf_op jit(solution)/shard_map/ppermute | solution.py:86
  44.1 6.3 %collective-permute-start.4 = (f32[64,256]{1,0:T(8,128)S(1)}, f32[64,256]{1,0:T(8,128)S(1)}, u32[]{:S(2)}, u32[]{:S(2)}) collective-permute-start(f32[64,256]{1,0:T(8,128)S(1)} %get-tuple-element.23), channel_id=1, source_target_pairs={{0,8},{2,10},{4,12},{6,14},{8,0},{10,2},{12,4},{14,6},{16,24},{18,... | collective-permute-start | bytes 196616 | tf_op jit(solution)/shard_map/ppermute | solution.py:86
  45.7 7.9 %collective-permute-start.5 = (f32[64,256]{1,0:T(8,128)S(1)}, f32[64,256]{1,0:T(8,128)S(1)}, u32[]{:S(2)}, u32[]{:S(2)}) collective-permute-start(f32[64,256]{1,0:T(8,128)S(1)} %get-tuple-element.22), channel_id=1, source_target_pairs={{0,12},{2,14},{4,8},{6,10},{8,4},{10,6},{12,0},{14,2},{16,28},{18,... | collective-permute-start | bytes 196616 | tf_op jit(solution)/shard_map/ppermute | solution.py:86
  46.1 8.2 %collective-permute-start.6 = (f32[64,256]{1,0:T(8,128)S(1)}, f32[64,256]{1,0:T(8,128)S(1)}, u32[]{:S(2)}, u32[]{:S(2)}) collective-permute-start(f32[64,256]{1,0:T(8,128)S(1)} %get-tuple-element.21), channel_id=1, source_target_pairs={{0,16},{2,18},{4,20},{6,22},{8,24},{10,26},{12,28},{14,30},{16,0},... | collective-permute-start | bytes 196616 | tf_op jit(solution)/shard_map/ppermute | solution.py:86
  48.7 10.3 %collective-permute-start.7 = (f32[64,256]{1,0:T(8,128)S(1)}, f32[64,256]{1,0:T(8,128)S(1)}, u32[]{:S(2)}, u32[]{:S(2)}) collective-permute-start(f32[64,256]{1,0:T(8,128)S(1)} %get-tuple-element.20), channel_id=1, source_target_pairs={{0,20},{2,22},{4,16},{6,18},{8,28},{10,30},{12,24},{14,26},{16,4},... | collective-permute-start | bytes 196616 | tf_op jit(solution)/shard_map/ppermute | solution.py:86
  50.4 8.6 %collective-permute-start.8 = (f32[64,256]{1,0:T(8,128)S(1)}, f32[64,256]{1,0:T(8,128)S(1)}, u32[]{:S(2)}, u32[]{:S(2)}) collective-permute-start(f32[64,256]{1,0:T(8,128)S(1)} %get-tuple-element.19), channel_id=1, source_target_pairs={{0,24},{2,26},{4,28},{6,30},{8,16},{10,18},{12,20},{14,22},{16,8},... | collective-permute-start | bytes 196616 | tf_op jit(solution)/shard_map/ppermute | solution.py:86
  53.6 7.1 %collective-permute-start.9 = (f32[64,256]{1,0:T(8,128)S(1)}, f32[64,256]{1,0:T(8,128)S(1)}, u32[]{:S(2)}, u32[]{:S(2)}) collective-permute-start(f32[64,256]{1,0:T(8,128)S(1)} %get-tuple-element.18), channel_id=1, source_target_pairs={{0,28},{2,30},{4,24},{6,26},{8,20},{10,22},{12,16},{14,18},{16,12}... | collective-permute-start | bytes 196616 | tf_op jit(solution)/shard_map/ppermute | solution.py:86
  60.7 7.1 %collective-permute-start.10 = (bf16[64,256]{1,0:T(8,128)(2,1)S(1)}, bf16[64,256]{1,0:T(8,128)(2,1)S(1)}, u32[]{:S(2)}, u32[]{:S(2)}) collective-permute-start(bf16[64,256]{1,0:T(8,128)(2,1)S(1)} %get-tuple-element.12), channel_id=1, source_target_pairs={{0,4},{2,6},{4,0},{6,2},{8,12},{10,14},{12,8},{14,10},{16,20},{18,... | collective-permute-start | bytes 98312 | tf_op jit(solution)/shard_map/ppermute | solution.py:97
  61.5 8.7 %collective-permute-start.11 = (bf16[64,256]{1,0:T(8,128)(2,1)S(1)}, bf16[64,256]{1,0:T(8,128)(2,1)S(1)}, u32[]{:S(2)}, u32[]{:S(2)}) collective-permute-start(bf16[64,256]{1,0:T(8,128)(2,1)S(1)} %get-tuple-element.12), channel_id=1, source_target_pairs={{0,8},{2,10},{4,12},{6,14},{8,0},{10,2},{12,4},{14,6},{16,24},{18,... | collective-permute-start | bytes 98312 | tf_op jit(solution)/shard_map/ppermute | solution.py:97
  63.8 8.5 %collective-permute-start.12 = (bf16[64,256]{1,0:T(8,128)(2,1)S(1)}, bf16[64,256]{1,0:T(8,128)(2,1)S(1)}, u32[]{:S(2)}, u32[]{:S(2)}) collective-permute-start(bf16[64,256]{1,0:T(8,128)(2,1)S(1)} %get-tuple-element.12), channel_id=1, source_target_pairs={{0,12},{2,14},{4,8},{6,10},{8,4},{10,6},{12,0},{14,2},{16,28},{18,... | collective-permute-start | bytes 98312 | tf_op jit(solution)/shard_map/ppermute | solution.py:97
  64.5 7.8 %collective-permute-start.13 = (bf16[64,256]{1,0:T(8,128)(2,1)S(1)}, bf16[64,256]{1,0:T(8,128)(2,1)S(1)}, u32[]{:S(2)}, u32[]{:S(2)}) collective-permute-start(bf16[64,256]{1,0:T(8,128)(2,1)S(1)} %get-tuple-element.12), channel_id=1, source_target_pairs={{0,16},{2,18},{4,20},{6,22},{8,24},{10,26},{12,28},{14,30},{16,0},... | collective-permute-start | bytes 98312 | tf_op jit(solution)/shard_map/ppermute | solution.py:97
  67.6 5.8 %collective-permute-start.14 = (bf16[64,256]{1,0:T(8,128)(2,1)S(1)}, bf16[64,256]{1,0:T(8,128)(2,1)S(1)}, u32[]{:S(2)}, u32[]{:S(2)}) collective-permute-start(bf16[64,256]{1,0:T(8,128)(2,1)S(1)} %get-tuple-element.12), channel_id=1, source_target_pairs={{0,20},{2,22},{4,16},{6,18},{8,28},{10,30},{12,24},{14,26},{16,4},... | collective-permute-start | bytes 98312 | tf_op jit(solution)/shard_map/ppermute | solution.py:97
  67.8 5.8 %collective-permute-start.15 = (bf16[64,256]{1,0:T(8,128)(2,1)S(1)}, bf16[64,256]{1,0:T(8,128)(2,1)S(1)}, u32[]{:S(2)}, u32[]{:S(2)}) collective-permute-start(bf16[64,256]{1,0:T(8,128)(2,1)S(1)} %get-tuple-element.12), channel_id=1, source_target_pairs={{0,24},{2,26},{4,28},{6,30},{8,16},{10,18},{12,20},{14,22},{16,8},... | collective-permute-start | bytes 98312 | tf_op jit(solution)/shard_map/ppermute | solution.py:97
  70.2 6.6 %collective-permute-start.16 = (bf16[64,256]{1,0:T(8,128)(2,1)S(1)}, bf16[64,256]{1,0:T(8,128)(2,1)S(1)}, u32[]{:S(2)}, u32[]{:S(2)}) collective-permute-start(bf16[64,256]{1,0:T(8,128)(2,1)S(1)} %get-tuple-element.12), channel_id=1, source_target_pairs={{0,28},{2,30},{4,24},{6,26},{8,20},{10,22},{12,16},{14,18},{16,12}... | collective-permute-start | bytes 98312 | tf_op jit(solution)/shard_map/ppermute | solution.py:97
  77.0 1.8 %collective-permute-start.17 = (bf16[512,256]{1,0:T(8,128)(2,1)S(1)}, bf16[512,256]{1,0:T(8,128)(2,1)S(1)}, u32[]{:S(2)}, u32[]{:S(2)}) collective-permute-start(bf16[512,256]{1,0:T(8,128)(2,1)S(1)} %constant_dynamic-update-slice_fusion.8), channel_id=1, source_target_pairs={{0,2},{2,0},{4,6},{6,4},{8,10},{10,8},{12,14},{14,12},{16,18},{18,... | collective-permute-start | bytes 786440 | tf_op jit(solution)/shard_map/ppermute | solution.py:97

commit v5 on v4

--- a/solution.py
+++ b/solution.py
@@ -184,18 +184,15 @@
     item_part = transposed_product(rating_errors, user_factors) + jnp.dot(
         link_errors, tag_factors, preferred_element_type=jnp.float32
     )
+    (item_share,), (item_offset,) = halving_scatter([item_part], "group", group_count, group_position)
     if got is not None:
-        item_part, _ = lax.optimization_barrier((item_part, got))
-    group_stages = radix_stages(group_count)
-    item_share, item_offset = radix_scatter(
-        item_part, "group", group_count, group_position, group_stages
-    )
+        item_share, _ = lax.optimization_barrier((item_share, got))
     fresh_items = advance(
         lax.dynamic_slice_in_dim(item_factors, item_offset, item_share.shape[0], 0),
         item_share,
         step_items,
     )
-    new_items = radix_gather(fresh_items, "group", group_count, group_position, group_stages)
+    (new_items,) = doubling_gather([fresh_items], "group", group_count, group_position)
     return (new_users, new_items, new_tags)
 
 

time: 80.1 us -> 74.1 us (0.925)
  starting transfers between devices: 28.1 us -> 16.1 us
  matrix products: 7.52 us -> 10.6 us
  other arithmetic: 5.82 us -> 8.25 us
  local copies, waits for them, and re-layouts: 6.55 us -> 7.38 us
    ppermute x1, waiting for transfers between devices: 20.1 us -> 8.87 us  [loop_pair_step(): got = lax.ppermute(sent, 'loop', [(0, 1), (1, 0)])]
    ppermute x16 -> x8, starting transfers between devices: 23.3 us -> 12.8 us  [the longest x4 8.01 us: halving_scatter(): got = lax.ppermute(tuple(sent), axis, xor_pairs(count, bit))]
    ppermute x16 -> x8, waiting for transfers between devices: 10.8 us -> 17.6 us  [the longest x4 9.96 us: halving_scatter(): got = lax.ppermute(tuple(sent), axis, xor_pairs(count, bit))]
    ppermute x1, waiting for transfers between devices: 0.01 us -> 4.1 us  [loop_pair_step(): other = lax.ppermute(fresh, 'loop', [(0, 1), (1, 0)])]
    dot_general x3, matrix products: 1.7 us -> 3.87 us  [transposed_product(): lax.dot_general(first_operand, second_operand, (((0,), (0,)), ((), ())),...]
    ppermute x1, starting transfers between devices: 2.97 us -> 1.52 us  [loop_pair_step(): got = lax.ppermute(sent, 'loop', [(0, 1), (1, 0)])]
    add x1, other arithmetic: 0.15 us -> 1.39 us  [loop_pair_step(): total = partial(side) + got]
    select_n x0 -> x4, other arithmetic: none -> 1.17 us  [doubling_gather(): jnp.where(side == 0, jnp.concatenate([m, g], 0), jnp.concatenate([g, m], 0))]
  transfers between devices with their start and end apart: 18 -> 10, of which waited for: 6 -> 10; matrix products, arithmetic and copies ran while one was open for 8% -> 7% of each run, Pallas kernels for 0% -> 0%
where the time goes in v5:
time: 74.1 us; the launch traced here: 73.7 us
  waiting for transfers between devices  30.6 us (41%)
  starting transfers between devices  16.1 us (22%)
  matrix products  10.6 us (14%)
  other arithmetic  8.25 us (11%)
  local copies, waits for them, and re-layouts  7.38 us (10%)
  between operations  0.89 us (1%)
    ppermute x4, waiting for transfers between devices, halving_scatter(): got = lax.ppermute(tuple(sent), axis, xor_pairs(count, bit))  9.96 us
    ppermute x1, waiting for transfers between devices, loop_pair_step(): got = lax.ppermute(sent, 'loop', [(0, 1), (1, 0)])  8.87 us
    ppermute x4, starting transfers between devices, halving_scatter(): got = lax.ppermute(tuple(sent), axis, xor_pairs(count, bit))  8.01 us
    ppermute x4, waiting for transfers between devices, doubling_gather(): got = lax.ppermute(tuple(parts), axis, xor_pairs(count, bit))  7.64 us
    unnamed x17, local copies, waits for them, and re-layouts  6.45 us
    ppermute x4, starting transfers between devices, doubling_gather(): got = lax.ppermute(tuple(parts), axis, xor_pairs(count, bit))  4.81 us
    ppermute x1, waiting for transfers between devices, loop_pair_step(): other = lax.ppermute(fresh, 'loop', [(0, 1), (1, 0)])  4.1 us
    dot_general x2, matrix products, partial(): jnp.dot(lax.dynamic_slice_in_dim(rating_errors, rows_side * user_half, us...  4.02 us
  transfers between devices with their start and end apart: 10, of which 10 were waited for; matrix products, arithmetic and copies ran while one was open for 7% of the time, Pallas kernels for 0%

profile of v5, /device:TPU:0, one launch (start us, length us, event | category | flops | bytes accessed | tf_op | source)
XLA Modules:
  0.0 73.7 jit_solution(16084552357609509867)
XLA Ops:
  1.4 1.1 %copy.11 = bf16[1024,128]{0,1:T(8,128)(2,1)S(1)} copy(bf16[1024,128]{1,0:T(8,128)(2,1)} %param.12) | data formatting | bytes 524288 | tf_op args[5]
  4.3 1.3 %copy-done.1 = bf16[2048,1024]{1,0:T(8,128)(2,1)S(1)} copy-done((bf16[2048,1024]{1,0:T(8,128)(2,1)S(1)}, bf16[2048,1024]{1,0:T(8,128)(2,1)}, u32[]{:S(2)}) %copy-start.1) | copy-done | bytes 4194328
  5.9 2.0 %fusion = bf16[2048,1024]{1,0:T(8,128)(2,1)S(1)} fusion(f32[256,8,8,128]{3,2,1,0:T(8,128)S(1)} %bitcast.22, bf16[2048,1024]{1,0:T(8,128)(2,1)S(1)} %copy-done.1, bf16[2048,256]{1,0:T(8,128)(2,1)S(1)} %copy-done.3, bf16[1024,256]{1,0:T(8,128)(2,1)S(1)} %copy-done), kind=kOutput, calls=%fused_computation.1 | convolution fusion | flops 1082130432 | bytes 18350080 | tf_op jit(solution)/shard_map/dot_general | solution.py:19
  7.9 1.9 %copy-done.2 = bf16[2048,1024]{1,0:T(8,128)(2,1)} copy-done((bf16[2048,1024]{1,0:T(8,128)(2,1)}, bf16[2048,1024]{1,0:T(8,128)(2,1)S(1)}, u32[]{:S(2)}) %copy-start.2) | copy-done | bytes 4194328
  9.9 1.7 %fusion.3 = f32[1024,256]{1,0:T(8,128)} fusion(bf16[1024,256]{1,0:T(8,128)(2,1)S(1)} %copy-done, bf16[2048,1024]{1,0:T(8,128)(2,1)S(1)} %fusion, s32[]{:T(128)S(6)} %select_n.87), kind=kOutput, calls=%fused_computation.4 | convolution fusion | flops 536870912 | bytes 3670020 | tf_op jit(solution)/shard_map/dot_general | solution.py:114
  13.9 3.5 %fusion.19 = f32[1024,256]{1,0:T(8,128)S(1)} fusion(bf16[2048,1024]{1,0:T(8,128)(2,1)} %copy-done.2, bf16[2048,256]{1,0:T(8,128)(2,1)S(1)} %copy-done.3), kind=kOutput, calls=%fused_computation.46 | convolution fusion | flops 1073741824 | bytes 6291456 | tf_op jit(solution)/shard_map/dot_general | solution.py:26
  18.2 1.7 %collective-permute-done.2 = f32[512,256]{1,0:T(8,128)} collective-permute-done((f32[512,256]{1,0:T(8,128)S(1)}, f32[512,256]{1,0:T(8,128)}, u32[]{:S(2)}, u32[]{:S(2)}) %collective-permute-start.2) | collective-permute-done | bytes 524320 | tf_op jit(solution)/shard_map/ppermute | solution.py:48
  19.9 1.1 %dynamic-slice_add_fusion = f32[512,256]{1,0:T(8,128)S(1)} fusion(f32[512,256]{1,0:T(8,128)} %collective-permute-done.2, f32[1024,256]{1,0:T(8,128)S(1)} %convolution_add_fusion, s32[]{:T(128)S(6)} %select_n.97), kind=kLoop, calls=%fused_computation.20 | loop fusion | flops 131072 | bytes 1572868 | tf_op jit(solution)/shard_map/add | solution.py:49
  21.1 2.9 %collective-permute-start.3 = (f32[256,256]{1,0:T(8,128)S(1)}, f32[256,256]{1,0:T(8,128)S(1)}, u32[]{:S(2)}, u32[]{:S(2)}) collective-permute-start(f32[256,256]{1,0:T(8,128)S(1)} %constant_dynamic-slice_fusion.2), channel_id=1, source_target_pairs={{0,4},{2,6},{4,0},{6,2},{8,12},{10,14},{12,8},{14,10},{16,20},{18,... | collective-permute-start | bytes 786440 | tf_op jit(solution)/shard_map/ppermute | solution.py:48
  24.0 1.5 %collective-permute-start = (f32[1088,256]{1,0:T(8,128)}, f32[1088,256]{1,0:T(8,128)}, u32[]{:S(2)}, u32[]{:S(2)}) collective-permute-start(f32[1088,256]{1,0:T(8,128)} %pad_maximum_fusion), channel_id=1, source_target_pairs={{0,1},{1,0},{2,3},{3,2},{4,5},{5,4},{6,7},{7,6},{8,9},{9,8},{10,11... | collective-permute-start | bytes 3342344 | tf_op jit(solution)/shard_map/ppermute | solution.py:127
  25.5 5.1 %collective-permute-done.3 = f32[256,256]{1,0:T(8,128)S(1)} collective-permute-done((f32[256,256]{1,0:T(8,128)S(1)}, f32[256,256]{1,0:T(8,128)S(1)}, u32[]{:S(2)}, u32[]{:S(2)}) %collective-permute-start.3) | collective-permute-done | bytes 262176 | tf_op jit(solution)/shard_map/ppermute | solution.py:48
  31.3 1.8 %collective-permute-start.4 = (f32[128,256]{1,0:T(8,128)S(1)}, f32[128,256]{1,0:T(8,128)S(1)}, u32[]{:S(2)}, u32[]{:S(2)}) collective-permute-start(f32[128,256]{1,0:T(8,128)S(1)} %constant_dynamic-slice_fusion.1), channel_id=1, source_target_pairs={{0,8},{2,10},{4,12},{6,14},{8,0},{10,2},{12,4},{14,6},{16,24},{18,... | collective-permute-start | bytes 393224 | tf_op jit(solution)/shard_map/ppermute | solution.py:48
  33.2 2.3 %fusion.1 = f32[1024,256]{1,0:T(8,128)S(1)} fusion(bf16[1024,256]{1,0:T(8,128)(2,1)S(1)} %copy-done, bf16[2048,1024]{1,0:T(8,128)(2,1)} %copy-done.2, s32[]{:T(128)S(6)} %select_n.86), kind=kOutput, calls=%fused_computation.2 | convolution fusion | flops 536870912 | bytes 3670020 | tf_op jit(solution)/shard_map/dot_general | solution.py:114
  36.5 2.7 %collective-permute-start.5 = (f32[64,256]{1,0:T(8,128)S(1)}, f32[64,256]{1,0:T(8,128)S(1)}, u32[]{:S(2)}, u32[]{:S(2)}) collective-permute-start(f32[64,256]{1,0:T(8,128)S(1)} %constant_dynamic-slice_fusion), channel_id=1, source_target_pairs={{0,16},{2,18},{4,20},{6,22},{8,24},{10,26},{12,28},{14,30},{16,0},... | collective-permute-start | bytes 196616 | tf_op jit(solution)/shard_map/ppermute | solution.py:48
  39.5 2.3 %collective-permute-done.5 = f32[64,256]{1,0:T(8,128)S(1)} collective-permute-done((f32[64,256]{1,0:T(8,128)S(1)}, f32[64,256]{1,0:T(8,128)S(1)}, u32[]{:S(2)}, u32[]{:S(2)}) %collective-permute-start.5) | collective-permute-done | bytes 65568 | tf_op jit(solution)/shard_map/ppermute | solution.py:48
  41.8 8.9 %collective-permute-done = f32[1088,256]{1,0:T(8,128)} collective-permute-done((f32[1088,256]{1,0:T(8,128)}, f32[1088,256]{1,0:T(8,128)}, u32[]{:S(2)}, u32[]{:S(2)}) %collective-permute-start) | collective-permute-done | bytes 1114144 | tf_op jit(solution)/shard_map/ppermute | solution.py:127
  50.6 2.7 %collective-permute-start.6 = (bf16[64,256]{1,0:T(8,128)(2,1)S(1)}, bf16[64,256]{1,0:T(8,128)(2,1)S(1)}, u32[]{:S(2)}, u32[]{:S(2)}) collective-permute-start(bf16[64,256]{1,0:T(8,128)(2,1)S(1)} %add_convert_fusion), channel_id=1, source_target_pairs={{0,16},{2,18},{4,20},{6,22},{8,24},{10,26},{12,28},{14,30},{16,0},... | collective-permute-start | bytes 98312 | tf_op jit(solution)/shard_map/ppermute | solution.py:58
  53.3 1.4 %maximum_add_fusion = f32[1088,256]{1,0:T(8,128)S(1)} fusion(f32[1088,256]{1,0:T(8,128)} %collective-permute-done, f32[64,256]{1,0:T(8,128)S(1)} %fusion.9, f32[1024,256]{1,0:T(8,128)S(1)} %fusion.1), kind=kLoop, calls=%fused_computation.11 | loop fusion | flops 557056 | bytes 3342336 | tf_op jit(solution)/shard_map/add | solution.py:128
  55.5 1.6 %collective-permute-start.7 = (bf16[128,256]{1,0:T(8,128)(2,1)S(1)}, bf16[128,256]{1,0:T(8,128)(2,1)S(1)}, u32[]{:S(2)}, u32[]{:S(2)}) collective-permute-start(bf16[128,256]{1,0:T(8,128)(2,1)S(1)} %maximum_select_fusion.3), channel_id=1, source_target_pairs={{0,8},{2,10},{4,12},{6,14},{8,0},{10,2},{12,4},{14,6},{16,24},{18,... | collective-permute-start | bytes 196616 | tf_op jit(solution)/shard_map/ppermute | solution.py:58
  57.2 2.7 %collective-permute-done.7 = bf16[128,256]{1,0:T(8,128)(2,1)S(1)} collective-permute-done((bf16[128,256]{1,0:T(8,128)(2,1)S(1)}, bf16[128,256]{1,0:T(8,128)(2,1)S(1)}, u32[]{:S(2)}, u32[]{:S(2)}) %collective-permute-start.7) | collective-permute-done | bytes 65568 | tf_op jit(solution)/shard_map/ppermute | solution.py:58
  60.4 1.8 %collective-permute-start.1 = (bf16[1088,256]{1,0:T(8,128)(2,1)S(1)}, bf16[1088,256]{1,0:T(8,128)(2,1)S(1)}, u32[]{:S(2)}, u32[]{:S(2)}) collective-permute-start(bf16[1088,256]{1,0:T(8,128)(2,1)S(1)} %pad_maximum_fusion.2), channel_id=1, source_target_pairs={{0,1},{1,0},{2,3},{3,2},{4,5},{5,4},{6,7},{7,6},{8,9},{9,8},{10,11... | collective-permute-start | bytes 1671176 | tf_op jit(solution)/shard_map/ppermute | solution.py:144
  62.1 2.8 %collective-permute-done.8 = bf16[256,256]{1,0:T(8,128)(2,1)S(1)} collective-permute-done((bf16[256,256]{1,0:T(8,128)(2,1)S(1)}, bf16[256,256]{1,0:T(8,128)(2,1)S(1)}, u32[]{:S(2)}, u32[]{:S(2)}) %collective-permute-start.8) | collective-permute-done | bytes 131104 | tf_op jit(solution)/shard_map/ppermute | solution.py:58
  65.1 1.5 %collective-permute-done.9 = bf16[512,256]{1,0:T(8,128)(2,1)S(1)} collective-permute-done((bf16[512,256]{1,0:T(8,128)(2,1)S(1)}, bf16[512,256]{1,0:T(8,128)(2,1)S(1)}, u32[]{:S(2)}, u32[]{:S(2)}) %collective-permute-start.9) | collective-permute-done | bytes 262176 | tf_op jit(solution)/shard_map/ppermute | solution.py:58
  67.7 4.1 %collective-permute-done.1 = bf16[1088,256]{1,0:T(8,128)(2,1)S(1)} collective-permute-done((bf16[1088,256]{1,0:T(8,128)(2,1)S(1)}, bf16[1088,256]{1,0:T(8,128)(2,1)S(1)}, u32[]{:S(2)}, u32[]{:S(2)}) %collective-permute-start.1) | collective-permute-done | bytes 557088 | tf_op jit(solution)/shard_map/ppermute | solution.py:144
  (51 shorter events, 12.4 us)
Async XLA Ops:
  3.2 1.0 %copy-start = (bf16[1024,256]{1,0:T(8,128)(2,1)S(1)}, bf16[1024,256]{1,0:T(8,128)(2,1)}, u32[]{:S(2)}) copy-start(bf16[1024,256]{1,0:T(8,128)(2,1)} %param.8) | copy-start | bytes 1572868
  3.2 2.4 %copy-start.1 = (bf16[2048,1024]{1,0:T(8,128)(2,1)S(1)}, bf16[2048,1024]{1,0:T(8,128)(2,1)}, u32[]{:S(2)}) copy-start(bf16[2048,1024]{1,0:T(8,128)(2,1)} %param.10) | copy-start | bytes 12582916
  3.2 2.6 %copy-start.3 = (bf16[2048,256]{1,0:T(8,128)(2,1)S(1)}, bf16[2048,256]{1,0:T(8,128)(2,1)}, u32[]{:S(2)}) copy-start(bf16[2048,256]{1,0:T(8,128)(2,1)} %param.7) | copy-start | bytes 3145732
  7.9 2.0 %copy-start.2 = (bf16[2048,1024]{1,0:T(8,128)(2,1)}, bf16[2048,1024]{1,0:T(8,128)(2,1)S(1)}, u32[]{:S(2)}) copy-start(bf16[2048,1024]{1,0:T(8,128)(2,1)S(1)} %fusion) | copy-start | bytes 12582916
  9.9 1.7 %copy-start.7 = (bf16[128,256]{1,0:T(8,128)(2,1)S(1)}, bf16[128,256]{1,0:T(8,128)(2,1)}, u32[]{:S(2)}) copy-start(bf16[128,256]{1,0:T(8,128)(2,1)} %param.9) | copy-start | bytes 196612
  11.6 1.2 %copy-start.4 = (f32[1024,256]{1,0:T(8,128)S(1)}, f32[1024,256]{1,0:T(8,128)}, u32[]{:S(2)}) copy-start(f32[1024,256]{1,0:T(8,128)} %fusion.3) | copy-start | bytes 3145732
  17.7 2.2 %collective-permute-start.2 = (f32[512,256]{1,0:T(8,128)S(1)}, f32[512,256]{1,0:T(8,128)}, u32[]{:S(2)}, u32[]{:S(2)}) collective-permute-start(f32[512,256]{1,0:T(8,128)S(1)} %constant_dynamic-slice_fusion.3), channel_id=1, source_target_pairs={{0,2},{2,0},{4,6},{6,4},{8,10},{10,8},{12,14},{14,12},{16,18},{18,... | collective-permute-start | bytes 1572872 | tf_op jit(solution)/shard_map/ppermute | solution.py:48
  21.1 9.5 %collective-permute-start.3 = (f32[256,256]{1,0:T(8,128)S(1)}, f32[256,256]{1,0:T(8,128)S(1)}, u32[]{:S(2)}, u32[]{:S(2)}) collective-permute-start(f32[256,256]{1,0:T(8,128)S(1)} %constant_dynamic-slice_fusion.2), channel_id=1, source_target_pairs={{0,4},{2,6},{4,0},{6,2},{8,12},{10,14},{12,8},{14,10},{16,20},{18,... | collective-permute-start | bytes 786440 | tf_op jit(solution)/shard_map/ppermute | solution.py:48
  24.0 26.6 %collective-permute-start = (f32[1088,256]{1,0:T(8,128)}, f32[1088,256]{1,0:T(8,128)}, u32[]{:S(2)}, u32[]{:S(2)}) collective-permute-start(f32[1088,256]{1,0:T(8,128)} %pad_maximum_fusion), channel_id=1, source_target_pairs={{0,1},{1,0},{2,3},{3,2},{4,5},{5,4},{6,7},{7,6},{8,9},{9,8},{10,11... | collective-permute-start | bytes 3342344 | tf_op jit(solution)/shard_map/ppermute | solution.py:127
  30.6 0.7 copy-start.5
  31.3 5.1 %collective-permute-start.4 = (f32[128,256]{1,0:T(8,128)S(1)}, f32[128,256]{1,0:T(8,128)S(1)}, u32[]{:S(2)}, u32[]{:S(2)}) collective-permute-start(f32[128,256]{1,0:T(8,128)S(1)} %constant_dynamic-slice_fusion.1), channel_id=1, source_target_pairs={{0,8},{2,10},{4,12},{6,14},{8,0},{10,2},{12,4},{14,6},{16,24},{18,... | collective-permute-start | bytes 393224 | tf_op jit(solution)/shard_map/ppermute | solution.py:48
  33.2 3.3 %copy-start.6 = (f32[256,256]{1,0:T(8,128)S(1)}, f32[256,256]{1,0:T(8,128)}, u32[]{:S(2)}) copy-start(f32[256,256]{1,0:T(8,128)} %copy-done.5) | copy-start | bytes 786436
  36.5 5.2 %collective-permute-start.5 = (f32[64,256]{1,0:T(8,128)S(1)}, f32[64,256]{1,0:T(8,128)S(1)}, u32[]{:S(2)}, u32[]{:S(2)}) collective-permute-start(f32[64,256]{1,0:T(8,128)S(1)} %constant_dynamic-slice_fusion), channel_id=1, source_target_pairs={{0,16},{2,18},{4,20},{6,22},{8,24},{10,26},{12,28},{14,30},{16,0},... | collective-permute-start | bytes 196616 | tf_op jit(solution)/shard_map/ppermute | solution.py:48
  50.6 4.9 %collective-permute-start.6 = (bf16[64,256]{1,0:T(8,128)(2,1)S(1)}, bf16[64,256]{1,0:T(8,128)(2,1)S(1)}, u32[]{:S(2)}, u32[]{:S(2)}) collective-permute-start(bf16[64,256]{1,0:T(8,128)(2,1)S(1)} %add_convert_fusion), channel_id=1, source_target_pairs={{0,16},{2,18},{4,20},{6,22},{8,24},{10,26},{12,28},{14,30},{16,0},... | collective-permute-start | bytes 98312 | tf_op jit(solution)/shard_map/ppermute | solution.py:58
  55.5 4.3 %collective-permute-start.7 = (bf16[128,256]{1,0:T(8,128)(2,1)S(1)}, bf16[128,256]{1,0:T(8,128)(2,1)S(1)}, u32[]{:S(2)}, u32[]{:S(2)}) collective-permute-start(bf16[128,256]{1,0:T(8,128)(2,1)S(1)} %maximum_select_fusion.3), channel_id=1, source_target_pairs={{0,8},{2,10},{4,12},{6,14},{8,0},{10,2},{12,4},{14,6},{16,24},{18,... | collective-permute-start | bytes 196616 | tf_op jit(solution)/shard_map/ppermute | solution.py:58
  59.9 5.0 %collective-permute-start.8 = (bf16[256,256]{1,0:T(8,128)(2,1)S(1)}, bf16[256,256]{1,0:T(8,128)(2,1)S(1)}, u32[]{:S(2)}, u32[]{:S(2)}) collective-permute-start(bf16[256,256]{1,0:T(8,128)(2,1)S(1)} %maximum_select_fusion.2), channel_id=1, source_target_pairs={{0,4},{2,6},{4,0},{6,2},{8,12},{10,14},{12,8},{14,10},{16,20},{18,... | collective-permute-start | bytes 393224 | tf_op jit(solution)/shard_map/ppermute | solution.py:58
  60.4 11.4 %collective-permute-start.1 = (bf16[1088,256]{1,0:T(8,128)(2,1)S(1)}, bf16[1088,256]{1,0:T(8,128)(2,1)S(1)}, u32[]{:S(2)}, u32[]{:S(2)}) collective-permute-start(bf16[1088,256]{1,0:T(8,128)(2,1)S(1)} %pad_maximum_fusion.2), channel_id=1, source_target_pairs={{0,1},{1,0},{2,3},{3,2},{4,5},{5,4},{6,7},{7,6},{8,9},{9,8},{10,11... | collective-permute-start | bytes 1671176 | tf_op jit(solution)/shard_map/ppermute | solution.py:144
  65.0 1.6 %collective-permute-start.9 = (bf16[512,256]{1,0:T(8,128)(2,1)S(1)}, bf16[512,256]{1,0:T(8,128)(2,1)S(1)}, u32[]{:S(2)}, u32[]{:S(2)}) collective-permute-start(bf16[512,256]{1,0:T(8,128)(2,1)S(1)} %maximum_select_fusion.1), channel_id=1, source_target_pairs={{0,2},{2,0},{4,6},{6,4},{8,10},{10,8},{12,14},{14,12},{16,18},{18,... | collective-permute-start | bytes 786440 | tf_op jit(solution)/shard_map/ppermute | solution.py:58

commit v6 on v3

--- a/solution.py
+++ b/solution.py
@@ -50,9 +50,11 @@
     return parts, offsets
 
 
-def doubling_gather(parts, axis, count, position):
+def doubling_gather(parts, axis, count, position, tie=None, tie_step=-1):
     steps = count.bit_length() - 1
     for bit in reversed(range(steps)):
+        if bit == tie_step and tie is not None:
+            parts, _ = lax.optimization_barrier((parts, tie))
         side = (position >> bit) & 1
         got = lax.ppermute(tuple(parts), axis, xor_pairs(count, bit))
         parts = [
@@ -103,7 +105,9 @@
         item_share,
         step_items,
     )
-    (new_items,) = doubling_gather([fresh_items], "group", group_count, group_position)
+    (new_items,) = doubling_gather(
+        [fresh_items], "group", group_count, group_position, new_joint, 1
+    )
     return (new_users, new_items, new_tags)
 
 

time: 64.7 us -> 67.4 us (1.042)
  waiting for transfers between devices: 25.2 us -> 28.6 us
  starting transfers between devices: 17.9 us -> 16.6 us
    ppermute x5, waiting for transfers between devices: 11.4 us -> 16.8 us  [halving_scatter(): got = lax.ppermute(tuple(sent), axis, xor_pairs(count, bit))]
    ppermute x5, waiting for transfers between devices: 13.8 us -> 11.8 us  [doubling_gather(): got = lax.ppermute(tuple(parts), axis, xor_pairs(count, bit))]
    ppermute x5, starting transfers between devices: 9.65 us -> 8.84 us  [halving_scatter(): got = lax.ppermute(tuple(sent), axis, xor_pairs(count, bit))]
  transfers between devices with their start and end apart: 10 -> 10, of which waited for: 8 -> 7; matrix products, arithmetic and copies ran while one was open for 8% -> 11% of each run, Pallas kernels for 0% -> 0%
where the time goes in v6:
time: 67.4 us; the launch traced here: 67.1 us
  waiting for transfers between devices  28.6 us (42%)
  starting transfers between devices  16.6 us (25%)
  matrix products  7.55 us (11%)
  local copies, waits for them, and re-layouts  7.28 us (11%)
  other arithmetic  6.3 us (9%)
  between operations  0.82 us (1%)
    ppermute x5, waiting for transfers between devices, halving_scatter(): got = lax.ppermute(tuple(sent), axis, xor_pairs(count, bit))  16.8 us
    ppermute x5, waiting for transfers between devices, doubling_gather(): got = lax.ppermute(tuple(parts), axis, xor_pairs(count, bit))  11.8 us
    ppermute x5, starting transfers between devices, halving_scatter(): got = lax.ppermute(tuple(sent), axis, xor_pairs(count, bit))  8.84 us
    ppermute x5, starting transfers between devices, doubling_gather(): got = lax.ppermute(tuple(parts), axis, xor_pairs(count, bit))  7.73 us
    unnamed x14, local copies, waits for them, and re-layouts  3.05 us
    dot_general x2, matrix products, transposed_product(): lax.dot_general(first_operand, second_operand, (((0,), (0,)), ((), ())),...  2.52 us
    add x3, other arithmetic, halving_scatter(): parts = [k + g for k, g in zip(kept, got)]  2.27 us
    dot_general x2, matrix products, residual_of(): lax.dot_general(row_factors, column_factors, (((1,), (1,)), ((), ())), pr...  2.26 us
  transfers between devices with their start and end apart: 10, of which 7 were waited for; matrix products, arithmetic and copies ran while one was open for 11% of the time, Pallas kernels for 0%

profile of v6, /device:TPU:0, one launch (start us, length us, event | category | flops | bytes accessed | tf_op | source)
XLA Modules:
  0.0 67.1 jit_solution(7905640311379476022)
XLA Ops:
  2.8 1.3 %copy-done.3 = bf16[2048,1024]{1,0:T(8,128)(2,1)S(1)} copy-done((bf16[2048,1024]{1,0:T(8,128)(2,1)S(1)}, bf16[2048,1024]{1,0:T(8,128)(2,1)}, u32[]{:S(2)}) %copy-start.3) | copy-done | bytes 4194328
  4.1 1.9 %fusion = bf16[2048,1024]{1,0:T(8,128)(2,1)S(1)} fusion(f32[256,8,8,128]{3,2,1,0:T(8,128)S(1)} %bitcast.22, bf16[2048,1024]{1,0:T(8,128)(2,1)S(1)} %copy-done.3, bf16[2048,256]{1,0:T(8,128)(2,1)S(1)} %copy-done.1, bf16[1024,256]{1,0:T(8,128)(2,1)S(1)} %copy-done), kind=kOutput, calls=%fused_computation.1 | convolution fusion | flops 1082130432 | bytes 18350080 | tf_op jit(solution)/shard_map/dot_general | solution.py:19
  6.1 1.3 %fusion.4 = f32[2048,256]{1,0:T(8,128)S(1)} fusion(bf16[2048,1024]{1,0:T(8,128)(2,1)S(1)} %fusion, bf16[1024,256]{1,0:T(8,128)(2,1)S(1)} %copy-done), kind=kOutput, calls=%fused_computation.27 | convolution fusion | flops 1073741824 | bytes 6815744 | tf_op jit(solution)/shard_map/dot_general | solution.py:75
  8.2 2.2 %fusion.6 = f32[1024,256]{1,0:T(8,128)} fusion(bf16[2048,1024]{1,0:T(8,128)(2,1)S(1)} %fusion, bf16[2048,256]{1,0:T(8,128)(2,1)S(1)} %copy-done.1), kind=kOutput, calls=%fused_computation.29 | convolution fusion | flops 1073741824 | bytes 6291456 | tf_op jit(solution)/shard_map/dot_general | solution.py:26
  10.5 1.5 %convolution_add_fusion = f32[1024,256]{1,0:T(8,128)S(1)} fusion(f32[1024,256]{1,0:T(8,128)} %fusion.6, bf16[1024,128]{1,0:T(8,128)(2,1)S(1)} %fusion.2, bf16[128,256]{1,0:T(8,128)(2,1)S(1)} %copy-done.4), kind=kOutput, calls=%fused_computation.3 | convolution fusion | flops 67371008 | bytes 2424832 | tf_op jit(solution)/shard_map/dot_general | solution.py:85
  13.5 1.1 %constant_dynamic-slice_fusion.3 = f32[1088,256]{1,0:T(8,128)} fusion(f32[2176,256]{1,0:T(8,128)S(1)} %pad_maximum_fusion, s32[]{:T(128)S(6)} %select_n.78), kind=kLoop, calls=%fused_computation.23 | loop fusion | bytes 2228228 | tf_op jit(solution)/shard_map/dynamic_slice | solution.py:46
  14.6 2.5 %collective-permute-start = (f32[1088,256]{1,0:T(8,128)}, f32[1088,256]{1,0:T(8,128)}, u32[]{:S(2)}, u32[]{:S(2)}) collective-permute-start(f32[1088,256]{1,0:T(8,128)} %constant_dynamic-slice_fusion.3), channel_id=1, source_target_pairs={{0,1},{1,0},{2,3},{3,2},{4,5},{5,4},{6,7},{7,6},{8,9},{9,8},{10,11... | collective-permute-start | bytes 3342344 | tf_op jit(solution)/shard_map/ppermute | solution.py:47
  17.1 1.3 %dynamic-slice_add_fusion = f32[512,256]{1,0:T(8,128)S(1)} fusion(f32[512,256]{1,0:T(8,128)} %collective-permute-done.2, f32[1024,256]{1,0:T(8,128)} %copy-done.2, s32[]{:T(128)S(6)} %select_n.85), kind=kLoop, calls=%fused_computation.13 | loop fusion | flops 131072 | bytes 1572868 | tf_op jit(solution)/shard_map/add | solution.py:48
  18.4 1.6 %collective-permute-start.3 = (f32[256,256]{1,0:T(8,128)S(1)}, f32[256,256]{1,0:T(8,128)}, u32[]{:S(2)}, u32[]{:S(2)}) collective-permute-start(f32[256,256]{1,0:T(8,128)S(1)} %constant_dynamic-slice_fusion.1), channel_id=1, source_target_pairs={{0,4},{2,6},{4,0},{6,2},{8,12},{10,14},{12,8},{14,10},{16,20},{18,... | collective-permute-start | bytes 786440 | tf_op jit(solution)/shard_map/ppermute | solution.py:47
  20.0 7.0 %collective-permute-done.3 = f32[256,256]{1,0:T(8,128)} collective-permute-done((f32[256,256]{1,0:T(8,128)S(1)}, f32[256,256]{1,0:T(8,128)}, u32[]{:S(2)}, u32[]{:S(2)}) %collective-permute-start.3) | collective-permute-done | bytes 262176 | tf_op jit(solution)/shard_map/ppermute | solution.py:47
  28.0 1.6 %collective-permute-start.4 = (f32[128,256]{1,0:T(8,128)S(1)}, f32[128,256]{1,0:T(8,128)S(1)}, u32[]{:S(2)}, u32[]{:S(2)}) collective-permute-start(f32[128,256]{1,0:T(8,128)S(1)} %constant_dynamic-slice_fusion), channel_id=1, source_target_pairs={{0,8},{2,10},{4,12},{6,14},{8,0},{10,2},{12,4},{14,6},{16,24},{18,... | collective-permute-start | bytes 393224 | tf_op jit(solution)/shard_map/ppermute | solution.py:47
  29.7 3.4 %collective-permute-done.4 = f32[128,256]{1,0:T(8,128)S(1)} collective-permute-done((f32[128,256]{1,0:T(8,128)S(1)}, f32[128,256]{1,0:T(8,128)S(1)}, u32[]{:S(2)}, u32[]{:S(2)}) %collective-permute-start.4) | collective-permute-done | bytes 131104 | tf_op jit(solution)/shard_map/ppermute | solution.py:47
  33.7 2.6 %collective-permute-start.5 = (f32[64,256]{1,0:T(8,128)}, f32[64,256]{1,0:T(8,128)S(1)}, u32[]{:S(2)}, u32[]{:S(2)}) collective-permute-start(f32[64,256]{1,0:T(8,128)} %constant_dynamic-slice_fusion.4), channel_id=1, source_target_pairs={{0,16},{2,18},{4,20},{6,22},{8,24},{10,26},{12,28},{14,30},{16,0},... | collective-permute-start | bytes 196616 | tf_op jit(solution)/shard_map/ppermute | solution.py:47
  36.3 6.3 %collective-permute-done = f32[1088,256]{1,0:T(8,128)} collective-permute-done((f32[1088,256]{1,0:T(8,128)}, f32[1088,256]{1,0:T(8,128)}, u32[]{:S(2)}, u32[]{:S(2)}) %collective-permute-start) | collective-permute-done | bytes 1114144 | tf_op jit(solution)/shard_map/ppermute | solution.py:47
  42.6 1.8 %add_convert_fusion = bf16[1088,256]{1,0:T(8,128)(2,1)S(1)} fusion(f32[1088,256]{1,0:T(8,128)} %collective-permute-done, f32[2176,256]{1,0:T(8,128)S(1)} %pad_maximum_fusion, s32[]{:T(128)S(6)} %select_n.77, bf16[2048,256]{1,0:T(8,128)(2,1)} %param.7, bf16[128,256]{1,0:T(8,128)(2,1)} %param.9), kind=kLoop, calls=%fused_computation.10 | loop fusion | flops 2228224 | bytes 3899396 | tf_op jit(solution)/shard_map/convert_element_type | solution.py:32
  44.4 1.8 %collective-permute-start.1 = (bf16[1088,256]{1,0:T(8,128)(2,1)S(1)}, bf16[1088,256]{1,0:T(8,128)(2,1)S(1)}, u32[]{:S(2)}, u32[]{:S(2)}) collective-permute-start(bf16[1088,256]{1,0:T(8,128)(2,1)S(1)} %add_convert_fusion), channel_id=1, source_target_pairs={{0,1},{1,0},{2,3},{3,2},{4,5},{5,4},{6,7},{7,6},{8,9},{9,8},{10,11... | collective-permute-start | bytes 1671176 | tf_op jit(solution)/shard_map/ppermute | solution.py:59
  46.2 2.6 %collective-permute-start.6 = (bf16[64,256]{1,0:T(8,128)(2,1)S(1)}, bf16[64,256]{1,0:T(8,128)(2,1)S(1)}, u32[]{:S(2)}, u32[]{:S(2)}) collective-permute-start(bf16[64,256]{1,0:T(8,128)(2,1)S(1)} %add_convert_fusion.1), channel_id=1, source_target_pairs={{0,16},{2,18},{4,20},{6,22},{8,24},{10,26},{12,28},{14,30},{16,0},... | collective-permute-start | bytes 98312 | tf_op jit(solution)/shard_map/ppermute | solution.py:59
  48.9 2.2 %collective-permute-done.6 = bf16[64,256]{1,0:T(8,128)(2,1)S(1)} collective-permute-done((bf16[64,256]{1,0:T(8,128)(2,1)S(1)}, bf16[64,256]{1,0:T(8,128)(2,1)S(1)}, u32[]{:S(2)}, u32[]{:S(2)}) %collective-permute-start.6) | collective-permute-done | bytes 32800 | tf_op jit(solution)/shard_map/ppermute | solution.py:59
  51.1 1.6 %collective-permute-start.7 = (bf16[128,256]{1,0:T(8,128)(2,1)S(1)}, bf16[128,256]{1,0:T(8,128)(2,1)S(1)}, u32[]{:S(2)}, u32[]{:S(2)}) collective-permute-start(bf16[128,256]{1,0:T(8,128)(2,1)S(1)} %maximum_select_fusion.4), channel_id=1, source_target_pairs={{0,8},{2,10},{4,12},{6,14},{8,0},{10,2},{12,4},{14,6},{16,24},{18,... | collective-permute-start | bytes 196616 | tf_op jit(solution)/shard_map/ppermute | solution.py:59
  52.7 2.7 %collective-permute-done.7 = bf16[128,256]{1,0:T(8,128)(2,1)S(1)} collective-permute-done((bf16[128,256]{1,0:T(8,128)(2,1)S(1)}, bf16[128,256]{1,0:T(8,128)(2,1)S(1)}, u32[]{:S(2)}, u32[]{:S(2)}) %collective-permute-start.7) | collective-permute-done | bytes 65568 | tf_op jit(solution)/shard_map/ppermute | solution.py:59
  55.5 3.4 %collective-permute-done.1 = bf16[1088,256]{1,0:T(8,128)(2,1)S(1)} collective-permute-done((bf16[1088,256]{1,0:T(8,128)(2,1)S(1)}, bf16[1088,256]{1,0:T(8,128)(2,1)S(1)}, u32[]{:S(2)}, u32[]{:S(2)}) %collective-permute-start.1) | collective-permute-done | bytes 557088 | tf_op jit(solution)/shard_map/ppermute | solution.py:59
  59.2 1.6 %collective-permute-start.8 = (bf16[256,256]{1,0:T(8,128)(2,1)S(1)}, bf16[256,256]{1,0:T(8,128)(2,1)S(1)}, u32[]{:S(2)}, u32[]{:S(2)}) collective-permute-start(bf16[256,256]{1,0:T(8,128)(2,1)S(1)} %maximum_select_fusion.3), channel_id=1, source_target_pairs={{0,4},{2,6},{4,0},{6,2},{8,12},{10,14},{12,8},{14,10},{16,20},{18,... | collective-permute-start | bytes 393224 | tf_op jit(solution)/shard_map/ppermute | solution.py:59
  60.8 3.4 %collective-permute-done.8 = bf16[256,256]{1,0:T(8,128)(2,1)S(1)} collective-permute-done((bf16[256,256]{1,0:T(8,128)(2,1)S(1)}, bf16[256,256]{1,0:T(8,128)(2,1)S(1)}, u32[]{:S(2)}, u32[]{:S(2)}) %collective-permute-start.8) | collective-permute-done | bytes 131104 | tf_op jit(solution)/shard_map/ppermute | solution.py:59
  64.4 1.0 %slice.8 = bf16[2048,256]{1,0:T(8,128)(2,1)} slice(bf16[2176,256]{1,0:T(8,128)(2,1)S(1)} %maximum_select_fusion), slice={[0:2048], [0:256]} | slice | bytes 2097152 | tf_op jit(solution)/shard_map/slice | solution.py:99
  (39 shorter events, 8.3 us)
Async XLA Ops:
  1.4 1.0 %copy-start = (bf16[1024,256]{1,0:T(8,128)(2,1)S(1)}, bf16[1024,256]{1,0:T(8,128)(2,1)}, u32[]{:S(2)}) copy-start(bf16[1024,256]{1,0:T(8,128)(2,1)} %param.8) | copy-start | bytes 1572868
  1.4 1.4 %copy-start.1 = (bf16[2048,256]{1,0:T(8,128)(2,1)S(1)}, bf16[2048,256]{1,0:T(8,128)(2,1)}, u32[]{:S(2)}) copy-start(bf16[2048,256]{1,0:T(8,128)(2,1)} %param.7) | copy-start | bytes 3145732
  1.4 2.7 %copy-start.3 = (bf16[2048,1024]{1,0:T(8,128)(2,1)S(1)}, bf16[2048,1024]{1,0:T(8,128)(2,1)}, u32[]{:S(2)}) copy-start(bf16[2048,1024]{1,0:T(8,128)(2,1)} %param.10) | copy-start | bytes 12582916
  6.0 1.3 %copy-start.6 = (s32[8,1]{0,1:T(1,128)S(1)}, s32[8,1]{0,1:T(1,128)}, u32[]{:S(2)}) copy-start(s32[8,1]{0,1:T(1,128)} %param.13) | copy-start | bytes 100
  6.1 1.4 %copy-start.4 = (bf16[128,256]{1,0:T(8,128)(2,1)S(1)}, bf16[128,256]{1,0:T(8,128)(2,1)}, u32[]{:S(2)}) copy-start(bf16[128,256]{1,0:T(8,128)(2,1)} %param.9) | copy-start | bytes 196612
  6.1 1.4 %copy-start.5 = (bf16[1024,128]{1,0:T(8,128)(2,1)S(1)}, bf16[1024,128]{1,0:T(8,128)(2,1)}, u32[]{:S(2)}) copy-start(bf16[1024,128]{1,0:T(8,128)(2,1)} %param.12) | copy-start | bytes 786436
  12.0 1.0 %copy-start.2 = (f32[1024,256]{1,0:T(8,128)}, f32[1024,256]{1,0:T(8,128)S(1)}, u32[]{:S(2)}) copy-start(f32[1024,256]{1,0:T(8,128)S(1)} %convolution_add_fusion) | copy-start | bytes 3145732
  13.0 4.1 %collective-permute-start.2 = (f32[512,256]{1,0:T(8,128)S(1)}, f32[512,256]{1,0:T(8,128)}, u32[]{:S(2)}, u32[]{:S(2)}) collective-permute-start(f32[512,256]{1,0:T(8,128)S(1)} %constant_dynamic-slice_fusion.2), channel_id=1, source_target_pairs={{0,2},{2,0},{4,6},{6,4},{8,10},{10,8},{12,14},{14,12},{16,18},{18,... | collective-permute-start | bytes 1572872 | tf_op jit(solution)/shard_map/ppermute | solution.py:47
  14.6 28.1 %collective-permute-start = (f32[1088,256]{1,0:T(8,128)}, f32[1088,256]{1,0:T(8,128)}, u32[]{:S(2)}, u32[]{:S(2)}) collective-permute-start(f32[1088,256]{1,0:T(8,128)} %constant_dynamic-slice_fusion.3), channel_id=1, source_target_pairs={{0,1},{1,0},{2,3},{3,2},{4,5},{5,4},{6,7},{7,6},{8,9},{9,8},{10,11... | collective-permute-start | bytes 3342344 | tf_op jit(solution)/shard_map/ppermute | solution.py:47
  18.4 8.6 %collective-permute-start.3 = (f32[256,256]{1,0:T(8,128)S(1)}, f32[256,256]{1,0:T(8,128)}, u32[]{:S(2)}, u32[]{:S(2)}) collective-permute-start(f32[256,256]{1,0:T(8,128)S(1)} %constant_dynamic-slice_fusion.1), channel_id=1, source_target_pairs={{0,4},{2,6},{4,0},{6,2},{8,12},{10,14},{12,8},{14,10},{16,20},{18,... | collective-permute-start | bytes 786440 | tf_op jit(solution)/shard_map/ppermute | solution.py:47
  28.0 5.0 %collective-permute-start.4 = (f32[128,256]{1,0:T(8,128)S(1)}, f32[128,256]{1,0:T(8,128)S(1)}, u32[]{:S(2)}, u32[]{:S(2)}) collective-permute-start(f32[128,256]{1,0:T(8,128)S(1)} %constant_dynamic-slice_fusion), channel_id=1, source_target_pairs={{0,8},{2,10},{4,12},{6,14},{8,0},{10,2},{12,4},{14,6},{16,24},{18,... | collective-permute-start | bytes 393224 | tf_op jit(solution)/shard_map/ppermute | solution.py:47
  33.7 12.5 %collective-permute-start.5 = (f32[64,256]{1,0:T(8,128)}, f32[64,256]{1,0:T(8,128)S(1)}, u32[]{:S(2)}, u32[]{:S(2)}) collective-permute-start(f32[64,256]{1,0:T(8,128)} %constant_dynamic-slice_fusion.4), channel_id=1, source_target_pairs={{0,16},{2,18},{4,20},{6,22},{8,24},{10,26},{12,28},{14,30},{16,0},... | collective-permute-start | bytes 196616 | tf_op jit(solution)/shard_map/ppermute | solution.py:47
  44.4 14.5 %collective-permute-start.1 = (bf16[1088,256]{1,0:T(8,128)(2,1)S(1)}, bf16[1088,256]{1,0:T(8,128)(2,1)S(1)}, u32[]{:S(2)}, u32[]{:S(2)}) collective-permute-start(bf16[1088,256]{1,0:T(8,128)(2,1)S(1)} %add_convert_fusion), channel_id=1, source_target_pairs={{0,1},{1,0},{2,3},{3,2},{4,5},{5,4},{6,7},{7,6},{8,9},{9,8},{10,11... | collective-permute-start | bytes 1671176 | tf_op jit(solution)/shard_map/ppermute | solution.py:59
  46.2 4.9 %collective-permute-start.6 = (bf16[64,256]{1,0:T(8,128)(2,1)S(1)}, bf16[64,256]{1,0:T(8,128)(2,1)S(1)}, u32[]{:S(2)}, u32[]{:S(2)}) collective-permute-start(bf16[64,256]{1,0:T(8,128)(2,1)S(1)} %add_convert_fusion.1), channel_id=1, source_target_pairs={{0,16},{2,18},{4,20},{6,22},{8,24},{10,26},{12,28},{14,30},{16,0},... | collective-permute-start | bytes 98312 | tf_op jit(solution)/shard_map/ppermute | solution.py:59
  51.1 4.3 %collective-permute-start.7 = (bf16[128,256]{1,0:T(8,128)(2,1)S(1)}, bf16[128,256]{1,0:T(8,128)(2,1)S(1)}, u32[]{:S(2)}, u32[]{:S(2)}) collective-permute-start(bf16[128,256]{1,0:T(8,128)(2,1)S(1)} %maximum_select_fusion.4), channel_id=1, source_target_pairs={{0,8},{2,10},{4,12},{6,14},{8,0},{10,2},{12,4},{14,6},{16,24},{18,... | collective-permute-start | bytes 196616 | tf_op jit(solution)/shard_map/ppermute | solution.py:59
  59.2 5.0 %collective-permute-start.8 = (bf16[256,256]{1,0:T(8,128)(2,1)S(1)}, bf16[256,256]{1,0:T(8,128)(2,1)S(1)}, u32[]{:S(2)}, u32[]{:S(2)}) collective-permute-start(bf16[256,256]{1,0:T(8,128)(2,1)S(1)} %maximum_select_fusion.3), channel_id=1, source_target_pairs={{0,4},{2,6},{4,0},{6,2},{8,12},{10,14},{12,8},{14,10},{16,20},{18,... | collective-permute-start | bytes 393224 | tf_op jit(solution)/shard_map/ppermute | solution.py:59
  64.3 1.8 %collective-permute-start.9 = (bf16[512,256]{1,0:T(8,128)(2,1)S(1)}, bf16[512,256]{1,0:T(8,128)(2,1)S(1)}, u32[]{:S(2)}, u32[]{:S(2)}) collective-permute-start(bf16[512,256]{1,0:T(8,128)(2,1)S(1)} %maximum_select_fusion.2), channel_id=1, source_target_pairs={{0,2},{2,0},{4,6},{6,4},{8,10},{10,8},{12,14},{14,12},{16,18},{18,... | collective-permute-start | bytes 786440 | tf_op jit(solution)/shard_map/ppermute | solution.py:59

commit v7 on v3

--- a/solution.py
+++ b/solution.py
@@ -36,10 +36,12 @@
     return [(i, i ^ (1 << bit)) for i in range(count)]
 
 
-def halving_scatter(parts, axis, count, position):
+def halving_scatter(parts, axis, count, position, tie=None, tie_step=-1):
     steps = count.bit_length() - 1
     offsets = [0 for _ in parts]
     for bit in range(steps):
+        if bit == tie_step and tie is not None:
+            parts, _ = lax.optimization_barrier((parts, tie))
         side = (position >> bit) & 1
         halves = [p.shape[0] // 2 for p in parts]
         kept = [lax.dynamic_slice_in_dim(p, side * h, h, 0) for p, h in zip(parts, halves)]
@@ -97,7 +99,9 @@
     new_users = new_joint[: user_factors.shape[0]]
     new_tags = new_joint[user_factors.shape[0] :]
 
-    (item_share,), (item_offset,) = halving_scatter([item_part], "group", group_count, group_position)
+    (item_share,), (item_offset,) = halving_scatter(
+        [item_part], "group", group_count, group_position, joint_share, 3
+    )
     fresh_items = advance(
         lax.dynamic_slice_in_dim(item_factors, item_offset, item_share.shape[0], 0),
         item_share,

time: 64.7 us -> 68.9 us (1.065)
  waiting for transfers between devices: 25.2 us -> 32.3 us
  starting transfers between devices: 17.9 us -> 14.9 us
    ppermute x5, waiting for transfers between devices: 11.4 us -> 23.7 us  [halving_scatter(): got = lax.ppermute(tuple(sent), axis, xor_pairs(count, bit))]
    ppermute x5, waiting for transfers between devices: 13.8 us -> 8.59 us  [doubling_gather(): got = lax.ppermute(tuple(parts), axis, xor_pairs(count, bit))]
    ppermute x5, starting transfers between devices: 8.21 us -> 5.74 us  [doubling_gather(): got = lax.ppermute(tuple(parts), axis, xor_pairs(count, bit))]
  transfers between devices with their start and end apart: 10 -> 10, of which waited for: 8 -> 7; matrix products, arithmetic and copies ran while one was open for 8% -> 8% of each run, Pallas kernels for 0% -> 0%
where the time goes in v7:
time: 68.9 us; the launch traced here: 68.5 us
  waiting for transfers between devices  32.3 us (47%)
  starting transfers between devices  14.9 us (22%)
  matrix products  7.55 us (11%)
  local copies, waits for them, and re-layouts  6.65 us (10%)
  other arithmetic  6.34 us (9%)
  between operations  0.83 us (1%)
    ppermute x5, waiting for transfers between devices, halving_scatter(): got = lax.ppermute(tuple(sent), axis, xor_pairs(count, bit))  23.7 us
    ppermute x5, starting transfers between devices, halving_scatter(): got = lax.ppermute(tuple(sent), axis, xor_pairs(count, bit))  9.13 us
    ppermute x5, waiting for transfers between devices, doubling_gather(): got = lax.ppermute(tuple(parts), axis, xor_pairs(count, bit))  8.59 us
    ppermute x5, starting transfers between devices, doubling_gather(): got = lax.ppermute(tuple(parts), axis, xor_pairs(count, bit))  5.74 us
    unnamed x14, local copies, waits for them, and re-layouts  3.05 us
    dot_general x2, matrix products, transposed_product(): lax.dot_general(first_operand, second_operand, (((0,), (0,)), ((), ())),...  2.52 us
    add x3, other arithmetic, halving_scatter(): parts = [k + g for k, g in zip(kept, got)]  2.27 us
    dot_general x2, matrix products, residual_of(): lax.dot_general(row_factors, column_factors, (((1,), (1,)), ((), ())), pr...  2.26 us
  transfers between devices with their start and end apart: 10, of which 7 were waited for; matrix products, arithmetic and copies ran while one was open for 8% of the time, Pallas kernels for 0%

profile of v7, /device:TPU:0, one launch (start us, length us, event | category | flops | bytes accessed | tf_op | source)
XLA Modules:
  0.0 68.5 jit_solution(14599995229720999425)
XLA Ops:
  2.8 1.3 %copy-done.3 = bf16[2048,1024]{1,0:T(8,128)(2,1)S(1)} copy-done((bf16[2048,1024]{1,0:T(8,128)(2,1)S(1)}, bf16[2048,1024]{1,0:T(8,128)(2,1)}, u32[]{:S(2)}) %copy-start.3) | copy-done | bytes 4194328
  4.1 1.9 %fusion = bf16[2048,1024]{1,0:T(8,128)(2,1)S(1)} fusion(f32[256,8,8,128]{3,2,1,0:T(8,128)S(1)} %bitcast.22, bf16[2048,1024]{1,0:T(8,128)(2,1)S(1)} %copy-done.3, bf16[2048,256]{1,0:T(8,128)(2,1)S(1)} %copy-done.1, bf16[1024,256]{1,0:T(8,128)(2,1)S(1)} %copy-done), kind=kOutput, calls=%fused_computation.1 | convolution fusion | flops 1082130432 | bytes 18350080 | tf_op jit(solution)/shard_map/dot_general | solution.py:19
  6.1 1.3 %fusion.4 = f32[2048,256]{1,0:T(8,128)S(1)} fusion(bf16[2048,1024]{1,0:T(8,128)(2,1)S(1)} %fusion, bf16[1024,256]{1,0:T(8,128)(2,1)S(1)} %copy-done), kind=kOutput, calls=%fused_computation.28 | convolution fusion | flops 1073741824 | bytes 6815744 | tf_op jit(solution)/shard_map/dot_general | solution.py:75
  8.2 2.2 %fusion.6 = f32[1024,256]{1,0:T(8,128)} fusion(bf16[2048,1024]{1,0:T(8,128)(2,1)S(1)} %fusion, bf16[2048,256]{1,0:T(8,128)(2,1)S(1)} %copy-done.1), kind=kOutput, calls=%fused_computation.30 | convolution fusion | flops 1073741824 | bytes 6291456 | tf_op jit(solution)/shard_map/dot_general | solution.py:26
  10.5 1.5 %convolution_add_fusion = f32[1024,256]{1,0:T(8,128)S(1)} fusion(f32[1024,256]{1,0:T(8,128)} %fusion.6, bf16[1024,128]{1,0:T(8,128)(2,1)S(1)} %fusion.2, bf16[128,256]{1,0:T(8,128)(2,1)S(1)} %copy-done.4), kind=kOutput, calls=%fused_computation.3 | convolution fusion | flops 67371008 | bytes 2424832 | tf_op jit(solution)/shard_map/dot_general | solution.py:85
  13.5 1.1 %constant_dynamic-slice_fusion.4 = f32[1088,256]{1,0:T(8,128)} fusion(f32[2176,256]{1,0:T(8,128)S(1)} %pad_maximum_fusion, s32[]{:T(128)S(6)} %select_n.78), kind=kLoop, calls=%fused_computation.25 | loop fusion | bytes 2228228 | tf_op jit(solution)/shard_map/dynamic_slice | solution.py:48
  14.6 2.5 %collective-permute-start = (f32[1088,256]{1,0:T(8,128)}, f32[1088,256]{1,0:T(8,128)}, u32[]{:S(2)}, u32[]{:S(2)}) collective-permute-start(f32[1088,256]{1,0:T(8,128)} %constant_dynamic-slice_fusion.4), channel_id=1, source_target_pairs={{0,1},{1,0},{2,3},{3,2},{4,5},{5,4},{6,7},{7,6},{8,9},{9,8},{10,11... | collective-permute-start | bytes 3342344 | tf_op jit(solution)/shard_map/ppermute | solution.py:49
  17.1 1.3 %dynamic-slice_add_fusion.1 = f32[512,256]{1,0:T(8,128)S(1)} fusion(f32[512,256]{1,0:T(8,128)} %collective-permute-done.2, f32[1024,256]{1,0:T(8,128)} %copy-done.2, s32[]{:T(128)S(6)} %select_n.85), kind=kLoop, calls=%fused_computation.14 | loop fusion | flops 131072 | bytes 1572868 | tf_op jit(solution)/shard_map/add | solution.py:50
  18.4 1.6 %collective-permute-start.3 = (f32[256,256]{1,0:T(8,128)S(1)}, f32[256,256]{1,0:T(8,128)}, u32[]{:S(2)}, u32[]{:S(2)}) collective-permute-start(f32[256,256]{1,0:T(8,128)S(1)} %constant_dynamic-slice_fusion.1), channel_id=1, source_target_pairs={{0,4},{2,6},{4,0},{6,2},{8,12},{10,14},{12,8},{14,10},{16,20},{18,... | collective-permute-start | bytes 786440 | tf_op jit(solution)/shard_map/ppermute | solution.py:49
  20.0 7.0 %collective-permute-done.3 = f32[256,256]{1,0:T(8,128)} collective-permute-done((f32[256,256]{1,0:T(8,128)S(1)}, f32[256,256]{1,0:T(8,128)}, u32[]{:S(2)}, u32[]{:S(2)}) %collective-permute-start.3) | collective-permute-done | bytes 262176 | tf_op jit(solution)/shard_map/ppermute | solution.py:49
  28.0 1.6 %collective-permute-start.4 = (f32[128,256]{1,0:T(8,128)S(1)}, f32[128,256]{1,0:T(8,128)S(1)}, u32[]{:S(2)}, u32[]{:S(2)}) collective-permute-start(f32[128,256]{1,0:T(8,128)S(1)} %constant_dynamic-slice_fusion), channel_id=1, source_target_pairs={{0,8},{2,10},{4,12},{6,14},{8,0},{10,2},{12,4},{14,6},{16,24},{18,... | collective-permute-start | bytes 393224 | tf_op jit(solution)/shard_map/ppermute | solution.py:49
  29.7 3.4 %collective-permute-done.4 = f32[128,256]{1,0:T(8,128)S(1)} collective-permute-done((f32[128,256]{1,0:T(8,128)S(1)}, f32[128,256]{1,0:T(8,128)S(1)}, u32[]{:S(2)}, u32[]{:S(2)}) %collective-permute-start.4) | collective-permute-done | bytes 131104 | tf_op jit(solution)/shard_map/ppermute | solution.py:49
  33.1 9.6 %collective-permute-done = f32[1088,256]{1,0:T(8,128)} collective-permute-done((f32[1088,256]{1,0:T(8,128)}, f32[1088,256]{1,0:T(8,128)}, u32[]{:S(2)}, u32[]{:S(2)}) %collective-permute-start) | collective-permute-done | bytes 1114144 | tf_op jit(solution)/shard_map/ppermute | solution.py:49
  42.6 1.8 %add_convert_fusion = bf16[1088,256]{1,0:T(8,128)(2,1)S(1)} fusion(s32[]{:T(128)S(6)} %select_n.77, bf16[2048,256]{1,0:T(8,128)(2,1)} %param.7, bf16[128,256]{1,0:T(8,128)(2,1)} %param.9, f32[1088,256]{1,0:T(8,128)} %collective-permute-done, f32[2176,256]{1,0:T(8,128)S(1)} %pad_maximum_fusion), kind=kLoop, calls=%fused_computation.10 | loop fusion | flops 2228224 | bytes 3899396 | tf_op jit(solution)/shard_map/convert_element_type | solution.py:32
  44.5 2.9 %collective-permute-start.5 = (f32[64,256]{1,0:T(8,128)S(1)}, f32[64,256]{1,0:T(8,128)S(1)}, u32[]{:S(2)}, u32[]{:S(2)}) collective-permute-start(f32[64,256]{1,0:T(8,128)S(1)} %constant_dynamic-slice_fusion.3), channel_id=1, source_target_pairs={{0,16},{2,18},{4,20},{6,22},{8,24},{10,26},{12,28},{14,30},{16,0},... | collective-permute-start | bytes 196616 | tf_op jit(solution)/shard_map/ppermute | solution.py:49
  47.3 3.7 %collective-permute-done.5 = f32[64,256]{1,0:T(8,128)S(1)} collective-permute-done((f32[64,256]{1,0:T(8,128)S(1)}, f32[64,256]{1,0:T(8,128)S(1)}, u32[]{:S(2)}, u32[]{:S(2)}) %collective-permute-start.5) | collective-permute-done | bytes 65568 | tf_op jit(solution)/shard_map/ppermute | solution.py:49
  51.1 1.6 %collective-permute-start.6 = (bf16[64,256]{1,0:T(8,128)(2,1)S(1)}, bf16[64,256]{1,0:T(8,128)(2,1)S(1)}, u32[]{:S(2)}, u32[]{:S(2)}) collective-permute-start(bf16[64,256]{1,0:T(8,128)(2,1)S(1)} %add_convert_fusion.1), channel_id=1, source_target_pairs={{0,16},{2,18},{4,20},{6,22},{8,24},{10,26},{12,28},{14,30},{16,0},... | collective-permute-start | bytes 98312 | tf_op jit(solution)/shard_map/ppermute | solution.py:59
  52.7 1.5 %collective-permute-start.1 = (bf16[1088,256]{1,0:T(8,128)(2,1)S(1)}, bf16[1088,256]{1,0:T(8,128)(2,1)S(1)}, u32[]{:S(2)}, u32[]{:S(2)}) collective-permute-start(bf16[1088,256]{1,0:T(8,128)(2,1)S(1)} %add_convert_fusion), channel_id=1, source_target_pairs={{0,1},{1,0},{2,3},{3,2},{4,5},{5,4},{6,7},{7,6},{8,9},{9,8},{10,11... | collective-permute-start | bytes 1671176 | tf_op jit(solution)/shard_map/ppermute | solution.py:59
  54.2 1.8 %collective-permute-done.6 = bf16[64,256]{1,0:T(8,128)(2,1)S(1)} collective-permute-done((bf16[64,256]{1,0:T(8,128)(2,1)S(1)}, bf16[64,256]{1,0:T(8,128)(2,1)S(1)}, u32[]{:S(2)}, u32[]{:S(2)}) %collective-permute-start.6) | collective-permute-done | bytes 32800 | tf_op jit(solution)/shard_map/ppermute | solution.py:59
  57.0 3.4 %collective-permute-done.7 = bf16[128,256]{1,0:T(8,128)(2,1)S(1)} collective-permute-done((bf16[128,256]{1,0:T(8,128)(2,1)S(1)}, bf16[128,256]{1,0:T(8,128)(2,1)S(1)}, u32[]{:S(2)}, u32[]{:S(2)}) %collective-permute-start.7) | collective-permute-done | bytes 65568 | tf_op jit(solution)/shard_map/ppermute | solution.py:59
  60.3 1.6 %collective-permute-start.8 = (bf16[256,256]{1,0:T(8,128)(2,1)S(1)}, bf16[256,256]{1,0:T(8,128)(2,1)S(1)}, u32[]{:S(2)}, u32[]{:S(2)}) collective-permute-start(bf16[256,256]{1,0:T(8,128)(2,1)S(1)} %maximum_select_fusion.3), channel_id=1, source_target_pairs={{0,4},{2,6},{4,0},{6,2},{8,12},{10,14},{12,8},{14,10},{16,20},{18,... | collective-permute-start | bytes 393224 | tf_op jit(solution)/shard_map/ppermute | solution.py:59
  61.9 3.5 %collective-permute-done.8 = bf16[256,256]{1,0:T(8,128)(2,1)S(1)} collective-permute-done((bf16[256,256]{1,0:T(8,128)(2,1)S(1)}, bf16[256,256]{1,0:T(8,128)(2,1)S(1)}, u32[]{:S(2)}, u32[]{:S(2)}) %collective-permute-start.8) | collective-permute-done | bytes 131104 | tf_op jit(solution)/shard_map/ppermute | solution.py:59
  65.8 1.0 %slice.8 = bf16[2048,256]{1,0:T(8,128)(2,1)} slice(bf16[2176,256]{1,0:T(8,128)(2,1)S(1)} %maximum_select_fusion), slice={[0:2048], [0:256]} | slice | bytes 2097152 | tf_op jit(solution)/shard_map/slice | solution.py:99
  67.5 1.0 %maximum_select_fusion.1 = bf16[1024,256]{1,0:T(8,128)(2,1)} fusion(bf16[512,256]{1,0:T(8,128)(2,1)S(1)} %collective-permute-done.9, bf16[512,256]{1,0:T(8,128)(2,1)S(1)} %maximum_select_fusion.2, pred[]{:T(512)S(6)} %eq.16), kind=kLoop, calls=%fused_computation.13 | loop fusion | flops 2359296 | bytes 1048577 | tf_op jit(solution)/shard_map/jit(_where)/select_n | solution.py:61
  (39 shorter events, 7.6 us)
Async XLA Ops:
  1.4 1.0 %copy-start = (bf16[1024,256]{1,0:T(8,128)(2,1)S(1)}, bf16[1024,256]{1,0:T(8,128)(2,1)}, u32[]{:S(2)}) copy-start(bf16[1024,256]{1,0:T(8,128)(2,1)} %param.8) | copy-start | bytes 1572868
  1.4 1.4 %copy-start.1 = (bf16[2048,256]{1,0:T(8,128)(2,1)S(1)}, bf16[2048,256]{1,0:T(8,128)(2,1)}, u32[]{:S(2)}) copy-start(bf16[2048,256]{1,0:T(8,128)(2,1)} %param.7) | copy-start | bytes 3145732
  1.4 2.7 %copy-start.3 = (bf16[2048,1024]{1,0:T(8,128)(2,1)S(1)}, bf16[2048,1024]{1,0:T(8,128)(2,1)}, u32[]{:S(2)}) copy-start(bf16[2048,1024]{1,0:T(8,128)(2,1)} %param.10) | copy-start | bytes 12582916
  6.0 1.3 %copy-start.6 = (s32[8,1]{0,1:T(1,128)S(1)}, s32[8,1]{0,1:T(1,128)}, u32[]{:S(2)}) copy-start(s32[8,1]{0,1:T(1,128)} %param.13) | copy-start | bytes 100
  6.1 1.4 %copy-start.4 = (bf16[128,256]{1,0:T(8,128)(2,1)S(1)}, bf16[128,256]{1,0:T(8,128)(2,1)}, u32[]{:S(2)}) copy-start(bf16[128,256]{1,0:T(8,128)(2,1)} %param.9) | copy-start | bytes 196612
  6.1 1.4 %copy-start.5 = (bf16[1024,128]{1,0:T(8,128)(2,1)S(1)}, bf16[1024,128]{1,0:T(8,128)(2,1)}, u32[]{:S(2)}) copy-start(bf16[1024,128]{1,0:T(8,128)(2,1)} %param.12) | copy-start | bytes 786436
  12.0 1.0 %copy-start.2 = (f32[1024,256]{1,0:T(8,128)}, f32[1024,256]{1,0:T(8,128)S(1)}, u32[]{:S(2)}) copy-start(f32[1024,256]{1,0:T(8,128)S(1)} %convolution_add_fusion) | copy-start | bytes 3145732
  13.0 4.1 %collective-permute-start.2 = (f32[512,256]{1,0:T(8,128)S(1)}, f32[512,256]{1,0:T(8,128)}, u32[]{:S(2)}, u32[]{:S(2)}) collective-permute-start(f32[512,256]{1,0:T(8,128)S(1)} %constant_dynamic-slice_fusion.2), channel_id=1, source_target_pairs={{0,2},{2,0},{4,6},{6,4},{8,10},{10,8},{12,14},{14,12},{16,18},{18,... | collective-permute-start | bytes 1572872 | tf_op jit(solution)/shard_map/ppermute | solution.py:49
  14.6 28.1 %collective-permute-start = (f32[1088,256]{1,0:T(8,128)}, f32[1088,256]{1,0:T(8,128)}, u32[]{:S(2)}, u32[]{:S(2)}) collective-permute-start(f32[1088,256]{1,0:T(8,128)} %constant_dynamic-slice_fusion.4), channel_id=1, source_target_pairs={{0,1},{1,0},{2,3},{3,2},{4,5},{5,4},{6,7},{7,6},{8,9},{9,8},{10,11... | collective-permute-start | bytes 3342344 | tf_op jit(solution)/shard_map/ppermute | solution.py:49
  18.4 8.6 %collective-permute-start.3 = (f32[256,256]{1,0:T(8,128)S(1)}, f32[256,256]{1,0:T(8,128)}, u32[]{:S(2)}, u32[]{:S(2)}) collective-permute-start(f32[256,256]{1,0:T(8,128)S(1)} %constant_dynamic-slice_fusion.1), channel_id=1, source_target_pairs={{0,4},{2,6},{4,0},{6,2},{8,12},{10,14},{12,8},{14,10},{16,20},{18,... | collective-permute-start | bytes 786440 | tf_op jit(solution)/shard_map/ppermute | solution.py:49
  28.0 5.0 %collective-permute-start.4 = (f32[128,256]{1,0:T(8,128)S(1)}, f32[128,256]{1,0:T(8,128)S(1)}, u32[]{:S(2)}, u32[]{:S(2)}) collective-permute-start(f32[128,256]{1,0:T(8,128)S(1)} %constant_dynamic-slice_fusion), channel_id=1, source_target_pairs={{0,8},{2,10},{4,12},{6,14},{8,0},{10,2},{12,4},{14,6},{16,24},{18,... | collective-permute-start | bytes 393224 | tf_op jit(solution)/shard_map/ppermute | solution.py:49
  44.5 6.6 %collective-permute-start.5 = (f32[64,256]{1,0:T(8,128)S(1)}, f32[64,256]{1,0:T(8,128)S(1)}, u32[]{:S(2)}, u32[]{:S(2)}) collective-permute-start(f32[64,256]{1,0:T(8,128)S(1)} %constant_dynamic-slice_fusion.3), channel_id=1, source_target_pairs={{0,16},{2,18},{4,20},{6,22},{8,24},{10,26},{12,28},{14,30},{16,0},... | collective-permute-start | bytes 196616 | tf_op jit(solution)/shard_map/ppermute | solution.py:49
  51.1 4.9 %collective-permute-start.6 = (bf16[64,256]{1,0:T(8,128)(2,1)S(1)}, bf16[64,256]{1,0:T(8,128)(2,1)S(1)}, u32[]{:S(2)}, u32[]{:S(2)}) collective-permute-start(bf16[64,256]{1,0:T(8,128)(2,1)S(1)} %add_convert_fusion.1), channel_id=1, source_target_pairs={{0,16},{2,18},{4,20},{6,22},{8,24},{10,26},{12,28},{14,30},{16,0},... | collective-permute-start | bytes 98312 | tf_op jit(solution)/shard_map/ppermute | solution.py:59
  52.7 12.9 %collective-permute-start.1 = (bf16[1088,256]{1,0:T(8,128)(2,1)S(1)}, bf16[1088,256]{1,0:T(8,128)(2,1)S(1)}, u32[]{:S(2)}, u32[]{:S(2)}) collective-permute-start(bf16[1088,256]{1,0:T(8,128)(2,1)S(1)} %add_convert_fusion), channel_id=1, source_target_pairs={{0,1},{1,0},{2,3},{3,2},{4,5},{5,4},{6,7},{7,6},{8,9},{9,8},{10,11... | collective-permute-start | bytes 1671176 | tf_op jit(solution)/shard_map/ppermute | solution.py:59
  56.0 4.3 %collective-permute-start.7 = (bf16[128,256]{1,0:T(8,128)(2,1)S(1)}, bf16[128,256]{1,0:T(8,128)(2,1)S(1)}, u32[]{:S(2)}, u32[]{:S(2)}) collective-permute-start(bf16[128,256]{1,0:T(8,128)(2,1)S(1)} %maximum_select_fusion.4), channel_id=1, source_target_pairs={{0,8},{2,10},{4,12},{6,14},{8,0},{10,2},{12,4},{14,6},{16,24},{18,... | collective-permute-start | bytes 196616 | tf_op jit(solution)/shard_map/ppermute | solution.py:59
  60.3 5.0 %collective-permute-start.8 = (bf16[256,256]{1,0:T(8,128)(2,1)S(1)}, bf16[256,256]{1,0:T(8,128)(2,1)S(1)}, u32[]{:S(2)}, u32[]{:S(2)}) collective-permute-start(bf16[256,256]{1,0:T(8,128)(2,1)S(1)} %maximum_select_fusion.3), channel_id=1, source_target_pairs={{0,4},{2,6},{4,0},{6,2},{8,12},{10,14},{12,8},{14,10},{16,20},{18,... | collective-permute-start | bytes 393224 | tf_op jit(solution)/shard_map/ppermute | solution.py:59
  65.5 2.0 %collective-permute-start.9 = (bf16[512,256]{1,0:T(8,128)(2,1)S(1)}, bf16[512,256]{1,0:T(8,128)(2,1)S(1)}, u32[]{:S(2)}, u32[]{:S(2)}) collective-permute-start(bf16[512,256]{1,0:T(8,128)(2,1)S(1)} %maximum_select_fusion.2), channel_id=1, source_target_pairs={{0,2},{2,0},{4,6},{6,4},{8,10},{10,8},{12,14},{14,12},{16,18},{18,... | collective-permute-start | bytes 786440 | tf_op jit(solution)/shard_map/ppermute | solution.py:59

commit v8 on v3

--- a/solution.py
+++ b/solution.py
@@ -36,7 +36,7 @@
     return [(i, i ^ (1 << bit)) for i in range(count)]
 
 
-def halving_scatter(parts, axis, count, position):
+def halving_scatter(parts, axis, count, position, tie=None):
     steps = count.bit_length() - 1
     offsets = [0 for _ in parts]
     for bit in range(steps):
@@ -45,14 +45,18 @@
         kept = [lax.dynamic_slice_in_dim(p, side * h, h, 0) for p, h in zip(parts, halves)]
         sent = [lax.dynamic_slice_in_dim(p, (1 - side) * h, h, 0) for p, h in zip(parts, halves)]
         got = lax.ppermute(tuple(sent), axis, xor_pairs(count, bit))
+        if tie is not None:
+            got, tie = lax.optimization_barrier((got, tie))
         parts = [k + g for k, g in zip(kept, got)]
         offsets = [o + side * h for o, h in zip(offsets, halves)]
+    if tie is not None:
+        return parts, offsets, tie
     return parts, offsets
 
 
-def doubling_gather(parts, axis, count, position):
+def doubling_gather(parts, axis, count, position, bits=None):
     steps = count.bit_length() - 1
-    for bit in reversed(range(steps)):
+    for bit in reversed(range(steps)) if bits is None else bits:
         side = (position >> bit) & 1
         got = lax.ppermute(tuple(parts), axis, xor_pairs(count, bit))
         parts = [
@@ -74,14 +78,38 @@
     tag_part = transposed_product(link_errors, item_factors)
     joint_part = jnp.concatenate([user_part, tag_part], 0)
 
-    joint_part, rating_errors, link_errors = lax.optimization_barrier(
-        (joint_part, rating_errors, link_errors)
-    )
-    (joint_share,), (joint_offset,) = halving_scatter(
-        [joint_part], "loop", loop_count, loop_position
-    )
     item_part = transposed_product(rating_errors, user_factors) + jnp.dot(
         link_errors, tag_factors, preferred_element_type=jnp.float32
+    )
+    group_steps = group_count.bit_length() - 1
+    late_bits = [bit for bit in (1, 0) if bit < group_steps]
+    early_bits = [bit for bit in reversed(range(group_steps)) if bit not in late_bits]
+    always = group_position >= 0
+
+    def group_early(item_part, item_factors):
+        (item_share,), (item_offset,) = halving_scatter(
+            [item_part], "group", group_count, group_position
+        )
+        fresh_items = advance(
+            lax.dynamic_slice_in_dim(item_factors, item_offset, item_share.shape[0], 0),
+            item_share,
+            step_items,
+        )
+        (partly,) = doubling_gather(
+            [fresh_items], "group", group_count, group_position, early_bits
+        )
+        return partly
+
+    partly_rows = item_factors.shape[0] >> len(late_bits)
+    partly = lax.cond(
+        always,
+        group_early,
+        lambda p, f: jnp.zeros((partly_rows, f.shape[1]), jnp.bfloat16),
+        item_part,
+        item_factors,
+    )
+    (joint_share,), (joint_offset,), partly = halving_scatter(
+        [joint_part], "loop", loop_count, loop_position, partly
     )
     joint_factors = jnp.concatenate([user_factors, tag_factors], 0)
     fresh_joint = advance(
@@ -97,13 +125,18 @@
     new_users = new_joint[: user_factors.shape[0]]
     new_tags = new_joint[user_factors.shape[0] :]
 
-    (item_share,), (item_offset,) = halving_scatter([item_part], "group", group_count, group_position)
-    fresh_items = advance(
-        lax.dynamic_slice_in_dim(item_factors, item_offset, item_share.shape[0], 0),
-        item_share,
-        step_items,
+    partly, _ = lax.optimization_barrier((partly, fresh_joint))
+
+    def group_late(partly):
+        (whole,) = doubling_gather([partly], "group", group_count, group_position, late_bits)
+        return whole
+
+    new_items = lax.cond(
+        always,
+        group_late,
+        lambda p: jnp.zeros(item_factors.shape, jnp.bfloat16),
+        partly,
     )
-    (new_items,) = doubling_gather([fresh_items], "group", group_count, group_position)
     return (new_users, new_items, new_tags)
 
 

time: 64.7 us -> 71.3 us (1.10)
  other arithmetic: 6.3 us -> 9.87 us
  matrix products: 7.55 us -> 9.89 us
  starting transfers between devices: 17.9 us -> 15.9 us
  waiting for transfers between devices: 25.2 us -> 27 us
  local copies, waits for them, and re-layouts: 6.65 us -> 7.56 us
    ppermute x5, waiting for transfers between devices: 11.4 us -> 15.1 us  [halving_scatter(): got = lax.ppermute(tuple(sent), axis, xor_pairs(count, bit))]
    dot_general x2, matrix products: 2.52 us -> 5 us  [transposed_product(): lax.dot_general(first_operand, second_operand, (((0,), (0,)), ((), ())),...]
    ppermute x5, waiting for transfers between devices: 13.8 us -> 11.9 us  [doubling_gather(): got = lax.ppermute(tuple(parts), axis, xor_pairs(count, bit))]
    cond x0 -> x4, local copies, waits for them, and re-layouts: none -> 1.69 us
    add x0 -> x1, other arithmetic: none -> 1.67 us  [shards(): transposed_product(rating_errors, user_factors)]
    ppermute x5, starting transfers between devices: 8.21 us -> 7.01 us  [doubling_gather(): got = lax.ppermute(tuple(parts), axis, xor_pairs(count, bit))]
    concatenate x1, other arithmetic: 0.15 us -> 1.31 us  [shards(): joint_part = jnp.concatenate([user_part, tag_part], 0)]
    add x3, other arithmetic: 2.27 us -> 3.17 us  [halving_scatter(): parts = [k + g for k, g in zip(kept, got)]]
  transfers between devices with their start and end apart: 10 -> 10, of which waited for: 8 -> 9; matrix products, arithmetic and copies ran while one was open for 8% -> 17% of each run, Pallas kernels for 0% -> 0%
where the time goes in v8:
time: 71.3 us; the launch traced here: 71 us
  waiting for transfers between devices  27 us (38%)
  starting transfers between devices  15.9 us (22%)
  matrix products  9.89 us (14%)
  other arithmetic  9.87 us (14%)
  local copies, waits for them, and re-layouts  7.56 us (11%)
  between operations  0.75 us (1%)
    ppermute x5, waiting for transfers between devices, halving_scatter(): got = lax.ppermute(tuple(sent), axis, xor_pairs(count, bit))  15.1 us
    ppermute x5, waiting for transfers between devices, doubling_gather(): got = lax.ppermute(tuple(parts), axis, xor_pairs(count, bit))  11.9 us
    ppermute x5, starting transfers between devices, halving_scatter(): got = lax.ppermute(tuple(sent), axis, xor_pairs(count, bit))  8.84 us
    ppermute x5, starting transfers between devices, doubling_gather(): got = lax.ppermute(tuple(parts), axis, xor_pairs(count, bit))  7.01 us
    dot_general x2, matrix products, transposed_product(): lax.dot_general(first_operand, second_operand, (((0,), (0,)), ((), ())),...  5 us
    add x3, other arithmetic, halving_scatter(): parts = [k + g for k, g in zip(kept, got)]  3.17 us
    unnamed x16, local copies, waits for them, and re-layouts  2.67 us
    convert_element_type x2, other arithmetic, advance(): return (factors.astype(jnp.float32) + rate * gradient).astype(jnp.bfloat16)  2.39 us
  transfers between devices with their start and end apart: 10, of which 9 were waited for; matrix products, arithmetic and copies ran while one was open for 17% of the time, Pallas kernels for 0%

profile of v8, /device:TPU:0, one launch (start us, length us, event | category | flops | bytes accessed | tf_op | source)
XLA Modules:
  0.0 71.0 jit_solution(4039576606199339552)
XLA Ops:
  4.1 2.0 %fusion = bf16[2048,1024]{1,0:T(8,128)(2,1)S(1)} fusion(f32[256,8,8,128]{3,2,1,0:T(8,128)S(1)} %bitcast.22, bf16[2048,1024]{1,0:T(8,128)(2,1)S(1)} %copy-done.3, bf16[2048,256]{1,0:T(8,128)(2,1)S(1)} %copy-done.2, bf16[1024,256]{1,0:T(8,128)(2,1)S(1)} %copy-done), kind=kOutput, calls=%fused_computation.13 | convolution fusion | flops 1082130432 | bytes 18350080 | tf_op jit(solution)/shard_map/dot_general | solution.py:19
  6.2 1.3 %fusion.10 = f32[2048,256]{1,0:T(8,128)S(1)} fusion(bf16[2048,1024]{1,0:T(8,128)(2,1)S(1)} %fusion, bf16[1024,256]{1,0:T(8,128)(2,1)S(1)} %copy-done), kind=kOutput, calls=%fused_computation.33 | convolution fusion | flops 1073741824 | bytes 6815744 | tf_op jit(solution)/shard_map/dot_general | solution.py:77
  8.7 1.3 %fusion.3 = f32[1088,256]{1,0:T(8,128)} fusion(s32[]{:T(128)S(6)} %select_n.78, f32[2048,256]{1,0:T(8,128)S(1)} %fusion.10, f32[128,256]{1,0:T(8,128)S(1)} %fusion.11), kind=kLoop, calls=%fused_computation.21 | loop fusion | flops 278528 | bytes 3342340 | tf_op jit(solution)/shard_map/concatenate | solution.py:79
  10.0 3.0 %collective-permute-start.8 = (f32[1088,256]{1,0:T(8,128)}, f32[1088,256]{1,0:T(8,128)}, u32[]{:S(2)}, u32[]{:S(2)}) collective-permute-start(f32[1088,256]{1,0:T(8,128)} %fusion.3), channel_id=1, source_target_pairs={{0,1},{1,0},{2,3},{3,2},{4,5},{5,4},{6,7},{7,6},{8,9},{9,8},{10,11... | collective-permute-start | bytes 3342344 | tf_op jit(solution)/shard_map/ppermute | solution.py:47
  14.2 4.7 %fusion.12 = f32[1024,256]{1,0:T(8,128)} fusion(bf16[2048,1024]{1,0:T(8,128)(2,1)} %copy-done.4, bf16[2048,256]{1,0:T(8,128)(2,1)} %param.11), kind=kOutput, calls=%fused_computation.35 | convolution fusion | flops 1073741824 | bytes 6291456 | tf_op jit(solution)/shard_map/dot_general | solution.py:26
  19.0 37.8 %conditional.2 = (bf16[256,256]{1,0:T(8,128)(2,1)S(1)}) conditional(s32[]{:T(128)} %convert_element_type.41, () %tuple.22, (s32[]{:T(128)}, bf16[1024,256]{1,0:T(8,128)(2,1)S(1)}, f32[1024,256]{1,0:T(8,128)}, f32[1024,256]{1,0:T(8,128)}) %tuple.33), branch_computations={%region_0.0_spmd, %region_1.2_spmd} | conditional | flops 1458228 | bytes 18023336 | solution.py:104
  19.0 1.7 %add.52 = f32[1024,256]{1,0:T(8,128)S(1)} add(f32[1024,256]{1,0:T(8,128)} %get-tuple-element.21, f32[1024,256]{1,0:T(8,128)} %get-tuple-element.22) | non-fusion elementwise | flops 262144 | bytes 3145728 | tf_op jit(solution)/shard_map/add | solution.py:81
  21.8 2.0 %collective-permute-done = f32[512,256]{1,0:T(8,128)} collective-permute-done((f32[512,256]{1,0:T(8,128)S(1)}, f32[512,256]{1,0:T(8,128)}, u32[]{:S(2)}, u32[]{:S(2)}) %collective-permute-start) | collective-permute-done | bytes 524320 | tf_op jit(solution)/shard_map/cond/branch_1_fun/ppermute | solution.py:47
  25.8 1.5 %collective-permute-start.1 = (f32[256,256]{1,0:T(8,128)}, f32[256,256]{1,0:T(8,128)}, u32[]{:S(2)}, u32[]{:S(2)}) collective-permute-start(f32[256,256]{1,0:T(8,128)} %constant_dynamic-slice_fusion.1), channel_id=1, source_target_pairs={{0,4},{2,6},{4,0},{6,2},{8,12},{10,14},{12,8},{14,10},{16,20},{18,... | collective-permute-start | bytes 786440 | tf_op jit(solution)/shard_map/cond/branch_1_fun/ppermute | solution.py:47
  27.3 7.2 %collective-permute-done.1 = f32[256,256]{1,0:T(8,128)} collective-permute-done((f32[256,256]{1,0:T(8,128)}, f32[256,256]{1,0:T(8,128)}, u32[]{:S(2)}, u32[]{:S(2)}) %collective-permute-start.1) | collective-permute-done | bytes 262176 | tf_op jit(solution)/shard_map/cond/branch_1_fun/ppermute | solution.py:47
  36.2 1.6 %collective-permute-start.2 = (f32[128,256]{1,0:T(8,128)S(1)}, f32[128,256]{1,0:T(8,128)S(1)}, u32[]{:S(2)}, u32[]{:S(2)}) collective-permute-start(f32[128,256]{1,0:T(8,128)S(1)} %constant_dynamic-slice_fusion), channel_id=1, source_target_pairs={{0,8},{2,10},{4,12},{6,14},{8,0},{10,2},{12,4},{14,6},{16,24},{18,... | collective-permute-start | bytes 393224 | tf_op jit(solution)/shard_map/cond/branch_1_fun/ppermute | solution.py:47
  37.8 3.4 %collective-permute-done.2 = f32[128,256]{1,0:T(8,128)S(1)} collective-permute-done((f32[128,256]{1,0:T(8,128)S(1)}, f32[128,256]{1,0:T(8,128)S(1)}, u32[]{:S(2)}, u32[]{:S(2)}) %collective-permute-start.2) | collective-permute-done | bytes 131104 | tf_op jit(solution)/shard_map/cond/branch_1_fun/ppermute | solution.py:47
  42.1 2.7 %collective-permute-start.3 = (f32[64,256]{1,0:T(8,128)S(1)}, f32[64,256]{1,0:T(8,128)S(1)}, u32[]{:S(2)}, u32[]{:S(2)}) collective-permute-start(f32[64,256]{1,0:T(8,128)S(1)} %constant_dynamic-slice_fusion.3), channel_id=1, source_target_pairs={{0,16},{2,18},{4,20},{6,22},{8,24},{10,26},{12,28},{14,30},{16,0},... | collective-permute-start | bytes 196616 | tf_op jit(solution)/shard_map/cond/branch_1_fun/ppermute | solution.py:47
  44.8 2.6 %collective-permute-done.3 = f32[64,256]{1,0:T(8,128)S(1)} collective-permute-done((f32[64,256]{1,0:T(8,128)S(1)}, f32[64,256]{1,0:T(8,128)S(1)}, u32[]{:S(2)}, u32[]{:S(2)}) %collective-permute-start.3) | collective-permute-done | bytes 65568 | tf_op jit(solution)/shard_map/cond/branch_1_fun/ppermute | solution.py:47
  47.4 2.7 %collective-permute-start.4 = (bf16[64,256]{1,0:T(8,128)(2,1)S(1)}, bf16[64,256]{1,0:T(8,128)(2,1)S(1)}, u32[]{:S(2)}, u32[]{:S(2)}) collective-permute-start(bf16[64,256]{1,0:T(8,128)(2,1)S(1)} %add_convert_fusion), channel_id=1, source_target_pairs={{0,16},{2,18},{4,20},{6,22},{8,24},{10,26},{12,28},{14,30},{16,0},... | collective-permute-start | bytes 98312 | tf_op jit(solution)/shard_map/cond/branch_1_fun/ppermute | solution.py:61
  50.1 2.2 %collective-permute-done.4 = bf16[64,256]{1,0:T(8,128)(2,1)S(1)} collective-permute-done((bf16[64,256]{1,0:T(8,128)(2,1)S(1)}, bf16[64,256]{1,0:T(8,128)(2,1)S(1)}, u32[]{:S(2)}, u32[]{:S(2)}) %collective-permute-start.4) | collective-permute-done | bytes 32800 | tf_op jit(solution)/shard_map/cond/branch_1_fun/ppermute | solution.py:61
  52.3 2.2 %collective-permute-start.5 = (bf16[128,256]{1,0:T(8,128)(2,1)S(1)}, bf16[128,256]{1,0:T(8,128)(2,1)S(1)}, u32[]{:S(2)}, u32[]{:S(2)}) collective-permute-start(bf16[128,256]{1,0:T(8,128)(2,1)S(1)} %maximum_select_fusion.1), channel_id=1, source_target_pairs={{0,8},{2,10},{4,12},{6,14},{8,0},{10,2},{12,4},{14,6},{16,24},{18,... | collective-permute-start | bytes 196616 | tf_op jit(solution)/shard_map/cond/branch_1_fun/ppermute | solution.py:61
  54.5 2.2 %collective-permute-done.5 = bf16[128,256]{1,0:T(8,128)(2,1)S(1)} collective-permute-done((bf16[128,256]{1,0:T(8,128)(2,1)S(1)}, bf16[128,256]{1,0:T(8,128)(2,1)S(1)}, u32[]{:S(2)}, u32[]{:S(2)}) %collective-permute-start.5) | collective-permute-done | bytes 65568 | tf_op jit(solution)/shard_map/cond/branch_1_fun/ppermute | solution.py:61
  56.8 2.4 %fusion.8 = bf16[1088,256]{1,0:T(8,128)(2,1)S(1)} fusion(f32[1088,256]{1,0:T(8,128)} %collective-permute-done.8, s32[]{:T(128)S(6)} %select_n.77, f32[2048,256]{1,0:T(8,128)S(1)} %fusion.10, f32[128,256]{1,0:T(8,128)S(1)} %fusion.11, bf16[2048,256]{1,0:T(8,128)(2,1)} %param.11, bf16[128,256]{1,0:T(8,128)(2,1)S(1)} %copy-done.6), kind=kLoop, calls=%fused_computation.26 | loop fusion | flops 2506752 | bytes 5013508 | tf_op jit(solution)/shard_map/convert_element_type | solution.py:32
  59.7 6.9 %conditional.3 = (bf16[1024,256]{1,0:T(8,128)(2,1)S(1)}) conditional(s32[]{:T(128)} %convert_element_type.41, () %tuple.25, (s32[]{:T(128)}, bf16[256,256]{1,0:T(8,128)(2,1)S(1)}) %tuple.27), branch_computations={%region_2.3_spmd, %region_3.4_spmd} | conditional | flops 3538950 | bytes 3145884 | solution.py:134
  59.7 1.5 %collective-permute-start.6 = (bf16[256,256]{1,0:T(8,128)(2,1)S(1)}, bf16[256,256]{1,0:T(8,128)(2,1)S(1)}, u32[]{:S(2)}, u32[]{:S(2)}) collective-permute-start(bf16[256,256]{1,0:T(8,128)(2,1)S(1)} %get-tuple-element.24), channel_id=1, source_target_pairs={{0,4},{2,6},{4,0},{6,2},{8,12},{10,14},{12,8},{14,10},{16,20},{18,... | collective-permute-start | bytes 393224 | tf_op jit(solution)/shard_map/cond/branch_1_fun/ppermute | solution.py:61
  61.2 3.5 %collective-permute-done.6 = bf16[256,256]{1,0:T(8,128)(2,1)S(1)} collective-permute-done((bf16[256,256]{1,0:T(8,128)(2,1)S(1)}, bf16[256,256]{1,0:T(8,128)(2,1)S(1)}, u32[]{:S(2)}, u32[]{:S(2)}) %collective-permute-start.6) | collective-permute-done | bytes 131104 | tf_op jit(solution)/shard_map/cond/branch_1_fun/ppermute | solution.py:61
  64.9 1.5 %collective-permute-done.7 = bf16[512,256]{1,0:T(8,128)(2,1)S(1)} collective-permute-done((bf16[512,256]{1,0:T(8,128)(2,1)S(1)}, bf16[512,256]{1,0:T(8,128)(2,1)S(1)}, u32[]{:S(2)}, u32[]{:S(2)}) %collective-permute-start.7) | collective-permute-done | bytes 262176 | tf_op jit(solution)/shard_map/cond/branch_1_fun/ppermute | solution.py:61
  66.7 2.4 %collective-permute-done.9 = bf16[1088,256]{1,0:T(8,128)(2,1)S(1)} collective-permute-done((bf16[1088,256]{1,0:T(8,128)(2,1)S(1)}, bf16[1088,256]{1,0:T(8,128)(2,1)S(1)}, u32[]{:S(2)}, u32[]{:S(2)}) %collective-permute-start.9) | collective-permute-done | bytes 557088 | tf_op jit(solution)/shard_map/ppermute | solution.py:61
  (47 shorter events, 14.6 us)
Async XLA Ops:
  1.4 1.0 %copy-start = (bf16[1024,256]{1,0:T(8,128)(2,1)S(1)}, bf16[1024,256]{1,0:T(8,128)(2,1)}, u32[]{:S(2)}) copy-start(bf16[1024,256]{1,0:T(8,128)(2,1)} %param.12) | copy-start | bytes 1572868
  1.4 1.4 %copy-start.2 = (bf16[2048,256]{1,0:T(8,128)(2,1)S(1)}, bf16[2048,256]{1,0:T(8,128)(2,1)}, u32[]{:S(2)}) copy-start(bf16[2048,256]{1,0:T(8,128)(2,1)} %param.11) | copy-start | bytes 3145732
  1.4 2.7 %copy-start.3 = (bf16[2048,1024]{1,0:T(8,128)(2,1)S(1)}, bf16[2048,1024]{1,0:T(8,128)(2,1)}, u32[]{:S(2)}) copy-start(bf16[2048,1024]{1,0:T(8,128)(2,1)} %param.14) | copy-start | bytes 12582916
  6.1 1.9 %copy-start.4 = (bf16[2048,1024]{1,0:T(8,128)(2,1)}, bf16[2048,1024]{1,0:T(8,128)(2,1)S(1)}, u32[]{:S(2)}) copy-start(bf16[2048,1024]{1,0:T(8,128)(2,1)S(1)} %fusion) | copy-start | bytes 12582916
  6.1 1.9 %copy-start.9 = (s32[8,1]{0,1:T(1,128)S(1)}, s32[8,1]{0,1:T(1,128)}, u32[]{:S(2)}) copy-start(s32[8,1]{0,1:T(1,128)} %param.17) | copy-start | bytes 100
  6.1 2.0 %copy-start.6 = (bf16[128,256]{1,0:T(8,128)(2,1)S(1)}, bf16[128,256]{1,0:T(8,128)(2,1)}, u32[]{:S(2)}) copy-start(bf16[128,256]{1,0:T(8,128)(2,1)} %param.13) | copy-start | bytes 196612
  6.2 2.0 %copy-start.8 = (bf16[1024,128]{1,0:T(8,128)(2,1)S(1)}, bf16[1024,128]{1,0:T(8,128)(2,1)}, u32[]{:S(2)}) copy-start(bf16[1024,128]{1,0:T(8,128)(2,1)} %param.16) | copy-start | bytes 786436
  10.0 46.7 %collective-permute-start.8 = (f32[1088,256]{1,0:T(8,128)}, f32[1088,256]{1,0:T(8,128)}, u32[]{:S(2)}, u32[]{:S(2)}) collective-permute-start(f32[1088,256]{1,0:T(8,128)} %fusion.3), channel_id=1, source_target_pairs={{0,1},{1,0},{2,3},{3,2},{4,5},{5,4},{6,7},{7,6},{8,9},{9,8},{10,11... | collective-permute-start | bytes 3342344 | tf_op jit(solution)/shard_map/ppermute | solution.py:47
  20.7 1.0 %copy-start.1 = (f32[1024,256]{1,0:T(8,128)}, f32[1024,256]{1,0:T(8,128)S(1)}, u32[]{:S(2)}) copy-start(f32[1024,256]{1,0:T(8,128)S(1)} %add.52) | copy-start | bytes 3145732 | tf_op jit(solution)/shard_map/cond
  21.7 2.1 %collective-permute-start = (f32[512,256]{1,0:T(8,128)S(1)}, f32[512,256]{1,0:T(8,128)}, u32[]{:S(2)}, u32[]{:S(2)}) collective-permute-start(f32[512,256]{1,0:T(8,128)S(1)} %constant_dynamic-slice_fusion.2), channel_id=1, source_target_pairs={{0,2},{2,0},{4,6},{6,4},{8,10},{10,8},{12,14},{14,12},{16,18},{18,... | collective-permute-start | bytes 1572872 | tf_op jit(solution)/shard_map/cond/branch_1_fun/ppermute | solution.py:47
  25.8 8.7 %collective-permute-start.1 = (f32[256,256]{1,0:T(8,128)}, f32[256,256]{1,0:T(8,128)}, u32[]{:S(2)}, u32[]{:S(2)}) collective-permute-start(f32[256,256]{1,0:T(8,128)} %constant_dynamic-slice_fusion.1), channel_id=1, source_target_pairs={{0,4},{2,6},{4,0},{6,2},{8,12},{10,14},{12,8},{14,10},{16,20},{18,... | collective-permute-start | bytes 786440 | tf_op jit(solution)/shard_map/cond/branch_1_fun/ppermute | solution.py:47
  35.5 0.7 copy-start.5
  36.2 5.0 %collective-permute-start.2 = (f32[128,256]{1,0:T(8,128)S(1)}, f32[128,256]{1,0:T(8,128)S(1)}, u32[]{:S(2)}, u32[]{:S(2)}) collective-permute-start(f32[128,256]{1,0:T(8,128)S(1)} %constant_dynamic-slice_fusion), channel_id=1, source_target_pairs={{0,8},{2,10},{4,12},{6,14},{8,0},{10,2},{12,4},{14,6},{16,24},{18,... | collective-permute-start | bytes 393224 | tf_op jit(solution)/shard_map/cond/branch_1_fun/ppermute | solution.py:47
  42.1 5.2 %collective-permute-start.3 = (f32[64,256]{1,0:T(8,128)S(1)}, f32[64,256]{1,0:T(8,128)S(1)}, u32[]{:S(2)}, u32[]{:S(2)}) collective-permute-start(f32[64,256]{1,0:T(8,128)S(1)} %constant_dynamic-slice_fusion.3), channel_id=1, source_target_pairs={{0,16},{2,18},{4,20},{6,22},{8,24},{10,26},{12,28},{14,30},{16,0},... | collective-permute-start | bytes 196616 | tf_op jit(solution)/shard_map/cond/branch_1_fun/ppermute | solution.py:47
  47.4 4.9 %collective-permute-start.4 = (bf16[64,256]{1,0:T(8,128)(2,1)S(1)}, bf16[64,256]{1,0:T(8,128)(2,1)S(1)}, u32[]{:S(2)}, u32[]{:S(2)}) collective-permute-start(bf16[64,256]{1,0:T(8,128)(2,1)S(1)} %add_convert_fusion), channel_id=1, source_target_pairs={{0,16},{2,18},{4,20},{6,22},{8,24},{10,26},{12,28},{14,30},{16,0},... | collective-permute-start | bytes 98312 | tf_op jit(solution)/shard_map/cond/branch_1_fun/ppermute | solution.py:61
  52.3 4.4 %collective-permute-start.5 = (bf16[128,256]{1,0:T(8,128)(2,1)S(1)}, bf16[128,256]{1,0:T(8,128)(2,1)S(1)}, u32[]{:S(2)}, u32[]{:S(2)}) collective-permute-start(bf16[128,256]{1,0:T(8,128)(2,1)S(1)} %maximum_select_fusion.1), channel_id=1, source_target_pairs={{0,8},{2,10},{4,12},{6,14},{8,0},{10,2},{12,4},{14,6},{16,24},{18,... | collective-permute-start | bytes 196616 | tf_op jit(solution)/shard_map/cond/branch_1_fun/ppermute | solution.py:61
  59.2 9.9 %collective-permute-start.9 = (bf16[1088,256]{1,0:T(8,128)(2,1)S(1)}, bf16[1088,256]{1,0:T(8,128)(2,1)S(1)}, u32[]{:S(2)}, u32[]{:S(2)}) collective-permute-start(bf16[1088,256]{1,0:T(8,128)(2,1)S(1)} %fusion.8), channel_id=1, source_target_pairs={{0,1},{1,0},{2,3},{3,2},{4,5},{5,4},{6,7},{7,6},{8,9},{9,8},{10,11... | collective-permute-start | bytes 1671176 | tf_op jit(solution)/shard_map/ppermute | solution.py:61
  59.7 5.0 %collective-permute-start.6 = (bf16[256,256]{1,0:T(8,128)(2,1)S(1)}, bf16[256,256]{1,0:T(8,128)(2,1)S(1)}, u32[]{:S(2)}, u32[]{:S(2)}) collective-permute-start(bf16[256,256]{1,0:T(8,128)(2,1)S(1)} %get-tuple-element.24), channel_id=1, source_target_pairs={{0,4},{2,6},{4,0},{6,2},{8,12},{10,14},{12,8},{14,10},{16,20},{18,... | collective-permute-start | bytes 393224 | tf_op jit(solution)/shard_map/cond/branch_1_fun/ppermute | solution.py:61
  64.8 1.6 %collective-permute-start.7 = (bf16[512,256]{1,0:T(8,128)(2,1)S(1)}, bf16[512,256]{1,0:T(8,128)(2,1)S(1)}, u32[]{:S(2)}, u32[]{:S(2)}) collective-permute-start(bf16[512,256]{1,0:T(8,128)(2,1)S(1)} %maximum_select_fusion.3), channel_id=1, source_target_pairs={{0,2},{2,0},{4,6},{6,4},{8,10},{10,8},{12,14},{14,12},{16,18},{18,... | collective-permute-start | bytes 786440 | tf_op jit(solution)/shard_map/cond/branch_1_fun/ppermute | solution.py:61
  66.6 3.8 %copy-start.7 = (bf16[1024,256]{1,0:T(8,128)(2,1)}, bf16[1024,256]{1,0:T(8,128)(2,1)S(1)}, u32[]{:S(2)}) copy-start(bf16[1024,256]{1,0:T(8,128)(2,1)S(1)} %get-tuple-element.35) | copy-start | bytes 1572868

commit v9 on v3

--- a/solution.py
+++ b/solution.py
@@ -1,6 +1,8 @@
 import jax
 import jax.numpy as jnp
 from jax import lax
+from jax.experimental import pallas as pl
+from jax.experimental.pallas import tpu as pltpu
 from jax.sharding import PartitionSpec as P
 
 step_users = 0.015
@@ -62,6 +64,52 @@
     return parts
 
 
+def rating_kernel(flags_ref, u_ref, i_ref, r_ref, user_ref, item_ref):
+    block = pl.program_id(0)
+    users = u_ref[...]
+    items = i_ref[...]
+    predicted = lax.dot_general(users, items, (((1,), (1,)), ((), ())), preferred_element_type=jnp.float32)
+    residual = r_ref[...].astype(jnp.float32) - predicted
+    column_tile = lax.broadcasted_iota(jnp.int32, (1, residual.shape[1]), 1) // 128
+    mask = jnp.zeros((1, residual.shape[1]), jnp.float32)
+    for tile in range(residual.shape[1] // 128):
+        mask = jnp.where(column_tile == tile, flags_ref[block, tile].astype(jnp.float32), mask)
+    errors = (residual * mask).astype(jnp.bfloat16)
+    user_ref[...] = jnp.dot(errors, items, preferred_element_type=jnp.float32)
+
+    @pl.when(block == 0)
+    def _():
+        item_ref[...] = jnp.zeros_like(item_ref)
+
+    item_ref[...] += lax.dot_general(errors, users, (((0,), (0,)), ((), ())), preferred_element_type=jnp.float32)
+
+
+def rating_partials(user_factors, item_factors, ratings, rating_tiles):
+    rows, rank = user_factors.shape
+    cols = item_factors.shape[0]
+    return pl.pallas_call(
+        rating_kernel,
+        grid_spec=pltpu.PrefetchScalarGridSpec(
+            num_scalar_prefetch=1,
+            grid=(rows // 128,),
+            in_specs=[
+                pl.BlockSpec((128, rank), lambda b, f: (b, 0)),
+                pl.BlockSpec((cols, rank), lambda b, f: (0, 0)),
+                pl.BlockSpec((128, cols), lambda b, f: (b, 0)),
+            ],
+            out_specs=[
+                pl.BlockSpec((128, rank), lambda b, f: (b, 0)),
+                pl.BlockSpec((cols, rank), lambda b, f: (0, 0)),
+            ],
+        ),
+        out_shape=[
+            jax.ShapeDtypeStruct((rows, rank), jnp.float32),
+            jax.ShapeDtypeStruct((cols, rank), jnp.float32),
+        ],
+        compiler_params=pltpu.CompilerParams(dimension_semantics=("arbitrary",)),
+    )(rating_tiles, user_factors, item_factors, ratings)
+
+
 def shards(user_factors, item_factors, tag_factors, ratings, rating_tiles, tag_links, link_tiles):
     group_count = lax.axis_size("group")
     loop_count = lax.axis_size("loop")
@@ -69,19 +117,16 @@
     loop_position = lax.axis_index("loop")
 
     link_errors = residual_of(tag_links, item_factors, tag_factors, link_tiles)
-    rating_errors = residual_of(ratings, user_factors, item_factors, rating_tiles)
-    user_part = jnp.dot(rating_errors, item_factors, preferred_element_type=jnp.float32)
+    user_part, rating_item_part = rating_partials(
+        user_factors, item_factors, ratings, rating_tiles
+    )
     tag_part = transposed_product(link_errors, item_factors)
     joint_part = jnp.concatenate([user_part, tag_part], 0)
-
-    joint_part, rating_errors, link_errors = lax.optimization_barrier(
-        (joint_part, rating_errors, link_errors)
+    item_part = rating_item_part + jnp.dot(
+        link_errors, tag_factors, preferred_element_type=jnp.float32
     )
     (joint_share,), (joint_offset,) = halving_scatter(
         [joint_part], "loop", loop_count, loop_position
-    )
-    item_part = transposed_product(rating_errors, user_factors) + jnp.dot(
-        link_errors, tag_factors, preferred_element_type=jnp.float32
     )
     joint_factors = jnp.concatenate([user_factors, tag_factors], 0)
     fresh_joint = advance(

time: 64.7 us -> 76.6 us (1.18)
  Pallas kernels: 0 us -> 19 us
  matrix products: 7.55 us -> 0.85 us
  local copies, waits for them, and re-layouts: 6.65 us -> 5.08 us
  other arithmetic: 6.3 us -> 7.5 us
    pallas_call x0 -> x1, Pallas kernels: none -> 19 us  [rating_partials(): pl.pallas_call(rating_kernel, grid_spec=pltpu.PrefetchScalarGridSpec(num_...]
    dot_general x2 -> x1, matrix products: 2.52 us -> 0.26 us  [transposed_product(): lax.dot_general(first_operand, second_operand, (((0,), (0,)), ((), ())),...]
    dot_general x2 -> x1, matrix products: 2.26 us -> 0.31 us  [residual_of(): lax.dot_general(row_factors, column_factors, (((1,), (1,)), ((), ())), pr...]
    dot_general x1 -> x0, matrix products: 1.28 us -> none  [shards(): jnp.dot(rating_errors, item_factors, preferred_element_type=jnp.float32)]
    dot_general x1, matrix products: 1.5 us -> 0.28 us  [shards(): jnp.dot(link_errors, tag_factors, preferred_element_type=jnp.float32)]
    concatenate x1, other arithmetic: 0.15 us -> 1.29 us  [shards(): joint_part = jnp.concatenate([user_part, tag_part], 0)]
    dynamic_slice x5 -> x4, local copies, waits for them, and re-layouts: 1.18 us -> 0.09 us  [halving_scatter(): lax.dynamic_slice_in_dim(p, (1 - side) * h, h, 0)]
    unnamed x14 -> x13, local copies, waits for them, and re-layouts: 3.05 us -> 3.24 us
  transfers between devices with their start and end apart: 10 -> 10, of which waited for: 8 -> 8; matrix products, arithmetic and copies ran while one was open for 8% -> 7% of each run, Pallas kernels for 0% -> 0%
where the time goes in v9:
time: 76.6 us; the launch traced here: 76 us
  waiting for transfers between devices  24.8 us (32%)
  Pallas kernels  19 us (25%)
  starting transfers between devices  17.9 us (23%)
  other arithmetic  7.5 us (10%)
  local copies, waits for them, and re-layouts  5.08 us (7%)
  matrix products  0.85 us (1%)
  between operations  0.8 us (1%)
    pallas_call x1, Pallas kernels, rating_partials(): pl.pallas_call(rating_kernel, grid_spec=pltpu.PrefetchScalarGridSpec(num_...  19 us
    ppermute x5, waiting for transfers between devices, doubling_gather(): got = lax.ppermute(tuple(parts), axis, xor_pairs(count, bit))  14 us
    ppermute x5, waiting for transfers between devices, halving_scatter(): got = lax.ppermute(tuple(sent), axis, xor_pairs(count, bit))  10.9 us
    ppermute x5, starting transfers between devices, halving_scatter(): got = lax.ppermute(tuple(sent), axis, xor_pairs(count, bit))  9.68 us
    ppermute x5, starting transfers between devices, doubling_gather(): got = lax.ppermute(tuple(parts), axis, xor_pairs(count, bit))  8.25 us
    unnamed x13, local copies, waits for them, and re-layouts  3.24 us
    add x3, other arithmetic, halving_scatter(): parts = [k + g for k, g in zip(kept, got)]  2.27 us
    convert_element_type x2, other arithmetic, advance(): return (factors.astype(jnp.float32) + rate * gradient).astype(jnp.bfloat16)  1.86 us
  transfers between devices with their start and end apart: 10, of which 8 were waited for; matrix products, arithmetic and copies ran while one was open for 7% of the time, Pallas kernels for 0%

profile of v9, /device:TPU:0, one launch (start us, length us, event | category | flops | bytes accessed | tf_op | source)
XLA Modules:
  0.0 76.0 jit_solution(18314771504772130897)
XLA Ops:
  0.6 1.4 %copy.10.flags_ref = s32[16,8]{1,0:T(8,128)} copy(s32[16,8]{0,1:T(8,128)} %param.11) | data formatting | bytes 1024 | tf_op args[4]
  2.7 19.0 %shard_map.94 = (f32[2048,256]{1,0:T(8,128)}, f32[1024,256]{1,0:T(8,128)}) custom-call(s32[16,8]{1,0:T(8,128)} %copy.10.flags_ref, bf16[2048,256]{1,0:T(8,128)(2,1)} %u_ref.1, bf16[1024,256]{1,0:T(8,128)(2,1)} %i_ref.1, bf16[2048,1024]{1,0:T(8,128)(2,1)} %r_ref.1), custom_call_target="tpu_custom_call" | custom-call | tf_op jit(solution)/shard_map/pallas_call | solution.py:90
  25.1 1.4 %collective-permute-done.2 = f32[512,256]{1,0:T(8,128)} collective-permute-done((f32[512,256]{1,0:T(8,128)S(1)}, f32[512,256]{1,0:T(8,128)}, u32[]{:S(2)}, u32[]{:S(2)}) %collective-permute-start.2) | collective-permute-done | bytes 524320 | tf_op jit(solution)/shard_map/ppermute | solution.py:49
  26.5 1.3 %dynamic-slice_add_fusion = f32[512,256]{1,0:T(8,128)S(1)} fusion(f32[512,256]{1,0:T(8,128)} %collective-permute-done.2, f32[1024,256]{1,0:T(8,128)} %copy-done.2, s32[]{:T(128)S(6)} %select_n.85), kind=kLoop, calls=%fused_computation.19 | loop fusion | flops 131072 | bytes 1572868 | tf_op jit(solution)/shard_map/add | solution.py:50
  27.8 2.9 %collective-permute-start.3 = (f32[256,256]{1,0:T(8,128)S(1)}, f32[256,256]{1,0:T(8,128)}, u32[]{:S(2)}, u32[]{:S(2)}) collective-permute-start(f32[256,256]{1,0:T(8,128)S(1)} %constant_dynamic-slice_fusion.1), channel_id=1, source_target_pairs={{0,4},{2,6},{4,0},{6,2},{8,12},{10,14},{12,8},{14,10},{16,20},{18,... | collective-permute-start | bytes 786440 | tf_op jit(solution)/shard_map/ppermute | solution.py:49
  30.7 1.3 %fusion.2 = f32[1088,256]{1,0:T(8,128)} fusion(s32[]{:T(128)S(6)} %select_n.78, f32[2048,256]{1,0:T(8,128)S(1)} %copy-done, f32[128,256]{1,0:T(8,128)S(1)} %fusion.9), kind=kLoop, calls=%fused_computation.8 | loop fusion | flops 278528 | bytes 3342340 | tf_op jit(solution)/shard_map/concatenate | solution.py:124
  32.0 1.5 %collective-permute-start = (f32[1088,256]{1,0:T(8,128)}, f32[1088,256]{1,0:T(8,128)}, u32[]{:S(2)}, u32[]{:S(2)}) collective-permute-start(f32[1088,256]{1,0:T(8,128)} %fusion.2), channel_id=1, source_target_pairs={{0,1},{1,0},{2,3},{3,2},{4,5},{5,4},{6,7},{7,6},{8,9},{9,8},{10,11... | collective-permute-start | bytes 3342344 | tf_op jit(solution)/shard_map/ppermute | solution.py:49
  33.5 3.9 %collective-permute-done.3 = f32[256,256]{1,0:T(8,128)} collective-permute-done((f32[256,256]{1,0:T(8,128)S(1)}, f32[256,256]{1,0:T(8,128)}, u32[]{:S(2)}, u32[]{:S(2)}) %collective-permute-start.3) | collective-permute-done | bytes 262176 | tf_op jit(solution)/shard_map/ppermute | solution.py:49
  37.4 1.0 %dynamic-slice_add_fusion.1 = f32[256,256]{1,0:T(8,128)S(1)} fusion(f32[256,256]{1,0:T(8,128)} %collective-permute-done.3, f32[512,256]{1,0:T(8,128)S(1)} %dynamic-slice_add_fusion, s32[]{:T(128)S(6)} %select_n.87), kind=kLoop, calls=%fused_computation.21 | loop fusion | flops 65536 | bytes 786436 | tf_op jit(solution)/shard_map/add | solution.py:50
  38.4 1.9 %collective-permute-start.4 = (f32[128,256]{1,0:T(8,128)S(1)}, f32[128,256]{1,0:T(8,128)S(1)}, u32[]{:S(2)}, u32[]{:S(2)}) collective-permute-start(f32[128,256]{1,0:T(8,128)S(1)} %constant_dynamic-slice_fusion), channel_id=1, source_target_pairs={{0,8},{2,10},{4,12},{6,14},{8,0},{10,2},{12,4},{14,6},{16,24},{18,... | collective-permute-start | bytes 393224 | tf_op jit(solution)/shard_map/ppermute | solution.py:49
  40.3 3.2 %collective-permute-done.4 = f32[128,256]{1,0:T(8,128)S(1)} collective-permute-done((f32[128,256]{1,0:T(8,128)S(1)}, f32[128,256]{1,0:T(8,128)S(1)}, u32[]{:S(2)}, u32[]{:S(2)}) %collective-permute-start.4) | collective-permute-done | bytes 131104 | tf_op jit(solution)/shard_map/ppermute | solution.py:49
  43.6 2.8 %collective-permute-start.5 = (f32[64,256]{1,0:T(8,128)S(1)}, f32[64,256]{1,0:T(8,128)S(1)}, u32[]{:S(2)}, u32[]{:S(2)}) collective-permute-start(f32[64,256]{1,0:T(8,128)S(1)} %constant_dynamic-slice_fusion.3), channel_id=1, source_target_pairs={{0,16},{2,18},{4,20},{6,22},{8,24},{10,26},{12,28},{14,30},{16,0},... | collective-permute-start | bytes 196616 | tf_op jit(solution)/shard_map/ppermute | solution.py:49
  46.4 2.4 %collective-permute-done.5 = f32[64,256]{1,0:T(8,128)S(1)} collective-permute-done((f32[64,256]{1,0:T(8,128)S(1)}, f32[64,256]{1,0:T(8,128)S(1)}, u32[]{:S(2)}, u32[]{:S(2)}) %collective-permute-start.5) | collective-permute-done | bytes 65568 | tf_op jit(solution)/shard_map/ppermute | solution.py:49
  48.8 2.9 %collective-permute-start.6 = (bf16[64,256]{1,0:T(8,128)(2,1)S(1)}, bf16[64,256]{1,0:T(8,128)(2,1)S(1)}, u32[]{:S(2)}, u32[]{:S(2)}) collective-permute-start(bf16[64,256]{1,0:T(8,128)(2,1)S(1)} %add_convert_fusion), channel_id=1, source_target_pairs={{0,16},{2,18},{4,20},{6,22},{8,24},{10,26},{12,28},{14,30},{16,0},... | collective-permute-start | bytes 98312 | tf_op jit(solution)/shard_map/ppermute | solution.py:59
  51.7 2.1 %collective-permute-done.6 = bf16[64,256]{1,0:T(8,128)(2,1)S(1)} collective-permute-done((bf16[64,256]{1,0:T(8,128)(2,1)S(1)}, bf16[64,256]{1,0:T(8,128)(2,1)S(1)}, u32[]{:S(2)}, u32[]{:S(2)}) %collective-permute-start.6) | collective-permute-done | bytes 32800 | tf_op jit(solution)/shard_map/ppermute | solution.py:59
  53.8 2.0 %collective-permute-start.7 = (bf16[128,256]{1,0:T(8,128)(2,1)S(1)}, bf16[128,256]{1,0:T(8,128)(2,1)S(1)}, u32[]{:S(2)}, u32[]{:S(2)}) collective-permute-start(bf16[128,256]{1,0:T(8,128)(2,1)S(1)} %maximum_select_fusion.4), channel_id=1, source_target_pairs={{0,8},{2,10},{4,12},{6,14},{8,0},{10,2},{12,4},{14,6},{16,24},{18,... | collective-permute-start | bytes 196616 | tf_op jit(solution)/shard_map/ppermute | solution.py:59
  55.8 2.4 %collective-permute-done.7 = bf16[128,256]{1,0:T(8,128)(2,1)S(1)} collective-permute-done((bf16[128,256]{1,0:T(8,128)(2,1)S(1)}, bf16[128,256]{1,0:T(8,128)(2,1)S(1)}, u32[]{:S(2)}, u32[]{:S(2)}) %collective-permute-start.7) | collective-permute-done | bytes 65568 | tf_op jit(solution)/shard_map/ppermute | solution.py:59
  58.2 1.7 %collective-permute-start.8 = (bf16[256,256]{1,0:T(8,128)(2,1)S(1)}, bf16[256,256]{1,0:T(8,128)(2,1)S(1)}, u32[]{:S(2)}, u32[]{:S(2)}) collective-permute-start(bf16[256,256]{1,0:T(8,128)(2,1)S(1)} %maximum_select_fusion.3), channel_id=1, source_target_pairs={{0,4},{2,6},{4,0},{6,2},{8,12},{10,14},{12,8},{14,10},{16,20},{18,... | collective-permute-start | bytes 393224 | tf_op jit(solution)/shard_map/ppermute | solution.py:59
  59.9 1.8 %fusion.7 = bf16[1088,256]{1,0:T(8,128)(2,1)S(1)} fusion(f32[1088,256]{1,0:T(8,128)} %collective-permute-done, s32[]{:T(128)S(6)} %select_n.77, f32[2048,256]{1,0:T(8,128)S(1)} %copy-done, f32[128,256]{1,0:T(8,128)S(1)} %fusion.9, bf16[2048,256]{1,0:T(8,128)(2,1)} %u_ref.1, bf16[128,256]{1,0:T(8,128)(2,1)} %param.9), kind=kLoop, calls=%fused_computation.13 | loop fusion | flops 2506752 | bytes 5013508 | tf_op jit(solution)/shard_map/convert_element_type | solution.py:34
  61.8 1.6 %collective-permute-start.1 = (bf16[1088,256]{1,0:T(8,128)(2,1)S(1)}, bf16[1088,256]{1,0:T(8,128)(2,1)S(1)}, u32[]{:S(2)}, u32[]{:S(2)}) collective-permute-start(bf16[1088,256]{1,0:T(8,128)(2,1)S(1)} %fusion.7), channel_id=1, source_target_pairs={{0,1},{1,0},{2,3},{3,2},{4,5},{5,4},{6,7},{7,6},{8,9},{9,8},{10,11... | collective-permute-start | bytes 1671176 | tf_op jit(solution)/shard_map/ppermute | solution.py:59
  63.6 1.5 %collective-permute-done.9 = bf16[512,256]{1,0:T(8,128)(2,1)S(1)} collective-permute-done((bf16[512,256]{1,0:T(8,128)(2,1)S(1)}, bf16[512,256]{1,0:T(8,128)(2,1)S(1)}, u32[]{:S(2)}, u32[]{:S(2)}) %collective-permute-start.9) | collective-permute-done | bytes 262176 | tf_op jit(solution)/shard_map/ppermute | solution.py:59
  65.1 1.0 %maximum_select_fusion.1 = bf16[1024,256]{1,0:T(8,128)(2,1)} fusion(bf16[512,256]{1,0:T(8,128)(2,1)S(1)} %collective-permute-done.9, bf16[512,256]{1,0:T(8,128)(2,1)S(1)} %maximum_select_fusion.2, pred[]{:T(512)S(6)} %eq.16), kind=kLoop, calls=%fused_computation.18 | loop fusion | flops 2359296 | bytes 1048577 | tf_op jit(solution)/shard_map/jit(_where)/select_n | solution.py:61
  66.1 8.0 %collective-permute-done.1 = bf16[1088,256]{1,0:T(8,128)(2,1)S(1)} collective-permute-done((bf16[1088,256]{1,0:T(8,128)(2,1)S(1)}, bf16[1088,256]{1,0:T(8,128)(2,1)S(1)}, u32[]{:S(2)}, u32[]{:S(2)}) %collective-permute-start.1) | collective-permute-done | bytes 557088 | tf_op jit(solution)/shard_map/ppermute | solution.py:59
  74.3 1.0 %slice.8 = bf16[2048,256]{1,0:T(8,128)(2,1)} slice(bf16[2176,256]{1,0:T(8,128)(2,1)S(1)} %maximum_select_fusion), slice={[0:2048], [0:256]} | slice | bytes 2097152 | tf_op jit(solution)/shard_map/slice | solution.py:142
  (32 shorter events, 5.2 us)
Async XLA Ops:
  2.7 19.0 %copy-start.1 = (bf16[1024,256]{1,0:T(8,128)(2,1)S(1)}, bf16[1024,256]{1,0:T(8,128)(2,1)}, u32[]{:S(2)}) copy-start(bf16[1024,256]{1,0:T(8,128)(2,1)} %i_ref.1) | copy-start | bytes 1572868
  2.7 19.0 %copy-start.4 = (bf16[128,256]{1,0:T(8,128)(2,1)S(1)}, bf16[128,256]{1,0:T(8,128)(2,1)}, u32[]{:S(2)}) copy-start(bf16[128,256]{1,0:T(8,128)(2,1)} %param.9) | copy-start | bytes 196612
  2.7 19.0 %copy-start.5 = (bf16[1024,128]{1,0:T(8,128)(2,1)S(1)}, bf16[1024,128]{1,0:T(8,128)(2,1)}, u32[]{:S(2)}) copy-start(bf16[1024,128]{1,0:T(8,128)(2,1)} %param.12) | copy-start | bytes 786436
  21.8 1.2 %copy-start.3 = (f32[1024,256]{1,0:T(8,128)S(1)}, f32[1024,256]{1,0:T(8,128)}, u32[]{:S(2)}) copy-start(f32[1024,256]{1,0:T(8,128)} %get-tuple-element.6) | copy-start | bytes 3145732
  23.3 1.0 %copy-start.2 = (f32[1024,256]{1,0:T(8,128)}, f32[1024,256]{1,0:T(8,128)S(1)}, u32[]{:S(2)}) copy-start(f32[1024,256]{1,0:T(8,128)S(1)} %convolution_add_fusion) | copy-start | bytes 3145732
  24.3 2.2 %collective-permute-start.2 = (f32[512,256]{1,0:T(8,128)S(1)}, f32[512,256]{1,0:T(8,128)}, u32[]{:S(2)}, u32[]{:S(2)}) collective-permute-start(f32[512,256]{1,0:T(8,128)S(1)} %constant_dynamic-slice_fusion.2), channel_id=1, source_target_pairs={{0,2},{2,0},{4,6},{6,4},{8,10},{10,8},{12,14},{14,12},{16,18},{18,... | collective-permute-start | bytes 1572872 | tf_op jit(solution)/shard_map/ppermute | solution.py:49
  25.1 5.6 %copy-start = (f32[2048,256]{1,0:T(8,128)S(1)}, f32[2048,256]{1,0:T(8,128)}, u32[]{:S(2)}) copy-start(f32[2048,256]{1,0:T(8,128)} %get-tuple-element.5) | copy-start | bytes 6291460
  27.8 9.6 %collective-permute-start.3 = (f32[256,256]{1,0:T(8,128)S(1)}, f32[256,256]{1,0:T(8,128)}, u32[]{:S(2)}, u32[]{:S(2)}) collective-permute-start(f32[256,256]{1,0:T(8,128)S(1)} %constant_dynamic-slice_fusion.1), channel_id=1, source_target_pairs={{0,4},{2,6},{4,0},{6,2},{8,12},{10,14},{12,8},{14,10},{16,20},{18,... | collective-permute-start | bytes 786440 | tf_op jit(solution)/shard_map/ppermute | solution.py:49
  32.0 27.9 %collective-permute-start = (f32[1088,256]{1,0:T(8,128)}, f32[1088,256]{1,0:T(8,128)}, u32[]{:S(2)}, u32[]{:S(2)}) collective-permute-start(f32[1088,256]{1,0:T(8,128)} %fusion.2), channel_id=1, source_target_pairs={{0,1},{1,0},{2,3},{3,2},{4,5},{5,4},{6,7},{7,6},{8,9},{9,8},{10,11... | collective-permute-start | bytes 3342344 | tf_op jit(solution)/shard_map/ppermute | solution.py:49
  38.4 5.1 %collective-permute-start.4 = (f32[128,256]{1,0:T(8,128)S(1)}, f32[128,256]{1,0:T(8,128)S(1)}, u32[]{:S(2)}, u32[]{:S(2)}) collective-permute-start(f32[128,256]{1,0:T(8,128)S(1)} %constant_dynamic-slice_fusion), channel_id=1, source_target_pairs={{0,8},{2,10},{4,12},{6,14},{8,0},{10,2},{12,4},{14,6},{16,24},{18,... | collective-permute-start | bytes 393224 | tf_op jit(solution)/shard_map/ppermute | solution.py:49
  43.6 5.2 %collective-permute-start.5 = (f32[64,256]{1,0:T(8,128)S(1)}, f32[64,256]{1,0:T(8,128)S(1)}, u32[]{:S(2)}, u32[]{:S(2)}) collective-permute-start(f32[64,256]{1,0:T(8,128)S(1)} %constant_dynamic-slice_fusion.3), channel_id=1, source_target_pairs={{0,16},{2,18},{4,20},{6,22},{8,24},{10,26},{12,28},{14,30},{16,0},... | collective-permute-start | bytes 196616 | tf_op jit(solution)/shard_map/ppermute | solution.py:49
  48.8 5.0 %collective-permute-start.6 = (bf16[64,256]{1,0:T(8,128)(2,1)S(1)}, bf16[64,256]{1,0:T(8,128)(2,1)S(1)}, u32[]{:S(2)}, u32[]{:S(2)}) collective-permute-start(bf16[64,256]{1,0:T(8,128)(2,1)S(1)} %add_convert_fusion), channel_id=1, source_target_pairs={{0,16},{2,18},{4,20},{6,22},{8,24},{10,26},{12,28},{14,30},{16,0},... | collective-permute-start | bytes 98312 | tf_op jit(solution)/shard_map/ppermute | solution.py:59
  53.8 4.3 %collective-permute-start.7 = (bf16[128,256]{1,0:T(8,128)(2,1)S(1)}, bf16[128,256]{1,0:T(8,128)(2,1)S(1)}, u32[]{:S(2)}, u32[]{:S(2)}) collective-permute-start(bf16[128,256]{1,0:T(8,128)(2,1)S(1)} %maximum_select_fusion.4), channel_id=1, source_target_pairs={{0,8},{2,10},{4,12},{6,14},{8,0},{10,2},{12,4},{14,6},{16,24},{18,... | collective-permute-start | bytes 196616 | tf_op jit(solution)/shard_map/ppermute | solution.py:59
  58.2 5.2 %collective-permute-start.8 = (bf16[256,256]{1,0:T(8,128)(2,1)S(1)}, bf16[256,256]{1,0:T(8,128)(2,1)S(1)}, u32[]{:S(2)}, u32[]{:S(2)}) collective-permute-start(bf16[256,256]{1,0:T(8,128)(2,1)S(1)} %maximum_select_fusion.3), channel_id=1, source_target_pairs={{0,4},{2,6},{4,0},{6,2},{8,12},{10,14},{12,8},{14,10},{16,20},{18,... | collective-permute-start | bytes 393224 | tf_op jit(solution)/shard_map/ppermute | solution.py:59
  61.8 12.3 %collective-permute-start.1 = (bf16[1088,256]{1,0:T(8,128)(2,1)S(1)}, bf16[1088,256]{1,0:T(8,128)(2,1)S(1)}, u32[]{:S(2)}, u32[]{:S(2)}) collective-permute-start(bf16[1088,256]{1,0:T(8,128)(2,1)S(1)} %fusion.7), channel_id=1, source_target_pairs={{0,1},{1,0},{2,3},{3,2},{4,5},{5,4},{6,7},{7,6},{8,9},{9,8},{10,11... | collective-permute-start | bytes 1671176 | tf_op jit(solution)/shard_map/ppermute | solution.py:59
  63.5 1.6 %collective-permute-start.9 = (bf16[512,256]{1,0:T(8,128)(2,1)S(1)}, bf16[512,256]{1,0:T(8,128)(2,1)S(1)}, u32[]{:S(2)}, u32[]{:S(2)}) collective-permute-start(bf16[512,256]{1,0:T(8,128)(2,1)S(1)} %maximum_select_fusion.2), channel_id=1, source_target_pairs={{0,2},{2,0},{4,6},{6,4},{8,10},{10,8},{12,14},{14,12},{16,18},{18,... | collective-permute-start | bytes 786440 | tf_op jit(solution)/shard_map/ppermute | solution.py:59

commit v10 on v9

--- a/solution.py
+++ b/solution.py
@@ -64,17 +64,23 @@
     return parts
 
 
-def rating_kernel(flags_ref, u_ref, i_ref, r_ref, user_ref, item_ref):
+def rating_kernel(flags_ref, u_ref, i_ref, r_ref, user_ref, item_ref, err_ref):
     block = pl.program_id(0)
     users = u_ref[...]
     items = i_ref[...]
+    block_rows, cols = err_ref.shape
     predicted = lax.dot_general(users, items, (((1,), (1,)), ((), ())), preferred_element_type=jnp.float32)
-    residual = r_ref[...].astype(jnp.float32) - predicted
-    column_tile = lax.broadcasted_iota(jnp.int32, (1, residual.shape[1]), 1) // 128
-    mask = jnp.zeros((1, residual.shape[1]), jnp.float32)
-    for tile in range(residual.shape[1] // 128):
-        mask = jnp.where(column_tile == tile, flags_ref[block, tile].astype(jnp.float32), mask)
-    errors = (residual * mask).astype(jnp.bfloat16)
+    column_tile = lax.broadcasted_iota(jnp.int32, (1, cols), 1) // 128
+    row_tiles = block_rows // 128
+    for row_tile in range(row_tiles):
+        rows = slice(row_tile * 128, (row_tile + 1) * 128)
+        mask = jnp.zeros((1, cols), jnp.float32)
+        for tile in range(cols // 128):
+            flag = flags_ref[block * row_tiles + row_tile, tile].astype(jnp.float32)
+            mask = jnp.where(column_tile == tile, flag, mask)
+        residual = r_ref[rows, :].astype(jnp.float32) - predicted[rows, :]
+        err_ref[rows, :] = (residual * mask).astype(jnp.bfloat16)
+    errors = err_ref[...]
     user_ref[...] = jnp.dot(errors, items, preferred_element_type=jnp.float32)
 
     @pl.when(block == 0)
@@ -87,20 +93,22 @@
 def rating_partials(user_factors, item_factors, ratings, rating_tiles):
     rows, rank = user_factors.shape
     cols = item_factors.shape[0]
+    block_rows = 512 if rows % 512 == 0 else 128
     return pl.pallas_call(
         rating_kernel,
         grid_spec=pltpu.PrefetchScalarGridSpec(
             num_scalar_prefetch=1,
-            grid=(rows // 128,),
+            grid=(rows // block_rows,),
             in_specs=[
-                pl.BlockSpec((128, rank), lambda b, f: (b, 0)),
+                pl.BlockSpec((block_rows, rank), lambda b, f: (b, 0)),
                 pl.BlockSpec((cols, rank), lambda b, f: (0, 0)),
-                pl.BlockSpec((128, cols), lambda b, f: (b, 0)),
+                pl.BlockSpec((block_rows, cols), lambda b, f: (b, 0)),
             ],
             out_specs=[
-                pl.BlockSpec((128, rank), lambda b, f: (b, 0)),
+                pl.BlockSpec((block_rows, rank), lambda b, f: (b, 0)),
                 pl.BlockSpec((cols, rank), lambda b, f: (0, 0)),
             ],
+            scratch_shapes=[pltpu.VMEM((block_rows, cols), jnp.bfloat16)],
         ),
         out_shape=[
             jax.ShapeDtypeStruct((rows, rank), jnp.float32),

time: 76.6 us -> 67.7 us (0.88)
  Pallas kernels: 19 us -> 10.4 us
    pallas_call x1, Pallas kernels: 19 us -> 10.4 us  [rating_partials(): pl.pallas_call(rating_kernel, grid_spec=pltpu.PrefetchScalarGridSpec(num_...]
  transfers between devices with their start and end apart: 10 -> 10, of which waited for: 8 -> 8; matrix products, arithmetic and copies ran while one was open for 7% -> 8% of each run, Pallas kernels for 0% -> 0%
where the time goes in v10:
time: 67.7 us; the launch traced here: 67.4 us
  waiting for transfers between devices  24.8 us (37%)
  starting transfers between devices  18 us (27%)
  Pallas kernels  10.4 us (15%)
  other arithmetic  7.5 us (11%)
  local copies, waits for them, and re-layouts  5.08 us (8%)
  matrix products  0.85 us (1%)
  between operations  0.8 us (1%)
    ppermute x5, waiting for transfers between devices, doubling_gather(): got = lax.ppermute(tuple(parts), axis, xor_pairs(count, bit))  13.9 us
    ppermute x5, waiting for transfers between devices, halving_scatter(): got = lax.ppermute(tuple(sent), axis, xor_pairs(count, bit))  10.9 us
    pallas_call x1, Pallas kernels, rating_partials(): pl.pallas_call(rating_kernel, grid_spec=pltpu.PrefetchScalarGridSpec(num_...  10.4 us
    ppermute x5, starting transfers between devices, halving_scatter(): got = lax.ppermute(tuple(sent), axis, xor_pairs(count, bit))  9.7 us
    ppermute x5, starting transfers between devices, doubling_gather(): got = lax.ppermute(tuple(parts), axis, xor_pairs(count, bit))  8.27 us
    unnamed x13, local copies, waits for them, and re-layouts  3.24 us
    add x3, other arithmetic, halving_scatter(): parts = [k + g for k, g in zip(kept, got)]  2.27 us
    convert_element_type x2, other arithmetic, advance(): return (factors.astype(jnp.float32) + rate * gradient).astype(jnp.bfloat16)  1.86 us
  transfers between devices with their start and end apart: 10, of which 8 were waited for; matrix products, arithmetic and copies ran while one was open for 8% of the time, Pallas kernels for 0%

profile of v10, /device:TPU:0, one launch (start us, length us, event | category | flops | bytes accessed | tf_op | source)
XLA Modules:
  0.0 67.4 jit_solution(14165222100597969979)
XLA Ops:
  0.6 1.4 %copy.10.flags_ref = s32[16,8]{1,0:T(8,128)} copy(s32[16,8]{0,1:T(8,128)} %param.11) | data formatting | bytes 1024 | tf_op args[4]
  2.7 10.4 %shard_map.94 = (f32[2048,256]{1,0:T(8,128)}, f32[1024,256]{1,0:T(8,128)}) custom-call(s32[16,8]{1,0:T(8,128)} %copy.10.flags_ref, bf16[2048,256]{1,0:T(8,128)(2,1)} %u_ref.1, bf16[1024,256]{1,0:T(8,128)(2,1)} %i_ref.1, bf16[2048,1024]{1,0:T(8,128)(2,1)} %r_ref.1), custom_call_target="tpu_custom_call" | custom-call | tf_op jit(solution)/shard_map/pallas_call | solution.py:97
  16.5 1.4 %collective-permute-done.2 = f32[512,256]{1,0:T(8,128)} collective-permute-done((f32[512,256]{1,0:T(8,128)S(1)}, f32[512,256]{1,0:T(8,128)}, u32[]{:S(2)}, u32[]{:S(2)}) %collective-permute-start.2) | collective-permute-done | bytes 524320 | tf_op jit(solution)/shard_map/ppermute | solution.py:49
  17.9 1.3 %dynamic-slice_add_fusion = f32[512,256]{1,0:T(8,128)S(1)} fusion(f32[512,256]{1,0:T(8,128)} %collective-permute-done.2, f32[1024,256]{1,0:T(8,128)} %copy-done.2, s32[]{:T(128)S(6)} %select_n.85), kind=kLoop, calls=%fused_computation.19 | loop fusion | flops 131072 | bytes 1572868 | tf_op jit(solution)/shard_map/add | solution.py:50
  19.2 2.9 %collective-permute-start.3 = (f32[256,256]{1,0:T(8,128)S(1)}, f32[256,256]{1,0:T(8,128)}, u32[]{:S(2)}, u32[]{:S(2)}) collective-permute-start(f32[256,256]{1,0:T(8,128)S(1)} %constant_dynamic-slice_fusion.1), channel_id=1, source_target_pairs={{0,4},{2,6},{4,0},{6,2},{8,12},{10,14},{12,8},{14,10},{16,20},{18,... | collective-permute-start | bytes 786440 | tf_op jit(solution)/shard_map/ppermute | solution.py:49
  22.1 1.3 %fusion.2 = f32[1088,256]{1,0:T(8,128)} fusion(s32[]{:T(128)S(6)} %select_n.78, f32[2048,256]{1,0:T(8,128)S(1)} %copy-done, f32[128,256]{1,0:T(8,128)S(1)} %fusion.9), kind=kLoop, calls=%fused_computation.8 | loop fusion | flops 278528 | bytes 3342340 | tf_op jit(solution)/shard_map/concatenate | solution.py:132
  23.4 1.5 %collective-permute-start = (f32[1088,256]{1,0:T(8,128)}, f32[1088,256]{1,0:T(8,128)}, u32[]{:S(2)}, u32[]{:S(2)}) collective-permute-start(f32[1088,256]{1,0:T(8,128)} %fusion.2), channel_id=1, source_target_pairs={{0,1},{1,0},{2,3},{3,2},{4,5},{5,4},{6,7},{7,6},{8,9},{9,8},{10,11... | collective-permute-start | bytes 3342344 | tf_op jit(solution)/shard_map/ppermute | solution.py:49
  24.9 3.9 %collective-permute-done.3 = f32[256,256]{1,0:T(8,128)} collective-permute-done((f32[256,256]{1,0:T(8,128)S(1)}, f32[256,256]{1,0:T(8,128)}, u32[]{:S(2)}, u32[]{:S(2)}) %collective-permute-start.3) | collective-permute-done | bytes 262176 | tf_op jit(solution)/shard_map/ppermute | solution.py:49
  28.8 1.0 %dynamic-slice_add_fusion.1 = f32[256,256]{1,0:T(8,128)S(1)} fusion(f32[256,256]{1,0:T(8,128)} %collective-permute-done.3, f32[512,256]{1,0:T(8,128)S(1)} %dynamic-slice_add_fusion, s32[]{:T(128)S(6)} %select_n.87), kind=kLoop, calls=%fused_computation.21 | loop fusion | flops 65536 | bytes 786436 | tf_op jit(solution)/shard_map/add | solution.py:50
  29.9 1.9 %collective-permute-start.4 = (f32[128,256]{1,0:T(8,128)S(1)}, f32[128,256]{1,0:T(8,128)S(1)}, u32[]{:S(2)}, u32[]{:S(2)}) collective-permute-start(f32[128,256]{1,0:T(8,128)S(1)} %constant_dynamic-slice_fusion), channel_id=1, source_target_pairs={{0,8},{2,10},{4,12},{6,14},{8,0},{10,2},{12,4},{14,6},{16,24},{18,... | collective-permute-start | bytes 393224 | tf_op jit(solution)/shard_map/ppermute | solution.py:49
  31.8 3.2 %collective-permute-done.4 = f32[128,256]{1,0:T(8,128)S(1)} collective-permute-done((f32[128,256]{1,0:T(8,128)S(1)}, f32[128,256]{1,0:T(8,128)S(1)}, u32[]{:S(2)}, u32[]{:S(2)}) %collective-permute-start.4) | collective-permute-done | bytes 131104 | tf_op jit(solution)/shard_map/ppermute | solution.py:49
  35.0 2.8 %collective-permute-start.5 = (f32[64,256]{1,0:T(8,128)S(1)}, f32[64,256]{1,0:T(8,128)S(1)}, u32[]{:S(2)}, u32[]{:S(2)}) collective-permute-start(f32[64,256]{1,0:T(8,128)S(1)} %constant_dynamic-slice_fusion.3), channel_id=1, source_target_pairs={{0,16},{2,18},{4,20},{6,22},{8,24},{10,26},{12,28},{14,30},{16,0},... | collective-permute-start | bytes 196616 | tf_op jit(solution)/shard_map/ppermute | solution.py:49
  37.8 2.4 %collective-permute-done.5 = f32[64,256]{1,0:T(8,128)S(1)} collective-permute-done((f32[64,256]{1,0:T(8,128)S(1)}, f32[64,256]{1,0:T(8,128)S(1)}, u32[]{:S(2)}, u32[]{:S(2)}) %collective-permute-start.5) | collective-permute-done | bytes 65568 | tf_op jit(solution)/shard_map/ppermute | solution.py:49
  40.2 2.9 %collective-permute-start.6 = (bf16[64,256]{1,0:T(8,128)(2,1)S(1)}, bf16[64,256]{1,0:T(8,128)(2,1)S(1)}, u32[]{:S(2)}, u32[]{:S(2)}) collective-permute-start(bf16[64,256]{1,0:T(8,128)(2,1)S(1)} %add_convert_fusion), channel_id=1, source_target_pairs={{0,16},{2,18},{4,20},{6,22},{8,24},{10,26},{12,28},{14,30},{16,0},... | collective-permute-start | bytes 98312 | tf_op jit(solution)/shard_map/ppermute | solution.py:59
  43.2 2.1 %collective-permute-done.6 = bf16[64,256]{1,0:T(8,128)(2,1)S(1)} collective-permute-done((bf16[64,256]{1,0:T(8,128)(2,1)S(1)}, bf16[64,256]{1,0:T(8,128)(2,1)S(1)}, u32[]{:S(2)}, u32[]{:S(2)}) %collective-permute-start.6) | collective-permute-done | bytes 32800 | tf_op jit(solution)/shard_map/ppermute | solution.py:59
  45.2 2.0 %collective-permute-start.7 = (bf16[128,256]{1,0:T(8,128)(2,1)S(1)}, bf16[128,256]{1,0:T(8,128)(2,1)S(1)}, u32[]{:S(2)}, u32[]{:S(2)}) collective-permute-start(bf16[128,256]{1,0:T(8,128)(2,1)S(1)} %maximum_select_fusion.4), channel_id=1, source_target_pairs={{0,8},{2,10},{4,12},{6,14},{8,0},{10,2},{12,4},{14,6},{16,24},{18,... | collective-permute-start | bytes 196616 | tf_op jit(solution)/shard_map/ppermute | solution.py:59
  47.2 2.3 %collective-permute-done.7 = bf16[128,256]{1,0:T(8,128)(2,1)S(1)} collective-permute-done((bf16[128,256]{1,0:T(8,128)(2,1)S(1)}, bf16[128,256]{1,0:T(8,128)(2,1)S(1)}, u32[]{:S(2)}, u32[]{:S(2)}) %collective-permute-start.7) | collective-permute-done | bytes 65568 | tf_op jit(solution)/shard_map/ppermute | solution.py:59
  49.6 1.7 %collective-permute-start.8 = (bf16[256,256]{1,0:T(8,128)(2,1)S(1)}, bf16[256,256]{1,0:T(8,128)(2,1)S(1)}, u32[]{:S(2)}, u32[]{:S(2)}) collective-permute-start(bf16[256,256]{1,0:T(8,128)(2,1)S(1)} %maximum_select_fusion.3), channel_id=1, source_target_pairs={{0,4},{2,6},{4,0},{6,2},{8,12},{10,14},{12,8},{14,10},{16,20},{18,... | collective-permute-start | bytes 393224 | tf_op jit(solution)/shard_map/ppermute | solution.py:59
  51.4 1.8 %fusion.7 = bf16[1088,256]{1,0:T(8,128)(2,1)S(1)} fusion(f32[1088,256]{1,0:T(8,128)} %collective-permute-done, s32[]{:T(128)S(6)} %select_n.77, f32[2048,256]{1,0:T(8,128)S(1)} %copy-done, f32[128,256]{1,0:T(8,128)S(1)} %fusion.9, bf16[2048,256]{1,0:T(8,128)(2,1)} %u_ref.1, bf16[128,256]{1,0:T(8,128)(2,1)} %param.9), kind=kLoop, calls=%fused_computation.13 | loop fusion | flops 2506752 | bytes 5013508 | tf_op jit(solution)/shard_map/convert_element_type | solution.py:34
  53.2 1.6 %collective-permute-start.1 = (bf16[1088,256]{1,0:T(8,128)(2,1)S(1)}, bf16[1088,256]{1,0:T(8,128)(2,1)S(1)}, u32[]{:S(2)}, u32[]{:S(2)}) collective-permute-start(bf16[1088,256]{1,0:T(8,128)(2,1)S(1)} %fusion.7), channel_id=1, source_target_pairs={{0,1},{1,0},{2,3},{3,2},{4,5},{5,4},{6,7},{7,6},{8,9},{9,8},{10,11... | collective-permute-start | bytes 1671176 | tf_op jit(solution)/shard_map/ppermute | solution.py:59
  55.0 1.5 %collective-permute-done.9 = bf16[512,256]{1,0:T(8,128)(2,1)S(1)} collective-permute-done((bf16[512,256]{1,0:T(8,128)(2,1)S(1)}, bf16[512,256]{1,0:T(8,128)(2,1)S(1)}, u32[]{:S(2)}, u32[]{:S(2)}) %collective-permute-start.9) | collective-permute-done | bytes 262176 | tf_op jit(solution)/shard_map/ppermute | solution.py:59
  56.5 1.0 %maximum_select_fusion.1 = bf16[1024,256]{1,0:T(8,128)(2,1)} fusion(bf16[512,256]{1,0:T(8,128)(2,1)S(1)} %collective-permute-done.9, bf16[512,256]{1,0:T(8,128)(2,1)S(1)} %maximum_select_fusion.2, pred[]{:T(512)S(6)} %eq.16), kind=kLoop, calls=%fused_computation.18 | loop fusion | flops 2359296 | bytes 1048577 | tf_op jit(solution)/shard_map/jit(_where)/select_n | solution.py:61
  57.5 8.0 %collective-permute-done.1 = bf16[1088,256]{1,0:T(8,128)(2,1)S(1)} collective-permute-done((bf16[1088,256]{1,0:T(8,128)(2,1)S(1)}, bf16[1088,256]{1,0:T(8,128)(2,1)S(1)}, u32[]{:S(2)}, u32[]{:S(2)}) %collective-permute-start.1) | collective-permute-done | bytes 557088 | tf_op jit(solution)/shard_map/ppermute | solution.py:59
  65.8 1.0 %slice.8 = bf16[2048,256]{1,0:T(8,128)(2,1)} slice(bf16[2176,256]{1,0:T(8,128)(2,1)S(1)} %maximum_select_fusion), slice={[0:2048], [0:256]} | slice | bytes 2097152 | tf_op jit(solution)/shard_map/slice | solution.py:150
  (32 shorter events, 5.2 us)
Async XLA Ops:
  2.7 10.4 %copy-start.1 = (bf16[1024,256]{1,0:T(8,128)(2,1)S(1)}, bf16[1024,256]{1,0:T(8,128)(2,1)}, u32[]{:S(2)}) copy-start(bf16[1024,256]{1,0:T(8,128)(2,1)} %i_ref.1) | copy-start | bytes 1572868
  2.7 10.4 %copy-start.4 = (bf16[128,256]{1,0:T(8,128)(2,1)S(1)}, bf16[128,256]{1,0:T(8,128)(2,1)}, u32[]{:S(2)}) copy-start(bf16[128,256]{1,0:T(8,128)(2,1)} %param.9) | copy-start | bytes 196612
  2.7 10.5 %copy-start.5 = (bf16[1024,128]{1,0:T(8,128)(2,1)S(1)}, bf16[1024,128]{1,0:T(8,128)(2,1)}, u32[]{:S(2)}) copy-start(bf16[1024,128]{1,0:T(8,128)(2,1)} %param.12) | copy-start | bytes 786436
  13.2 1.2 %copy-start.3 = (f32[1024,256]{1,0:T(8,128)S(1)}, f32[1024,256]{1,0:T(8,128)}, u32[]{:S(2)}) copy-start(f32[1024,256]{1,0:T(8,128)} %get-tuple-element.6) | copy-start | bytes 3145732
  14.7 1.0 %copy-start.2 = (f32[1024,256]{1,0:T(8,128)}, f32[1024,256]{1,0:T(8,128)S(1)}, u32[]{:S(2)}) copy-start(f32[1024,256]{1,0:T(8,128)S(1)} %convolution_add_fusion) | copy-start | bytes 3145732
  15.7 2.2 %collective-permute-start.2 = (f32[512,256]{1,0:T(8,128)S(1)}, f32[512,256]{1,0:T(8,128)}, u32[]{:S(2)}, u32[]{:S(2)}) collective-permute-start(f32[512,256]{1,0:T(8,128)S(1)} %constant_dynamic-slice_fusion.2), channel_id=1, source_target_pairs={{0,2},{2,0},{4,6},{6,4},{8,10},{10,8},{12,14},{14,12},{16,18},{18,... | collective-permute-start | bytes 1572872 | tf_op jit(solution)/shard_map/ppermute | solution.py:49
  16.5 5.6 %copy-start = (f32[2048,256]{1,0:T(8,128)S(1)}, f32[2048,256]{1,0:T(8,128)}, u32[]{:S(2)}) copy-start(f32[2048,256]{1,0:T(8,128)} %get-tuple-element.5) | copy-start | bytes 6291460
  19.2 9.6 %collective-permute-start.3 = (f32[256,256]{1,0:T(8,128)S(1)}, f32[256,256]{1,0:T(8,128)}, u32[]{:S(2)}, u32[]{:S(2)}) collective-permute-start(f32[256,256]{1,0:T(8,128)S(1)} %constant_dynamic-slice_fusion.1), channel_id=1, source_target_pairs={{0,4},{2,6},{4,0},{6,2},{8,12},{10,14},{12,8},{14,10},{16,20},{18,... | collective-permute-start | bytes 786440 | tf_op jit(solution)/shard_map/ppermute | solution.py:49
  23.4 27.9 %collective-permute-start = (f32[1088,256]{1,0:T(8,128)}, f32[1088,256]{1,0:T(8,128)}, u32[]{:S(2)}, u32[]{:S(2)}) collective-permute-start(f32[1088,256]{1,0:T(8,128)} %fusion.2), channel_id=1, source_target_pairs={{0,1},{1,0},{2,3},{3,2},{4,5},{5,4},{6,7},{7,6},{8,9},{9,8},{10,11... | collective-permute-start | bytes 3342344 | tf_op jit(solution)/shard_map/ppermute | solution.py:49
  29.9 5.1 %collective-permute-start.4 = (f32[128,256]{1,0:T(8,128)S(1)}, f32[128,256]{1,0:T(8,128)S(1)}, u32[]{:S(2)}, u32[]{:S(2)}) collective-permute-start(f32[128,256]{1,0:T(8,128)S(1)} %constant_dynamic-slice_fusion), channel_id=1, source_target_pairs={{0,8},{2,10},{4,12},{6,14},{8,0},{10,2},{12,4},{14,6},{16,24},{18,... | collective-permute-start | bytes 393224 | tf_op jit(solution)/shard_map/ppermute | solution.py:49
  35.0 5.2 %collective-permute-start.5 = (f32[64,256]{1,0:T(8,128)S(1)}, f32[64,256]{1,0:T(8,128)S(1)}, u32[]{:S(2)}, u32[]{:S(2)}) collective-permute-start(f32[64,256]{1,0:T(8,128)S(1)} %constant_dynamic-slice_fusion.3), channel_id=1, source_target_pairs={{0,16},{2,18},{4,20},{6,22},{8,24},{10,26},{12,28},{14,30},{16,0},... | collective-permute-start | bytes 196616 | tf_op jit(solution)/shard_map/ppermute | solution.py:49
  40.2 5.0 %collective-permute-start.6 = (bf16[64,256]{1,0:T(8,128)(2,1)S(1)}, bf16[64,256]{1,0:T(8,128)(2,1)S(1)}, u32[]{:S(2)}, u32[]{:S(2)}) collective-permute-start(bf16[64,256]{1,0:T(8,128)(2,1)S(1)} %add_convert_fusion), channel_id=1, source_target_pairs={{0,16},{2,18},{4,20},{6,22},{8,24},{10,26},{12,28},{14,30},{16,0},... | collective-permute-start | bytes 98312 | tf_op jit(solution)/shard_map/ppermute | solution.py:59
  45.2 4.3 %collective-permute-start.7 = (bf16[128,256]{1,0:T(8,128)(2,1)S(1)}, bf16[128,256]{1,0:T(8,128)(2,1)S(1)}, u32[]{:S(2)}, u32[]{:S(2)}) collective-permute-start(bf16[128,256]{1,0:T(8,128)(2,1)S(1)} %maximum_select_fusion.4), channel_id=1, source_target_pairs={{0,8},{2,10},{4,12},{6,14},{8,0},{10,2},{12,4},{14,6},{16,24},{18,... | collective-permute-start | bytes 196616 | tf_op jit(solution)/shard_map/ppermute | solution.py:59
  49.6 5.2 %collective-permute-start.8 = (bf16[256,256]{1,0:T(8,128)(2,1)S(1)}, bf16[256,256]{1,0:T(8,128)(2,1)S(1)}, u32[]{:S(2)}, u32[]{:S(2)}) collective-permute-start(bf16[256,256]{1,0:T(8,128)(2,1)S(1)} %maximum_select_fusion.3), channel_id=1, source_target_pairs={{0,4},{2,6},{4,0},{6,2},{8,12},{10,14},{12,8},{14,10},{16,20},{18,... | collective-permute-start | bytes 393224 | tf_op jit(solution)/shard_map/ppermute | solution.py:59
  53.2 12.3 %collective-permute-start.1 = (bf16[1088,256]{1,0:T(8,128)(2,1)S(1)}, bf16[1088,256]{1,0:T(8,128)(2,1)S(1)}, u32[]{:S(2)}, u32[]{:S(2)}) collective-permute-start(bf16[1088,256]{1,0:T(8,128)(2,1)S(1)} %fusion.7), channel_id=1, source_target_pairs={{0,1},{1,0},{2,3},{3,2},{4,5},{5,4},{6,7},{7,6},{8,9},{9,8},{10,11... | collective-permute-start | bytes 1671176 | tf_op jit(solution)/shard_map/ppermute | solution.py:59
  54.9 1.6 %collective-permute-start.9 = (bf16[512,256]{1,0:T(8,128)(2,1)S(1)}, bf16[512,256]{1,0:T(8,128)(2,1)S(1)}, u32[]{:S(2)}, u32[]{:S(2)}) collective-permute-start(bf16[512,256]{1,0:T(8,128)(2,1)S(1)} %maximum_select_fusion.2), channel_id=1, source_target_pairs={{0,2},{2,0},{4,6},{6,4},{8,10},{10,8},{12,14},{14,12},{16,18},{18,... | collective-permute-start | bytes 786440 | tf_op jit(solution)/shard_map/ppermute | solution.py:59

commit v11 on v10

--- a/solution.py
+++ b/solution.py
@@ -87,7 +87,7 @@
     def _():
         item_ref[...] = jnp.zeros_like(item_ref)
 
-    item_ref[...] += lax.dot_general(errors, users, (((0,), (0,)), ((), ())), preferred_element_type=jnp.float32)
+    item_ref[...] += lax.dot_general(users, errors, (((0,), (0,)), ((), ())), preferred_element_type=jnp.float32)
 
 
 def rating_partials(user_factors, item_factors, ratings, rating_tiles):
@@ -106,13 +106,13 @@
             ],
             out_specs=[
                 pl.BlockSpec((block_rows, rank), lambda b, f: (b, 0)),
-                pl.BlockSpec((cols, rank), lambda b, f: (0, 0)),
+                pl.BlockSpec((rank, cols), lambda b, f: (0, 0)),
             ],
             scratch_shapes=[pltpu.VMEM((block_rows, cols), jnp.bfloat16)],
         ),
         out_shape=[
             jax.ShapeDtypeStruct((rows, rank), jnp.float32),
-            jax.ShapeDtypeStruct((cols, rank), jnp.float32),
+            jax.ShapeDtypeStruct((rank, cols), jnp.float32),
         ],
         compiler_params=pltpu.CompilerParams(dimension_semantics=("arbitrary",)),
     )(rating_tiles, user_factors, item_factors, ratings)
@@ -130,7 +130,7 @@
     )
     tag_part = transposed_product(link_errors, item_factors)
     joint_part = jnp.concatenate([user_part, tag_part], 0)
-    item_part = rating_item_part + jnp.dot(
+    item_part = rating_item_part.T + jnp.dot(
         link_errors, tag_factors, preferred_element_type=jnp.float32
     )
     (joint_share,), (joint_offset,) = halving_scatter(

time: 67.7 us -> 75.5 us (1.12)
  waiting for transfers between devices: 24.8 us -> 34.3 us
  starting transfers between devices: 18 us -> 15.9 us
  local copies, waits for them, and re-layouts: 5.08 us -> 6.73 us
  other arithmetic: 7.5 us -> 6.16 us
    ppermute x5, waiting for transfers between devices: 10.9 us -> 18 us  [halving_scatter(): got = lax.ppermute(tuple(sent), axis, xor_pairs(count, bit))]
    ppermute x5, waiting for transfers between devices: 13.9 us -> 16.3 us  [doubling_gather(): got = lax.ppermute(tuple(parts), axis, xor_pairs(count, bit))]
    ppermute x5, starting transfers between devices: 8.27 us -> 6.27 us  [doubling_gather(): got = lax.ppermute(tuple(parts), axis, xor_pairs(count, bit))]
    add x3, other arithmetic: 2.27 us -> 1.08 us  [halving_scatter(): parts = [k + g for k, g in zip(kept, got)]]
    unnamed x13 -> x19, local copies, waits for them, and re-layouts: 3.24 us -> 4.1 us
    dynamic_slice x4, local copies, waits for them, and re-layouts: 0.09 us -> 0.88 us  [halving_scatter(): lax.dynamic_slice_in_dim(p, (1 - side) * h, h, 0)]
    select_n x5, other arithmetic: 1.42 us -> 0.65 us  [doubling_gather(): jnp.where(side == 0, jnp.concatenate([m, g], 0), jnp.concatenate([g, m], 0))]
  transfers between devices with their start and end apart: 10 -> 10, of which waited for: 8 -> 9; matrix products, arithmetic and copies ran while one was open for 8% -> 8% of each run, Pallas kernels for 0% -> 0%
where the time goes in v11:
time: 75.5 us; the launch traced here: 75.2 us
  waiting for transfers between devices  34.3 us (45%)
  starting transfers between devices  15.9 us (21%)
  Pallas kernels  10.4 us (14%)
  local copies, waits for them, and re-layouts  6.73 us (9%)
  other arithmetic  6.16 us (8%)
  matrix products  0.9 us (1%)
  between operations  0.82 us (1%)
    ppermute x5, waiting for transfers between devices, halving_scatter(): got = lax.ppermute(tuple(sent), axis, xor_pairs(count, bit))  18 us
    ppermute x5, waiting for transfers between devices, doubling_gather(): got = lax.ppermute(tuple(parts), axis, xor_pairs(count, bit))  16.3 us
    pallas_call x1, Pallas kernels, rating_partials(): pl.pallas_call(rating_kernel, grid_spec=pltpu.PrefetchScalarGridSpec(num_...  10.4 us
    ppermute x5, starting transfers between devices, halving_scatter(): got = lax.ppermute(tuple(sent), axis, xor_pairs(count, bit))  9.64 us
    ppermute x5, starting transfers between devices, doubling_gather(): got = lax.ppermute(tuple(parts), axis, xor_pairs(count, bit))  6.27 us
    unnamed x19, local copies, waits for them, and re-layouts  4.1 us
    convert_element_type x2, other arithmetic, advance(): return (factors.astype(jnp.float32) + rate * gradient).astype(jnp.bfloat16)  2.47 us
  transfers between devices with their start and end apart: 10, of which 9 were waited for; matrix products, arithmetic and copies ran while one was open for 8% of the time, Pallas kernels for 0%

profile of v11, /device:TPU:0, one launch (start us, length us, event | category | flops | bytes accessed | tf_op | source)
XLA Modules:
  0.0 75.2 jit_solution(11947927635489161361)
XLA Ops:
  0.6 1.4 %copy.10.flags_ref = s32[16,8]{1,0:T(8,128)} copy(s32[16,8]{0,1:T(8,128)} %param.11) | data formatting | bytes 1024 | tf_op args[4]
  2.7 10.4 %shard_map.94 = (f32[2048,256]{1,0:T(8,128)}, f32[256,1024]{1,0:T(8,128)}) custom-call(s32[16,8]{1,0:T(8,128)} %copy.10.flags_ref, bf16[2048,256]{1,0:T(8,128)(2,1)} %u_ref.1, bf16[1024,256]{1,0:T(8,128)(2,1)} %i_ref.1, bf16[2048,1024]{1,0:T(8,128)(2,1)} %r_ref.1), custom_call_target="tpu_custom_call" | custom-call | tf_op jit(solution)/shard_map/pallas_call | solution.py:97
  13.5 0.9 %copy-done.2 = f32[256,1024]{1,0:T(8,128)S(1)} copy-done((f32[256,1024]{1,0:T(8,128)S(1)}, f32[256,1024]{1,0:T(8,128)}, u32[]{:S(2)}) %copy-start.2) | copy-done | bytes 1048600
  15.3 1.5 %collective-permute-done.2 = f32[512,256]{0,1:T(8,128)S(1)} collective-permute-done((f32[512,256]{0,1:T(8,128)S(1)}, f32[512,256]{0,1:T(8,128)S(1)}, u32[]{:S(2)}, u32[]{:S(2)}) %collective-permute-start.2) | collective-permute-done | bytes 524320 | tf_op jit(solution)/shard_map/ppermute | solution.py:49
  17.7 2.9 %collective-permute-start.3 = (f32[256,256]{0,1:T(8,128)}, f32[256,256]{0,1:T(8,128)}, u32[]{:S(2)}, u32[]{:S(2)}) collective-permute-start(f32[256,256]{0,1:T(8,128)} %constant_dynamic-slice_fusion.1), channel_id=1, source_target_pairs={{0,4},{2,6},{4,0},{6,2},{8,12},{10,14},{12,8},{14,10},{16,20},{18,... | collective-permute-start | bytes 786440 | tf_op jit(solution)/shard_map/ppermute | solution.py:49
  20.8 6.6 %collective-permute-done.3 = f32[256,256]{0,1:T(8,128)} collective-permute-done((f32[256,256]{0,1:T(8,128)}, f32[256,256]{0,1:T(8,128)}, u32[]{:S(2)}, u32[]{:S(2)}) %collective-permute-start.3) | collective-permute-done | bytes 262176 | tf_op jit(solution)/shard_map/ppermute | solution.py:49
  27.5 1.0 %dynamic-slice_add_fusion.1 = f32[256,256]{0,1:T(8,128)S(1)} fusion(f32[256,256]{0,1:T(8,128)} %collective-permute-done.3, f32[512,256]{0,1:T(8,128)S(1)} %dynamic-slice_add_fusion, s32[]{:T(128)S(6)} %select_n.87), kind=kLoop, calls=%fused_computation.21 | loop fusion | flops 65536 | bytes 786436 | tf_op jit(solution)/shard_map/add | solution.py:50
  29.2 1.9 %collective-permute-start.4 = (f32[128,256]{0,1:T(8,128)S(1)}, f32[128,256]{0,1:T(8,128)S(1)}, u32[]{:S(2)}, u32[]{:S(2)}) collective-permute-start(f32[128,256]{0,1:T(8,128)S(1)} %constant_dynamic-slice_fusion), channel_id=1, source_target_pairs={{0,8},{2,10},{4,12},{6,14},{8,0},{10,2},{12,4},{14,6},{16,24},{18,... | collective-permute-start | bytes 393224 | tf_op jit(solution)/shard_map/ppermute | solution.py:49
  31.1 1.3 %fusion.2 = f32[1088,256]{1,0:T(8,128)} fusion(s32[]{:T(128)S(6)} %select_n.78, f32[2048,256]{1,0:T(8,128)S(1)} %copy-done, f32[128,256]{1,0:T(8,128)S(1)} %fusion.9), kind=kLoop, calls=%fused_computation.8 | loop fusion | flops 278528 | bytes 3342340 | tf_op jit(solution)/shard_map/concatenate | solution.py:132
  32.4 1.5 %collective-permute-start = (f32[1088,256]{1,0:T(8,128)}, f32[1088,256]{1,0:T(8,128)}, u32[]{:S(2)}, u32[]{:S(2)}) collective-permute-start(f32[1088,256]{1,0:T(8,128)} %fusion.2), channel_id=1, source_target_pairs={{0,1},{1,0},{2,3},{3,2},{4,5},{5,4},{6,7},{7,6},{8,9},{9,8},{10,11... | collective-permute-start | bytes 3342344 | tf_op jit(solution)/shard_map/ppermute | solution.py:49
  34.4 2.8 %collective-permute-start.5 = (f32[64,256]{0,1:T(8,128)S(1)}, f32[64,256]{0,1:T(8,128)S(1)}, u32[]{:S(2)}, u32[]{:S(2)}) collective-permute-start(f32[64,256]{0,1:T(8,128)S(1)} %constant_dynamic-slice_fusion.4), channel_id=1, source_target_pairs={{0,16},{2,18},{4,20},{6,22},{8,24},{10,26},{12,28},{14,30},{16,0},... | collective-permute-start | bytes 196616 | tf_op jit(solution)/shard_map/ppermute | solution.py:49
  37.4 4.9 %collective-permute-done.5 = f32[64,256]{0,1:T(8,128)S(1)} collective-permute-done((f32[64,256]{0,1:T(8,128)S(1)}, f32[64,256]{0,1:T(8,128)S(1)}, u32[]{:S(2)}, u32[]{:S(2)}) %collective-permute-start.5) | collective-permute-done | bytes 65568 | tf_op jit(solution)/shard_map/ppermute | solution.py:49
  42.4 1.0 %collective-permute-start.6 = (bf16[64,256]{0,1:T(8,128)(2,1)S(1)}, bf16[64,256]{0,1:T(8,128)(2,1)S(1)}, u32[]{:S(2)}, u32[]{:S(2)}) collective-permute-start(bf16[64,256]{0,1:T(8,128)(2,1)S(1)} %add_convert_fusion), channel_id=1, source_target_pairs={{0,16},{2,18},{4,20},{6,22},{8,24},{10,26},{12,28},{14,30},{16,0},... | collective-permute-start | bytes 98312 | tf_op jit(solution)/shard_map/ppermute | solution.py:59
  43.4 4.3 %collective-permute-done.6 = bf16[64,256]{0,1:T(8,128)(2,1)S(1)} collective-permute-done((bf16[64,256]{0,1:T(8,128)(2,1)S(1)}, bf16[64,256]{0,1:T(8,128)(2,1)S(1)}, u32[]{:S(2)}, u32[]{:S(2)}) %collective-permute-start.6) | collective-permute-done | bytes 32800 | tf_op jit(solution)/shard_map/ppermute | solution.py:59
  47.8 2.1 %collective-permute-start.7 = (bf16[128,256]{0,1:T(8,128)(2,1)S(1)}, bf16[128,256]{0,1:T(8,128)(2,1)S(1)}, u32[]{:S(2)}, u32[]{:S(2)}) collective-permute-start(bf16[128,256]{0,1:T(8,128)(2,1)S(1)} %maximum_select_fusion.4), channel_id=1, source_target_pairs={{0,8},{2,10},{4,12},{6,14},{8,0},{10,2},{12,4},{14,6},{16,24},{18,... | collective-permute-start | bytes 196616 | tf_op jit(solution)/shard_map/ppermute | solution.py:59
  49.9 2.2 %collective-permute-done.7 = bf16[128,256]{0,1:T(8,128)(2,1)S(1)} collective-permute-done((bf16[128,256]{0,1:T(8,128)(2,1)S(1)}, bf16[128,256]{0,1:T(8,128)(2,1)S(1)}, u32[]{:S(2)}, u32[]{:S(2)}) %collective-permute-start.7) | collective-permute-done | bytes 65568 | tf_op jit(solution)/shard_map/ppermute | solution.py:59
  52.2 1.6 %collective-permute-start.8 = (bf16[256,256]{0,1:T(8,128)(2,1)S(1)}, bf16[256,256]{0,1:T(8,128)(2,1)S(1)}, u32[]{:S(2)}, u32[]{:S(2)}) collective-permute-start(bf16[256,256]{0,1:T(8,128)(2,1)S(1)} %maximum_select_fusion.3), channel_id=1, source_target_pairs={{0,4},{2,6},{4,0},{6,2},{8,12},{10,14},{12,8},{14,10},{16,20},{18,... | collective-permute-start | bytes 393224 | tf_op jit(solution)/shard_map/ppermute | solution.py:59
  53.7 4.5 %collective-permute-done = f32[1088,256]{1,0:T(8,128)} collective-permute-done((f32[1088,256]{1,0:T(8,128)}, f32[1088,256]{1,0:T(8,128)}, u32[]{:S(2)}, u32[]{:S(2)}) %collective-permute-start) | collective-permute-done | bytes 1114144 | tf_op jit(solution)/shard_map/ppermute | solution.py:49
  58.2 2.4 %fusion.7 = bf16[1088,256]{1,0:T(8,128)(2,1)S(1)} fusion(f32[1088,256]{1,0:T(8,128)} %collective-permute-done, s32[]{:T(128)S(6)} %select_n.77, f32[2048,256]{1,0:T(8,128)S(1)} %copy-done, f32[128,256]{1,0:T(8,128)S(1)} %fusion.9, bf16[2048,256]{1,0:T(8,128)(2,1)} %u_ref.1, bf16[128,256]{1,0:T(8,128)(2,1)S(1)} %copy-done.6), kind=kLoop, calls=%fused_computation.13 | loop fusion | flops 2506752 | bytes 5013508 | tf_op jit(solution)/shard_map/convert_element_type | solution.py:34
  60.6 1.6 %collective-permute-start.1 = (bf16[1088,256]{1,0:T(8,128)(2,1)S(1)}, bf16[1088,256]{1,0:T(8,128)(2,1)S(1)}, u32[]{:S(2)}, u32[]{:S(2)}) collective-permute-start(bf16[1088,256]{1,0:T(8,128)(2,1)S(1)} %fusion.7), channel_id=1, source_target_pairs={{0,1},{1,0},{2,3},{3,2},{4,5},{5,4},{6,7},{7,6},{8,9},{9,8},{10,11... | collective-permute-start | bytes 1671176 | tf_op jit(solution)/shard_map/ppermute | solution.py:59
  62.4 1.5 %collective-permute-done.9 = bf16[512,256]{0,1:T(8,128)(2,1)S(1)} collective-permute-done((bf16[512,256]{0,1:T(8,128)(2,1)S(1)}, bf16[512,256]{0,1:T(8,128)(2,1)S(1)}, u32[]{:S(2)}, u32[]{:S(2)}) %collective-permute-start.9) | collective-permute-done | bytes 262176 | tf_op jit(solution)/shard_map/ppermute | solution.py:59
  64.0 1.0 %copy.13 = bf16[1024,256]{1,0:T(8,128)(2,1)} copy(bf16[1024,256]{0,1:T(8,128)(2,1)S(1)} %maximum_select_fusion.1) | data formatting | bytes 1048576
  65.0 8.3 %collective-permute-done.1 = bf16[1088,256]{1,0:T(8,128)(2,1)S(1)} collective-permute-done((bf16[1088,256]{1,0:T(8,128)(2,1)S(1)}, bf16[1088,256]{1,0:T(8,128)(2,1)S(1)}, u32[]{:S(2)}, u32[]{:S(2)}) %collective-permute-start.1) | collective-permute-done | bytes 557088 | tf_op jit(solution)/shard_map/ppermute | solution.py:59
  73.5 1.0 %slice.8 = bf16[2048,256]{1,0:T(8,128)(2,1)} slice(bf16[2176,256]{1,0:T(8,128)(2,1)S(1)} %maximum_select_fusion), slice={[0:2048], [0:256]} | slice | bytes 2097152 | tf_op jit(solution)/shard_map/slice | solution.py:150
  (39 shorter events, 5.8 us)
Async XLA Ops:
  2.7 10.5 %copy-start.1 = (bf16[1024,256]{1,0:T(8,128)(2,1)S(1)}, bf16[1024,256]{1,0:T(8,128)(2,1)}, u32[]{:S(2)}) copy-start(bf16[1024,256]{1,0:T(8,128)(2,1)} %i_ref.1) | copy-start | bytes 1572868
  2.7 10.5 %copy-start.5 = (bf16[128,256]{1,0:T(8,128)(2,1)S(1)}, bf16[128,256]{1,0:T(8,128)(2,1)}, u32[]{:S(2)}) copy-start(bf16[128,256]{1,0:T(8,128)(2,1)} %param.9) | copy-start | bytes 196612
  2.7 10.5 %copy-start.7 = (bf16[1024,128]{1,0:T(8,128)(2,1)S(1)}, bf16[1024,128]{1,0:T(8,128)(2,1)}, u32[]{:S(2)}) copy-start(bf16[1024,128]{1,0:T(8,128)(2,1)} %param.12) | copy-start | bytes 786436
  13.2 1.2 %copy-start.2 = (f32[256,1024]{1,0:T(8,128)S(1)}, f32[256,1024]{1,0:T(8,128)}, u32[]{:S(2)}) copy-start(f32[256,1024]{1,0:T(8,128)} %get-tuple-element.6) | copy-start | bytes 3145732
  14.8 2.1 %collective-permute-start.2 = (f32[512,256]{0,1:T(8,128)S(1)}, f32[512,256]{0,1:T(8,128)S(1)}, u32[]{:S(2)}, u32[]{:S(2)}) collective-permute-start(f32[512,256]{0,1:T(8,128)S(1)} %constant_dynamic-slice_fusion.2), channel_id=1, source_target_pairs={{0,2},{2,0},{4,6},{6,4},{8,10},{10,8},{12,14},{14,12},{16,18},{18,... | collective-permute-start | bytes 1572872 | tf_op jit(solution)/shard_map/ppermute | solution.py:49
  17.0 14.1 %copy-start = (f32[2048,256]{1,0:T(8,128)S(1)}, f32[2048,256]{1,0:T(8,128)}, u32[]{:S(2)}) copy-start(f32[2048,256]{1,0:T(8,128)} %get-tuple-element.5) | copy-start | bytes 6291460
  17.7 9.8 %collective-permute-start.3 = (f32[256,256]{0,1:T(8,128)}, f32[256,256]{0,1:T(8,128)}, u32[]{:S(2)}, u32[]{:S(2)}) collective-permute-start(f32[256,256]{0,1:T(8,128)} %constant_dynamic-slice_fusion.1), channel_id=1, source_target_pairs={{0,4},{2,6},{4,0},{6,2},{8,12},{10,14},{12,8},{14,10},{16,20},{18,... | collective-permute-start | bytes 786440 | tf_op jit(solution)/shard_map/ppermute | solution.py:49
  28.5 0.7 copy-start.3
  29.2 5.1 %collective-permute-start.4 = (f32[128,256]{0,1:T(8,128)S(1)}, f32[128,256]{0,1:T(8,128)S(1)}, u32[]{:S(2)}, u32[]{:S(2)}) collective-permute-start(f32[128,256]{0,1:T(8,128)S(1)} %constant_dynamic-slice_fusion), channel_id=1, source_target_pairs={{0,8},{2,10},{4,12},{6,14},{8,0},{10,2},{12,4},{14,6},{16,24},{18,... | collective-permute-start | bytes 393224 | tf_op jit(solution)/shard_map/ppermute | solution.py:49
  31.1 3.2 %copy-start.4 = (f32[256,256]{0,1:T(8,128)S(1)}, f32[256,256]{0,1:T(8,128)}, u32[]{:S(2)}) copy-start(f32[256,256]{0,1:T(8,128)} %copy-done.3) | copy-start | bytes 786436
  32.4 25.8 %copy-start.6 = (bf16[128,256]{1,0:T(8,128)(2,1)S(1)}, bf16[128,256]{1,0:T(8,128)(2,1)}, u32[]{:S(2)}) copy-start(bf16[128,256]{1,0:T(8,128)(2,1)} %param.9) | copy-start | bytes 196612
  32.4 25.8 %collective-permute-start = (f32[1088,256]{1,0:T(8,128)}, f32[1088,256]{1,0:T(8,128)}, u32[]{:S(2)}, u32[]{:S(2)}) collective-permute-start(f32[1088,256]{1,0:T(8,128)} %fusion.2), channel_id=1, source_target_pairs={{0,1},{1,0},{2,3},{3,2},{4,5},{5,4},{6,7},{7,6},{8,9},{9,8},{10,11... | collective-permute-start | bytes 3342344 | tf_op jit(solution)/shard_map/ppermute | solution.py:49
  34.4 7.9 %collective-permute-start.5 = (f32[64,256]{0,1:T(8,128)S(1)}, f32[64,256]{0,1:T(8,128)S(1)}, u32[]{:S(2)}, u32[]{:S(2)}) collective-permute-start(f32[64,256]{0,1:T(8,128)S(1)} %constant_dynamic-slice_fusion.4), channel_id=1, source_target_pairs={{0,16},{2,18},{4,20},{6,22},{8,24},{10,26},{12,28},{14,30},{16,0},... | collective-permute-start | bytes 196616 | tf_op jit(solution)/shard_map/ppermute | solution.py:49
  42.4 5.2 %collective-permute-start.6 = (bf16[64,256]{0,1:T(8,128)(2,1)S(1)}, bf16[64,256]{0,1:T(8,128)(2,1)S(1)}, u32[]{:S(2)}, u32[]{:S(2)}) collective-permute-start(bf16[64,256]{0,1:T(8,128)(2,1)S(1)} %add_convert_fusion), channel_id=1, source_target_pairs={{0,16},{2,18},{4,20},{6,22},{8,24},{10,26},{12,28},{14,30},{16,0},... | collective-permute-start | bytes 98312 | tf_op jit(solution)/shard_map/ppermute | solution.py:59
  47.8 4.3 %collective-permute-start.7 = (bf16[128,256]{0,1:T(8,128)(2,1)S(1)}, bf16[128,256]{0,1:T(8,128)(2,1)S(1)}, u32[]{:S(2)}, u32[]{:S(2)}) collective-permute-start(bf16[128,256]{0,1:T(8,128)(2,1)S(1)} %maximum_select_fusion.4), channel_id=1, source_target_pairs={{0,8},{2,10},{4,12},{6,14},{8,0},{10,2},{12,4},{14,6},{16,24},{18,... | collective-permute-start | bytes 196616 | tf_op jit(solution)/shard_map/ppermute | solution.py:59
  52.2 10.0 %collective-permute-start.8 = (bf16[256,256]{0,1:T(8,128)(2,1)S(1)}, bf16[256,256]{0,1:T(8,128)(2,1)S(1)}, u32[]{:S(2)}, u32[]{:S(2)}) collective-permute-start(bf16[256,256]{0,1:T(8,128)(2,1)S(1)} %maximum_select_fusion.3), channel_id=1, source_target_pairs={{0,4},{2,6},{4,0},{6,2},{8,12},{10,14},{12,8},{14,10},{16,20},{18,... | collective-permute-start | bytes 393224 | tf_op jit(solution)/shard_map/ppermute | solution.py:59
  60.6 12.7 %collective-permute-start.1 = (bf16[1088,256]{1,0:T(8,128)(2,1)S(1)}, bf16[1088,256]{1,0:T(8,128)(2,1)S(1)}, u32[]{:S(2)}, u32[]{:S(2)}) collective-permute-start(bf16[1088,256]{1,0:T(8,128)(2,1)S(1)} %fusion.7), channel_id=1, source_target_pairs={{0,1},{1,0},{2,3},{3,2},{4,5},{5,4},{6,7},{7,6},{8,9},{9,8},{10,11... | collective-permute-start | bytes 1671176 | tf_op jit(solution)/shard_map/ppermute | solution.py:59
  62.3 1.6 %collective-permute-start.9 = (bf16[512,256]{0,1:T(8,128)(2,1)S(1)}, bf16[512,256]{0,1:T(8,128)(2,1)S(1)}, u32[]{:S(2)}, u32[]{:S(2)}) collective-permute-start(bf16[512,256]{0,1:T(8,128)(2,1)S(1)} %maximum_select_fusion.2), channel_id=1, source_target_pairs={{0,2},{2,0},{4,6},{6,4},{8,10},{10,8},{12,14},{14,12},{16,18},{18,... | collective-permute-start | bytes 786440 | tf_op jit(solution)/shard_map/ppermute | solution.py:59

commit v12 on v7

--- a/solution.py
+++ b/solution.py
@@ -36,12 +36,10 @@
     return [(i, i ^ (1 << bit)) for i in range(count)]
 
 
-def halving_scatter(parts, axis, count, position, tie=None, tie_step=-1):
+def halving_scatter(parts, axis, count, position, bits=None):
     steps = count.bit_length() - 1
     offsets = [0 for _ in parts]
-    for bit in range(steps):
-        if bit == tie_step and tie is not None:
-            parts, _ = lax.optimization_barrier((parts, tie))
+    for bit in range(steps) if bits is None else bits:
         side = (position >> bit) & 1
         halves = [p.shape[0] // 2 for p in parts]
         kept = [lax.dynamic_slice_in_dim(p, side * h, h, 0) for p, h in zip(parts, halves)]
@@ -99,9 +97,26 @@
     new_users = new_joint[: user_factors.shape[0]]
     new_tags = new_joint[user_factors.shape[0] :]
 
+    group_steps = group_count.bit_length() - 1
+    first_bits = list(range(min(2, group_steps)))
+    first_rows = item_part.shape[0] >> len(first_bits)
+
+    def group_first(item_part):
+        (share,), (offset,) = halving_scatter(
+            [item_part], "group", group_count, group_position, first_bits
+        )
+        return share, offset
+
+    first_share, first_offset = lax.cond(
+        group_position >= 0,
+        group_first,
+        lambda p: (jnp.zeros((first_rows, p.shape[1]), p.dtype), jnp.int32(0)),
+        item_part,
+    )
     (item_share,), (item_offset,) = halving_scatter(
-        [item_part], "group", group_count, group_position, joint_share, 3
+        [first_share], "group", group_count, group_position, range(len(first_bits), group_steps)
     )
+    item_offset = first_offset + item_offset
     fresh_items = advance(
         lax.dynamic_slice_in_dim(item_factors, item_offset, item_share.shape[0], 0),
         item_share,

time: 68.9 us -> 69.8 us (1.013)
  waiting for transfers between devices: 32.3 us -> 28.1 us
  matrix products: 7.55 us -> 9.9 us
  other arithmetic: 6.34 us -> 7.98 us
    ppermute x5, waiting for transfers between devices: 23.7 us -> 15 us  [halving_scatter(): got = lax.ppermute(tuple(sent), axis, xor_pairs(count, bit))]
    ppermute x5, waiting for transfers between devices: 8.59 us -> 13.1 us  [doubling_gather(): got = lax.ppermute(tuple(parts), axis, xor_pairs(count, bit))]
    dot_general x2, matrix products: 2.52 us -> 5 us  [transposed_product(): lax.dot_general(first_operand, second_operand, (((0,), (0,)), ((), ())),...]
    add x0 -> x1, other arithmetic: none -> 1.67 us  [shards(): transposed_product(rating_errors, user_factors)]
    cond x0 -> x2, local copies, waits for them, and re-layouts: none -> 0.98 us
    ppermute x5, starting transfers between devices: 5.74 us -> 6.61 us  [doubling_gather(): got = lax.ppermute(tuple(parts), axis, xor_pairs(count, bit))]
  transfers between devices with their start and end apart: 10 -> 10, of which waited for: 7 -> 9; matrix products, arithmetic and copies ran while one was open for 8% -> 19% of each run, Pallas kernels for 0% -> 0%
where the time goes in v12:
time: 69.8 us; the launch traced here: 69.6 us
  waiting for transfers between devices  28.1 us (40%)
  starting transfers between devices  15.4 us (22%)
  matrix products  9.9 us (14%)
  other arithmetic  7.98 us (11%)
  local copies, waits for them, and re-layouts  7.29 us (10%)
  between operations  0.8 us (1%)
    ppermute x5, waiting for transfers between devices, halving_scatter(): got = lax.ppermute(tuple(sent), axis, xor_pairs(count, bit))  15 us
    ppermute x5, waiting for transfers between devices, doubling_gather(): got = lax.ppermute(tuple(parts), axis, xor_pairs(count, bit))  13.1 us
    ppermute x5, starting transfers between devices, halving_scatter(): got = lax.ppermute(tuple(sent), axis, xor_pairs(count, bit))  8.82 us
    ppermute x5, starting transfers between devices, doubling_gather(): got = lax.ppermute(tuple(parts), axis, xor_pairs(count, bit))  6.61 us
    dot_general x2, matrix products, transposed_product(): lax.dot_general(first_operand, second_operand, (((0,), (0,)), ((), ())),...  5 us
    unnamed x14, local copies, waits for them, and re-layouts  2.71 us
    dot_general x2, matrix products, residual_of(): lax.dot_general(row_factors, column_factors, (((1,), (1,)), ((), ())), pr...  2.36 us
    add x3, other arithmetic, halving_scatter(): parts = [k + g for k, g in zip(kept, got)]  2.27 us
  transfers between devices with their start and end apart: 10, of which 9 were waited for; matrix products, arithmetic and copies ran while one was open for 19% of the time, Pallas kernels for 0%

profile of v12, /device:TPU:0, one launch (start us, length us, event | category | flops | bytes accessed | tf_op | source)
XLA Modules:
  0.0 69.6 jit_solution(17419800365916042408)
XLA Ops:
  2.8 1.3 %copy-done.3 = bf16[2048,1024]{1,0:T(8,128)(2,1)S(1)} copy-done((bf16[2048,1024]{1,0:T(8,128)(2,1)S(1)}, bf16[2048,1024]{1,0:T(8,128)(2,1)}, u32[]{:S(2)}) %copy-start.3) | copy-done | bytes 4194328
  4.1 2.1 %fusion = bf16[2048,1024]{1,0:T(8,128)(2,1)S(1)} fusion(f32[256,8,8,128]{3,2,1,0:T(8,128)S(1)} %bitcast.22, bf16[2048,1024]{1,0:T(8,128)(2,1)S(1)} %copy-done.3, bf16[2048,256]{1,0:T(8,128)(2,1)S(1)} %copy-done.2, bf16[1024,256]{1,0:T(8,128)(2,1)S(1)} %copy-done), kind=kOutput, calls=%fused_computation.5 | convolution fusion | flops 1082130432 | bytes 18350080 | tf_op jit(solution)/shard_map/dot_general | solution.py:19
  6.2 1.3 %fusion.4 = f32[2048,256]{1,0:T(8,128)S(1)} fusion(bf16[2048,1024]{1,0:T(8,128)(2,1)S(1)} %fusion, bf16[1024,256]{1,0:T(8,128)(2,1)S(1)} %copy-done), kind=kOutput, calls=%fused_computation.26 | convolution fusion | flops 1073741824 | bytes 6815744 | tf_op jit(solution)/shard_map/dot_general | solution.py:73
  10.0 3.0 %collective-permute-start.2 = (f32[1088,256]{1,0:T(8,128)}, f32[1088,256]{1,0:T(8,128)}, u32[]{:S(2)}, u32[]{:S(2)}) collective-permute-start(f32[1088,256]{1,0:T(8,128)} %constant_dynamic-slice_fusion.3), channel_id=1, source_target_pairs={{0,1},{1,0},{2,3},{3,2},{4,5},{5,4},{6,7},{7,6},{8,9},{9,8},{10,11... | collective-permute-start | bytes 3342344 | tf_op jit(solution)/shard_map/ppermute | solution.py:47
  13.0 4.7 %fusion.6 = f32[1024,256]{1,0:T(8,128)} fusion(bf16[2048,1024]{1,0:T(8,128)(2,1)} %copy-done.4, bf16[2048,256]{1,0:T(8,128)(2,1)} %param.9), kind=kOutput, calls=%fused_computation.28 | convolution fusion | flops 1073741824 | bytes 6291456 | tf_op jit(solution)/shard_map/dot_general | solution.py:26
  17.7 1.3 %fusion.7 = f32[1024,256]{1,0:T(8,128)} fusion(bf16[1024,128]{1,0:T(8,128)(2,1)S(1)} %fusion.2, bf16[128,256]{1,0:T(8,128)(2,1)S(1)} %copy-done.5), kind=kOutput, calls=%fused_computation.29 | convolution fusion | flops 67108864 | bytes 1376256 | tf_op jit(solution)/shard_map/dot_general | solution.py:83
  19.0 15.6 %conditional.1 = (f32[256,256]{1,0:T(8,128)S(1)}, s32[]{:T(128)}) conditional(s32[]{:T(128)} %convert_element_type.41, () %tuple.18, (f32[1024,256]{1,0:T(8,128)}, f32[1024,256]{1,0:T(8,128)}, s32[]{:T(128)}) %tuple.19), branch_computations={%region_0.1_spmd, %region_1.2_spmd} | conditional | flops 458775 | bytes 14418328 | solution.py:110
  19.0 1.7 %add.28 = f32[1024,256]{1,0:T(8,128)S(1)} add(f32[1024,256]{1,0:T(8,128)} %get-tuple-element.7, f32[1024,256]{1,0:T(8,128)} %get-tuple-element.8) | non-fusion elementwise | flops 262144 | bytes 3145728 | tf_op jit(solution)/shard_map/add | solution.py:83
  21.8 2.0 %collective-permute-done = f32[512,256]{1,0:T(8,128)} collective-permute-done((f32[512,256]{1,0:T(8,128)S(1)}, f32[512,256]{1,0:T(8,128)}, u32[]{:S(2)}, u32[]{:S(2)}) %collective-permute-start) | collective-permute-done | bytes 524320 | tf_op jit(solution)/shard_map/cond/branch_1_fun/ppermute | solution.py:47
  23.8 1.3 %dynamic-slice_add_fusion = f32[512,256]{1,0:T(8,128)S(1)} fusion(f32[512,256]{1,0:T(8,128)} %collective-permute-done, f32[1024,256]{1,0:T(8,128)} %copy-done.1, s32[]{:T(128)S(6)} %select_n.55), kind=kLoop, calls=%fused_computation | loop fusion | flops 131072 | bytes 1572868 | tf_op jit(solution)/shard_map/cond/branch_1_fun/add | solution.py:48
  25.1 1.5 %collective-permute-start.1 = (f32[256,256]{1,0:T(8,128)S(1)}, f32[256,256]{1,0:T(8,128)}, u32[]{:S(2)}, u32[]{:S(2)}) collective-permute-start(f32[256,256]{1,0:T(8,128)S(1)} %constant_dynamic-slice_fusion), channel_id=1, source_target_pairs={{0,4},{2,6},{4,0},{6,2},{8,12},{10,14},{12,8},{14,10},{16,20},{18,... | collective-permute-start | bytes 786440 | tf_op jit(solution)/shard_map/cond/branch_1_fun/ppermute | solution.py:47
  26.6 7.0 %collective-permute-done.1 = f32[256,256]{1,0:T(8,128)} collective-permute-done((f32[256,256]{1,0:T(8,128)S(1)}, f32[256,256]{1,0:T(8,128)}, u32[]{:S(2)}, u32[]{:S(2)}) %collective-permute-start.1) | collective-permute-done | bytes 262176 | tf_op jit(solution)/shard_map/cond/branch_1_fun/ppermute | solution.py:47
  34.6 1.6 %collective-permute-start.4 = (f32[128,256]{1,0:T(8,128)S(1)}, f32[128,256]{1,0:T(8,128)S(1)}, u32[]{:S(2)}, u32[]{:S(2)}) collective-permute-start(f32[128,256]{1,0:T(8,128)S(1)} %constant_dynamic-slice_fusion.2), channel_id=1, source_target_pairs={{0,8},{2,10},{4,12},{6,14},{8,0},{10,2},{12,4},{14,6},{16,24},{18,... | collective-permute-start | bytes 393224 | tf_op jit(solution)/shard_map/ppermute | solution.py:47
  36.2 3.4 %collective-permute-done.4 = f32[128,256]{1,0:T(8,128)S(1)} collective-permute-done((f32[128,256]{1,0:T(8,128)S(1)}, f32[128,256]{1,0:T(8,128)S(1)}, u32[]{:S(2)}, u32[]{:S(2)}) %collective-permute-start.4) | collective-permute-done | bytes 131104 | tf_op jit(solution)/shard_map/ppermute | solution.py:47
  39.7 2.6 %collective-permute-start.5 = (f32[64,256]{1,0:T(8,128)S(1)}, f32[64,256]{1,0:T(8,128)S(1)}, u32[]{:S(2)}, u32[]{:S(2)}) collective-permute-start(f32[64,256]{1,0:T(8,128)S(1)} %constant_dynamic-slice_fusion.4), channel_id=1, source_target_pairs={{0,16},{2,18},{4,20},{6,22},{8,24},{10,26},{12,28},{14,30},{16,0},... | collective-permute-start | bytes 196616 | tf_op jit(solution)/shard_map/ppermute | solution.py:47
  42.3 2.6 %collective-permute-done.5 = f32[64,256]{1,0:T(8,128)S(1)} collective-permute-done((f32[64,256]{1,0:T(8,128)S(1)}, f32[64,256]{1,0:T(8,128)S(1)}, u32[]{:S(2)}, u32[]{:S(2)}) %collective-permute-start.5) | collective-permute-done | bytes 65568 | tf_op jit(solution)/shard_map/ppermute | solution.py:47
  44.9 2.7 %collective-permute-start.6 = (bf16[64,256]{1,0:T(8,128)(2,1)S(1)}, bf16[64,256]{1,0:T(8,128)(2,1)S(1)}, u32[]{:S(2)}, u32[]{:S(2)}) collective-permute-start(bf16[64,256]{1,0:T(8,128)(2,1)S(1)} %add_convert_fusion.1), channel_id=1, source_target_pairs={{0,16},{2,18},{4,20},{6,22},{8,24},{10,26},{12,28},{14,30},{16,0},... | collective-permute-start | bytes 98312 | tf_op jit(solution)/shard_map/ppermute | solution.py:57
  47.6 2.3 %collective-permute-done.6 = bf16[64,256]{1,0:T(8,128)(2,1)S(1)} collective-permute-done((bf16[64,256]{1,0:T(8,128)(2,1)S(1)}, bf16[64,256]{1,0:T(8,128)(2,1)S(1)}, u32[]{:S(2)}, u32[]{:S(2)}) %collective-permute-start.6) | collective-permute-done | bytes 32800 | tf_op jit(solution)/shard_map/ppermute | solution.py:57
  49.9 1.8 %collective-permute-start.7 = (bf16[128,256]{1,0:T(8,128)(2,1)S(1)}, bf16[128,256]{1,0:T(8,128)(2,1)S(1)}, u32[]{:S(2)}, u32[]{:S(2)}) collective-permute-start(bf16[128,256]{1,0:T(8,128)(2,1)S(1)} %maximum_select_fusion.4), channel_id=1, source_target_pairs={{0,8},{2,10},{4,12},{6,14},{8,0},{10,2},{12,4},{14,6},{16,24},{18,... | collective-permute-start | bytes 196616 | tf_op jit(solution)/shard_map/ppermute | solution.py:57
  51.7 2.6 %collective-permute-done.7 = bf16[128,256]{1,0:T(8,128)(2,1)S(1)} collective-permute-done((bf16[128,256]{1,0:T(8,128)(2,1)S(1)}, bf16[128,256]{1,0:T(8,128)(2,1)S(1)}, u32[]{:S(2)}, u32[]{:S(2)}) %collective-permute-start.7) | collective-permute-done | bytes 65568 | tf_op jit(solution)/shard_map/ppermute | solution.py:57
  54.3 1.5 %collective-permute-start.8 = (bf16[256,256]{1,0:T(8,128)(2,1)S(1)}, bf16[256,256]{1,0:T(8,128)(2,1)S(1)}, u32[]{:S(2)}, u32[]{:S(2)}) collective-permute-start(bf16[256,256]{1,0:T(8,128)(2,1)S(1)} %maximum_select_fusion.3), channel_id=1, source_target_pairs={{0,4},{2,6},{4,0},{6,2},{8,12},{10,14},{12,8},{14,10},{16,20},{18,... | collective-permute-start | bytes 393224 | tf_op jit(solution)/shard_map/ppermute | solution.py:57
  55.9 1.8 %add_convert_fusion = bf16[1088,256]{1,0:T(8,128)(2,1)S(1)} fusion(f32[1088,256]{1,0:T(8,128)} %collective-permute-done.2, f32[2176,256]{1,0:T(8,128)S(1)} %pad_maximum_fusion, s32[]{:T(128)S(6)} %select_n.77, bf16[2048,256]{1,0:T(8,128)(2,1)} %param.9, bf16[128,256]{1,0:T(8,128)(2,1)} %param.11), kind=kLoop, calls=%fused_computation.13 | loop fusion | flops 2228224 | bytes 3899396 | tf_op jit(solution)/shard_map/convert_element_type | solution.py:32
  59.5 1.5 %collective-permute-done.9 = bf16[512,256]{1,0:T(8,128)(2,1)S(1)} collective-permute-done((bf16[512,256]{1,0:T(8,128)(2,1)S(1)}, bf16[512,256]{1,0:T(8,128)(2,1)S(1)}, u32[]{:S(2)}, u32[]{:S(2)}) %collective-permute-start.9) | collective-permute-done | bytes 262176 | tf_op jit(solution)/shard_map/ppermute | solution.py:57
  62.1 5.6 %collective-permute-done.3 = bf16[1088,256]{1,0:T(8,128)(2,1)S(1)} collective-permute-done((bf16[1088,256]{1,0:T(8,128)(2,1)S(1)}, bf16[1088,256]{1,0:T(8,128)(2,1)S(1)}, u32[]{:S(2)}, u32[]{:S(2)}) %collective-permute-start.3) | collective-permute-done | bytes 557088 | tf_op jit(solution)/shard_map/ppermute | solution.py:57
  (43 shorter events, 11.7 us)
Async XLA Ops:
  1.4 1.0 %copy-start = (bf16[1024,256]{1,0:T(8,128)(2,1)S(1)}, bf16[1024,256]{1,0:T(8,128)(2,1)}, u32[]{:S(2)}) copy-start(bf16[1024,256]{1,0:T(8,128)(2,1)} %param.10) | copy-start | bytes 1572868
  1.4 1.4 %copy-start.2 = (bf16[2048,256]{1,0:T(8,128)(2,1)S(1)}, bf16[2048,256]{1,0:T(8,128)(2,1)}, u32[]{:S(2)}) copy-start(bf16[2048,256]{1,0:T(8,128)(2,1)} %param.9) | copy-start | bytes 3145732
  1.4 2.7 %copy-start.3 = (bf16[2048,1024]{1,0:T(8,128)(2,1)S(1)}, bf16[2048,1024]{1,0:T(8,128)(2,1)}, u32[]{:S(2)}) copy-start(bf16[2048,1024]{1,0:T(8,128)(2,1)} %param.12) | copy-start | bytes 12582916
  6.1 2.0 %copy-start.4 = (bf16[2048,1024]{1,0:T(8,128)(2,1)}, bf16[2048,1024]{1,0:T(8,128)(2,1)S(1)}, u32[]{:S(2)}) copy-start(bf16[2048,1024]{1,0:T(8,128)(2,1)S(1)} %fusion) | copy-start | bytes 12582916
  6.1 1.9 %copy-start.7 = (s32[8,1]{0,1:T(1,128)S(1)}, s32[8,1]{0,1:T(1,128)}, u32[]{:S(2)}) copy-start(s32[8,1]{0,1:T(1,128)} %param.15) | copy-start | bytes 100
  6.2 2.0 %copy-start.5 = (bf16[128,256]{1,0:T(8,128)(2,1)S(1)}, bf16[128,256]{1,0:T(8,128)(2,1)}, u32[]{:S(2)}) copy-start(bf16[128,256]{1,0:T(8,128)(2,1)} %param.11) | copy-start | bytes 196612
  6.2 2.0 %copy-start.6 = (bf16[1024,128]{1,0:T(8,128)(2,1)S(1)}, bf16[1024,128]{1,0:T(8,128)(2,1)}, u32[]{:S(2)}) copy-start(bf16[1024,128]{1,0:T(8,128)(2,1)} %param.14) | copy-start | bytes 786436
  10.0 45.9 %collective-permute-start.2 = (f32[1088,256]{1,0:T(8,128)}, f32[1088,256]{1,0:T(8,128)}, u32[]{:S(2)}, u32[]{:S(2)}) collective-permute-start(f32[1088,256]{1,0:T(8,128)} %constant_dynamic-slice_fusion.3), channel_id=1, source_target_pairs={{0,1},{1,0},{2,3},{3,2},{4,5},{5,4},{6,7},{7,6},{8,9},{9,8},{10,11... | collective-permute-start | bytes 3342344 | tf_op jit(solution)/shard_map/ppermute | solution.py:47
  20.6 1.0 %copy-start.1 = (f32[1024,256]{1,0:T(8,128)}, f32[1024,256]{1,0:T(8,128)S(1)}, u32[]{:S(2)}) copy-start(f32[1024,256]{1,0:T(8,128)S(1)} %add.28) | copy-start | bytes 3145732 | tf_op jit(solution)/shard_map/cond
  21.7 2.1 %collective-permute-start = (f32[512,256]{1,0:T(8,128)S(1)}, f32[512,256]{1,0:T(8,128)}, u32[]{:S(2)}, u32[]{:S(2)}) collective-permute-start(f32[512,256]{1,0:T(8,128)S(1)} %constant_dynamic-slice_fusion.1), channel_id=1, source_target_pairs={{0,2},{2,0},{4,6},{6,4},{8,10},{10,8},{12,14},{14,12},{16,18},{18,... | collective-permute-start | bytes 1572872 | tf_op jit(solution)/shard_map/cond/branch_1_fun/ppermute | solution.py:47
  25.1 8.5 %collective-permute-start.1 = (f32[256,256]{1,0:T(8,128)S(1)}, f32[256,256]{1,0:T(8,128)}, u32[]{:S(2)}, u32[]{:S(2)}) collective-permute-start(f32[256,256]{1,0:T(8,128)S(1)} %constant_dynamic-slice_fusion), channel_id=1, source_target_pairs={{0,4},{2,6},{4,0},{6,2},{8,12},{10,14},{12,8},{14,10},{16,20},{18,... | collective-permute-start | bytes 786440 | tf_op jit(solution)/shard_map/cond/branch_1_fun/ppermute | solution.py:47
  34.6 5.0 %collective-permute-start.4 = (f32[128,256]{1,0:T(8,128)S(1)}, f32[128,256]{1,0:T(8,128)S(1)}, u32[]{:S(2)}, u32[]{:S(2)}) collective-permute-start(f32[128,256]{1,0:T(8,128)S(1)} %constant_dynamic-slice_fusion.2), channel_id=1, source_target_pairs={{0,8},{2,10},{4,12},{6,14},{8,0},{10,2},{12,4},{14,6},{16,24},{18,... | collective-permute-start | bytes 393224 | tf_op jit(solution)/shard_map/ppermute | solution.py:47
  39.7 5.2 %collective-permute-start.5 = (f32[64,256]{1,0:T(8,128)S(1)}, f32[64,256]{1,0:T(8,128)S(1)}, u32[]{:S(2)}, u32[]{:S(2)}) collective-permute-start(f32[64,256]{1,0:T(8,128)S(1)} %constant_dynamic-slice_fusion.4), channel_id=1, source_target_pairs={{0,16},{2,18},{4,20},{6,22},{8,24},{10,26},{12,28},{14,30},{16,0},... | collective-permute-start | bytes 196616 | tf_op jit(solution)/shard_map/ppermute | solution.py:47
  44.9 5.0 %collective-permute-start.6 = (bf16[64,256]{1,0:T(8,128)(2,1)S(1)}, bf16[64,256]{1,0:T(8,128)(2,1)S(1)}, u32[]{:S(2)}, u32[]{:S(2)}) collective-permute-start(bf16[64,256]{1,0:T(8,128)(2,1)S(1)} %add_convert_fusion.1), channel_id=1, source_target_pairs={{0,16},{2,18},{4,20},{6,22},{8,24},{10,26},{12,28},{14,30},{16,0},... | collective-permute-start | bytes 98312 | tf_op jit(solution)/shard_map/ppermute | solution.py:57
  49.9 4.3 %collective-permute-start.7 = (bf16[128,256]{1,0:T(8,128)(2,1)S(1)}, bf16[128,256]{1,0:T(8,128)(2,1)S(1)}, u32[]{:S(2)}, u32[]{:S(2)}) collective-permute-start(bf16[128,256]{1,0:T(8,128)(2,1)S(1)} %maximum_select_fusion.4), channel_id=1, source_target_pairs={{0,8},{2,10},{4,12},{6,14},{8,0},{10,2},{12,4},{14,6},{16,24},{18,... | collective-permute-start | bytes 196616 | tf_op jit(solution)/shard_map/ppermute | solution.py:57
  54.3 5.0 %collective-permute-start.8 = (bf16[256,256]{1,0:T(8,128)(2,1)S(1)}, bf16[256,256]{1,0:T(8,128)(2,1)S(1)}, u32[]{:S(2)}, u32[]{:S(2)}) collective-permute-start(bf16[256,256]{1,0:T(8,128)(2,1)S(1)} %maximum_select_fusion.3), channel_id=1, source_target_pairs={{0,4},{2,6},{4,0},{6,2},{8,12},{10,14},{12,8},{14,10},{16,20},{18,... | collective-permute-start | bytes 393224 | tf_op jit(solution)/shard_map/ppermute | solution.py:57
  57.6 10.0 %collective-permute-start.3 = (bf16[1088,256]{1,0:T(8,128)(2,1)S(1)}, bf16[1088,256]{1,0:T(8,128)(2,1)S(1)}, u32[]{:S(2)}, u32[]{:S(2)}) collective-permute-start(bf16[1088,256]{1,0:T(8,128)(2,1)S(1)} %add_convert_fusion), channel_id=1, source_target_pairs={{0,1},{1,0},{2,3},{3,2},{4,5},{5,4},{6,7},{7,6},{8,9},{9,8},{10,11... | collective-permute-start | bytes 1671176 | tf_op jit(solution)/shard_map/ppermute | solution.py:57
  59.5 1.6 %collective-permute-start.9 = (bf16[512,256]{1,0:T(8,128)(2,1)S(1)}, bf16[512,256]{1,0:T(8,128)(2,1)S(1)}, u32[]{:S(2)}, u32[]{:S(2)}) collective-permute-start(bf16[512,256]{1,0:T(8,128)(2,1)S(1)} %maximum_select_fusion.2), channel_id=1, source_target_pairs={{0,2},{2,0},{4,6},{6,4},{8,10},{10,8},{12,14},{14,12},{16,18},{18,... | collective-permute-start | bytes 786440 | tf_op jit(solution)/shard_map/ppermute | solution.py:57

commit v13 on v12

--- a/solution.py
+++ b/solution.py
@@ -50,9 +50,9 @@
     return parts, offsets
 
 
-def doubling_gather(parts, axis, count, position):
+def doubling_gather(parts, axis, count, position, bits=None):
     steps = count.bit_length() - 1
-    for bit in reversed(range(steps)):
+    for bit in reversed(range(steps)) if bits is None else bits:
         side = (position >> bit) & 1
         got = lax.ppermute(tuple(parts), axis, xor_pairs(count, bit))
         parts = [
@@ -74,29 +74,13 @@
     tag_part = transposed_product(link_errors, item_factors)
     joint_part = jnp.concatenate([user_part, tag_part], 0)
 
-    joint_part, rating_errors, link_errors = lax.optimization_barrier(
-        (joint_part, rating_errors, link_errors)
+    item_part = transposed_product(rating_errors, user_factors) + jnp.dot(
+        link_errors, tag_factors, preferred_element_type=jnp.float32
     )
+    joint_part, item_part = lax.optimization_barrier((joint_part, item_part))
     (joint_share,), (joint_offset,) = halving_scatter(
         [joint_part], "loop", loop_count, loop_position
     )
-    item_part = transposed_product(rating_errors, user_factors) + jnp.dot(
-        link_errors, tag_factors, preferred_element_type=jnp.float32
-    )
-    joint_factors = jnp.concatenate([user_factors, tag_factors], 0)
-    fresh_joint = advance(
-        lax.dynamic_slice_in_dim(joint_factors, joint_offset, joint_share.shape[0], 0),
-        joint_share,
-        jnp.where(
-            joint_offset + jnp.arange(joint_share.shape[0])[:, None] < user_factors.shape[0],
-            step_users,
-            step_tags,
-        ),
-    )
-    (new_joint,) = doubling_gather([fresh_joint], "loop", loop_count, loop_position)
-    new_users = new_joint[: user_factors.shape[0]]
-    new_tags = new_joint[user_factors.shape[0] :]
-
     group_steps = group_count.bit_length() - 1
     first_bits = list(range(min(2, group_steps)))
     first_rows = item_part.shape[0] >> len(first_bits)
@@ -122,7 +106,34 @@
         item_share,
         step_items,
     )
-    (new_items,) = doubling_gather([fresh_items], "group", group_count, group_position)
+    gather_bits = list(reversed(range(group_steps)))
+    (partly,) = doubling_gather(
+        [fresh_items], "group", group_count, group_position, gather_bits[:1]
+    )
+    partly, joint_share = lax.optimization_barrier((partly, joint_share))
+    joint_factors = jnp.concatenate([user_factors, tag_factors], 0)
+    fresh_joint = advance(
+        lax.dynamic_slice_in_dim(joint_factors, joint_offset, joint_share.shape[0], 0),
+        joint_share,
+        jnp.where(
+            joint_offset + jnp.arange(joint_share.shape[0])[:, None] < user_factors.shape[0],
+            step_users,
+            step_tags,
+        ),
+    )
+    (new_joint,) = doubling_gather([fresh_joint], "loop", loop_count, loop_position)
+    new_users = new_joint[: user_factors.shape[0]]
+    new_tags = new_joint[user_factors.shape[0] :]
+
+    (partly,) = doubling_gather(
+        [partly], "group", group_count, group_position, gather_bits[1:2]
+    )
+    partly, new_joint = lax.optimization_barrier((partly, new_joint))
+    new_users = new_joint[: user_factors.shape[0]]
+    new_tags = new_joint[user_factors.shape[0] :]
+    (new_items,) = doubling_gather(
+        [partly], "group", group_count, group_position, gather_bits[2:]
+    )
     return (new_users, new_items, new_tags)
 
 

time: 69.8 us -> 65.3 us (0.936)
  matrix products: 9.9 us -> 6.33 us
  other arithmetic: 7.98 us -> 6.34 us
  starting transfers between devices: 15.4 us -> 16.5 us
    dot_general x2, matrix products: 5 us -> 1.55 us  [transposed_product(): lax.dot_general(first_operand, second_operand, (((0,), (0,)), ((), ())),...]
    add x1 -> x0, other arithmetic: 1.67 us -> none  [shards(): transposed_product(rating_errors, user_factors)]
    add x3 -> x4, other arithmetic: 2.27 us -> 3.66 us  [halving_scatter(): parts = [k + g for k, g in zip(kept, got)]]
    convert_element_type x2, other arithmetic: 1.78 us -> 0.42 us  [advance(): return (factors.astype(jnp.float32) + rate * gradient).astype(jnp.bfloat16)]
    dynamic_slice x5, local copies, waits for them, and re-layouts: 1.18 us -> 2.23 us  [halving_scatter(): lax.dynamic_slice_in_dim(p, (1 - side) * h, h, 0)]
    ppermute x5, starting transfers between devices: 6.61 us -> 7.59 us  [doubling_gather(): got = lax.ppermute(tuple(parts), axis, xor_pairs(count, bit))]
    cond x2 -> x0, local copies, waits for them, and re-layouts: 0.98 us -> none
  transfers between devices with their start and end apart: 10 -> 10, of which waited for: 9 -> 8; matrix products, arithmetic and copies ran while one was open for 19% -> 8% of each run, Pallas kernels for 0% -> 0%
where the time goes in v13:
time: 65.3 us; the launch traced here: 64.9 us
  waiting for transfers between devices  28.2 us (43%)
  starting transfers between devices  16.5 us (25%)
  local copies, waits for them, and re-layouts  6.74 us (10%)
  other arithmetic  6.34 us (10%)
  matrix products  6.33 us (10%)
  between operations  0.82 us (1%)
    ppermute x5, waiting for transfers between devices, halving_scatter(): got = lax.ppermute(tuple(sent), axis, xor_pairs(count, bit))  14.9 us
    ppermute x5, waiting for transfers between devices, doubling_gather(): got = lax.ppermute(tuple(parts), axis, xor_pairs(count, bit))  13.2 us
    ppermute x5, starting transfers between devices, halving_scatter(): got = lax.ppermute(tuple(sent), axis, xor_pairs(count, bit))  8.9 us
    ppermute x5, starting transfers between devices, doubling_gather(): got = lax.ppermute(tuple(parts), axis, xor_pairs(count, bit))  7.59 us
    add x4, other arithmetic, halving_scatter(): parts = [k + g for k, g in zip(kept, got)]  3.66 us
    dot_general x2, matrix products, residual_of(): lax.dot_general(row_factors, column_factors, (((1,), (1,)), ((), ())), pr...  2.26 us
    dynamic_slice x5, local copies, waits for them, and re-layouts, halving_scatter(): lax.dynamic_slice_in_dim(p, (1 - side) * h, h, 0)  2.23 us
    unnamed x14, local copies, waits for them, and re-layouts  2.09 us
  transfers between devices with their start and end apart: 10, of which 8 were waited for; matrix products, arithmetic and copies ran while one was open for 8% of the time, Pallas kernels for 0%

profile of v13, /device:TPU:0, one launch (start us, length us, event | category | flops | bytes accessed | tf_op | source)
XLA Modules:
  0.0 64.9 jit_solution(3764491652508887879)
XLA Ops:
  2.8 1.3 %copy-done.3 = bf16[2048,1024]{1,0:T(8,128)(2,1)S(1)} copy-done((bf16[2048,1024]{1,0:T(8,128)(2,1)S(1)}, bf16[2048,1024]{1,0:T(8,128)(2,1)}, u32[]{:S(2)}) %copy-start.3) | copy-done | bytes 4194328
  4.1 2.0 %fusion = bf16[2048,1024]{1,0:T(8,128)(2,1)S(1)} fusion(f32[256,8,8,128]{3,2,1,0:T(8,128)S(1)} %bitcast.22, bf16[2048,1024]{1,0:T(8,128)(2,1)S(1)} %copy-done.3, bf16[2048,256]{1,0:T(8,128)(2,1)S(1)} %copy-done.1, bf16[1024,256]{1,0:T(8,128)(2,1)S(1)} %copy-done), kind=kOutput, calls=%fused_computation.5 | convolution fusion | flops 1082130432 | bytes 18350080 | tf_op jit(solution)/shard_map/dot_general | solution.py:19
  6.0 1.3 %fusion.4 = f32[2048,256]{1,0:T(8,128)S(1)} fusion(bf16[2048,1024]{1,0:T(8,128)(2,1)S(1)} %fusion, bf16[1024,256]{1,0:T(8,128)(2,1)S(1)} %copy-done), kind=kOutput, calls=%fused_computation.28 | convolution fusion | flops 1073741824 | bytes 6815744 | tf_op jit(solution)/shard_map/dot_general | solution.py:73
  7.4 1.3 %fusion.6 = f32[1024,256]{1,0:T(8,128)S(1)} fusion(bf16[2048,1024]{1,0:T(8,128)(2,1)S(1)} %fusion, bf16[2048,256]{1,0:T(8,128)(2,1)S(1)} %copy-done.1), kind=kOutput, calls=%fused_computation.30 | convolution fusion | flops 1073741824 | bytes 6291456 | tf_op jit(solution)/shard_map/dot_general | solution.py:26
  9.3 1.2 %convolution_add_fusion = f32[1024,256]{1,0:T(8,128)} fusion(f32[1024,256]{1,0:T(8,128)S(1)} %fusion.6, bf16[1024,128]{1,0:T(8,128)(2,1)S(1)} %fusion.2, bf16[128,256]{1,0:T(8,128)(2,1)S(1)} %copy-done.4), kind=kOutput, calls=%fused_computation.7 | convolution fusion | flops 67371008 | bytes 2424832 | tf_op jit(solution)/shard_map/dot_general | solution.py:77
  11.8 3.0 %collective-permute-start.5 = (f32[1088,256]{1,0:T(8,128)}, f32[1088,256]{1,0:T(8,128)}, u32[]{:S(2)}, u32[]{:S(2)}) collective-permute-start(f32[1088,256]{1,0:T(8,128)} %constant_dynamic-slice_fusion.2), channel_id=1, source_target_pairs={{0,1},{1,0},{2,3},{3,2},{4,5},{5,4},{6,7},{7,6},{8,9},{9,8},{10,11... | collective-permute-start | bytes 3342344 | tf_op jit(solution)/shard_map/ppermute | solution.py:47
  14.8 14.0 %conditional.1 = (f32[256,256]{1,0:T(8,128)S(1)}, s32[]{:T(128)}) conditional(s32[]{:T(128)} %convert_element_type.33, () %tuple.19, (s32[]{:T(128)}, f32[1024,256]{1,0:T(8,128)}) %tuple.21), branch_computations={%region_0.0_spmd, %region_1.0_spmd} | conditional | flops 196631 | bytes 7078268 | solution.py:94
  16.0 2.0 %collective-permute-done = f32[512,256]{1,0:T(8,128)} collective-permute-done((f32[512,256]{1,0:T(8,128)S(1)}, f32[512,256]{1,0:T(8,128)}, u32[]{:S(2)}, u32[]{:S(2)}) %collective-permute-start) | collective-permute-done | bytes 524320 | tf_op jit(solution)/shard_map/cond/branch_1_fun/ppermute | solution.py:47
  18.0 1.3 %dynamic-slice_add_fusion = f32[512,256]{1,0:T(8,128)S(1)} fusion(f32[512,256]{1,0:T(8,128)} %collective-permute-done, f32[1024,256]{1,0:T(8,128)} %get-tuple-element.4, s32[]{:T(128)S(6)} %select_n.55), kind=kLoop, calls=%fused_computation | loop fusion | flops 131072 | bytes 1572868 | tf_op jit(solution)/shard_map/cond/branch_1_fun/add | solution.py:48
  19.3 1.6 %collective-permute-start.1 = (f32[256,256]{1,0:T(8,128)S(1)}, f32[256,256]{1,0:T(8,128)}, u32[]{:S(2)}, u32[]{:S(2)}) collective-permute-start(f32[256,256]{1,0:T(8,128)S(1)} %constant_dynamic-slice_fusion), channel_id=1, source_target_pairs={{0,4},{2,6},{4,0},{6,2},{8,12},{10,14},{12,8},{14,10},{16,20},{18,... | collective-permute-start | bytes 786440 | tf_op jit(solution)/shard_map/cond/branch_1_fun/ppermute | solution.py:47
  20.9 7.0 %collective-permute-done.1 = f32[256,256]{1,0:T(8,128)} collective-permute-done((f32[256,256]{1,0:T(8,128)S(1)}, f32[256,256]{1,0:T(8,128)}, u32[]{:S(2)}, u32[]{:S(2)}) %collective-permute-start.1) | collective-permute-done | bytes 262176 | tf_op jit(solution)/shard_map/cond/branch_1_fun/ppermute | solution.py:47
  28.8 1.6 %collective-permute-start.2 = (f32[128,256]{1,0:T(8,128)S(1)}, f32[128,256]{1,0:T(8,128)S(1)}, u32[]{:S(2)}, u32[]{:S(2)}) collective-permute-start(f32[128,256]{1,0:T(8,128)S(1)} %constant_dynamic-slice_fusion.4), channel_id=1, source_target_pairs={{0,8},{2,10},{4,12},{6,14},{8,0},{10,2},{12,4},{14,6},{16,24},{18,... | collective-permute-start | bytes 393224 | tf_op jit(solution)/shard_map/ppermute | solution.py:47
  30.5 3.4 %collective-permute-done.2 = f32[128,256]{1,0:T(8,128)S(1)} collective-permute-done((f32[128,256]{1,0:T(8,128)S(1)}, f32[128,256]{1,0:T(8,128)S(1)}, u32[]{:S(2)}, u32[]{:S(2)}) %collective-permute-start.2) | collective-permute-done | bytes 131104 | tf_op jit(solution)/shard_map/ppermute | solution.py:47
  33.9 2.7 %collective-permute-start.3 = (f32[64,256]{1,0:T(8,128)S(1)}, f32[64,256]{1,0:T(8,128)S(1)}, u32[]{:S(2)}, u32[]{:S(2)}) collective-permute-start(f32[64,256]{1,0:T(8,128)S(1)} %constant_dynamic-slice_fusion.3), channel_id=1, source_target_pairs={{0,16},{2,18},{4,20},{6,22},{8,24},{10,26},{12,28},{14,30},{16,0},... | collective-permute-start | bytes 196616 | tf_op jit(solution)/shard_map/ppermute | solution.py:47
  36.6 2.6 %collective-permute-done.3 = f32[64,256]{1,0:T(8,128)S(1)} collective-permute-done((f32[64,256]{1,0:T(8,128)S(1)}, f32[64,256]{1,0:T(8,128)S(1)}, u32[]{:S(2)}, u32[]{:S(2)}) %collective-permute-start.3) | collective-permute-done | bytes 65568 | tf_op jit(solution)/shard_map/ppermute | solution.py:47
  39.2 2.7 %collective-permute-start.4 = (bf16[64,256]{1,0:T(8,128)(2,1)S(1)}, bf16[64,256]{1,0:T(8,128)(2,1)S(1)}, u32[]{:S(2)}, u32[]{:S(2)}) collective-permute-start(bf16[64,256]{1,0:T(8,128)(2,1)S(1)} %add_convert_fusion.1), channel_id=1, source_target_pairs={{0,16},{2,18},{4,20},{6,22},{8,24},{10,26},{12,28},{14,30},{16,0},... | collective-permute-start | bytes 98312 | tf_op jit(solution)/shard_map/ppermute | solution.py:57
  41.9 2.1 %collective-permute-done.4 = bf16[64,256]{1,0:T(8,128)(2,1)S(1)} collective-permute-done((bf16[64,256]{1,0:T(8,128)(2,1)S(1)}, bf16[64,256]{1,0:T(8,128)(2,1)S(1)}, u32[]{:S(2)}, u32[]{:S(2)}) %collective-permute-start.4) | collective-permute-done | bytes 32800 | tf_op jit(solution)/shard_map/ppermute | solution.py:57
  44.1 1.4 %dynamic-slice_add_fusion.2 = f32[1088,256]{1,0:T(8,128)S(1)} fusion(f32[1088,256]{1,0:T(8,128)} %collective-permute-done.5, f32[2176,256]{1,0:T(8,128)S(1)} %pad_maximum_fusion, s32[]{:T(128)S(6)} %select_n.84), kind=kLoop, calls=%fused_computation.15 | loop fusion | flops 278528 | bytes 3342340 | tf_op jit(solution)/shard_map/add | solution.py:48
  45.9 1.2 %collective-permute-start.7 = (bf16[1088,256]{1,0:T(8,128)(2,1)S(1)}, bf16[1088,256]{1,0:T(8,128)(2,1)S(1)}, u32[]{:S(2)}, u32[]{:S(2)}) collective-permute-start(bf16[1088,256]{1,0:T(8,128)(2,1)S(1)} %add_convert_fusion), channel_id=1, source_target_pairs={{0,1},{1,0},{2,3},{3,2},{4,5},{5,4},{6,7},{7,6},{8,9},{9,8},{10,11... | collective-permute-start | bytes 1671176 | tf_op jit(solution)/shard_map/ppermute | solution.py:57
  47.1 2.0 %collective-permute-start.6 = (bf16[128,256]{1,0:T(8,128)(2,1)S(1)}, bf16[128,256]{1,0:T(8,128)(2,1)S(1)}, u32[]{:S(2)}, u32[]{:S(2)}) collective-permute-start(bf16[128,256]{1,0:T(8,128)(2,1)S(1)} %maximum_select_fusion.4), channel_id=1, source_target_pairs={{0,8},{2,10},{4,12},{6,14},{8,0},{10,2},{12,4},{14,6},{16,24},{18,... | collective-permute-start | bytes 196616 | tf_op jit(solution)/shard_map/ppermute | solution.py:57
  49.1 2.3 %collective-permute-done.6 = bf16[128,256]{1,0:T(8,128)(2,1)S(1)} collective-permute-done((bf16[128,256]{1,0:T(8,128)(2,1)S(1)}, bf16[128,256]{1,0:T(8,128)(2,1)S(1)}, u32[]{:S(2)}, u32[]{:S(2)}) %collective-permute-start.6) | collective-permute-done | bytes 65568 | tf_op jit(solution)/shard_map/ppermute | solution.py:57
  51.4 5.3 %collective-permute-done.7 = bf16[1088,256]{1,0:T(8,128)(2,1)S(1)} collective-permute-done((bf16[1088,256]{1,0:T(8,128)(2,1)S(1)}, bf16[1088,256]{1,0:T(8,128)(2,1)S(1)}, u32[]{:S(2)}, u32[]{:S(2)}) %collective-permute-start.7) | collective-permute-done | bytes 557088 | tf_op jit(solution)/shard_map/ppermute | solution.py:57
  57.0 1.6 %collective-permute-start.8 = (bf16[256,256]{1,0:T(8,128)(2,1)S(1)}, bf16[256,256]{1,0:T(8,128)(2,1)S(1)}, u32[]{:S(2)}, u32[]{:S(2)}) collective-permute-start(bf16[256,256]{1,0:T(8,128)(2,1)S(1)} %maximum_select_fusion.3), channel_id=1, source_target_pairs={{0,4},{2,6},{4,0},{6,2},{8,12},{10,14},{12,8},{14,10},{16,20},{18,... | collective-permute-start | bytes 393224 | tf_op jit(solution)/shard_map/ppermute | solution.py:57
  58.6 3.5 %collective-permute-done.8 = bf16[256,256]{1,0:T(8,128)(2,1)S(1)} collective-permute-done((bf16[256,256]{1,0:T(8,128)(2,1)S(1)}, bf16[256,256]{1,0:T(8,128)(2,1)S(1)}, u32[]{:S(2)}, u32[]{:S(2)}) %collective-permute-start.8) | collective-permute-done | bytes 131104 | tf_op jit(solution)/shard_map/ppermute | solution.py:57
  (41 shorter events, 9.9 us)
Async XLA Ops:
  1.4 1.0 %copy-start = (bf16[1024,256]{1,0:T(8,128)(2,1)S(1)}, bf16[1024,256]{1,0:T(8,128)(2,1)}, u32[]{:S(2)}) copy-start(bf16[1024,256]{1,0:T(8,128)(2,1)} %param.10) | copy-start | bytes 1572868
  1.4 1.4 %copy-start.1 = (bf16[2048,256]{1,0:T(8,128)(2,1)S(1)}, bf16[2048,256]{1,0:T(8,128)(2,1)}, u32[]{:S(2)}) copy-start(bf16[2048,256]{1,0:T(8,128)(2,1)} %param.9) | copy-start | bytes 3145732
  1.4 2.7 %copy-start.3 = (bf16[2048,1024]{1,0:T(8,128)(2,1)S(1)}, bf16[2048,1024]{1,0:T(8,128)(2,1)}, u32[]{:S(2)}) copy-start(bf16[2048,1024]{1,0:T(8,128)(2,1)} %param.12) | copy-start | bytes 12582916
  7.3 1.3 %copy-start.6 = (s32[8,1]{0,1:T(1,128)S(1)}, s32[8,1]{0,1:T(1,128)}, u32[]{:S(2)}) copy-start(s32[8,1]{0,1:T(1,128)} %param.15) | copy-start | bytes 100
  7.3 1.4 %copy-start.4 = (bf16[128,256]{1,0:T(8,128)(2,1)S(1)}, bf16[128,256]{1,0:T(8,128)(2,1)}, u32[]{:S(2)}) copy-start(bf16[128,256]{1,0:T(8,128)(2,1)} %param.11) | copy-start | bytes 196612
  7.3 1.4 %copy-start.5 = (bf16[1024,128]{1,0:T(8,128)(2,1)S(1)}, bf16[1024,128]{1,0:T(8,128)(2,1)}, u32[]{:S(2)}) copy-start(bf16[1024,128]{1,0:T(8,128)(2,1)} %param.14) | copy-start | bytes 786436
  11.8 32.2 %collective-permute-start.5 = (f32[1088,256]{1,0:T(8,128)}, f32[1088,256]{1,0:T(8,128)}, u32[]{:S(2)}, u32[]{:S(2)}) collective-permute-start(f32[1088,256]{1,0:T(8,128)} %constant_dynamic-slice_fusion.2), channel_id=1, source_target_pairs={{0,1},{1,0},{2,3},{3,2},{4,5},{5,4},{6,7},{7,6},{8,9},{9,8},{10,11... | collective-permute-start | bytes 3342344 | tf_op jit(solution)/shard_map/ppermute | solution.py:47
  15.9 2.1 %collective-permute-start = (f32[512,256]{1,0:T(8,128)S(1)}, f32[512,256]{1,0:T(8,128)}, u32[]{:S(2)}, u32[]{:S(2)}) collective-permute-start(f32[512,256]{1,0:T(8,128)S(1)} %constant_dynamic-slice_fusion.1), channel_id=1, source_target_pairs={{0,2},{2,0},{4,6},{6,4},{8,10},{10,8},{12,14},{14,12},{16,18},{18,... | collective-permute-start | bytes 1572872 | tf_op jit(solution)/shard_map/cond/branch_1_fun/ppermute | solution.py:47
  19.3 8.5 %collective-permute-start.1 = (f32[256,256]{1,0:T(8,128)S(1)}, f32[256,256]{1,0:T(8,128)}, u32[]{:S(2)}, u32[]{:S(2)}) collective-permute-start(f32[256,256]{1,0:T(8,128)S(1)} %constant_dynamic-slice_fusion), channel_id=1, source_target_pairs={{0,4},{2,6},{4,0},{6,2},{8,12},{10,14},{12,8},{14,10},{16,20},{18,... | collective-permute-start | bytes 786440 | tf_op jit(solution)/shard_map/cond/branch_1_fun/ppermute | solution.py:47
  28.8 5.0 %collective-permute-start.2 = (f32[128,256]{1,0:T(8,128)S(1)}, f32[128,256]{1,0:T(8,128)S(1)}, u32[]{:S(2)}, u32[]{:S(2)}) collective-permute-start(f32[128,256]{1,0:T(8,128)S(1)} %constant_dynamic-slice_fusion.4), channel_id=1, source_target_pairs={{0,8},{2,10},{4,12},{6,14},{8,0},{10,2},{12,4},{14,6},{16,24},{18,... | collective-permute-start | bytes 393224 | tf_op jit(solution)/shard_map/ppermute | solution.py:47
  33.9 5.2 %collective-permute-start.3 = (f32[64,256]{1,0:T(8,128)S(1)}, f32[64,256]{1,0:T(8,128)S(1)}, u32[]{:S(2)}, u32[]{:S(2)}) collective-permute-start(f32[64,256]{1,0:T(8,128)S(1)} %constant_dynamic-slice_fusion.3), channel_id=1, source_target_pairs={{0,16},{2,18},{4,20},{6,22},{8,24},{10,26},{12,28},{14,30},{16,0},... | collective-permute-start | bytes 196616 | tf_op jit(solution)/shard_map/ppermute | solution.py:47
  39.2 6.3 %copy-start.2 = (bf16[2048,256]{1,0:T(8,128)(2,1)S(1)}, bf16[2048,256]{1,0:T(8,128)(2,1)}, u32[]{:S(2)}) copy-start(bf16[2048,256]{1,0:T(8,128)(2,1)} %param.9) | copy-start | bytes 3145732
  39.2 4.9 %collective-permute-start.4 = (bf16[64,256]{1,0:T(8,128)(2,1)S(1)}, bf16[64,256]{1,0:T(8,128)(2,1)S(1)}, u32[]{:S(2)}, u32[]{:S(2)}) collective-permute-start(bf16[64,256]{1,0:T(8,128)(2,1)S(1)} %add_convert_fusion.1), channel_id=1, source_target_pairs={{0,16},{2,18},{4,20},{6,22},{8,24},{10,26},{12,28},{14,30},{16,0},... | collective-permute-start | bytes 98312 | tf_op jit(solution)/shard_map/ppermute | solution.py:57
  45.9 10.9 %collective-permute-start.7 = (bf16[1088,256]{1,0:T(8,128)(2,1)S(1)}, bf16[1088,256]{1,0:T(8,128)(2,1)S(1)}, u32[]{:S(2)}, u32[]{:S(2)}) collective-permute-start(bf16[1088,256]{1,0:T(8,128)(2,1)S(1)} %add_convert_fusion), channel_id=1, source_target_pairs={{0,1},{1,0},{2,3},{3,2},{4,5},{5,4},{6,7},{7,6},{8,9},{9,8},{10,11... | collective-permute-start | bytes 1671176 | tf_op jit(solution)/shard_map/ppermute | solution.py:57
  47.1 4.3 %collective-permute-start.6 = (bf16[128,256]{1,0:T(8,128)(2,1)S(1)}, bf16[128,256]{1,0:T(8,128)(2,1)S(1)}, u32[]{:S(2)}, u32[]{:S(2)}) collective-permute-start(bf16[128,256]{1,0:T(8,128)(2,1)S(1)} %maximum_select_fusion.4), channel_id=1, source_target_pairs={{0,8},{2,10},{4,12},{6,14},{8,0},{10,2},{12,4},{14,6},{16,24},{18,... | collective-permute-start | bytes 196616 | tf_op jit(solution)/shard_map/ppermute | solution.py:57
  57.0 5.0 %collective-permute-start.8 = (bf16[256,256]{1,0:T(8,128)(2,1)S(1)}, bf16[256,256]{1,0:T(8,128)(2,1)S(1)}, u32[]{:S(2)}, u32[]{:S(2)}) collective-permute-start(bf16[256,256]{1,0:T(8,128)(2,1)S(1)} %maximum_select_fusion.3), channel_id=1, source_target_pairs={{0,4},{2,6},{4,0},{6,2},{8,12},{10,14},{12,8},{14,10},{16,20},{18,... | collective-permute-start | bytes 393224 | tf_op jit(solution)/shard_map/ppermute | solution.py:57
  62.2 1.8 %collective-permute-start.9 = (bf16[512,256]{1,0:T(8,128)(2,1)S(1)}, bf16[512,256]{1,0:T(8,128)(2,1)S(1)}, u32[]{:S(2)}, u32[]{:S(2)}) collective-permute-start(bf16[512,256]{1,0:T(8,128)(2,1)S(1)} %maximum_select_fusion.2), channel_id=1, source_target_pairs={{0,2},{2,0},{4,6},{6,4},{8,10},{10,8},{12,14},{14,12},{16,18},{18,... | collective-permute-start | bytes 786440 | tf_op jit(solution)/shard_map/ppermute | solution.py:57

commit v14 on v13

--- a/solution.py
+++ b/solution.py
@@ -82,7 +82,8 @@
         [joint_part], "loop", loop_count, loop_position
     )
     group_steps = group_count.bit_length() - 1
-    first_bits = list(range(min(2, group_steps)))
+    group_bits = [bit for bit in range(group_steps) if bit != 1] + [1][: group_steps > 1]
+    first_bits = group_bits[:2]
     first_rows = item_part.shape[0] >> len(first_bits)
 
     def group_first(item_part):
@@ -98,7 +99,7 @@
         item_part,
     )
     (item_share,), (item_offset,) = halving_scatter(
-        [first_share], "group", group_count, group_position, range(len(first_bits), group_steps)
+        [first_share], "group", group_count, group_position, group_bits[2:]
     )
     item_offset = first_offset + item_offset
     fresh_items = advance(
@@ -106,7 +107,7 @@
         item_share,
         step_items,
     )
-    gather_bits = list(reversed(range(group_steps)))
+    gather_bits = list(reversed(group_bits))
     (partly,) = doubling_gather(
         [fresh_items], "group", group_count, group_position, gather_bits[:1]
     )

time: 65.3 us -> 67.6 us (1.035)
  waiting for transfers between devices: 28.2 us -> 33.2 us
  starting transfers between devices: 16.5 us -> 13.8 us
    ppermute x5, starting transfers between devices: 7.59 us -> 4.93 us  [doubling_gather(): got = lax.ppermute(tuple(parts), axis, xor_pairs(count, bit))]
    ppermute x5, waiting for transfers between devices: 14.9 us -> 17.5 us  [halving_scatter(): got = lax.ppermute(tuple(sent), axis, xor_pairs(count, bit))]
    ppermute x5, waiting for transfers between devices: 13.2 us -> 15.7 us  [doubling_gather(): got = lax.ppermute(tuple(parts), axis, xor_pairs(count, bit))]
where the time goes in v14:
time: 67.6 us; the launch traced here: 67.3 us
  waiting for transfers between devices  33.2 us (49%)
  starting transfers between devices  13.8 us (20%)
  local copies, waits for them, and re-layouts  6.74 us (10%)
  other arithmetic  6.34 us (9%)
  matrix products  6.33 us (9%)
  between operations  0.82 us (1%)
    ppermute x5, waiting for transfers between devices, halving_scatter(): got = lax.ppermute(tuple(sent), axis, xor_pairs(count, bit))  17.5 us
    ppermute x5, waiting for transfers between devices, doubling_gather(): got = lax.ppermute(tuple(parts), axis, xor_pairs(count, bit))  15.7 us
    ppermute x5, starting transfers between devices, halving_scatter(): got = lax.ppermute(tuple(sent), axis, xor_pairs(count, bit))  8.9 us
    ppermute x5, starting transfers between devices, doubling_gather(): got = lax.ppermute(tuple(parts), axis, xor_pairs(count, bit))  4.93 us
    add x4, other arithmetic, halving_scatter(): parts = [k + g for k, g in zip(kept, got)]  3.66 us
    dot_general x2, matrix products, residual_of(): lax.dot_general(row_factors, column_factors, (((1,), (1,)), ((), ())), pr...  2.26 us
    dynamic_slice x5, local copies, waits for them, and re-layouts, halving_scatter(): lax.dynamic_slice_in_dim(p, (1 - side) * h, h, 0)  2.23 us
    unnamed x14, local copies, waits for them, and re-layouts  2.09 us
  transfers between devices with their start and end apart: 10, of which 8 were waited for; matrix products, arithmetic and copies ran while one was open for 8% of the time, Pallas kernels for 0%

profile of v14, /device:TPU:0, one launch (start us, length us, event | category | flops | bytes accessed | tf_op | source)
XLA Modules:
  0.0 67.3 jit_solution(1791669561307500880)
XLA Ops:
  2.8 1.3 %copy-done.3 = bf16[2048,1024]{1,0:T(8,128)(2,1)S(1)} copy-done((bf16[2048,1024]{1,0:T(8,128)(2,1)S(1)}, bf16[2048,1024]{1,0:T(8,128)(2,1)}, u32[]{:S(2)}) %copy-start.3) | copy-done | bytes 4194328
  4.1 2.0 %fusion = bf16[2048,1024]{1,0:T(8,128)(2,1)S(1)} fusion(f32[256,8,8,128]{3,2,1,0:T(8,128)S(1)} %bitcast.22, bf16[2048,1024]{1,0:T(8,128)(2,1)S(1)} %copy-done.3, bf16[2048,256]{1,0:T(8,128)(2,1)S(1)} %copy-done.1, bf16[1024,256]{1,0:T(8,128)(2,1)S(1)} %copy-done), kind=kOutput, calls=%fused_computation.5 | convolution fusion | flops 1082130432 | bytes 18350080 | tf_op jit(solution)/shard_map/dot_general | solution.py:19
  6.0 1.3 %fusion.4 = f32[2048,256]{1,0:T(8,128)S(1)} fusion(bf16[2048,1024]{1,0:T(8,128)(2,1)S(1)} %fusion, bf16[1024,256]{1,0:T(8,128)(2,1)S(1)} %copy-done), kind=kOutput, calls=%fused_computation.28 | convolution fusion | flops 1073741824 | bytes 6815744 | tf_op jit(solution)/shard_map/dot_general | solution.py:73
  7.4 1.3 %fusion.6 = f32[1024,256]{1,0:T(8,128)S(1)} fusion(bf16[2048,1024]{1,0:T(8,128)(2,1)S(1)} %fusion, bf16[2048,256]{1,0:T(8,128)(2,1)S(1)} %copy-done.1), kind=kOutput, calls=%fused_computation.30 | convolution fusion | flops 1073741824 | bytes 6291456 | tf_op jit(solution)/shard_map/dot_general | solution.py:26
  9.3 1.2 %convolution_add_fusion = f32[1024,256]{1,0:T(8,128)} fusion(f32[1024,256]{1,0:T(8,128)S(1)} %fusion.6, bf16[1024,128]{1,0:T(8,128)(2,1)S(1)} %fusion.2, bf16[128,256]{1,0:T(8,128)(2,1)S(1)} %copy-done.4), kind=kOutput, calls=%fused_computation.7 | convolution fusion | flops 67371008 | bytes 2424832 | tf_op jit(solution)/shard_map/dot_general | solution.py:77
  10.7 1.1 %constant_dynamic-slice_fusion.2 = f32[1088,256]{1,0:T(8,128)} fusion(f32[2176,256]{1,0:T(8,128)S(1)} %pad_maximum_fusion, s32[]{:T(128)S(6)} %select_n.85), kind=kLoop, calls=%fused_computation.23 | loop fusion | bytes 2228228 | tf_op jit(solution)/shard_map/dynamic_slice | solution.py:46
  11.8 3.0 %collective-permute-start.5 = (f32[1088,256]{1,0:T(8,128)}, f32[1088,256]{1,0:T(8,128)}, u32[]{:S(2)}, u32[]{:S(2)}) collective-permute-start(f32[1088,256]{1,0:T(8,128)} %constant_dynamic-slice_fusion.2), channel_id=1, source_target_pairs={{0,1},{1,0},{2,3},{3,2},{4,5},{5,4},{6,7},{7,6},{8,9},{9,8},{10,11... | collective-permute-start | bytes 3342344 | tf_op jit(solution)/shard_map/ppermute | solution.py:47
  14.8 14.0 %conditional.1 = (f32[256,256]{1,0:T(8,128)S(1)}, s32[]{:T(128)}) conditional(s32[]{:T(128)} %convert_element_type.33, () %tuple.19, (s32[]{:T(128)}, f32[1024,256]{1,0:T(8,128)}) %tuple.21), branch_computations={%region_0.0_spmd, %region_1.0_spmd} | conditional | flops 196631 | bytes 7078268 | solution.py:95
  16.0 2.0 %collective-permute-done = f32[512,256]{1,0:T(8,128)} collective-permute-done((f32[512,256]{1,0:T(8,128)S(1)}, f32[512,256]{1,0:T(8,128)}, u32[]{:S(2)}, u32[]{:S(2)}) %collective-permute-start) | collective-permute-done | bytes 524320 | tf_op jit(solution)/shard_map/cond/branch_1_fun/ppermute | solution.py:47
  18.0 1.3 %dynamic-slice_add_fusion = f32[512,256]{1,0:T(8,128)S(1)} fusion(f32[512,256]{1,0:T(8,128)} %collective-permute-done, f32[1024,256]{1,0:T(8,128)} %get-tuple-element.4, s32[]{:T(128)S(6)} %select_n.55), kind=kLoop, calls=%fused_computation | loop fusion | flops 131072 | bytes 1572868 | tf_op jit(solution)/shard_map/cond/branch_1_fun/add | solution.py:48
  19.3 1.6 %collective-permute-start.1 = (f32[256,256]{1,0:T(8,128)S(1)}, f32[256,256]{1,0:T(8,128)}, u32[]{:S(2)}, u32[]{:S(2)}) collective-permute-start(f32[256,256]{1,0:T(8,128)S(1)} %constant_dynamic-slice_fusion), channel_id=1, source_target_pairs={{0,8},{2,10},{4,12},{6,14},{8,0},{10,2},{12,4},{14,6},{16,24},{18,... | collective-permute-start | bytes 786440 | tf_op jit(solution)/shard_map/cond/branch_1_fun/ppermute | solution.py:47
  20.9 6.9 %collective-permute-done.1 = f32[256,256]{1,0:T(8,128)} collective-permute-done((f32[256,256]{1,0:T(8,128)S(1)}, f32[256,256]{1,0:T(8,128)}, u32[]{:S(2)}, u32[]{:S(2)}) %collective-permute-start.1) | collective-permute-done | bytes 262176 | tf_op jit(solution)/shard_map/cond/branch_1_fun/ppermute | solution.py:47
  28.8 2.7 %collective-permute-start.2 = (f32[128,256]{1,0:T(8,128)S(1)}, f32[128,256]{1,0:T(8,128)S(1)}, u32[]{:S(2)}, u32[]{:S(2)}) collective-permute-start(f32[128,256]{1,0:T(8,128)S(1)} %constant_dynamic-slice_fusion.4), channel_id=1, source_target_pairs={{0,16},{2,18},{4,20},{6,22},{8,24},{10,26},{12,28},{14,30},{16,0},... | collective-permute-start | bytes 393224 | tf_op jit(solution)/shard_map/ppermute | solution.py:47
  31.5 5.8 %collective-permute-done.2 = f32[128,256]{1,0:T(8,128)S(1)} collective-permute-done((f32[128,256]{1,0:T(8,128)S(1)}, f32[128,256]{1,0:T(8,128)S(1)}, u32[]{:S(2)}, u32[]{:S(2)}) %collective-permute-start.2) | collective-permute-done | bytes 131104 | tf_op jit(solution)/shard_map/ppermute | solution.py:47
  37.4 1.6 %collective-permute-start.3 = (f32[64,256]{1,0:T(8,128)S(1)}, f32[64,256]{1,0:T(8,128)S(1)}, u32[]{:S(2)}, u32[]{:S(2)}) collective-permute-start(f32[64,256]{1,0:T(8,128)S(1)} %constant_dynamic-slice_fusion.3), channel_id=1, source_target_pairs={{0,4},{2,6},{4,0},{6,2},{8,12},{10,14},{12,8},{14,10},{16,20},{18,... | collective-permute-start | bytes 196616 | tf_op jit(solution)/shard_map/ppermute | solution.py:47
  38.9 2.8 %collective-permute-done.3 = f32[64,256]{1,0:T(8,128)S(1)} collective-permute-done((f32[64,256]{1,0:T(8,128)S(1)}, f32[64,256]{1,0:T(8,128)S(1)}, u32[]{:S(2)}, u32[]{:S(2)}) %collective-permute-start.3) | collective-permute-done | bytes 65568 | tf_op jit(solution)/shard_map/ppermute | solution.py:47
  41.7 1.6 %collective-permute-start.4 = (bf16[64,256]{1,0:T(8,128)(2,1)S(1)}, bf16[64,256]{1,0:T(8,128)(2,1)S(1)}, u32[]{:S(2)}, u32[]{:S(2)}) collective-permute-start(bf16[64,256]{1,0:T(8,128)(2,1)S(1)} %add_convert_fusion.1), channel_id=1, source_target_pairs={{0,4},{2,6},{4,0},{6,2},{8,12},{10,14},{12,8},{14,10},{16,20},{18,... | collective-permute-start | bytes 98312 | tf_op jit(solution)/shard_map/ppermute | solution.py:57
  43.3 2.4 %collective-permute-done.4 = bf16[64,256]{1,0:T(8,128)(2,1)S(1)} collective-permute-done((bf16[64,256]{1,0:T(8,128)(2,1)S(1)}, bf16[64,256]{1,0:T(8,128)(2,1)S(1)}, u32[]{:S(2)}, u32[]{:S(2)}) %collective-permute-start.4) | collective-permute-done | bytes 32800 | tf_op jit(solution)/shard_map/ppermute | solution.py:57
  45.7 1.4 %dynamic-slice_add_fusion.2 = f32[1088,256]{1,0:T(8,128)S(1)} fusion(f32[1088,256]{1,0:T(8,128)} %collective-permute-done.5, f32[2176,256]{1,0:T(8,128)S(1)} %pad_maximum_fusion, s32[]{:T(128)S(6)} %select_n.84), kind=kLoop, calls=%fused_computation.15 | loop fusion | flops 278528 | bytes 3342340 | tf_op jit(solution)/shard_map/add | solution.py:48
  47.5 1.6 %collective-permute-start.7 = (bf16[1088,256]{1,0:T(8,128)(2,1)S(1)}, bf16[1088,256]{1,0:T(8,128)(2,1)S(1)}, u32[]{:S(2)}, u32[]{:S(2)}) collective-permute-start(bf16[1088,256]{1,0:T(8,128)(2,1)S(1)} %add_convert_fusion), channel_id=1, source_target_pairs={{0,1},{1,0},{2,3},{3,2},{4,5},{5,4},{6,7},{7,6},{8,9},{9,8},{10,11... | collective-permute-start | bytes 1671176 | tf_op jit(solution)/shard_map/ppermute | solution.py:57
  49.1 5.9 %collective-permute-done.6 = bf16[128,256]{1,0:T(8,128)(2,1)S(1)} collective-permute-done((bf16[128,256]{1,0:T(8,128)(2,1)S(1)}, bf16[128,256]{1,0:T(8,128)(2,1)S(1)}, u32[]{:S(2)}, u32[]{:S(2)}) %collective-permute-start.6) | collective-permute-done | bytes 65568 | tf_op jit(solution)/shard_map/ppermute | solution.py:57
  55.0 4.1 %collective-permute-done.7 = bf16[1088,256]{1,0:T(8,128)(2,1)S(1)} collective-permute-done((bf16[1088,256]{1,0:T(8,128)(2,1)S(1)}, bf16[1088,256]{1,0:T(8,128)(2,1)S(1)}, u32[]{:S(2)}, u32[]{:S(2)}) %collective-permute-start.7) | collective-permute-done | bytes 557088 | tf_op jit(solution)/shard_map/ppermute | solution.py:57
  59.4 1.7 %collective-permute-start.8 = (bf16[256,256]{1,0:T(8,128)(2,1)S(1)}, bf16[256,256]{1,0:T(8,128)(2,1)S(1)}, u32[]{:S(2)}, u32[]{:S(2)}) collective-permute-start(bf16[256,256]{1,0:T(8,128)(2,1)S(1)} %maximum_select_fusion.3), channel_id=1, source_target_pairs={{0,8},{2,10},{4,12},{6,14},{8,0},{10,2},{12,4},{14,6},{16,24},{18,... | collective-permute-start | bytes 393224 | tf_op jit(solution)/shard_map/ppermute | solution.py:57
  61.1 3.3 %collective-permute-done.8 = bf16[256,256]{1,0:T(8,128)(2,1)S(1)} collective-permute-done((bf16[256,256]{1,0:T(8,128)(2,1)S(1)}, bf16[256,256]{1,0:T(8,128)(2,1)S(1)}, u32[]{:S(2)}, u32[]{:S(2)}) %collective-permute-start.8) | collective-permute-done | bytes 131104 | tf_op jit(solution)/shard_map/ppermute | solution.py:57
  (41 shorter events, 8.8 us)
Async XLA Ops:
  1.4 1.0 %copy-start = (bf16[1024,256]{1,0:T(8,128)(2,1)S(1)}, bf16[1024,256]{1,0:T(8,128)(2,1)}, u32[]{:S(2)}) copy-start(bf16[1024,256]{1,0:T(8,128)(2,1)} %param.10) | copy-start | bytes 1572868
  1.4 1.4 %copy-start.1 = (bf16[2048,256]{1,0:T(8,128)(2,1)S(1)}, bf16[2048,256]{1,0:T(8,128)(2,1)}, u32[]{:S(2)}) copy-start(bf16[2048,256]{1,0:T(8,128)(2,1)} %param.9) | copy-start | bytes 3145732
  1.4 2.7 %copy-start.3 = (bf16[2048,1024]{1,0:T(8,128)(2,1)S(1)}, bf16[2048,1024]{1,0:T(8,128)(2,1)}, u32[]{:S(2)}) copy-start(bf16[2048,1024]{1,0:T(8,128)(2,1)} %param.12) | copy-start | bytes 12582916
  7.3 1.3 %copy-start.6 = (s32[8,1]{0,1:T(1,128)S(1)}, s32[8,1]{0,1:T(1,128)}, u32[]{:S(2)}) copy-start(s32[8,1]{0,1:T(1,128)} %param.15) | copy-start | bytes 100
  7.3 1.4 %copy-start.4 = (bf16[128,256]{1,0:T(8,128)(2,1)S(1)}, bf16[128,256]{1,0:T(8,128)(2,1)}, u32[]{:S(2)}) copy-start(bf16[128,256]{1,0:T(8,128)(2,1)} %param.11) | copy-start | bytes 196612
  7.3 1.4 %copy-start.5 = (bf16[1024,128]{1,0:T(8,128)(2,1)S(1)}, bf16[1024,128]{1,0:T(8,128)(2,1)}, u32[]{:S(2)}) copy-start(bf16[1024,128]{1,0:T(8,128)(2,1)} %param.14) | copy-start | bytes 786436
  11.8 33.9 %collective-permute-start.5 = (f32[1088,256]{1,0:T(8,128)}, f32[1088,256]{1,0:T(8,128)}, u32[]{:S(2)}, u32[]{:S(2)}) collective-permute-start(f32[1088,256]{1,0:T(8,128)} %constant_dynamic-slice_fusion.2), channel_id=1, source_target_pairs={{0,1},{1,0},{2,3},{3,2},{4,5},{5,4},{6,7},{7,6},{8,9},{9,8},{10,11... | collective-permute-start | bytes 3342344 | tf_op jit(solution)/shard_map/ppermute | solution.py:47
  15.9 2.1 %collective-permute-start = (f32[512,256]{1,0:T(8,128)S(1)}, f32[512,256]{1,0:T(8,128)}, u32[]{:S(2)}, u32[]{:S(2)}) collective-permute-start(f32[512,256]{1,0:T(8,128)S(1)} %constant_dynamic-slice_fusion.1), channel_id=1, source_target_pairs={{0,2},{2,0},{4,6},{6,4},{8,10},{10,8},{12,14},{14,12},{16,18},{18,... | collective-permute-start | bytes 1572872 | tf_op jit(solution)/shard_map/cond/branch_1_fun/ppermute | solution.py:47
  19.3 8.5 %collective-permute-start.1 = (f32[256,256]{1,0:T(8,128)S(1)}, f32[256,256]{1,0:T(8,128)}, u32[]{:S(2)}, u32[]{:S(2)}) collective-permute-start(f32[256,256]{1,0:T(8,128)S(1)} %constant_dynamic-slice_fusion), channel_id=1, source_target_pairs={{0,8},{2,10},{4,12},{6,14},{8,0},{10,2},{12,4},{14,6},{16,24},{18,... | collective-permute-start | bytes 786440 | tf_op jit(solution)/shard_map/cond/branch_1_fun/ppermute | solution.py:47
  28.8 8.5 %collective-permute-start.2 = (f32[128,256]{1,0:T(8,128)S(1)}, f32[128,256]{1,0:T(8,128)S(1)}, u32[]{:S(2)}, u32[]{:S(2)}) collective-permute-start(f32[128,256]{1,0:T(8,128)S(1)} %constant_dynamic-slice_fusion.4), channel_id=1, source_target_pairs={{0,16},{2,18},{4,20},{6,22},{8,24},{10,26},{12,28},{14,30},{16,0},... | collective-permute-start | bytes 393224 | tf_op jit(solution)/shard_map/ppermute | solution.py:47
  37.4 4.3 %collective-permute-start.3 = (f32[64,256]{1,0:T(8,128)S(1)}, f32[64,256]{1,0:T(8,128)S(1)}, u32[]{:S(2)}, u32[]{:S(2)}) collective-permute-start(f32[64,256]{1,0:T(8,128)S(1)} %constant_dynamic-slice_fusion.3), channel_id=1, source_target_pairs={{0,4},{2,6},{4,0},{6,2},{8,12},{10,14},{12,8},{14,10},{16,20},{18,... | collective-permute-start | bytes 196616 | tf_op jit(solution)/shard_map/ppermute | solution.py:47
  41.7 5.4 %copy-start.2 = (bf16[2048,256]{1,0:T(8,128)(2,1)S(1)}, bf16[2048,256]{1,0:T(8,128)(2,1)}, u32[]{:S(2)}) copy-start(bf16[2048,256]{1,0:T(8,128)(2,1)} %param.9) | copy-start | bytes 3145732
  41.7 4.0 %collective-permute-start.4 = (bf16[64,256]{1,0:T(8,128)(2,1)S(1)}, bf16[64,256]{1,0:T(8,128)(2,1)S(1)}, u32[]{:S(2)}, u32[]{:S(2)}) collective-permute-start(bf16[64,256]{1,0:T(8,128)(2,1)S(1)} %add_convert_fusion.1), channel_id=1, source_target_pairs={{0,4},{2,6},{4,0},{6,2},{8,12},{10,14},{12,8},{14,10},{16,20},{18,... | collective-permute-start | bytes 98312 | tf_op jit(solution)/shard_map/ppermute | solution.py:57
  47.5 11.6 %collective-permute-start.7 = (bf16[1088,256]{1,0:T(8,128)(2,1)S(1)}, bf16[1088,256]{1,0:T(8,128)(2,1)S(1)}, u32[]{:S(2)}, u32[]{:S(2)}) collective-permute-start(bf16[1088,256]{1,0:T(8,128)(2,1)S(1)} %add_convert_fusion), channel_id=1, source_target_pairs={{0,1},{1,0},{2,3},{3,2},{4,5},{5,4},{6,7},{7,6},{8,9},{9,8},{10,11... | collective-permute-start | bytes 1671176 | tf_op jit(solution)/shard_map/ppermute | solution.py:57
  49.1 5.9 %collective-permute-start.6 = (bf16[128,256]{1,0:T(8,128)(2,1)S(1)}, bf16[128,256]{1,0:T(8,128)(2,1)S(1)}, u32[]{:S(2)}, u32[]{:S(2)}) collective-permute-start(bf16[128,256]{1,0:T(8,128)(2,1)S(1)} %maximum_select_fusion.4), channel_id=1, source_target_pairs={{0,16},{2,18},{4,20},{6,22},{8,24},{10,26},{12,28},{14,30},{16,0},... | collective-permute-start | bytes 196616 | tf_op jit(solution)/shard_map/ppermute | solution.py:57
  59.4 5.0 %collective-permute-start.8 = (bf16[256,256]{1,0:T(8,128)(2,1)S(1)}, bf16[256,256]{1,0:T(8,128)(2,1)S(1)}, u32[]{:S(2)}, u32[]{:S(2)}) collective-permute-start(bf16[256,256]{1,0:T(8,128)(2,1)S(1)} %maximum_select_fusion.3), channel_id=1, source_target_pairs={{0,8},{2,10},{4,12},{6,14},{8,0},{10,2},{12,4},{14,6},{16,24},{18,... | collective-permute-start | bytes 393224 | tf_op jit(solution)/shard_map/ppermute | solution.py:57
  64.5 1.8 %collective-permute-start.9 = (bf16[512,256]{1,0:T(8,128)(2,1)S(1)}, bf16[512,256]{1,0:T(8,128)(2,1)S(1)}, u32[]{:S(2)}, u32[]{:S(2)}) collective-permute-start(bf16[512,256]{1,0:T(8,128)(2,1)S(1)} %maximum_select_fusion.2), channel_id=1, source_target_pairs={{0,2},{2,0},{4,6},{6,4},{8,10},{10,8},{12,14},{14,12},{16,18},{18,... | collective-permute-start | bytes 786440 | tf_op jit(solution)/shard_map/ppermute | solution.py:57

commit v15 on v13

--- a/solution.py
+++ b/solution.py
@@ -125,14 +125,15 @@
     new_users = new_joint[: user_factors.shape[0]]
     new_tags = new_joint[user_factors.shape[0] :]
 
+    partly, _ = lax.optimization_barrier((partly, fresh_joint))
     (partly,) = doubling_gather(
-        [partly], "group", group_count, group_position, gather_bits[1:2]
+        [partly], "group", group_count, group_position, gather_bits[1:-1]
     )
     partly, new_joint = lax.optimization_barrier((partly, new_joint))
     new_users = new_joint[: user_factors.shape[0]]
     new_tags = new_joint[user_factors.shape[0] :]
     (new_items,) = doubling_gather(
-        [partly], "group", group_count, group_position, gather_bits[2:]
+        [partly], "group", group_count, group_position, gather_bits[-1:]
     )
     return (new_users, new_items, new_tags)
 

time: 65.3 us -> 60.1 us (0.920)
  waiting for transfers between devices: 28.2 us -> 22.8 us
    ppermute x5, waiting for transfers between devices: 13.2 us -> 7.91 us  [doubling_gather(): got = lax.ppermute(tuple(parts), axis, xor_pairs(count, bit))]
  transfers between devices with their start and end apart: 10 -> 10, of which waited for: 8 -> 8; matrix products, arithmetic and copies ran while one was open for 8% -> 9% of each run, Pallas kernels for 0% -> 0%
where the time goes in v15:
time: 60.1 us; the launch traced here: 59.8 us
  waiting for transfers between devices  22.8 us (38%)
  starting transfers between devices  16.7 us (28%)
  local copies, waits for them, and re-layouts  6.74 us (11%)
  other arithmetic  6.34 us (11%)
  matrix products  6.33 us (11%)
  between operations  0.82 us (1%)
    ppermute x5, waiting for transfers between devices, halving_scatter(): got = lax.ppermute(tuple(sent), axis, xor_pairs(count, bit))  14.9 us
    ppermute x5, starting transfers between devices, halving_scatter(): got = lax.ppermute(tuple(sent), axis, xor_pairs(count, bit))  8.9 us
    ppermute x5, waiting for transfers between devices, doubling_gather(): got = lax.ppermute(tuple(parts), axis, xor_pairs(count, bit))  7.91 us
    ppermute x5, starting transfers between devices, doubling_gather(): got = lax.ppermute(tuple(parts), axis, xor_pairs(count, bit))  7.79 us
    add x4, other arithmetic, halving_scatter(): parts = [k + g for k, g in zip(kept, got)]  3.66 us
    dot_general x2, matrix products, residual_of(): lax.dot_general(row_factors, column_factors, (((1,), (1,)), ((), ())), pr...  2.26 us
    dynamic_slice x5, local copies, waits for them, and re-layouts, halving_scatter(): lax.dynamic_slice_in_dim(p, (1 - side) * h, h, 0)  2.23 us
    unnamed x14, local copies, waits for them, and re-layouts  2.09 us
  transfers between devices with their start and end apart: 10, of which 8 were waited for; matrix products, arithmetic and copies ran while one was open for 9% of the time, Pallas kernels for 0%

profile of v15, /device:TPU:0, one launch (start us, length us, event | category | flops | bytes accessed | tf_op | source)
XLA Modules:
  0.0 59.8 jit_solution(8365143833848248734)
XLA Ops:
  2.8 1.3 %copy-done.3 = bf16[2048,1024]{1,0:T(8,128)(2,1)S(1)} copy-done((bf16[2048,1024]{1,0:T(8,128)(2,1)S(1)}, bf16[2048,1024]{1,0:T(8,128)(2,1)}, u32[]{:S(2)}) %copy-start.3) | copy-done | bytes 4194328
  4.1 2.0 %fusion = bf16[2048,1024]{1,0:T(8,128)(2,1)S(1)} fusion(f32[256,8,8,128]{3,2,1,0:T(8,128)S(1)} %bitcast.22, bf16[2048,1024]{1,0:T(8,128)(2,1)S(1)} %copy-done.3, bf16[2048,256]{1,0:T(8,128)(2,1)S(1)} %copy-done.1, bf16[1024,256]{1,0:T(8,128)(2,1)S(1)} %copy-done), kind=kOutput, calls=%fused_computation.5 | convolution fusion | flops 1082130432 | bytes 18350080 | tf_op jit(solution)/shard_map/dot_general | solution.py:19
  6.0 1.3 %fusion.4 = f32[2048,256]{1,0:T(8,128)S(1)} fusion(bf16[2048,1024]{1,0:T(8,128)(2,1)S(1)} %fusion, bf16[1024,256]{1,0:T(8,128)(2,1)S(1)} %copy-done), kind=kOutput, calls=%fused_computation.28 | convolution fusion | flops 1073741824 | bytes 6815744 | tf_op jit(solution)/shard_map/dot_general | solution.py:73
  7.4 1.3 %fusion.6 = f32[1024,256]{1,0:T(8,128)S(1)} fusion(bf16[2048,1024]{1,0:T(8,128)(2,1)S(1)} %fusion, bf16[2048,256]{1,0:T(8,128)(2,1)S(1)} %copy-done.1), kind=kOutput, calls=%fused_computation.30 | convolution fusion | flops 1073741824 | bytes 6291456 | tf_op jit(solution)/shard_map/dot_general | solution.py:26
  9.3 1.2 %convolution_add_fusion = f32[1024,256]{1,0:T(8,128)} fusion(f32[1024,256]{1,0:T(8,128)S(1)} %fusion.6, bf16[1024,128]{1,0:T(8,128)(2,1)S(1)} %fusion.2, bf16[128,256]{1,0:T(8,128)(2,1)S(1)} %copy-done.4), kind=kOutput, calls=%fused_computation.7 | convolution fusion | flops 67371008 | bytes 2424832 | tf_op jit(solution)/shard_map/dot_general | solution.py:77
  10.7 1.1 %constant_dynamic-slice_fusion.2 = f32[1088,256]{1,0:T(8,128)} fusion(f32[2176,256]{1,0:T(8,128)S(1)} %pad_maximum_fusion, s32[]{:T(128)S(6)} %select_n.86), kind=kLoop, calls=%fused_computation.23 | loop fusion | bytes 2228228 | tf_op jit(solution)/shard_map/dynamic_slice | solution.py:46
  11.8 3.0 %collective-permute-start.5 = (f32[1088,256]{1,0:T(8,128)}, f32[1088,256]{1,0:T(8,128)}, u32[]{:S(2)}, u32[]{:S(2)}) collective-permute-start(f32[1088,256]{1,0:T(8,128)} %constant_dynamic-slice_fusion.2), channel_id=1, source_target_pairs={{0,1},{1,0},{2,3},{3,2},{4,5},{5,4},{6,7},{7,6},{8,9},{9,8},{10,11... | collective-permute-start | bytes 3342344 | tf_op jit(solution)/shard_map/ppermute | solution.py:47
  14.8 14.0 %conditional.1 = (f32[256,256]{1,0:T(8,128)S(1)}, s32[]{:T(128)}) conditional(s32[]{:T(128)} %convert_element_type.33, () %tuple.20, (s32[]{:T(128)}, f32[1024,256]{1,0:T(8,128)}) %tuple.22), branch_computations={%region_0.0_spmd, %region_1.0_spmd} | conditional | flops 196631 | bytes 7078268 | solution.py:94
  16.0 2.0 %collective-permute-done = f32[512,256]{1,0:T(8,128)} collective-permute-done((f32[512,256]{1,0:T(8,128)S(1)}, f32[512,256]{1,0:T(8,128)}, u32[]{:S(2)}, u32[]{:S(2)}) %collective-permute-start) | collective-permute-done | bytes 524320 | tf_op jit(solution)/shard_map/cond/branch_1_fun/ppermute | solution.py:47
  18.0 1.3 %dynamic-slice_add_fusion = f32[512,256]{1,0:T(8,128)S(1)} fusion(f32[512,256]{1,0:T(8,128)} %collective-permute-done, f32[1024,256]{1,0:T(8,128)} %get-tuple-element.4, s32[]{:T(128)S(6)} %select_n.55), kind=kLoop, calls=%fused_computation | loop fusion | flops 131072 | bytes 1572868 | tf_op jit(solution)/shard_map/cond/branch_1_fun/add | solution.py:48
  19.3 1.6 %collective-permute-start.1 = (f32[256,256]{1,0:T(8,128)S(1)}, f32[256,256]{1,0:T(8,128)}, u32[]{:S(2)}, u32[]{:S(2)}) collective-permute-start(f32[256,256]{1,0:T(8,128)S(1)} %constant_dynamic-slice_fusion), channel_id=1, source_target_pairs={{0,4},{2,6},{4,0},{6,2},{8,12},{10,14},{12,8},{14,10},{16,20},{18,... | collective-permute-start | bytes 786440 | tf_op jit(solution)/shard_map/cond/branch_1_fun/ppermute | solution.py:47
  20.9 7.0 %collective-permute-done.1 = f32[256,256]{1,0:T(8,128)} collective-permute-done((f32[256,256]{1,0:T(8,128)S(1)}, f32[256,256]{1,0:T(8,128)}, u32[]{:S(2)}, u32[]{:S(2)}) %collective-permute-start.1) | collective-permute-done | bytes 262176 | tf_op jit(solution)/shard_map/cond/branch_1_fun/ppermute | solution.py:47
  28.8 1.6 %collective-permute-start.2 = (f32[128,256]{1,0:T(8,128)S(1)}, f32[128,256]{1,0:T(8,128)S(1)}, u32[]{:S(2)}, u32[]{:S(2)}) collective-permute-start(f32[128,256]{1,0:T(8,128)S(1)} %constant_dynamic-slice_fusion.4), channel_id=1, source_target_pairs={{0,8},{2,10},{4,12},{6,14},{8,0},{10,2},{12,4},{14,6},{16,24},{18,... | collective-permute-start | bytes 393224 | tf_op jit(solution)/shard_map/ppermute | solution.py:47
  30.5 3.4 %collective-permute-done.2 = f32[128,256]{1,0:T(8,128)S(1)} collective-permute-done((f32[128,256]{1,0:T(8,128)S(1)}, f32[128,256]{1,0:T(8,128)S(1)}, u32[]{:S(2)}, u32[]{:S(2)}) %collective-permute-start.2) | collective-permute-done | bytes 131104 | tf_op jit(solution)/shard_map/ppermute | solution.py:47
  33.9 2.7 %collective-permute-start.3 = (f32[64,256]{1,0:T(8,128)S(1)}, f32[64,256]{1,0:T(8,128)S(1)}, u32[]{:S(2)}, u32[]{:S(2)}) collective-permute-start(f32[64,256]{1,0:T(8,128)S(1)} %constant_dynamic-slice_fusion.3), channel_id=1, source_target_pairs={{0,16},{2,18},{4,20},{6,22},{8,24},{10,26},{12,28},{14,30},{16,0},... | collective-permute-start | bytes 196616 | tf_op jit(solution)/shard_map/ppermute | solution.py:47
  36.6 2.6 %collective-permute-done.3 = f32[64,256]{1,0:T(8,128)S(1)} collective-permute-done((f32[64,256]{1,0:T(8,128)S(1)}, f32[64,256]{1,0:T(8,128)S(1)}, u32[]{:S(2)}, u32[]{:S(2)}) %collective-permute-start.3) | collective-permute-done | bytes 65568 | tf_op jit(solution)/shard_map/ppermute | solution.py:47
  39.2 2.7 %collective-permute-start.4 = (bf16[64,256]{1,0:T(8,128)(2,1)S(1)}, bf16[64,256]{1,0:T(8,128)(2,1)S(1)}, u32[]{:S(2)}, u32[]{:S(2)}) collective-permute-start(bf16[64,256]{1,0:T(8,128)(2,1)S(1)} %add_convert_fusion.1), channel_id=1, source_target_pairs={{0,16},{2,18},{4,20},{6,22},{8,24},{10,26},{12,28},{14,30},{16,0},... | collective-permute-start | bytes 98312 | tf_op jit(solution)/shard_map/ppermute | solution.py:57
  41.9 2.1 %collective-permute-done.4 = bf16[64,256]{1,0:T(8,128)(2,1)S(1)} collective-permute-done((bf16[64,256]{1,0:T(8,128)(2,1)S(1)}, bf16[64,256]{1,0:T(8,128)(2,1)S(1)}, u32[]{:S(2)}, u32[]{:S(2)}) %collective-permute-start.4) | collective-permute-done | bytes 32800 | tf_op jit(solution)/shard_map/ppermute | solution.py:57
  44.1 1.4 %dynamic-slice_add_fusion.2 = f32[1088,256]{1,0:T(8,128)S(1)} fusion(f32[1088,256]{1,0:T(8,128)} %collective-permute-done.5, f32[2176,256]{1,0:T(8,128)S(1)} %pad_maximum_fusion, s32[]{:T(128)S(6)} %select_n.85), kind=kLoop, calls=%fused_computation.15 | loop fusion | flops 278528 | bytes 3342340 | tf_op jit(solution)/shard_map/add | solution.py:48
  45.9 1.2 %collective-permute-start.8 = (bf16[1088,256]{1,0:T(8,128)(2,1)S(1)}, bf16[1088,256]{1,0:T(8,128)(2,1)S(1)}, u32[]{:S(2)}, u32[]{:S(2)}) collective-permute-start(bf16[1088,256]{1,0:T(8,128)(2,1)S(1)} %add_convert_fusion), channel_id=1, source_target_pairs={{0,1},{1,0},{2,3},{3,2},{4,5},{5,4},{6,7},{7,6},{8,9},{9,8},{10,11... | collective-permute-start | bytes 1671176 | tf_op jit(solution)/shard_map/ppermute | solution.py:57
  47.1 2.0 %collective-permute-start.6 = (bf16[128,256]{1,0:T(8,128)(2,1)S(1)}, bf16[128,256]{1,0:T(8,128)(2,1)S(1)}, u32[]{:S(2)}, u32[]{:S(2)}) collective-permute-start(bf16[128,256]{1,0:T(8,128)(2,1)S(1)} %maximum_select_fusion.4), channel_id=1, source_target_pairs={{0,8},{2,10},{4,12},{6,14},{8,0},{10,2},{12,4},{14,6},{16,24},{18,... | collective-permute-start | bytes 196616 | tf_op jit(solution)/shard_map/ppermute | solution.py:57
  49.1 2.3 %collective-permute-done.6 = bf16[128,256]{1,0:T(8,128)(2,1)S(1)} collective-permute-done((bf16[128,256]{1,0:T(8,128)(2,1)S(1)}, bf16[128,256]{1,0:T(8,128)(2,1)S(1)}, u32[]{:S(2)}, u32[]{:S(2)}) %collective-permute-start.6) | collective-permute-done | bytes 65568 | tf_op jit(solution)/shard_map/ppermute | solution.py:57
  51.4 1.7 %collective-permute-start.7 = (bf16[256,256]{1,0:T(8,128)(2,1)S(1)}, bf16[256,256]{1,0:T(8,128)(2,1)S(1)}, u32[]{:S(2)}, u32[]{:S(2)}) collective-permute-start(bf16[256,256]{1,0:T(8,128)(2,1)S(1)} %maximum_select_fusion.3), channel_id=1, source_target_pairs={{0,4},{2,6},{4,0},{6,2},{8,12},{10,14},{12,8},{14,10},{16,20},{18,... | collective-permute-start | bytes 393224 | tf_op jit(solution)/shard_map/ppermute | solution.py:57
  53.2 3.3 %collective-permute-done.7 = bf16[256,256]{1,0:T(8,128)(2,1)S(1)} collective-permute-done((bf16[256,256]{1,0:T(8,128)(2,1)S(1)}, bf16[256,256]{1,0:T(8,128)(2,1)S(1)}, u32[]{:S(2)}, u32[]{:S(2)}) %collective-permute-start.7) | collective-permute-done | bytes 131104 | tf_op jit(solution)/shard_map/ppermute | solution.py:57
  (41 shorter events, 9.0 us)
Async XLA Ops:
  1.4 1.0 %copy-start = (bf16[1024,256]{1,0:T(8,128)(2,1)S(1)}, bf16[1024,256]{1,0:T(8,128)(2,1)}, u32[]{:S(2)}) copy-start(bf16[1024,256]{1,0:T(8,128)(2,1)} %param.10) | copy-start | bytes 1572868
  1.4 1.4 %copy-start.1 = (bf16[2048,256]{1,0:T(8,128)(2,1)S(1)}, bf16[2048,256]{1,0:T(8,128)(2,1)}, u32[]{:S(2)}) copy-start(bf16[2048,256]{1,0:T(8,128)(2,1)} %param.9) | copy-start | bytes 3145732
  1.4 2.7 %copy-start.3 = (bf16[2048,1024]{1,0:T(8,128)(2,1)S(1)}, bf16[2048,1024]{1,0:T(8,128)(2,1)}, u32[]{:S(2)}) copy-start(bf16[2048,1024]{1,0:T(8,128)(2,1)} %param.12) | copy-start | bytes 12582916
  7.3 1.3 %copy-start.6 = (s32[8,1]{0,1:T(1,128)S(1)}, s32[8,1]{0,1:T(1,128)}, u32[]{:S(2)}) copy-start(s32[8,1]{0,1:T(1,128)} %param.15) | copy-start | bytes 100
  7.3 1.4 %copy-start.4 = (bf16[128,256]{1,0:T(8,128)(2,1)S(1)}, bf16[128,256]{1,0:T(8,128)(2,1)}, u32[]{:S(2)}) copy-start(bf16[128,256]{1,0:T(8,128)(2,1)} %param.11) | copy-start | bytes 196612
  7.3 1.4 %copy-start.5 = (bf16[1024,128]{1,0:T(8,128)(2,1)S(1)}, bf16[1024,128]{1,0:T(8,128)(2,1)}, u32[]{:S(2)}) copy-start(bf16[1024,128]{1,0:T(8,128)(2,1)} %param.14) | copy-start | bytes 786436
  11.8 32.2 %collective-permute-start.5 = (f32[1088,256]{1,0:T(8,128)}, f32[1088,256]{1,0:T(8,128)}, u32[]{:S(2)}, u32[]{:S(2)}) collective-permute-start(f32[1088,256]{1,0:T(8,128)} %constant_dynamic-slice_fusion.2), channel_id=1, source_target_pairs={{0,1},{1,0},{2,3},{3,2},{4,5},{5,4},{6,7},{7,6},{8,9},{9,8},{10,11... | collective-permute-start | bytes 3342344 | tf_op jit(solution)/shard_map/ppermute | solution.py:47
  15.9 2.1 %collective-permute-start = (f32[512,256]{1,0:T(8,128)S(1)}, f32[512,256]{1,0:T(8,128)}, u32[]{:S(2)}, u32[]{:S(2)}) collective-permute-start(f32[512,256]{1,0:T(8,128)S(1)} %constant_dynamic-slice_fusion.1), channel_id=1, source_target_pairs={{0,2},{2,0},{4,6},{6,4},{8,10},{10,8},{12,14},{14,12},{16,18},{18,... | collective-permute-start | bytes 1572872 | tf_op jit(solution)/shard_map/cond/branch_1_fun/ppermute | solution.py:47
  19.3 8.5 %collective-permute-start.1 = (f32[256,256]{1,0:T(8,128)S(1)}, f32[256,256]{1,0:T(8,128)}, u32[]{:S(2)}, u32[]{:S(2)}) collective-permute-start(f32[256,256]{1,0:T(8,128)S(1)} %constant_dynamic-slice_fusion), channel_id=1, source_target_pairs={{0,4},{2,6},{4,0},{6,2},{8,12},{10,14},{12,8},{14,10},{16,20},{18,... | collective-permute-start | bytes 786440 | tf_op jit(solution)/shard_map/cond/branch_1_fun/ppermute | solution.py:47
  28.8 5.0 %collective-permute-start.2 = (f32[128,256]{1,0:T(8,128)S(1)}, f32[128,256]{1,0:T(8,128)S(1)}, u32[]{:S(2)}, u32[]{:S(2)}) collective-permute-start(f32[128,256]{1,0:T(8,128)S(1)} %constant_dynamic-slice_fusion.4), channel_id=1, source_target_pairs={{0,8},{2,10},{4,12},{6,14},{8,0},{10,2},{12,4},{14,6},{16,24},{18,... | collective-permute-start | bytes 393224 | tf_op jit(solution)/shard_map/ppermute | solution.py:47
  33.9 5.2 %collective-permute-start.3 = (f32[64,256]{1,0:T(8,128)S(1)}, f32[64,256]{1,0:T(8,128)S(1)}, u32[]{:S(2)}, u32[]{:S(2)}) collective-permute-start(f32[64,256]{1,0:T(8,128)S(1)} %constant_dynamic-slice_fusion.3), channel_id=1, source_target_pairs={{0,16},{2,18},{4,20},{6,22},{8,24},{10,26},{12,28},{14,30},{16,0},... | collective-permute-start | bytes 196616 | tf_op jit(solution)/shard_map/ppermute | solution.py:47
  39.2 6.3 %copy-start.2 = (bf16[2048,256]{1,0:T(8,128)(2,1)S(1)}, bf16[2048,256]{1,0:T(8,128)(2,1)}, u32[]{:S(2)}) copy-start(bf16[2048,256]{1,0:T(8,128)(2,1)} %param.9) | copy-start | bytes 3145732
  39.2 4.9 %collective-permute-start.4 = (bf16[64,256]{1,0:T(8,128)(2,1)S(1)}, bf16[64,256]{1,0:T(8,128)(2,1)S(1)}, u32[]{:S(2)}, u32[]{:S(2)}) collective-permute-start(bf16[64,256]{1,0:T(8,128)(2,1)S(1)} %add_convert_fusion.1), channel_id=1, source_target_pairs={{0,16},{2,18},{4,20},{6,22},{8,24},{10,26},{12,28},{14,30},{16,0},... | collective-permute-start | bytes 98312 | tf_op jit(solution)/shard_map/ppermute | solution.py:57
  45.9 10.9 %collective-permute-start.8 = (bf16[1088,256]{1,0:T(8,128)(2,1)S(1)}, bf16[1088,256]{1,0:T(8,128)(2,1)S(1)}, u32[]{:S(2)}, u32[]{:S(2)}) collective-permute-start(bf16[1088,256]{1,0:T(8,128)(2,1)S(1)} %add_convert_fusion), channel_id=1, source_target_pairs={{0,1},{1,0},{2,3},{3,2},{4,5},{5,4},{6,7},{7,6},{8,9},{9,8},{10,11... | collective-permute-start | bytes 1671176 | tf_op jit(solution)/shard_map/ppermute | solution.py:57
  47.1 4.3 %collective-permute-start.6 = (bf16[128,256]{1,0:T(8,128)(2,1)S(1)}, bf16[128,256]{1,0:T(8,128)(2,1)S(1)}, u32[]{:S(2)}, u32[]{:S(2)}) collective-permute-start(bf16[128,256]{1,0:T(8,128)(2,1)S(1)} %maximum_select_fusion.4), channel_id=1, source_target_pairs={{0,8},{2,10},{4,12},{6,14},{8,0},{10,2},{12,4},{14,6},{16,24},{18,... | collective-permute-start | bytes 196616 | tf_op jit(solution)/shard_map/ppermute | solution.py:57
  51.4 5.0 %collective-permute-start.7 = (bf16[256,256]{1,0:T(8,128)(2,1)S(1)}, bf16[256,256]{1,0:T(8,128)(2,1)S(1)}, u32[]{:S(2)}, u32[]{:S(2)}) collective-permute-start(bf16[256,256]{1,0:T(8,128)(2,1)S(1)} %maximum_select_fusion.3), channel_id=1, source_target_pairs={{0,4},{2,6},{4,0},{6,2},{8,12},{10,14},{12,8},{14,10},{16,20},{18,... | collective-permute-start | bytes 393224 | tf_op jit(solution)/shard_map/ppermute | solution.py:57
  57.0 1.8 %collective-permute-start.9 = (bf16[512,256]{1,0:T(8,128)(2,1)S(1)}, bf16[512,256]{1,0:T(8,128)(2,1)S(1)}, u32[]{:S(2)}, u32[]{:S(2)}) collective-permute-start(bf16[512,256]{1,0:T(8,128)(2,1)S(1)} %maximum_select_fusion.2), channel_id=1, source_target_pairs={{0,2},{2,0},{4,6},{6,4},{8,10},{10,8},{12,14},{14,12},{16,18},{18,... | collective-permute-start | bytes 786440 | tf_op jit(solution)/shard_map/ppermute | solution.py:57

commit v16 on v15

--- a/solution.py
+++ b/solution.py
@@ -56,7 +56,7 @@
         side = (position >> bit) & 1
         got = lax.ppermute(tuple(parts), axis, xor_pairs(count, bit))
         parts = [
-            jnp.where(side == 0, jnp.concatenate([m, g], 0), jnp.concatenate([g, m], 0))
+            jnp.concatenate([jnp.where(side == 0, m, g), jnp.where(side == 0, g, m)], 0)
             for m, g in zip(parts, got)
         ]
     return parts
@@ -121,17 +121,21 @@
             step_tags,
         ),
     )
-    (new_joint,) = doubling_gather([fresh_joint], "loop", loop_count, loop_position)
-    new_users = new_joint[: user_factors.shape[0]]
-    new_tags = new_joint[user_factors.shape[0] :]
+    if loop_count == 2:
+        other = lax.ppermute(fresh_joint, "loop", [(0, 1), (1, 0)])
+        low = jnp.where(loop_position == 0, fresh_joint, other)
+        high = jnp.where(loop_position == 0, other, fresh_joint)
+        spill = user_factors.shape[0] - low.shape[0]
+        new_joint = (jnp.concatenate([low, high[:spill]], 0), high[spill:])
+    else:
+        (new_joint,) = doubling_gather([fresh_joint], "loop", loop_count, loop_position)
+        new_joint = (new_joint[: user_factors.shape[0]], new_joint[user_factors.shape[0] :])
 
     partly, _ = lax.optimization_barrier((partly, fresh_joint))
     (partly,) = doubling_gather(
         [partly], "group", group_count, group_position, gather_bits[1:-1]
     )
-    partly, new_joint = lax.optimization_barrier((partly, new_joint))
-    new_users = new_joint[: user_factors.shape[0]]
-    new_tags = new_joint[user_factors.shape[0] :]
+    partly, (new_users, new_tags) = lax.optimization_barrier((partly, new_joint))
     (new_items,) = doubling_gather(
         [partly], "group", group_count, group_position, gather_bits[-1:]
     )

time: 60.1 us -> 75.9 us (1.26)
  waiting for transfers between devices: 22.8 us -> 37.3 us
  matrix products: 6.33 us -> 7.68 us
  local copies, waits for them, and re-layouts: 6.74 us -> 5.74 us
    ppermute x5, waiting for transfers between devices: 14.9 us -> 24.9 us  [halving_scatter(): got = lax.ppermute(tuple(sent), axis, xor_pairs(count, bit))]
    ppermute x0 -> x1, waiting for transfers between devices: none -> 4 us  [shards(): other = lax.ppermute(fresh_joint, 'loop', [(0, 1), (1, 0)])]
    ppermute x5 -> x4, starting transfers between devices: 7.79 us -> 5.03 us  [doubling_gather(): got = lax.ppermute(tuple(parts), axis, xor_pairs(count, bit))]
    ppermute x0 -> x1, starting transfers between devices: none -> 2.27 us  [shards(): other = lax.ppermute(fresh_joint, 'loop', [(0, 1), (1, 0)])]
    concatenate x0 -> x5, other arithmetic: none -> 1.9 us  [the longest x1 1.04 us: shards(): new_joint = (jnp.concatenate([low, high[:spill]], 0), high[spill:])]
    dot_general x1, matrix products: 1.28 us -> 2.62 us  [shards(): jnp.dot(rating_errors, item_factors, preferred_element_type=jnp.float32)]
    select_n x5, other arithmetic: 1.42 us -> 0.18 us  [the longest x4 0.11 us: doubling_gather(): jnp.where(side == 0, m, g)]
    slice x2, local copies, waits for them, and re-layouts: 1.67 us -> 0.67 us  [shards(): new_joint = (jnp.concatenate([low, high[:spill]], 0), high[spill:])]
  transfers between devices with their start and end apart: 10 -> 10, of which waited for: 8 -> 10; matrix products, arithmetic and copies ran while one was open for 9% -> 2% of each run, Pallas kernels for 0% -> 0%
where the time goes in v16:
time: 75.9 us; the launch traced here: 75.6 us
  waiting for transfers between devices  37.3 us (49%)
  starting transfers between devices  17 us (22%)
  matrix products  7.68 us (10%)
  other arithmetic  7 us (9%)
  local copies, waits for them, and re-layouts  5.74 us (8%)
  between operations  0.81 us (1%)
    ppermute x5, waiting for transfers between devices, halving_scatter(): got = lax.ppermute(tuple(sent), axis, xor_pairs(count, bit))  24.9 us
    ppermute x5, starting transfers between devices, halving_scatter(): got = lax.ppermute(tuple(sent), axis, xor_pairs(count, bit))  9.67 us
    ppermute x4, waiting for transfers between devices, doubling_gather(): got = lax.ppermute(tuple(parts), axis, xor_pairs(count, bit))  8.47 us
    ppermute x4, starting transfers between devices, doubling_gather(): got = lax.ppermute(tuple(parts), axis, xor_pairs(count, bit))  5.03 us
    ppermute x1, waiting for transfers between devices, shards(): other = lax.ppermute(fresh_joint, 'loop', [(0, 1), (1, 0)])  4 us
    add x4, other arithmetic, halving_scatter(): parts = [k + g for k, g in zip(kept, got)]  3.66 us
    dot_general x1, matrix products, shards(): jnp.dot(rating_errors, item_factors, preferred_element_type=jnp.float32)  2.62 us
    ppermute x1, starting transfers between devices, shards(): other = lax.ppermute(fresh_joint, 'loop', [(0, 1), (1, 0)])  2.27 us
  transfers between devices with their start and end apart: 10, of which 10 were waited for; matrix products, arithmetic and copies ran while one was open for 2% of the time, Pallas kernels for 0%

profile of v16, /device:TPU:0, one launch (start us, length us, event | category | flops | bytes accessed | tf_op | source)
XLA Modules:
  0.0 75.6 jit_solution(16947948285002280593)
XLA Ops:
  2.8 1.3 %copy-done.3 = bf16[2048,1024]{1,0:T(8,128)(2,1)S(1)} copy-done((bf16[2048,1024]{1,0:T(8,128)(2,1)S(1)}, bf16[2048,1024]{1,0:T(8,128)(2,1)}, u32[]{:S(2)}) %copy-start.3) | copy-done | bytes 4194328
  4.1 2.0 %fusion = bf16[2048,1024]{1,0:T(8,128)(2,1)S(1)} fusion(f32[256,8,8,128]{3,2,1,0:T(8,128)S(1)} %bitcast.22, bf16[2048,1024]{1,0:T(8,128)(2,1)S(1)} %copy-done.3, bf16[2048,256]{1,0:T(8,128)(2,1)S(1)} %copy-done.1, bf16[1024,256]{1,0:T(8,128)(2,1)S(1)} %copy-done), kind=kOutput, calls=%fused_computation.5 | convolution fusion | flops 1082130432 | bytes 18350080 | tf_op jit(solution)/shard_map/dot_general | solution.py:19
  6.0 2.6 %fusion.4 = f32[2048,256]{1,0:T(8,128)} fusion(bf16[2048,1024]{1,0:T(8,128)(2,1)S(1)} %fusion, bf16[1024,256]{1,0:T(8,128)(2,1)S(1)} %copy-done), kind=kOutput, calls=%fused_computation.38 | convolution fusion | flops 1073741824 | bytes 6815744 | tf_op jit(solution)/shard_map/dot_general | solution.py:73
  8.7 1.3 %fusion.6 = f32[1024,256]{1,0:T(8,128)S(1)} fusion(bf16[2048,1024]{1,0:T(8,128)(2,1)S(1)} %fusion, bf16[2048,256]{1,0:T(8,128)(2,1)S(1)} %copy-done.1), kind=kOutput, calls=%fused_computation.40 | convolution fusion | flops 1073741824 | bytes 6291456 | tf_op jit(solution)/shard_map/dot_general | solution.py:26
  10.7 1.2 %convolution_add_fusion = f32[1024,256]{1,0:T(8,128)} fusion(f32[1024,256]{1,0:T(8,128)S(1)} %fusion.6, bf16[1024,128]{1,0:T(8,128)(2,1)S(1)} %fusion.2, bf16[128,256]{1,0:T(8,128)(2,1)S(1)} %copy-done.5), kind=kOutput, calls=%fused_computation.7 | convolution fusion | flops 67371008 | bytes 2424832 | tf_op jit(solution)/shard_map/dot_general | solution.py:77
  12.1 15.2 %conditional.1 = (f32[256,256]{1,0:T(8,128)S(1)}, s32[]{:T(128)}) conditional(s32[]{:T(128)} %convert_element_type.33, () %tuple.20, (s32[]{:T(128)}, f32[1024,256]{1,0:T(8,128)}) %tuple.22), branch_computations={%region_0.0_spmd, %region_1.0_spmd} | conditional | flops 196631 | bytes 7078268 | solution.py:94
  13.7 1.7 %collective-permute-done = f32[512,256]{1,0:T(8,128)} collective-permute-done((f32[512,256]{1,0:T(8,128)S(1)}, f32[512,256]{1,0:T(8,128)}, u32[]{:S(2)}, u32[]{:S(2)}) %collective-permute-start) | collective-permute-done | bytes 524320 | tf_op jit(solution)/shard_map/cond/branch_1_fun/ppermute | solution.py:47
  15.3 1.3 %dynamic-slice_add_fusion = f32[512,256]{1,0:T(8,128)S(1)} fusion(f32[512,256]{1,0:T(8,128)} %collective-permute-done, f32[1024,256]{1,0:T(8,128)} %get-tuple-element.4, s32[]{:T(128)S(6)} %select_n.70), kind=kLoop, calls=%fused_computation | loop fusion | flops 131072 | bytes 1572868 | tf_op jit(solution)/shard_map/cond/branch_1_fun/add | solution.py:48
  16.6 2.9 %collective-permute-start.1 = (f32[256,256]{1,0:T(8,128)S(1)}, f32[256,256]{1,0:T(8,128)}, u32[]{:S(2)}, u32[]{:S(2)}) collective-permute-start(f32[256,256]{1,0:T(8,128)S(1)} %constant_dynamic-slice_fusion), channel_id=1, source_target_pairs={{0,4},{2,6},{4,0},{6,2},{8,12},{10,14},{12,8},{14,10},{16,20},{18,... | collective-permute-start | bytes 786440 | tf_op jit(solution)/shard_map/cond/branch_1_fun/ppermute | solution.py:47
  19.6 6.7 %collective-permute-done.1 = f32[256,256]{1,0:T(8,128)} collective-permute-done((f32[256,256]{1,0:T(8,128)S(1)}, f32[256,256]{1,0:T(8,128)}, u32[]{:S(2)}, u32[]{:S(2)}) %collective-permute-start.1) | collective-permute-done | bytes 262176 | tf_op jit(solution)/shard_map/cond/branch_1_fun/ppermute | solution.py:47
  27.3 1.9 %collective-permute-start.2 = (f32[128,256]{1,0:T(8,128)S(1)}, f32[128,256]{1,0:T(8,128)S(1)}, u32[]{:S(2)}, u32[]{:S(2)}) collective-permute-start(f32[128,256]{1,0:T(8,128)S(1)} %constant_dynamic-slice_fusion.4), channel_id=1, source_target_pairs={{0,8},{2,10},{4,12},{6,14},{8,0},{10,2},{12,4},{14,6},{16,24},{18,... | collective-permute-start | bytes 393224 | tf_op jit(solution)/shard_map/ppermute | solution.py:47
  30.3 1.5 %collective-permute-start.5 = (f32[1088,256]{1,0:T(8,128)}, f32[1088,256]{1,0:T(8,128)}, u32[]{:S(2)}, u32[]{:S(2)}) collective-permute-start(f32[1088,256]{1,0:T(8,128)} %constant_dynamic-slice_fusion.2), channel_id=1, source_target_pairs={{0,1},{1,0},{2,3},{3,2},{4,5},{5,4},{6,7},{7,6},{8,9},{9,8},{10,11... | collective-permute-start | bytes 3342344 | tf_op jit(solution)/shard_map/ppermute | solution.py:47
  32.4 2.8 %collective-permute-start.3 = (f32[64,256]{1,0:T(8,128)S(1)}, f32[64,256]{1,0:T(8,128)S(1)}, u32[]{:S(2)}, u32[]{:S(2)}) collective-permute-start(f32[64,256]{1,0:T(8,128)S(1)} %constant_dynamic-slice_fusion.3), channel_id=1, source_target_pairs={{0,16},{2,18},{4,20},{6,22},{8,24},{10,26},{12,28},{14,30},{16,0},... | collective-permute-start | bytes 196616 | tf_op jit(solution)/shard_map/ppermute | solution.py:47
  35.3 2.4 %collective-permute-done.3 = f32[64,256]{1,0:T(8,128)S(1)} collective-permute-done((f32[64,256]{1,0:T(8,128)S(1)}, f32[64,256]{1,0:T(8,128)S(1)}, u32[]{:S(2)}, u32[]{:S(2)}) %collective-permute-start.3) | collective-permute-done | bytes 65568 | tf_op jit(solution)/shard_map/ppermute | solution.py:47
  37.7 2.9 %collective-permute-start.4 = (bf16[64,256]{1,0:T(8,128)(2,1)S(1)}, bf16[64,256]{1,0:T(8,128)(2,1)S(1)}, u32[]{:S(2)}, u32[]{:S(2)}) collective-permute-start(bf16[64,256]{1,0:T(8,128)(2,1)S(1)} %add_convert_fusion.1), channel_id=1, source_target_pairs={{0,16},{2,18},{4,20},{6,22},{8,24},{10,26},{12,28},{14,30},{16,0},... | collective-permute-start | bytes 98312 | tf_op jit(solution)/shard_map/ppermute | solution.py:57
  40.6 2.0 %collective-permute-done.4 = bf16[64,256]{1,0:T(8,128)(2,1)S(1)} collective-permute-done((bf16[64,256]{1,0:T(8,128)(2,1)S(1)}, bf16[64,256]{1,0:T(8,128)(2,1)S(1)}, u32[]{:S(2)}, u32[]{:S(2)}) %collective-permute-start.4) | collective-permute-done | bytes 32800 | tf_op jit(solution)/shard_map/ppermute | solution.py:57
  42.6 13.5 %collective-permute-done.5 = f32[1088,256]{1,0:T(8,128)} collective-permute-done((f32[1088,256]{1,0:T(8,128)}, f32[1088,256]{1,0:T(8,128)}, u32[]{:S(2)}, u32[]{:S(2)}) %collective-permute-start.5) | collective-permute-done | bytes 1114144 | tf_op jit(solution)/shard_map/ppermute | solution.py:47
  56.1 1.4 %dynamic-slice_add_fusion.2 = f32[1088,256]{1,0:T(8,128)S(1)} fusion(f32[1088,256]{1,0:T(8,128)} %collective-permute-done.5, f32[2176,256]{1,0:T(8,128)S(1)} %pad_maximum_fusion, s32[]{:T(128)S(6)} %select_n.106), kind=kLoop, calls=%fused_computation.14 | loop fusion | flops 278528 | bytes 3342340 | tf_op jit(solution)/shard_map/add | solution.py:48
  58.5 2.3 %collective-permute-start.8 = (bf16[1088,256]{1,0:T(8,128)(2,1)S(1)}, bf16[1088,256]{1,0:T(8,128)(2,1)S(1)}, u32[]{:S(2)}, u32[]{:S(2)}) collective-permute-start(bf16[1088,256]{1,0:T(8,128)(2,1)S(1)} %add_convert_fusion), channel_id=1, source_target_pairs={{0,1},{1,0},{2,3},{3,2},{4,5},{5,4},{6,7},{7,6},{8,9},{9,8},{10,11... | collective-permute-start | bytes 1671176 | tf_op jit(solution)/shard_map/ppermute | solution.py:125
  60.8 1.5 %collective-permute-done.6 = bf16[128,256]{1,0:T(8,128)(2,1)S(1)} collective-permute-done((bf16[128,256]{1,0:T(8,128)(2,1)S(1)}, bf16[128,256]{1,0:T(8,128)(2,1)S(1)}, u32[]{:S(2)}, u32[]{:S(2)}) %collective-permute-start.6) | collective-permute-done | bytes 65568 | tf_op jit(solution)/shard_map/ppermute | solution.py:57
  62.3 1.6 %collective-permute-start.7 = (bf16[256,256]{1,0:T(8,128)(2,1)S(1)}, bf16[256,256]{1,0:T(8,128)(2,1)S(1)}, u32[]{:S(2)}, u32[]{:S(2)}) collective-permute-start(bf16[256,256]{1,0:T(8,128)(2,1)S(1)} %pad_maximum_fusion.4), channel_id=1, source_target_pairs={{0,4},{2,6},{4,0},{6,2},{8,12},{10,14},{12,8},{14,10},{16,20},{18,... | collective-permute-start | bytes 393224 | tf_op jit(solution)/shard_map/ppermute | solution.py:57
  63.8 3.5 %collective-permute-done.7 = bf16[256,256]{1,0:T(8,128)(2,1)S(1)} collective-permute-done((bf16[256,256]{1,0:T(8,128)(2,1)S(1)}, bf16[256,256]{1,0:T(8,128)(2,1)S(1)}, u32[]{:S(2)}, u32[]{:S(2)}) %collective-permute-start.7) | collective-permute-done | bytes 131104 | tf_op jit(solution)/shard_map/ppermute | solution.py:57
  67.4 4.0 %collective-permute-done.8 = bf16[1088,256]{1,0:T(8,128)(2,1)S(1)} collective-permute-done((bf16[1088,256]{1,0:T(8,128)(2,1)S(1)}, bf16[1088,256]{1,0:T(8,128)(2,1)S(1)}, u32[]{:S(2)}, u32[]{:S(2)}) %collective-permute-start.8) | collective-permute-done | bytes 557088 | tf_op jit(solution)/shard_map/ppermute | solution.py:125
  73.2 1.5 %collective-permute-done.9 = bf16[512,256]{1,0:T(8,128)(2,1)S(1)} collective-permute-done((bf16[512,256]{1,0:T(8,128)(2,1)S(1)}, bf16[512,256]{1,0:T(8,128)(2,1)S(1)}, u32[]{:S(2)}, u32[]{:S(2)}) %collective-permute-start.9) | collective-permute-done | bytes 262176 | tf_op jit(solution)/shard_map/ppermute | solution.py:57
  (48 shorter events, 11.1 us)
Async XLA Ops:
  1.4 1.0 %copy-start = (bf16[1024,256]{1,0:T(8,128)(2,1)S(1)}, bf16[1024,256]{1,0:T(8,128)(2,1)}, u32[]{:S(2)}) copy-start(bf16[1024,256]{1,0:T(8,128)(2,1)} %param.10) | copy-start | bytes 1572868
  1.4 1.4 %copy-start.1 = (bf16[2048,256]{1,0:T(8,128)(2,1)S(1)}, bf16[2048,256]{1,0:T(8,128)(2,1)}, u32[]{:S(2)}) copy-start(bf16[2048,256]{1,0:T(8,128)(2,1)} %param.9) | copy-start | bytes 3145732
  1.4 2.7 %copy-start.3 = (bf16[2048,1024]{1,0:T(8,128)(2,1)S(1)}, bf16[2048,1024]{1,0:T(8,128)(2,1)}, u32[]{:S(2)}) copy-start(bf16[2048,1024]{1,0:T(8,128)(2,1)} %param.12) | copy-start | bytes 12582916
  8.7 1.3 %copy-start.7 = (s32[8,1]{0,1:T(1,128)S(1)}, s32[8,1]{0,1:T(1,128)}, u32[]{:S(2)}) copy-start(s32[8,1]{0,1:T(1,128)} %param.15) | copy-start | bytes 100
  8.7 1.4 %copy-start.5 = (bf16[128,256]{1,0:T(8,128)(2,1)S(1)}, bf16[128,256]{1,0:T(8,128)(2,1)}, u32[]{:S(2)}) copy-start(bf16[128,256]{1,0:T(8,128)(2,1)} %param.11) | copy-start | bytes 196612
  8.7 1.4 %copy-start.6 = (bf16[1024,128]{1,0:T(8,128)(2,1)S(1)}, bf16[1024,128]{1,0:T(8,128)(2,1)}, u32[]{:S(2)}) copy-start(bf16[1024,128]{1,0:T(8,128)(2,1)} %param.14) | copy-start | bytes 786436
  10.1 1.9 %copy-start.4 = (f32[2048,256]{1,0:T(8,128)S(1)}, f32[2048,256]{1,0:T(8,128)}, u32[]{:S(2)}) copy-start(f32[2048,256]{1,0:T(8,128)} %fusion.4) | copy-start | bytes 6291460
  13.2 2.2 %collective-permute-start = (f32[512,256]{1,0:T(8,128)S(1)}, f32[512,256]{1,0:T(8,128)}, u32[]{:S(2)}, u32[]{:S(2)}) collective-permute-start(f32[512,256]{1,0:T(8,128)S(1)} %constant_dynamic-slice_fusion.1), channel_id=1, source_target_pairs={{0,2},{2,0},{4,6},{6,4},{8,10},{10,8},{12,14},{14,12},{16,18},{18,... | collective-permute-start | bytes 1572872 | tf_op jit(solution)/shard_map/cond/branch_1_fun/ppermute | solution.py:47
  16.6 9.7 %collective-permute-start.1 = (f32[256,256]{1,0:T(8,128)S(1)}, f32[256,256]{1,0:T(8,128)}, u32[]{:S(2)}, u32[]{:S(2)}) collective-permute-start(f32[256,256]{1,0:T(8,128)S(1)} %constant_dynamic-slice_fusion), channel_id=1, source_target_pairs={{0,4},{2,6},{4,0},{6,2},{8,12},{10,14},{12,8},{14,10},{16,20},{18,... | collective-permute-start | bytes 786440 | tf_op jit(solution)/shard_map/cond/branch_1_fun/ppermute | solution.py:47
  27.3 5.1 %collective-permute-start.2 = (f32[128,256]{1,0:T(8,128)S(1)}, f32[128,256]{1,0:T(8,128)S(1)}, u32[]{:S(2)}, u32[]{:S(2)}) collective-permute-start(f32[128,256]{1,0:T(8,128)S(1)} %constant_dynamic-slice_fusion.4), channel_id=1, source_target_pairs={{0,8},{2,10},{4,12},{6,14},{8,0},{10,2},{12,4},{14,6},{16,24},{18,... | collective-permute-start | bytes 393224 | tf_op jit(solution)/shard_map/ppermute | solution.py:47
  30.3 25.8 %collective-permute-start.5 = (f32[1088,256]{1,0:T(8,128)}, f32[1088,256]{1,0:T(8,128)}, u32[]{:S(2)}, u32[]{:S(2)}) collective-permute-start(f32[1088,256]{1,0:T(8,128)} %constant_dynamic-slice_fusion.2), channel_id=1, source_target_pairs={{0,1},{1,0},{2,3},{3,2},{4,5},{5,4},{6,7},{7,6},{8,9},{9,8},{10,11... | collective-permute-start | bytes 3342344 | tf_op jit(solution)/shard_map/ppermute | solution.py:47
  32.4 5.2 %collective-permute-start.3 = (f32[64,256]{1,0:T(8,128)S(1)}, f32[64,256]{1,0:T(8,128)S(1)}, u32[]{:S(2)}, u32[]{:S(2)}) collective-permute-start(f32[64,256]{1,0:T(8,128)S(1)} %constant_dynamic-slice_fusion.3), channel_id=1, source_target_pairs={{0,16},{2,18},{4,20},{6,22},{8,24},{10,26},{12,28},{14,30},{16,0},... | collective-permute-start | bytes 196616 | tf_op jit(solution)/shard_map/ppermute | solution.py:47
  37.7 19.8 %copy-start.2 = (bf16[2048,256]{1,0:T(8,128)(2,1)S(1)}, bf16[2048,256]{1,0:T(8,128)(2,1)}, u32[]{:S(2)}) copy-start(bf16[2048,256]{1,0:T(8,128)(2,1)} %param.9) | copy-start | bytes 3145732
  37.7 4.9 %collective-permute-start.4 = (bf16[64,256]{1,0:T(8,128)(2,1)S(1)}, bf16[64,256]{1,0:T(8,128)(2,1)S(1)}, u32[]{:S(2)}, u32[]{:S(2)}) collective-permute-start(bf16[64,256]{1,0:T(8,128)(2,1)S(1)} %add_convert_fusion.1), channel_id=1, source_target_pairs={{0,16},{2,18},{4,20},{6,22},{8,24},{10,26},{12,28},{14,30},{16,0},... | collective-permute-start | bytes 98312 | tf_op jit(solution)/shard_map/ppermute | solution.py:57
  57.9 4.3 %collective-permute-start.6 = (bf16[128,256]{1,0:T(8,128)(2,1)S(1)}, bf16[128,256]{1,0:T(8,128)(2,1)S(1)}, u32[]{:S(2)}, u32[]{:S(2)}) collective-permute-start(bf16[128,256]{1,0:T(8,128)(2,1)S(1)} %pad_maximum_fusion.5), channel_id=1, source_target_pairs={{0,8},{2,10},{4,12},{6,14},{8,0},{10,2},{12,4},{14,6},{16,24},{18,... | collective-permute-start | bytes 196616 | tf_op jit(solution)/shard_map/ppermute | solution.py:57
  58.5 12.9 %collective-permute-start.8 = (bf16[1088,256]{1,0:T(8,128)(2,1)S(1)}, bf16[1088,256]{1,0:T(8,128)(2,1)S(1)}, u32[]{:S(2)}, u32[]{:S(2)}) collective-permute-start(bf16[1088,256]{1,0:T(8,128)(2,1)S(1)} %add_convert_fusion), channel_id=1, source_target_pairs={{0,1},{1,0},{2,3},{3,2},{4,5},{5,4},{6,7},{7,6},{8,9},{9,8},{10,11... | collective-permute-start | bytes 1671176 | tf_op jit(solution)/shard_map/ppermute | solution.py:125
  62.3 5.0 %collective-permute-start.7 = (bf16[256,256]{1,0:T(8,128)(2,1)S(1)}, bf16[256,256]{1,0:T(8,128)(2,1)S(1)}, u32[]{:S(2)}, u32[]{:S(2)}) collective-permute-start(bf16[256,256]{1,0:T(8,128)(2,1)S(1)} %pad_maximum_fusion.4), channel_id=1, source_target_pairs={{0,4},{2,6},{4,0},{6,2},{8,12},{10,14},{12,8},{14,10},{16,20},{18,... | collective-permute-start | bytes 393224 | tf_op jit(solution)/shard_map/ppermute | solution.py:57
  73.2 1.5 %collective-permute-start.9 = (bf16[512,256]{1,0:T(8,128)(2,1)S(1)}, bf16[512,256]{1,0:T(8,128)(2,1)S(1)}, u32[]{:S(2)}, u32[]{:S(2)}) collective-permute-start(bf16[512,256]{1,0:T(8,128)(2,1)S(1)} %pad_maximum_fusion.3), channel_id=1, source_target_pairs={{0,2},{2,0},{4,6},{6,4},{8,10},{10,8},{12,14},{14,12},{16,18},{18,... | collective-permute-start | bytes 786440 | tf_op jit(solution)/shard_map/ppermute | solution.py:57

commit v17 on v16

--- a/solution.py
+++ b/solution.py
@@ -56,7 +56,7 @@
         side = (position >> bit) & 1
         got = lax.ppermute(tuple(parts), axis, xor_pairs(count, bit))
         parts = [
-            jnp.concatenate([jnp.where(side == 0, m, g), jnp.where(side == 0, g, m)], 0)
+            jnp.where(side == 0, jnp.concatenate([m, g], 0), jnp.concatenate([g, m], 0))
             for m, g in zip(parts, got)
         ]
     return parts

time: 75.9 us -> 61.4 us (0.81)
  waiting for transfers between devices: 37.3 us -> 24.4 us
  matrix products: 7.68 us -> 6.33 us
    ppermute x5, waiting for transfers between devices: 24.9 us -> 14.9 us  [halving_scatter(): got = lax.ppermute(tuple(sent), axis, xor_pairs(count, bit))]
    ppermute x1, waiting for transfers between devices: 4 us -> 0.21 us  [shards(): other = lax.ppermute(fresh_joint, 'loop', [(0, 1), (1, 0)])]
    ppermute x4, starting transfers between devices: 5.03 us -> 6.48 us  [doubling_gather(): got = lax.ppermute(tuple(parts), axis, xor_pairs(count, bit))]
    dot_general x1, matrix products: 2.62 us -> 1.28 us  [shards(): jnp.dot(rating_errors, item_factors, preferred_element_type=jnp.float32)]
    select_n x4, other arithmetic: 0.11 us -> 1.17 us  [doubling_gather(): jnp.where(side == 0, jnp.concatenate([m, g], 0), jnp.concatenate([g, m], 0))]
    ppermute x1, starting transfers between devices: 2.27 us -> 1.23 us  [shards(): other = lax.ppermute(fresh_joint, 'loop', [(0, 1), (1, 0)])]
    concatenate x4 -> x0, other arithmetic: 0.87 us -> none  [doubling_gather(): jnp.concatenate([jnp.where(side == 0, m, g), jnp.where(side == 0, g, m)], 0)]
    ppermute x5, starting transfers between devices: 9.67 us -> 8.9 us  [halving_scatter(): got = lax.ppermute(tuple(sent), axis, xor_pairs(count, bit))]
  transfers between devices with their start and end apart: 10 -> 10, of which waited for: 10 -> 9; matrix products, arithmetic and copies ran while one was open for 2% -> 6% of each run, Pallas kernels for 0% -> 0%
where the time goes in v17:
time: 61.4 us; the launch traced here: 61.1 us
  waiting for transfers between devices  24.4 us (40%)
  starting transfers between devices  16.6 us (27%)
  other arithmetic  7.2 us (12%)
  matrix products  6.33 us (10%)
  local copies, waits for them, and re-layouts  5.74 us (9%)
  between operations  0.82 us (1%)
    ppermute x5, waiting for transfers between devices, halving_scatter(): got = lax.ppermute(tuple(sent), axis, xor_pairs(count, bit))  14.9 us
    ppermute x4, waiting for transfers between devices, doubling_gather(): got = lax.ppermute(tuple(parts), axis, xor_pairs(count, bit))  9.23 us
    ppermute x5, starting transfers between devices, halving_scatter(): got = lax.ppermute(tuple(sent), axis, xor_pairs(count, bit))  8.9 us
    ppermute x4, starting transfers between devices, doubling_gather(): got = lax.ppermute(tuple(parts), axis, xor_pairs(count, bit))  6.48 us
    add x4, other arithmetic, halving_scatter(): parts = [k + g for k, g in zip(kept, got)]  3.66 us
    dot_general x2, matrix products, residual_of(): lax.dot_general(row_factors, column_factors, (((1,), (1,)), ((), ())), pr...  2.26 us
    dynamic_slice x5, local copies, waits for them, and re-layouts, halving_scatter(): lax.dynamic_slice_in_dim(p, (1 - side) * h, h, 0)  2.23 us
    unnamed x14, local copies, waits for them, and re-layouts  2.09 us
  transfers between devices with their start and end apart: 10, of which 9 were waited for; matrix products, arithmetic and copies ran while one was open for 6% of the time, Pallas kernels for 0%

profile of v17, /device:TPU:0, one launch (start us, length us, event | category | flops | bytes accessed | tf_op | source)
XLA Modules:
  0.0 61.1 jit_solution(6776531334379710930)
XLA Ops:
  2.8 1.3 %copy-done.3 = bf16[2048,1024]{1,0:T(8,128)(2,1)S(1)} copy-done((bf16[2048,1024]{1,0:T(8,128)(2,1)S(1)}, bf16[2048,1024]{1,0:T(8,128)(2,1)}, u32[]{:S(2)}) %copy-start.3) | copy-done | bytes 4194328
  4.1 2.0 %fusion = bf16[2048,1024]{1,0:T(8,128)(2,1)S(1)} fusion(f32[256,8,8,128]{3,2,1,0:T(8,128)S(1)} %bitcast.22, bf16[2048,1024]{1,0:T(8,128)(2,1)S(1)} %copy-done.3, bf16[2048,256]{1,0:T(8,128)(2,1)S(1)} %copy-done.1, bf16[1024,256]{1,0:T(8,128)(2,1)S(1)} %copy-done), kind=kOutput, calls=%fused_computation.5 | convolution fusion | flops 1082130432 | bytes 18350080 | tf_op jit(solution)/shard_map/dot_general | solution.py:19
  6.0 1.3 %fusion.4 = f32[2048,256]{1,0:T(8,128)S(1)} fusion(bf16[2048,1024]{1,0:T(8,128)(2,1)S(1)} %fusion, bf16[1024,256]{1,0:T(8,128)(2,1)S(1)} %copy-done), kind=kOutput, calls=%fused_computation.30 | convolution fusion | flops 1073741824 | bytes 6815744 | tf_op jit(solution)/shard_map/dot_general | solution.py:73
  7.4 1.3 %fusion.6 = f32[1024,256]{1,0:T(8,128)S(1)} fusion(bf16[2048,1024]{1,0:T(8,128)(2,1)S(1)} %fusion, bf16[2048,256]{1,0:T(8,128)(2,1)S(1)} %copy-done.1), kind=kOutput, calls=%fused_computation.32 | convolution fusion | flops 1073741824 | bytes 6291456 | tf_op jit(solution)/shard_map/dot_general | solution.py:26
  9.3 1.2 %convolution_add_fusion = f32[1024,256]{1,0:T(8,128)} fusion(f32[1024,256]{1,0:T(8,128)S(1)} %fusion.6, bf16[1024,128]{1,0:T(8,128)(2,1)S(1)} %fusion.2, bf16[128,256]{1,0:T(8,128)(2,1)S(1)} %copy-done.4), kind=kOutput, calls=%fused_computation.7 | convolution fusion | flops 67371008 | bytes 2424832 | tf_op jit(solution)/shard_map/dot_general | solution.py:77
  11.8 3.0 %collective-permute-start.5 = (f32[1088,256]{1,0:T(8,128)}, f32[1088,256]{1,0:T(8,128)}, u32[]{:S(2)}, u32[]{:S(2)}) collective-permute-start(f32[1088,256]{1,0:T(8,128)} %constant_dynamic-slice_fusion.2), channel_id=1, source_target_pairs={{0,1},{1,0},{2,3},{3,2},{4,5},{5,4},{6,7},{7,6},{8,9},{9,8},{10,11... | collective-permute-start | bytes 3342344 | tf_op jit(solution)/shard_map/ppermute | solution.py:47
  14.8 14.0 %conditional.1 = (f32[256,256]{1,0:T(8,128)S(1)}, s32[]{:T(128)}) conditional(s32[]{:T(128)} %convert_element_type.33, () %tuple.20, (s32[]{:T(128)}, f32[1024,256]{1,0:T(8,128)}) %tuple.22), branch_computations={%region_0.0_spmd, %region_1.0_spmd} | conditional | flops 196631 | bytes 7078268 | solution.py:94
  16.0 2.0 %collective-permute-done = f32[512,256]{1,0:T(8,128)} collective-permute-done((f32[512,256]{1,0:T(8,128)S(1)}, f32[512,256]{1,0:T(8,128)}, u32[]{:S(2)}, u32[]{:S(2)}) %collective-permute-start) | collective-permute-done | bytes 524320 | tf_op jit(solution)/shard_map/cond/branch_1_fun/ppermute | solution.py:47
  18.0 1.3 %dynamic-slice_add_fusion = f32[512,256]{1,0:T(8,128)S(1)} fusion(f32[512,256]{1,0:T(8,128)} %collective-permute-done, f32[1024,256]{1,0:T(8,128)} %get-tuple-element.4, s32[]{:T(128)S(6)} %select_n.58), kind=kLoop, calls=%fused_computation | loop fusion | flops 131072 | bytes 1572868 | tf_op jit(solution)/shard_map/cond/branch_1_fun/add | solution.py:48
  19.3 1.6 %collective-permute-start.1 = (f32[256,256]{1,0:T(8,128)S(1)}, f32[256,256]{1,0:T(8,128)}, u32[]{:S(2)}, u32[]{:S(2)}) collective-permute-start(f32[256,256]{1,0:T(8,128)S(1)} %constant_dynamic-slice_fusion), channel_id=1, source_target_pairs={{0,4},{2,6},{4,0},{6,2},{8,12},{10,14},{12,8},{14,10},{16,20},{18,... | collective-permute-start | bytes 786440 | tf_op jit(solution)/shard_map/cond/branch_1_fun/ppermute | solution.py:47
  20.8 7.0 %collective-permute-done.1 = f32[256,256]{1,0:T(8,128)} collective-permute-done((f32[256,256]{1,0:T(8,128)S(1)}, f32[256,256]{1,0:T(8,128)}, u32[]{:S(2)}, u32[]{:S(2)}) %collective-permute-start.1) | collective-permute-done | bytes 262176 | tf_op jit(solution)/shard_map/cond/branch_1_fun/ppermute | solution.py:47
  28.8 1.6 %collective-permute-start.2 = (f32[128,256]{1,0:T(8,128)S(1)}, f32[128,256]{1,0:T(8,128)S(1)}, u32[]{:S(2)}, u32[]{:S(2)}) collective-permute-start(f32[128,256]{1,0:T(8,128)S(1)} %constant_dynamic-slice_fusion.4), channel_id=1, source_target_pairs={{0,8},{2,10},{4,12},{6,14},{8,0},{10,2},{12,4},{14,6},{16,24},{18,... | collective-permute-start | bytes 393224 | tf_op jit(solution)/shard_map/ppermute | solution.py:47
  30.5 3.4 %collective-permute-done.2 = f32[128,256]{1,0:T(8,128)S(1)} collective-permute-done((f32[128,256]{1,0:T(8,128)S(1)}, f32[128,256]{1,0:T(8,128)S(1)}, u32[]{:S(2)}, u32[]{:S(2)}) %collective-permute-start.2) | collective-permute-done | bytes 131104 | tf_op jit(solution)/shard_map/ppermute | solution.py:47
  33.9 2.7 %collective-permute-start.3 = (f32[64,256]{1,0:T(8,128)S(1)}, f32[64,256]{1,0:T(8,128)S(1)}, u32[]{:S(2)}, u32[]{:S(2)}) collective-permute-start(f32[64,256]{1,0:T(8,128)S(1)} %constant_dynamic-slice_fusion.3), channel_id=1, source_target_pairs={{0,16},{2,18},{4,20},{6,22},{8,24},{10,26},{12,28},{14,30},{16,0},... | collective-permute-start | bytes 196616 | tf_op jit(solution)/shard_map/ppermute | solution.py:47
  36.6 2.6 %collective-permute-done.3 = f32[64,256]{1,0:T(8,128)S(1)} collective-permute-done((f32[64,256]{1,0:T(8,128)S(1)}, f32[64,256]{1,0:T(8,128)S(1)}, u32[]{:S(2)}, u32[]{:S(2)}) %collective-permute-start.3) | collective-permute-done | bytes 65568 | tf_op jit(solution)/shard_map/ppermute | solution.py:47
  39.2 2.7 %collective-permute-start.4 = (bf16[64,256]{1,0:T(8,128)(2,1)S(1)}, bf16[64,256]{1,0:T(8,128)(2,1)S(1)}, u32[]{:S(2)}, u32[]{:S(2)}) collective-permute-start(bf16[64,256]{1,0:T(8,128)(2,1)S(1)} %add_convert_fusion.1), channel_id=1, source_target_pairs={{0,16},{2,18},{4,20},{6,22},{8,24},{10,26},{12,28},{14,30},{16,0},... | collective-permute-start | bytes 98312 | tf_op jit(solution)/shard_map/ppermute | solution.py:57
  41.9 2.1 %collective-permute-done.4 = bf16[64,256]{1,0:T(8,128)(2,1)S(1)} collective-permute-done((bf16[64,256]{1,0:T(8,128)(2,1)S(1)}, bf16[64,256]{1,0:T(8,128)(2,1)S(1)}, u32[]{:S(2)}, u32[]{:S(2)}) %collective-permute-start.4) | collective-permute-done | bytes 32800 | tf_op jit(solution)/shard_map/ppermute | solution.py:57
  44.1 1.4 %dynamic-slice_add_fusion.2 = f32[1088,256]{1,0:T(8,128)S(1)} fusion(f32[1088,256]{1,0:T(8,128)} %collective-permute-done.5, f32[2176,256]{1,0:T(8,128)S(1)} %pad_maximum_fusion, s32[]{:T(128)S(6)} %select_n.89), kind=kLoop, calls=%fused_computation.14 | loop fusion | flops 278528 | bytes 3342340 | tf_op jit(solution)/shard_map/add | solution.py:48
  45.9 1.2 %collective-permute-start.8 = (bf16[1088,256]{1,0:T(8,128)(2,1)S(1)}, bf16[1088,256]{1,0:T(8,128)(2,1)S(1)}, u32[]{:S(2)}, u32[]{:S(2)}) collective-permute-start(bf16[1088,256]{1,0:T(8,128)(2,1)S(1)} %add_convert_fusion), channel_id=1, source_target_pairs={{0,1},{1,0},{2,3},{3,2},{4,5},{5,4},{6,7},{7,6},{8,9},{9,8},{10,11... | collective-permute-start | bytes 1671176 | tf_op jit(solution)/shard_map/ppermute | solution.py:125
  47.1 2.0 %collective-permute-start.6 = (bf16[128,256]{1,0:T(8,128)(2,1)S(1)}, bf16[128,256]{1,0:T(8,128)(2,1)S(1)}, u32[]{:S(2)}, u32[]{:S(2)}) collective-permute-start(bf16[128,256]{1,0:T(8,128)(2,1)S(1)} %maximum_select_fusion.3), channel_id=1, source_target_pairs={{0,8},{2,10},{4,12},{6,14},{8,0},{10,2},{12,4},{14,6},{16,24},{18,... | collective-permute-start | bytes 196616 | tf_op jit(solution)/shard_map/ppermute | solution.py:57
  49.1 2.3 %collective-permute-done.6 = bf16[128,256]{1,0:T(8,128)(2,1)S(1)} collective-permute-done((bf16[128,256]{1,0:T(8,128)(2,1)S(1)}, bf16[128,256]{1,0:T(8,128)(2,1)S(1)}, u32[]{:S(2)}, u32[]{:S(2)}) %collective-permute-start.6) | collective-permute-done | bytes 65568 | tf_op jit(solution)/shard_map/ppermute | solution.py:57
  51.4 1.7 %collective-permute-start.7 = (bf16[256,256]{1,0:T(8,128)(2,1)S(1)}, bf16[256,256]{1,0:T(8,128)(2,1)S(1)}, u32[]{:S(2)}, u32[]{:S(2)}) collective-permute-start(bf16[256,256]{1,0:T(8,128)(2,1)S(1)} %maximum_select_fusion.2), channel_id=1, source_target_pairs={{0,4},{2,6},{4,0},{6,2},{8,12},{10,14},{12,8},{14,10},{16,20},{18,... | collective-permute-start | bytes 393224 | tf_op jit(solution)/shard_map/ppermute | solution.py:57
  53.2 3.3 %collective-permute-done.7 = bf16[256,256]{1,0:T(8,128)(2,1)S(1)} collective-permute-done((bf16[256,256]{1,0:T(8,128)(2,1)S(1)}, bf16[256,256]{1,0:T(8,128)(2,1)S(1)}, u32[]{:S(2)}, u32[]{:S(2)}) %collective-permute-start.7) | collective-permute-done | bytes 131104 | tf_op jit(solution)/shard_map/ppermute | solution.py:57
  58.6 1.5 %collective-permute-done.9 = bf16[512,256]{1,0:T(8,128)(2,1)S(1)} collective-permute-done((bf16[512,256]{1,0:T(8,128)(2,1)S(1)}, bf16[512,256]{1,0:T(8,128)(2,1)S(1)}, u32[]{:S(2)}, u32[]{:S(2)}) %collective-permute-start.9) | collective-permute-done | bytes 262176 | tf_op jit(solution)/shard_map/ppermute | solution.py:57
  (42 shorter events, 9.8 us)
Async XLA Ops:
  1.4 1.0 %copy-start = (bf16[1024,256]{1,0:T(8,128)(2,1)S(1)}, bf16[1024,256]{1,0:T(8,128)(2,1)}, u32[]{:S(2)}) copy-start(bf16[1024,256]{1,0:T(8,128)(2,1)} %param.10) | copy-start | bytes 1572868
  1.4 1.4 %copy-start.1 = (bf16[2048,256]{1,0:T(8,128)(2,1)S(1)}, bf16[2048,256]{1,0:T(8,128)(2,1)}, u32[]{:S(2)}) copy-start(bf16[2048,256]{1,0:T(8,128)(2,1)} %param.9) | copy-start | bytes 3145732
  1.4 2.7 %copy-start.3 = (bf16[2048,1024]{1,0:T(8,128)(2,1)S(1)}, bf16[2048,1024]{1,0:T(8,128)(2,1)}, u32[]{:S(2)}) copy-start(bf16[2048,1024]{1,0:T(8,128)(2,1)} %param.12) | copy-start | bytes 12582916
  7.3 1.3 %copy-start.6 = (s32[8,1]{0,1:T(1,128)S(1)}, s32[8,1]{0,1:T(1,128)}, u32[]{:S(2)}) copy-start(s32[8,1]{0,1:T(1,128)} %param.15) | copy-start | bytes 100
  7.3 1.4 %copy-start.4 = (bf16[128,256]{1,0:T(8,128)(2,1)S(1)}, bf16[128,256]{1,0:T(8,128)(2,1)}, u32[]{:S(2)}) copy-start(bf16[128,256]{1,0:T(8,128)(2,1)} %param.11) | copy-start | bytes 196612
  7.3 1.4 %copy-start.5 = (bf16[1024,128]{1,0:T(8,128)(2,1)S(1)}, bf16[1024,128]{1,0:T(8,128)(2,1)}, u32[]{:S(2)}) copy-start(bf16[1024,128]{1,0:T(8,128)(2,1)} %param.14) | copy-start | bytes 786436
  11.8 32.2 %collective-permute-start.5 = (f32[1088,256]{1,0:T(8,128)}, f32[1088,256]{1,0:T(8,128)}, u32[]{:S(2)}, u32[]{:S(2)}) collective-permute-start(f32[1088,256]{1,0:T(8,128)} %constant_dynamic-slice_fusion.2), channel_id=1, source_target_pairs={{0,1},{1,0},{2,3},{3,2},{4,5},{5,4},{6,7},{7,6},{8,9},{9,8},{10,11... | collective-permute-start | bytes 3342344 | tf_op jit(solution)/shard_map/ppermute | solution.py:47
  15.9 2.1 %collective-permute-start = (f32[512,256]{1,0:T(8,128)S(1)}, f32[512,256]{1,0:T(8,128)}, u32[]{:S(2)}, u32[]{:S(2)}) collective-permute-start(f32[512,256]{1,0:T(8,128)S(1)} %constant_dynamic-slice_fusion.1), channel_id=1, source_target_pairs={{0,2},{2,0},{4,6},{6,4},{8,10},{10,8},{12,14},{14,12},{16,18},{18,... | collective-permute-start | bytes 1572872 | tf_op jit(solution)/shard_map/cond/branch_1_fun/ppermute | solution.py:47
  19.3 8.5 %collective-permute-start.1 = (f32[256,256]{1,0:T(8,128)S(1)}, f32[256,256]{1,0:T(8,128)}, u32[]{:S(2)}, u32[]{:S(2)}) collective-permute-start(f32[256,256]{1,0:T(8,128)S(1)} %constant_dynamic-slice_fusion), channel_id=1, source_target_pairs={{0,4},{2,6},{4,0},{6,2},{8,12},{10,14},{12,8},{14,10},{16,20},{18,... | collective-permute-start | bytes 786440 | tf_op jit(solution)/shard_map/cond/branch_1_fun/ppermute | solution.py:47
  28.8 5.0 %collective-permute-start.2 = (f32[128,256]{1,0:T(8,128)S(1)}, f32[128,256]{1,0:T(8,128)S(1)}, u32[]{:S(2)}, u32[]{:S(2)}) collective-permute-start(f32[128,256]{1,0:T(8,128)S(1)} %constant_dynamic-slice_fusion.4), channel_id=1, source_target_pairs={{0,8},{2,10},{4,12},{6,14},{8,0},{10,2},{12,4},{14,6},{16,24},{18,... | collective-permute-start | bytes 393224 | tf_op jit(solution)/shard_map/ppermute | solution.py:47
  33.9 5.2 %collective-permute-start.3 = (f32[64,256]{1,0:T(8,128)S(1)}, f32[64,256]{1,0:T(8,128)S(1)}, u32[]{:S(2)}, u32[]{:S(2)}) collective-permute-start(f32[64,256]{1,0:T(8,128)S(1)} %constant_dynamic-slice_fusion.3), channel_id=1, source_target_pairs={{0,16},{2,18},{4,20},{6,22},{8,24},{10,26},{12,28},{14,30},{16,0},... | collective-permute-start | bytes 196616 | tf_op jit(solution)/shard_map/ppermute | solution.py:47
  39.1 6.3 %copy-start.2 = (bf16[2048,256]{1,0:T(8,128)(2,1)S(1)}, bf16[2048,256]{1,0:T(8,128)(2,1)}, u32[]{:S(2)}) copy-start(bf16[2048,256]{1,0:T(8,128)(2,1)} %param.9) | copy-start | bytes 3145732
  39.2 4.9 %collective-permute-start.4 = (bf16[64,256]{1,0:T(8,128)(2,1)S(1)}, bf16[64,256]{1,0:T(8,128)(2,1)S(1)}, u32[]{:S(2)}, u32[]{:S(2)}) collective-permute-start(bf16[64,256]{1,0:T(8,128)(2,1)S(1)} %add_convert_fusion.1), channel_id=1, source_target_pairs={{0,16},{2,18},{4,20},{6,22},{8,24},{10,26},{12,28},{14,30},{16,0},... | collective-permute-start | bytes 98312 | tf_op jit(solution)/shard_map/ppermute | solution.py:57
  45.9 10.9 %collective-permute-start.8 = (bf16[1088,256]{1,0:T(8,128)(2,1)S(1)}, bf16[1088,256]{1,0:T(8,128)(2,1)S(1)}, u32[]{:S(2)}, u32[]{:S(2)}) collective-permute-start(bf16[1088,256]{1,0:T(8,128)(2,1)S(1)} %add_convert_fusion), channel_id=1, source_target_pairs={{0,1},{1,0},{2,3},{3,2},{4,5},{5,4},{6,7},{7,6},{8,9},{9,8},{10,11... | collective-permute-start | bytes 1671176 | tf_op jit(solution)/shard_map/ppermute | solution.py:125
  47.1 4.3 %collective-permute-start.6 = (bf16[128,256]{1,0:T(8,128)(2,1)S(1)}, bf16[128,256]{1,0:T(8,128)(2,1)S(1)}, u32[]{:S(2)}, u32[]{:S(2)}) collective-permute-start(bf16[128,256]{1,0:T(8,128)(2,1)S(1)} %maximum_select_fusion.3), channel_id=1, source_target_pairs={{0,8},{2,10},{4,12},{6,14},{8,0},{10,2},{12,4},{14,6},{16,24},{18,... | collective-permute-start | bytes 196616 | tf_op jit(solution)/shard_map/ppermute | solution.py:57
  51.4 5.0 %collective-permute-start.7 = (bf16[256,256]{1,0:T(8,128)(2,1)S(1)}, bf16[256,256]{1,0:T(8,128)(2,1)S(1)}, u32[]{:S(2)}, u32[]{:S(2)}) collective-permute-start(bf16[256,256]{1,0:T(8,128)(2,1)S(1)} %maximum_select_fusion.2), channel_id=1, source_target_pairs={{0,4},{2,6},{4,0},{6,2},{8,12},{10,14},{12,8},{14,10},{16,20},{18,... | collective-permute-start | bytes 393224 | tf_op jit(solution)/shard_map/ppermute | solution.py:57
  58.6 1.5 %collective-permute-start.9 = (bf16[512,256]{1,0:T(8,128)(2,1)S(1)}, bf16[512,256]{1,0:T(8,128)(2,1)S(1)}, u32[]{:S(2)}, u32[]{:S(2)}) collective-permute-start(bf16[512,256]{1,0:T(8,128)(2,1)S(1)} %maximum_select_fusion.1), channel_id=1, source_target_pairs={{0,2},{2,0},{4,6},{6,4},{8,10},{10,8},{12,14},{14,12},{16,18},{18,... | collective-permute-start | bytes 786440 | tf_op jit(solution)/shard_map/ppermute | solution.py:57

commit v18 on v15

--- a/solution.py
+++ b/solution.py
@@ -107,10 +107,7 @@
         step_items,
     )
     gather_bits = list(reversed(range(group_steps)))
-    (partly,) = doubling_gather(
-        [fresh_items], "group", group_count, group_position, gather_bits[:1]
-    )
-    partly, joint_share = lax.optimization_barrier((partly, joint_share))
+    fresh_items, joint_share = lax.optimization_barrier((fresh_items, joint_share))
     joint_factors = jnp.concatenate([user_factors, tag_factors], 0)
     fresh_joint = advance(
         lax.dynamic_slice_in_dim(joint_factors, joint_offset, joint_share.shape[0], 0),
@@ -122,12 +119,9 @@
         ),
     )
     (new_joint,) = doubling_gather([fresh_joint], "loop", loop_count, loop_position)
-    new_users = new_joint[: user_factors.shape[0]]
-    new_tags = new_joint[user_factors.shape[0] :]
-
-    partly, _ = lax.optimization_barrier((partly, fresh_joint))
+    partly, _ = lax.optimization_barrier((fresh_items, fresh_joint))
     (partly,) = doubling_gather(
-        [partly], "group", group_count, group_position, gather_bits[1:-1]
+        [partly], "group", group_count, group_position, gather_bits[:-1]
     )
     partly, new_joint = lax.optimization_barrier((partly, new_joint))
     new_users = new_joint[: user_factors.shape[0]]

time: 60.1 us -> 61.5 us (1.023)
    unnamed x14 -> x16, local copies, waits for them, and re-layouts: 2.09 us -> 2.1 us
  transfers between devices with their start and end apart: 10 -> 10, of which waited for: 8 -> 9; matrix products, arithmetic and copies ran while one was open for 9% -> 9% of each run, Pallas kernels for 0% -> 0%
where the time goes in v18:
time: 61.5 us; the launch traced here: 61.2 us
  waiting for transfers between devices  23.3 us (38%)
  starting transfers between devices  17 us (28%)
  other arithmetic  6.83 us (11%)
  local copies, waits for them, and re-layouts  6.74 us (11%)
  matrix products  6.44 us (10%)
  between operations  0.82 us (1%)
    ppermute x5, waiting for transfers between devices, halving_scatter(): got = lax.ppermute(tuple(sent), axis, xor_pairs(count, bit))  15.5 us
    ppermute x5, starting transfers between devices, halving_scatter(): got = lax.ppermute(tuple(sent), axis, xor_pairs(count, bit))  8.87 us
    ppermute x5, starting transfers between devices, doubling_gather(): got = lax.ppermute(tuple(parts), axis, xor_pairs(count, bit))  8.13 us
    ppermute x5, waiting for transfers between devices, doubling_gather(): got = lax.ppermute(tuple(parts), axis, xor_pairs(count, bit))  7.88 us
    add x4, other arithmetic, halving_scatter(): parts = [k + g for k, g in zip(kept, got)]  3.66 us
    dot_general x2, matrix products, residual_of(): lax.dot_general(row_factors, column_factors, (((1,), (1,)), ((), ())), pr...  2.36 us
    dynamic_slice x5, local copies, waits for them, and re-layouts, halving_scatter(): lax.dynamic_slice_in_dim(p, (1 - side) * h, h, 0)  2.23 us
    unnamed x16, local copies, waits for them, and re-layouts  2.1 us
  transfers between devices with their start and end apart: 10, of which 9 were waited for; matrix products, arithmetic and copies ran while one was open for 9% of the time, Pallas kernels for 0%

profile of v18, /device:TPU:0, one launch (start us, length us, event | category | flops | bytes accessed | tf_op | source)
XLA Modules:
  0.0 61.2 jit_solution(17744318521907650826)
XLA Ops:
  2.8 1.3 %copy-done.3 = bf16[2048,1024]{1,0:T(8,128)(2,1)S(1)} copy-done((bf16[2048,1024]{1,0:T(8,128)(2,1)S(1)}, bf16[2048,1024]{1,0:T(8,128)(2,1)}, u32[]{:S(2)}) %copy-start.3) | copy-done | bytes 4194328
  4.1 2.1 %fusion = bf16[2048,1024]{1,0:T(8,128)(2,1)S(1)} fusion(f32[256,8,8,128]{3,2,1,0:T(8,128)S(1)} %bitcast.22, bf16[2048,1024]{1,0:T(8,128)(2,1)S(1)} %copy-done.3, bf16[2048,256]{1,0:T(8,128)(2,1)S(1)} %copy-done.1, bf16[1024,256]{1,0:T(8,128)(2,1)S(1)} %copy-done), kind=kOutput, calls=%fused_computation.5 | convolution fusion | flops 1082130432 | bytes 18350080 | tf_op jit(solution)/shard_map/dot_general | solution.py:19
  6.1 1.3 %fusion.4 = f32[2048,256]{1,0:T(8,128)S(1)} fusion(bf16[2048,1024]{1,0:T(8,128)(2,1)S(1)} %fusion, bf16[1024,256]{1,0:T(8,128)(2,1)S(1)} %copy-done), kind=kOutput, calls=%fused_computation.28 | convolution fusion | flops 1073741824 | bytes 6815744 | tf_op jit(solution)/shard_map/dot_general | solution.py:73
  7.5 1.3 %fusion.6 = f32[1024,256]{1,0:T(8,128)S(1)} fusion(bf16[2048,1024]{1,0:T(8,128)(2,1)S(1)} %fusion, bf16[2048,256]{1,0:T(8,128)(2,1)S(1)} %copy-done.1), kind=kOutput, calls=%fused_computation.30 | convolution fusion | flops 1073741824 | bytes 6291456 | tf_op jit(solution)/shard_map/dot_general | solution.py:26
  9.4 1.2 %convolution_add_fusion = f32[1024,256]{1,0:T(8,128)} fusion(f32[1024,256]{1,0:T(8,128)S(1)} %fusion.6, bf16[1024,128]{1,0:T(8,128)(2,1)S(1)} %fusion.2, bf16[128,256]{1,0:T(8,128)(2,1)S(1)} %copy-done.4), kind=kOutput, calls=%fused_computation.7 | convolution fusion | flops 67371008 | bytes 2424832 | tf_op jit(solution)/shard_map/dot_general | solution.py:77
  10.8 1.1 %constant_dynamic-slice_fusion.2 = f32[1088,256]{1,0:T(8,128)} fusion(f32[2176,256]{1,0:T(8,128)S(1)} %pad_maximum_fusion, s32[]{:T(128)S(6)} %select_n.85), kind=kLoop, calls=%fused_computation.23 | loop fusion | bytes 2228228 | tf_op jit(solution)/shard_map/dynamic_slice | solution.py:46
  11.9 3.0 %collective-permute-start.4 = (f32[1088,256]{1,0:T(8,128)}, f32[1088,256]{1,0:T(8,128)}, u32[]{:S(2)}, u32[]{:S(2)}) collective-permute-start(f32[1088,256]{1,0:T(8,128)} %constant_dynamic-slice_fusion.2), channel_id=1, source_target_pairs={{0,1},{1,0},{2,3},{3,2},{4,5},{5,4},{6,7},{7,6},{8,9},{9,8},{10,11... | collective-permute-start | bytes 3342344 | tf_op jit(solution)/shard_map/ppermute | solution.py:47
  14.9 14.0 %conditional.1 = (f32[256,256]{1,0:T(8,128)S(1)}, s32[]{:T(128)}) conditional(s32[]{:T(128)} %convert_element_type.33, () %tuple.20, (s32[]{:T(128)}, f32[1024,256]{1,0:T(8,128)}) %tuple.22), branch_computations={%region_0.0_spmd, %region_1.0_spmd} | conditional | flops 196631 | bytes 7078268 | solution.py:94
  16.1 2.0 %collective-permute-done = f32[512,256]{1,0:T(8,128)} collective-permute-done((f32[512,256]{1,0:T(8,128)S(1)}, f32[512,256]{1,0:T(8,128)}, u32[]{:S(2)}, u32[]{:S(2)}) %collective-permute-start) | collective-permute-done | bytes 524320 | tf_op jit(solution)/shard_map/cond/branch_1_fun/ppermute | solution.py:47
  18.1 1.3 %dynamic-slice_add_fusion = f32[512,256]{1,0:T(8,128)S(1)} fusion(f32[512,256]{1,0:T(8,128)} %collective-permute-done, f32[1024,256]{1,0:T(8,128)} %get-tuple-element.4, s32[]{:T(128)S(6)} %select_n.55), kind=kLoop, calls=%fused_computation | loop fusion | flops 131072 | bytes 1572868 | tf_op jit(solution)/shard_map/cond/branch_1_fun/add | solution.py:48
  19.4 1.6 %collective-permute-start.1 = (f32[256,256]{1,0:T(8,128)S(1)}, f32[256,256]{1,0:T(8,128)}, u32[]{:S(2)}, u32[]{:S(2)}) collective-permute-start(f32[256,256]{1,0:T(8,128)S(1)} %constant_dynamic-slice_fusion), channel_id=1, source_target_pairs={{0,4},{2,6},{4,0},{6,2},{8,12},{10,14},{12,8},{14,10},{16,20},{18,... | collective-permute-start | bytes 786440 | tf_op jit(solution)/shard_map/cond/branch_1_fun/ppermute | solution.py:47
  20.9 7.0 %collective-permute-done.1 = f32[256,256]{1,0:T(8,128)} collective-permute-done((f32[256,256]{1,0:T(8,128)S(1)}, f32[256,256]{1,0:T(8,128)}, u32[]{:S(2)}, u32[]{:S(2)}) %collective-permute-start.1) | collective-permute-done | bytes 262176 | tf_op jit(solution)/shard_map/cond/branch_1_fun/ppermute | solution.py:47
  28.9 1.6 %collective-permute-start.2 = (f32[128,256]{1,0:T(8,128)S(1)}, f32[128,256]{1,0:T(8,128)S(1)}, u32[]{:S(2)}, u32[]{:S(2)}) collective-permute-start(f32[128,256]{1,0:T(8,128)S(1)} %constant_dynamic-slice_fusion.4), channel_id=1, source_target_pairs={{0,8},{2,10},{4,12},{6,14},{8,0},{10,2},{12,4},{14,6},{16,24},{18,... | collective-permute-start | bytes 393224 | tf_op jit(solution)/shard_map/ppermute | solution.py:47
  30.6 3.4 %collective-permute-done.2 = f32[128,256]{1,0:T(8,128)S(1)} collective-permute-done((f32[128,256]{1,0:T(8,128)S(1)}, f32[128,256]{1,0:T(8,128)S(1)}, u32[]{:S(2)}, u32[]{:S(2)}) %collective-permute-start.2) | collective-permute-done | bytes 131104 | tf_op jit(solution)/shard_map/ppermute | solution.py:47
  34.0 2.6 %collective-permute-start.3 = (f32[64,256]{1,0:T(8,128)S(1)}, f32[64,256]{1,0:T(8,128)S(1)}, u32[]{:S(2)}, u32[]{:S(2)}) collective-permute-start(f32[64,256]{1,0:T(8,128)S(1)} %constant_dynamic-slice_fusion.3), channel_id=1, source_target_pairs={{0,16},{2,18},{4,20},{6,22},{8,24},{10,26},{12,28},{14,30},{16,0},... | collective-permute-start | bytes 196616 | tf_op jit(solution)/shard_map/ppermute | solution.py:47
  36.7 2.6 %collective-permute-done.3 = f32[64,256]{1,0:T(8,128)S(1)} collective-permute-done((f32[64,256]{1,0:T(8,128)S(1)}, f32[64,256]{1,0:T(8,128)S(1)}, u32[]{:S(2)}, u32[]{:S(2)}) %collective-permute-start.3) | collective-permute-done | bytes 65568 | tf_op jit(solution)/shard_map/ppermute | solution.py:47
  39.8 1.4 %dynamic-slice_add_fusion.2 = f32[1088,256]{1,0:T(8,128)S(1)} fusion(f32[1088,256]{1,0:T(8,128)} %collective-permute-done.4, f32[2176,256]{1,0:T(8,128)S(1)} %pad_maximum_fusion, s32[]{:T(128)S(6)} %select_n.84), kind=kLoop, calls=%fused_computation.15 | loop fusion | flops 278528 | bytes 3342340 | tf_op jit(solution)/shard_map/add | solution.py:48
  42.1 2.9 %collective-permute-start.5 = (bf16[64,256]{1,0:T(8,128)(2,1)S(1)}, bf16[64,256]{1,0:T(8,128)(2,1)S(1)}, u32[]{:S(2)}, u32[]{:S(2)}) collective-permute-start(bf16[64,256]{1,0:T(8,128)(2,1)S(1)} %add_convert_fusion.1), channel_id=1, source_target_pairs={{0,16},{2,18},{4,20},{6,22},{8,24},{10,26},{12,28},{14,30},{16,0},... | collective-permute-start | bytes 98312 | tf_op jit(solution)/shard_map/ppermute | solution.py:57
  45.0 1.5 %collective-permute-start.8 = (bf16[1088,256]{1,0:T(8,128)(2,1)S(1)}, bf16[1088,256]{1,0:T(8,128)(2,1)S(1)}, u32[]{:S(2)}, u32[]{:S(2)}) collective-permute-start(bf16[1088,256]{1,0:T(8,128)(2,1)S(1)} %add_convert_fusion), channel_id=1, source_target_pairs={{0,1},{1,0},{2,3},{3,2},{4,5},{5,4},{6,7},{7,6},{8,9},{9,8},{10,11... | collective-permute-start | bytes 1671176 | tf_op jit(solution)/shard_map/ppermute | solution.py:57
  47.0 1.9 %collective-permute-start.6 = (bf16[128,256]{1,0:T(8,128)(2,1)S(1)}, bf16[128,256]{1,0:T(8,128)(2,1)S(1)}, u32[]{:S(2)}, u32[]{:S(2)}) collective-permute-start(bf16[128,256]{1,0:T(8,128)(2,1)S(1)} %maximum_select_fusion.4), channel_id=1, source_target_pairs={{0,8},{2,10},{4,12},{6,14},{8,0},{10,2},{12,4},{14,6},{16,24},{18,... | collective-permute-start | bytes 196616 | tf_op jit(solution)/shard_map/ppermute | solution.py:57
  48.8 2.5 %collective-permute-done.6 = bf16[128,256]{1,0:T(8,128)(2,1)S(1)} collective-permute-done((bf16[128,256]{1,0:T(8,128)(2,1)S(1)}, bf16[128,256]{1,0:T(8,128)(2,1)S(1)}, u32[]{:S(2)}, u32[]{:S(2)}) %collective-permute-start.6) | collective-permute-done | bytes 65568 | tf_op jit(solution)/shard_map/ppermute | solution.py:57
  51.3 1.8 %collective-permute-start.7 = (bf16[256,256]{1,0:T(8,128)(2,1)S(1)}, bf16[256,256]{1,0:T(8,128)(2,1)S(1)}, u32[]{:S(2)}, u32[]{:S(2)}) collective-permute-start(bf16[256,256]{1,0:T(8,128)(2,1)S(1)} %maximum_select_fusion.3), channel_id=1, source_target_pairs={{0,4},{2,6},{4,0},{6,2},{8,12},{10,14},{12,8},{14,10},{16,20},{18,... | collective-permute-start | bytes 393224 | tf_op jit(solution)/shard_map/ppermute | solution.py:57
  53.1 3.2 %collective-permute-done.7 = bf16[256,256]{1,0:T(8,128)(2,1)S(1)} collective-permute-done((bf16[256,256]{1,0:T(8,128)(2,1)S(1)}, bf16[256,256]{1,0:T(8,128)(2,1)S(1)}, u32[]{:S(2)}, u32[]{:S(2)}) %collective-permute-start.7) | collective-permute-done | bytes 131104 | tf_op jit(solution)/shard_map/ppermute | solution.py:57
  56.5 1.7 %collective-permute-done.8 = bf16[1088,256]{1,0:T(8,128)(2,1)S(1)} collective-permute-done((bf16[1088,256]{1,0:T(8,128)(2,1)S(1)}, bf16[1088,256]{1,0:T(8,128)(2,1)S(1)}, u32[]{:S(2)}, u32[]{:S(2)}) %collective-permute-start.8) | collective-permute-done | bytes 557088 | tf_op jit(solution)/shard_map/ppermute | solution.py:57
  (43 shorter events, 10.2 us)
Async XLA Ops:
  1.4 1.0 %copy-start = (bf16[1024,256]{1,0:T(8,128)(2,1)S(1)}, bf16[1024,256]{1,0:T(8,128)(2,1)}, u32[]{:S(2)}) copy-start(bf16[1024,256]{1,0:T(8,128)(2,1)} %param.10) | copy-start | bytes 1572868
  1.4 1.4 %copy-start.1 = (bf16[2048,256]{1,0:T(8,128)(2,1)S(1)}, bf16[2048,256]{1,0:T(8,128)(2,1)}, u32[]{:S(2)}) copy-start(bf16[2048,256]{1,0:T(8,128)(2,1)} %param.9) | copy-start | bytes 3145732
  1.4 2.7 %copy-start.3 = (bf16[2048,1024]{1,0:T(8,128)(2,1)S(1)}, bf16[2048,1024]{1,0:T(8,128)(2,1)}, u32[]{:S(2)}) copy-start(bf16[2048,1024]{1,0:T(8,128)(2,1)} %param.12) | copy-start | bytes 12582916
  7.4 1.3 %copy-start.7 = (s32[8,1]{0,1:T(1,128)S(1)}, s32[8,1]{0,1:T(1,128)}, u32[]{:S(2)}) copy-start(s32[8,1]{0,1:T(1,128)} %param.15) | copy-start | bytes 100
  7.4 1.4 %copy-start.4 = (bf16[128,256]{1,0:T(8,128)(2,1)S(1)}, bf16[128,256]{1,0:T(8,128)(2,1)}, u32[]{:S(2)}) copy-start(bf16[128,256]{1,0:T(8,128)(2,1)} %param.11) | copy-start | bytes 196612
  7.4 1.4 %copy-start.6 = (bf16[1024,128]{1,0:T(8,128)(2,1)S(1)}, bf16[1024,128]{1,0:T(8,128)(2,1)}, u32[]{:S(2)}) copy-start(bf16[1024,128]{1,0:T(8,128)(2,1)} %param.14) | copy-start | bytes 786436
  11.9 27.8 %collective-permute-start.4 = (f32[1088,256]{1,0:T(8,128)}, f32[1088,256]{1,0:T(8,128)}, u32[]{:S(2)}, u32[]{:S(2)}) collective-permute-start(f32[1088,256]{1,0:T(8,128)} %constant_dynamic-slice_fusion.2), channel_id=1, source_target_pairs={{0,1},{1,0},{2,3},{3,2},{4,5},{5,4},{6,7},{7,6},{8,9},{9,8},{10,11... | collective-permute-start | bytes 3342344 | tf_op jit(solution)/shard_map/ppermute | solution.py:47
  16.0 2.1 %collective-permute-start = (f32[512,256]{1,0:T(8,128)S(1)}, f32[512,256]{1,0:T(8,128)}, u32[]{:S(2)}, u32[]{:S(2)}) collective-permute-start(f32[512,256]{1,0:T(8,128)S(1)} %constant_dynamic-slice_fusion.1), channel_id=1, source_target_pairs={{0,2},{2,0},{4,6},{6,4},{8,10},{10,8},{12,14},{14,12},{16,18},{18,... | collective-permute-start | bytes 1572872 | tf_op jit(solution)/shard_map/cond/branch_1_fun/ppermute | solution.py:47
  19.4 8.5 %collective-permute-start.1 = (f32[256,256]{1,0:T(8,128)S(1)}, f32[256,256]{1,0:T(8,128)}, u32[]{:S(2)}, u32[]{:S(2)}) collective-permute-start(f32[256,256]{1,0:T(8,128)S(1)} %constant_dynamic-slice_fusion), channel_id=1, source_target_pairs={{0,4},{2,6},{4,0},{6,2},{8,12},{10,14},{12,8},{14,10},{16,20},{18,... | collective-permute-start | bytes 786440 | tf_op jit(solution)/shard_map/cond/branch_1_fun/ppermute | solution.py:47
  28.9 12.3 %copy-start.5 = (bf16[128,256]{1,0:T(8,128)(2,1)S(1)}, bf16[128,256]{1,0:T(8,128)(2,1)}, u32[]{:S(2)}) copy-start(bf16[128,256]{1,0:T(8,128)(2,1)} %param.11) | copy-start | bytes 196612
  28.9 5.0 %collective-permute-start.2 = (f32[128,256]{1,0:T(8,128)S(1)}, f32[128,256]{1,0:T(8,128)S(1)}, u32[]{:S(2)}, u32[]{:S(2)}) collective-permute-start(f32[128,256]{1,0:T(8,128)S(1)} %constant_dynamic-slice_fusion.4), channel_id=1, source_target_pairs={{0,8},{2,10},{4,12},{6,14},{8,0},{10,2},{12,4},{14,6},{16,24},{18,... | collective-permute-start | bytes 393224 | tf_op jit(solution)/shard_map/ppermute | solution.py:47
  34.0 5.2 %collective-permute-start.3 = (f32[64,256]{1,0:T(8,128)S(1)}, f32[64,256]{1,0:T(8,128)S(1)}, u32[]{:S(2)}, u32[]{:S(2)}) collective-permute-start(f32[64,256]{1,0:T(8,128)S(1)} %constant_dynamic-slice_fusion.3), channel_id=1, source_target_pairs={{0,16},{2,18},{4,20},{6,22},{8,24},{10,26},{12,28},{14,30},{16,0},... | collective-permute-start | bytes 196616 | tf_op jit(solution)/shard_map/ppermute | solution.py:47
  36.7 4.5 %copy-start.2 = (bf16[2048,256]{1,0:T(8,128)(2,1)S(1)}, bf16[2048,256]{1,0:T(8,128)(2,1)}, u32[]{:S(2)}) copy-start(bf16[2048,256]{1,0:T(8,128)(2,1)} %param.9) | copy-start | bytes 3145732
  42.1 4.9 %collective-permute-start.5 = (bf16[64,256]{1,0:T(8,128)(2,1)S(1)}, bf16[64,256]{1,0:T(8,128)(2,1)S(1)}, u32[]{:S(2)}, u32[]{:S(2)}) collective-permute-start(bf16[64,256]{1,0:T(8,128)(2,1)S(1)} %add_convert_fusion.1), channel_id=1, source_target_pairs={{0,16},{2,18},{4,20},{6,22},{8,24},{10,26},{12,28},{14,30},{16,0},... | collective-permute-start | bytes 98312 | tf_op jit(solution)/shard_map/ppermute | solution.py:57
  45.0 13.2 %collective-permute-start.8 = (bf16[1088,256]{1,0:T(8,128)(2,1)S(1)}, bf16[1088,256]{1,0:T(8,128)(2,1)S(1)}, u32[]{:S(2)}, u32[]{:S(2)}) collective-permute-start(bf16[1088,256]{1,0:T(8,128)(2,1)S(1)} %add_convert_fusion), channel_id=1, source_target_pairs={{0,1},{1,0},{2,3},{3,2},{4,5},{5,4},{6,7},{7,6},{8,9},{9,8},{10,11... | collective-permute-start | bytes 1671176 | tf_op jit(solution)/shard_map/ppermute | solution.py:57
  47.0 4.3 %collective-permute-start.6 = (bf16[128,256]{1,0:T(8,128)(2,1)S(1)}, bf16[128,256]{1,0:T(8,128)(2,1)S(1)}, u32[]{:S(2)}, u32[]{:S(2)}) collective-permute-start(bf16[128,256]{1,0:T(8,128)(2,1)S(1)} %maximum_select_fusion.4), channel_id=1, source_target_pairs={{0,8},{2,10},{4,12},{6,14},{8,0},{10,2},{12,4},{14,6},{16,24},{18,... | collective-permute-start | bytes 196616 | tf_op jit(solution)/shard_map/ppermute | solution.py:57
  51.3 5.0 %collective-permute-start.7 = (bf16[256,256]{1,0:T(8,128)(2,1)S(1)}, bf16[256,256]{1,0:T(8,128)(2,1)S(1)}, u32[]{:S(2)}, u32[]{:S(2)}) collective-permute-start(bf16[256,256]{1,0:T(8,128)(2,1)S(1)} %maximum_select_fusion.3), channel_id=1, source_target_pairs={{0,4},{2,6},{4,0},{6,2},{8,12},{10,14},{12,8},{14,10},{16,20},{18,... | collective-permute-start | bytes 393224 | tf_op jit(solution)/shard_map/ppermute | solution.py:57
  58.4 1.8 %collective-permute-start.9 = (bf16[512,256]{1,0:T(8,128)(2,1)S(1)}, bf16[512,256]{1,0:T(8,128)(2,1)S(1)}, u32[]{:S(2)}, u32[]{:S(2)}) collective-permute-start(bf16[512,256]{1,0:T(8,128)(2,1)S(1)} %maximum_select_fusion.2), channel_id=1, source_target_pairs={{0,2},{2,0},{4,6},{6,4},{8,10},{10,8},{12,14},{14,12},{16,18},{18,... | collective-permute-start | bytes 786440 | tf_op jit(solution)/shard_map/ppermute | solution.py:57

commit v19 on v15

--- a/solution.py
+++ b/solution.py
@@ -50,15 +50,21 @@
     return parts, offsets
 
 
-def doubling_gather(parts, axis, count, position, bits=None):
+def doubling_gather(parts, axis, count, position, bits=None, select_halves=False):
     steps = count.bit_length() - 1
     for bit in reversed(range(steps)) if bits is None else bits:
         side = (position >> bit) & 1
         got = lax.ppermute(tuple(parts), axis, xor_pairs(count, bit))
-        parts = [
-            jnp.where(side == 0, jnp.concatenate([m, g], 0), jnp.concatenate([g, m], 0))
-            for m, g in zip(parts, got)
-        ]
+        if select_halves:
+            parts = [
+                jnp.concatenate([jnp.where(side == 0, m, g), jnp.where(side == 0, g, m)], 0)
+                for m, g in zip(parts, got)
+            ]
+        else:
+            parts = [
+                jnp.where(side == 0, jnp.concatenate([m, g], 0), jnp.concatenate([g, m], 0))
+                for m, g in zip(parts, got)
+            ]
     return parts
 
 
@@ -133,7 +139,7 @@
     new_users = new_joint[: user_factors.shape[0]]
     new_tags = new_joint[user_factors.shape[0] :]
     (new_items,) = doubling_gather(
-        [partly], "group", group_count, group_position, gather_bits[-1:]
+        [partly], "group", group_count, group_position, gather_bits[-1:], True
     )
     return (new_users, new_items, new_tags)
 

time: 60.1 us -> 60 us (level)
    select_n x5 -> x4, other arithmetic: 1.42 us -> 0.4 us  [doubling_gather(): jnp.where(side == 0, jnp.concatenate([m, g], 0), jnp.concatenate([g, m], 0))]
    concatenate x0 -> x1, other arithmetic: none -> 0.83 us  [doubling_gather(): jnp.concatenate([jnp.where(side == 0, m, g), jnp.where(side == 0, g, m)], 0)]
where the time goes in v19:
time: 60 us; the launch traced here: 59.7 us
  waiting for transfers between devices  22.8 us (38%)
  starting transfers between devices  16.7 us (28%)
  local copies, waits for them, and re-layouts  6.74 us (11%)
  matrix products  6.33 us (11%)
  other arithmetic  6.19 us (10%)
  between operations  0.83 us (1%)
    ppermute x5, waiting for transfers between devices, halving_scatter(): got = lax.ppermute(tuple(sent), axis, xor_pairs(count, bit))  14.9 us
    ppermute x5, starting transfers between devices, halving_scatter(): got = lax.ppermute(tuple(sent), axis, xor_pairs(count, bit))  8.9 us
    ppermute x5, waiting for transfers between devices, doubling_gather(): got = lax.ppermute(tuple(parts), axis, xor_pairs(count, bit))  7.91 us
    ppermute x5, starting transfers between devices, doubling_gather(): got = lax.ppermute(tuple(parts), axis, xor_pairs(count, bit))  7.79 us
    add x4, other arithmetic, halving_scatter(): parts = [k + g for k, g in zip(kept, got)]  3.66 us
    dot_general x2, matrix products, residual_of(): lax.dot_general(row_factors, column_factors, (((1,), (1,)), ((), ())), pr...  2.26 us
    dynamic_slice x5, local copies, waits for them, and re-layouts, halving_scatter(): lax.dynamic_slice_in_dim(p, (1 - side) * h, h, 0)  2.23 us
    unnamed x14, local copies, waits for them, and re-layouts  2.09 us
  transfers between devices with their start and end apart: 10, of which 8 were waited for; matrix products, arithmetic and copies ran while one was open for 9% of the time, Pallas kernels for 0%

profile of v19, /device:TPU:0, one launch (start us, length us, event | category | flops | bytes accessed | tf_op | source)
XLA Modules:
  0.0 59.7 jit_solution(13885847704739305977)
XLA Ops:
  2.8 1.3 %copy-done.3 = bf16[2048,1024]{1,0:T(8,128)(2,1)S(1)} copy-done((bf16[2048,1024]{1,0:T(8,128)(2,1)S(1)}, bf16[2048,1024]{1,0:T(8,128)(2,1)}, u32[]{:S(2)}) %copy-start.3) | copy-done | bytes 4194328
  4.1 2.0 %fusion = bf16[2048,1024]{1,0:T(8,128)(2,1)S(1)} fusion(f32[256,8,8,128]{3,2,1,0:T(8,128)S(1)} %bitcast.22, bf16[2048,1024]{1,0:T(8,128)(2,1)S(1)} %copy-done.3, bf16[2048,256]{1,0:T(8,128)(2,1)S(1)} %copy-done.1, bf16[1024,256]{1,0:T(8,128)(2,1)S(1)} %copy-done), kind=kOutput, calls=%fused_computation.5 | convolution fusion | flops 1082130432 | bytes 18350080 | tf_op jit(solution)/shard_map/dot_general | solution.py:19
  6.0 1.3 %fusion.4 = f32[2048,256]{1,0:T(8,128)S(1)} fusion(bf16[2048,1024]{1,0:T(8,128)(2,1)S(1)} %fusion, bf16[1024,256]{1,0:T(8,128)(2,1)S(1)} %copy-done), kind=kOutput, calls=%fused_computation.30 | convolution fusion | flops 1073741824 | bytes 6815744 | tf_op jit(solution)/shard_map/dot_general | solution.py:79
  7.4 1.3 %fusion.6 = f32[1024,256]{1,0:T(8,128)S(1)} fusion(bf16[2048,1024]{1,0:T(8,128)(2,1)S(1)} %fusion, bf16[2048,256]{1,0:T(8,128)(2,1)S(1)} %copy-done.1), kind=kOutput, calls=%fused_computation.32 | convolution fusion | flops 1073741824 | bytes 6291456 | tf_op jit(solution)/shard_map/dot_general | solution.py:26
  9.3 1.2 %convolution_add_fusion = f32[1024,256]{1,0:T(8,128)} fusion(f32[1024,256]{1,0:T(8,128)S(1)} %fusion.6, bf16[1024,128]{1,0:T(8,128)(2,1)S(1)} %fusion.2, bf16[128,256]{1,0:T(8,128)(2,1)S(1)} %copy-done.4), kind=kOutput, calls=%fused_computation.7 | convolution fusion | flops 67371008 | bytes 2424832 | tf_op jit(solution)/shard_map/dot_general | solution.py:83
  10.7 1.1 %constant_dynamic-slice_fusion.2 = f32[1088,256]{1,0:T(8,128)} fusion(f32[2176,256]{1,0:T(8,128)S(1)} %pad_maximum_fusion, s32[]{:T(128)S(6)} %select_n.88), kind=kLoop, calls=%fused_computation.25 | loop fusion | bytes 2228228 | tf_op jit(solution)/shard_map/dynamic_slice | solution.py:46
  11.8 3.0 %collective-permute-start.5 = (f32[1088,256]{1,0:T(8,128)}, f32[1088,256]{1,0:T(8,128)}, u32[]{:S(2)}, u32[]{:S(2)}) collective-permute-start(f32[1088,256]{1,0:T(8,128)} %constant_dynamic-slice_fusion.2), channel_id=1, source_target_pairs={{0,1},{1,0},{2,3},{3,2},{4,5},{5,4},{6,7},{7,6},{8,9},{9,8},{10,11... | collective-permute-start | bytes 3342344 | tf_op jit(solution)/shard_map/ppermute | solution.py:47
  14.8 14.0 %conditional.1 = (f32[256,256]{1,0:T(8,128)S(1)}, s32[]{:T(128)}) conditional(s32[]{:T(128)} %convert_element_type.33, () %tuple.20, (s32[]{:T(128)}, f32[1024,256]{1,0:T(8,128)}) %tuple.22), branch_computations={%region_0.0_spmd, %region_1.0_spmd} | conditional | flops 196631 | bytes 7078268 | solution.py:100
  16.0 2.0 %collective-permute-done = f32[512,256]{1,0:T(8,128)} collective-permute-done((f32[512,256]{1,0:T(8,128)S(1)}, f32[512,256]{1,0:T(8,128)}, u32[]{:S(2)}, u32[]{:S(2)}) %collective-permute-start) | collective-permute-done | bytes 524320 | tf_op jit(solution)/shard_map/cond/branch_1_fun/ppermute | solution.py:47
  18.0 1.3 %dynamic-slice_add_fusion = f32[512,256]{1,0:T(8,128)S(1)} fusion(f32[512,256]{1,0:T(8,128)} %collective-permute-done, f32[1024,256]{1,0:T(8,128)} %get-tuple-element.4, s32[]{:T(128)S(6)} %select_n.56), kind=kLoop, calls=%fused_computation | loop fusion | flops 131072 | bytes 1572868 | tf_op jit(solution)/shard_map/cond/branch_1_fun/add | solution.py:48
  19.3 1.6 %collective-permute-start.1 = (f32[256,256]{1,0:T(8,128)S(1)}, f32[256,256]{1,0:T(8,128)}, u32[]{:S(2)}, u32[]{:S(2)}) collective-permute-start(f32[256,256]{1,0:T(8,128)S(1)} %constant_dynamic-slice_fusion), channel_id=1, source_target_pairs={{0,4},{2,6},{4,0},{6,2},{8,12},{10,14},{12,8},{14,10},{16,20},{18,... | collective-permute-start | bytes 786440 | tf_op jit(solution)/shard_map/cond/branch_1_fun/ppermute | solution.py:47
  20.8 7.0 %collective-permute-done.1 = f32[256,256]{1,0:T(8,128)} collective-permute-done((f32[256,256]{1,0:T(8,128)S(1)}, f32[256,256]{1,0:T(8,128)}, u32[]{:S(2)}, u32[]{:S(2)}) %collective-permute-start.1) | collective-permute-done | bytes 262176 | tf_op jit(solution)/shard_map/cond/branch_1_fun/ppermute | solution.py:47
  28.8 1.6 %collective-permute-start.2 = (f32[128,256]{1,0:T(8,128)S(1)}, f32[128,256]{1,0:T(8,128)S(1)}, u32[]{:S(2)}, u32[]{:S(2)}) collective-permute-start(f32[128,256]{1,0:T(8,128)S(1)} %constant_dynamic-slice_fusion.4), channel_id=1, source_target_pairs={{0,8},{2,10},{4,12},{6,14},{8,0},{10,2},{12,4},{14,6},{16,24},{18,... | collective-permute-start | bytes 393224 | tf_op jit(solution)/shard_map/ppermute | solution.py:47
  30.5 3.4 %collective-permute-done.2 = f32[128,256]{1,0:T(8,128)S(1)} collective-permute-done((f32[128,256]{1,0:T(8,128)S(1)}, f32[128,256]{1,0:T(8,128)S(1)}, u32[]{:S(2)}, u32[]{:S(2)}) %collective-permute-start.2) | collective-permute-done | bytes 131104 | tf_op jit(solution)/shard_map/ppermute | solution.py:47
  33.9 2.7 %collective-permute-start.3 = (f32[64,256]{1,0:T(8,128)S(1)}, f32[64,256]{1,0:T(8,128)S(1)}, u32[]{:S(2)}, u32[]{:S(2)}) collective-permute-start(f32[64,256]{1,0:T(8,128)S(1)} %constant_dynamic-slice_fusion.3), channel_id=1, source_target_pairs={{0,16},{2,18},{4,20},{6,22},{8,24},{10,26},{12,28},{14,30},{16,0},... | collective-permute-start | bytes 196616 | tf_op jit(solution)/shard_map/ppermute | solution.py:47
  36.6 2.6 %collective-permute-done.3 = f32[64,256]{1,0:T(8,128)S(1)} collective-permute-done((f32[64,256]{1,0:T(8,128)S(1)}, f32[64,256]{1,0:T(8,128)S(1)}, u32[]{:S(2)}, u32[]{:S(2)}) %collective-permute-start.3) | collective-permute-done | bytes 65568 | tf_op jit(solution)/shard_map/ppermute | solution.py:47
  39.2 2.7 %collective-permute-start.4 = (bf16[64,256]{1,0:T(8,128)(2,1)S(1)}, bf16[64,256]{1,0:T(8,128)(2,1)S(1)}, u32[]{:S(2)}, u32[]{:S(2)}) collective-permute-start(bf16[64,256]{1,0:T(8,128)(2,1)S(1)} %add_convert_fusion.1), channel_id=1, source_target_pairs={{0,16},{2,18},{4,20},{6,22},{8,24},{10,26},{12,28},{14,30},{16,0},... | collective-permute-start | bytes 98312 | tf_op jit(solution)/shard_map/ppermute | solution.py:57
  41.9 2.1 %collective-permute-done.4 = bf16[64,256]{1,0:T(8,128)(2,1)S(1)} collective-permute-done((bf16[64,256]{1,0:T(8,128)(2,1)S(1)}, bf16[64,256]{1,0:T(8,128)(2,1)S(1)}, u32[]{:S(2)}, u32[]{:S(2)}) %collective-permute-start.4) | collective-permute-done | bytes 32800 | tf_op jit(solution)/shard_map/ppermute | solution.py:57
  44.1 1.4 %dynamic-slice_add_fusion.2 = f32[1088,256]{1,0:T(8,128)S(1)} fusion(f32[1088,256]{1,0:T(8,128)} %collective-permute-done.5, f32[2176,256]{1,0:T(8,128)S(1)} %pad_maximum_fusion, s32[]{:T(128)S(6)} %select_n.87), kind=kLoop, calls=%fused_computation.15 | loop fusion | flops 278528 | bytes 3342340 | tf_op jit(solution)/shard_map/add | solution.py:48
  45.9 1.2 %collective-permute-start.8 = (bf16[1088,256]{1,0:T(8,128)(2,1)S(1)}, bf16[1088,256]{1,0:T(8,128)(2,1)S(1)}, u32[]{:S(2)}, u32[]{:S(2)}) collective-permute-start(bf16[1088,256]{1,0:T(8,128)(2,1)S(1)} %add_convert_fusion), channel_id=1, source_target_pairs={{0,1},{1,0},{2,3},{3,2},{4,5},{5,4},{6,7},{7,6},{8,9},{9,8},{10,11... | collective-permute-start | bytes 1671176 | tf_op jit(solution)/shard_map/ppermute | solution.py:57
  47.1 2.0 %collective-permute-start.6 = (bf16[128,256]{1,0:T(8,128)(2,1)S(1)}, bf16[128,256]{1,0:T(8,128)(2,1)S(1)}, u32[]{:S(2)}, u32[]{:S(2)}) collective-permute-start(bf16[128,256]{1,0:T(8,128)(2,1)S(1)} %maximum_select_fusion.3), channel_id=1, source_target_pairs={{0,8},{2,10},{4,12},{6,14},{8,0},{10,2},{12,4},{14,6},{16,24},{18,... | collective-permute-start | bytes 196616 | tf_op jit(solution)/shard_map/ppermute | solution.py:57
  49.1 2.3 %collective-permute-done.6 = bf16[128,256]{1,0:T(8,128)(2,1)S(1)} collective-permute-done((bf16[128,256]{1,0:T(8,128)(2,1)S(1)}, bf16[128,256]{1,0:T(8,128)(2,1)S(1)}, u32[]{:S(2)}, u32[]{:S(2)}) %collective-permute-start.6) | collective-permute-done | bytes 65568 | tf_op jit(solution)/shard_map/ppermute | solution.py:57
  51.4 1.7 %collective-permute-start.7 = (bf16[256,256]{1,0:T(8,128)(2,1)S(1)}, bf16[256,256]{1,0:T(8,128)(2,1)S(1)}, u32[]{:S(2)}, u32[]{:S(2)}) collective-permute-start(bf16[256,256]{1,0:T(8,128)(2,1)S(1)} %maximum_select_fusion.2), channel_id=1, source_target_pairs={{0,4},{2,6},{4,0},{6,2},{8,12},{10,14},{12,8},{14,10},{16,20},{18,... | collective-permute-start | bytes 393224 | tf_op jit(solution)/shard_map/ppermute | solution.py:57
  53.2 3.3 %collective-permute-done.7 = bf16[256,256]{1,0:T(8,128)(2,1)S(1)} collective-permute-done((bf16[256,256]{1,0:T(8,128)(2,1)S(1)}, bf16[256,256]{1,0:T(8,128)(2,1)S(1)}, u32[]{:S(2)}, u32[]{:S(2)}) %collective-permute-start.7) | collective-permute-done | bytes 131104 | tf_op jit(solution)/shard_map/ppermute | solution.py:57
  (42 shorter events, 8.8 us)
Async XLA Ops:
  1.4 1.0 %copy-start = (bf16[1024,256]{1,0:T(8,128)(2,1)S(1)}, bf16[1024,256]{1,0:T(8,128)(2,1)}, u32[]{:S(2)}) copy-start(bf16[1024,256]{1,0:T(8,128)(2,1)} %param.10) | copy-start | bytes 1572868
  1.4 1.4 %copy-start.1 = (bf16[2048,256]{1,0:T(8,128)(2,1)S(1)}, bf16[2048,256]{1,0:T(8,128)(2,1)}, u32[]{:S(2)}) copy-start(bf16[2048,256]{1,0:T(8,128)(2,1)} %param.9) | copy-start | bytes 3145732
  1.4 2.7 %copy-start.3 = (bf16[2048,1024]{1,0:T(8,128)(2,1)S(1)}, bf16[2048,1024]{1,0:T(8,128)(2,1)}, u32[]{:S(2)}) copy-start(bf16[2048,1024]{1,0:T(8,128)(2,1)} %param.12) | copy-start | bytes 12582916
  7.3 1.3 %copy-start.6 = (s32[8,1]{0,1:T(1,128)S(1)}, s32[8,1]{0,1:T(1,128)}, u32[]{:S(2)}) copy-start(s32[8,1]{0,1:T(1,128)} %param.15) | copy-start | bytes 100
  7.3 1.4 %copy-start.4 = (bf16[128,256]{1,0:T(8,128)(2,1)S(1)}, bf16[128,256]{1,0:T(8,128)(2,1)}, u32[]{:S(2)}) copy-start(bf16[128,256]{1,0:T(8,128)(2,1)} %param.11) | copy-start | bytes 196612
  7.3 1.4 %copy-start.5 = (bf16[1024,128]{1,0:T(8,128)(2,1)S(1)}, bf16[1024,128]{1,0:T(8,128)(2,1)}, u32[]{:S(2)}) copy-start(bf16[1024,128]{1,0:T(8,128)(2,1)} %param.14) | copy-start | bytes 786436
  11.8 32.2 %collective-permute-start.5 = (f32[1088,256]{1,0:T(8,128)}, f32[1088,256]{1,0:T(8,128)}, u32[]{:S(2)}, u32[]{:S(2)}) collective-permute-start(f32[1088,256]{1,0:T(8,128)} %constant_dynamic-slice_fusion.2), channel_id=1, source_target_pairs={{0,1},{1,0},{2,3},{3,2},{4,5},{5,4},{6,7},{7,6},{8,9},{9,8},{10,11... | collective-permute-start | bytes 3342344 | tf_op jit(solution)/shard_map/ppermute | solution.py:47
  15.9 2.1 %collective-permute-start = (f32[512,256]{1,0:T(8,128)S(1)}, f32[512,256]{1,0:T(8,128)}, u32[]{:S(2)}, u32[]{:S(2)}) collective-permute-start(f32[512,256]{1,0:T(8,128)S(1)} %constant_dynamic-slice_fusion.1), channel_id=1, source_target_pairs={{0,2},{2,0},{4,6},{6,4},{8,10},{10,8},{12,14},{14,12},{16,18},{18,... | collective-permute-start | bytes 1572872 | tf_op jit(solution)/shard_map/cond/branch_1_fun/ppermute | solution.py:47
  19.3 8.5 %collective-permute-start.1 = (f32[256,256]{1,0:T(8,128)S(1)}, f32[256,256]{1,0:T(8,128)}, u32[]{:S(2)}, u32[]{:S(2)}) collective-permute-start(f32[256,256]{1,0:T(8,128)S(1)} %constant_dynamic-slice_fusion), channel_id=1, source_target_pairs={{0,4},{2,6},{4,0},{6,2},{8,12},{10,14},{12,8},{14,10},{16,20},{18,... | collective-permute-start | bytes 786440 | tf_op jit(solution)/shard_map/cond/branch_1_fun/ppermute | solution.py:47
  28.8 5.0 %collective-permute-start.2 = (f32[128,256]{1,0:T(8,128)S(1)}, f32[128,256]{1,0:T(8,128)S(1)}, u32[]{:S(2)}, u32[]{:S(2)}) collective-permute-start(f32[128,256]{1,0:T(8,128)S(1)} %constant_dynamic-slice_fusion.4), channel_id=1, source_target_pairs={{0,8},{2,10},{4,12},{6,14},{8,0},{10,2},{12,4},{14,6},{16,24},{18,... | collective-permute-start | bytes 393224 | tf_op jit(solution)/shard_map/ppermute | solution.py:47
  33.9 5.2 %collective-permute-start.3 = (f32[64,256]{1,0:T(8,128)S(1)}, f32[64,256]{1,0:T(8,128)S(1)}, u32[]{:S(2)}, u32[]{:S(2)}) collective-permute-start(f32[64,256]{1,0:T(8,128)S(1)} %constant_dynamic-slice_fusion.3), channel_id=1, source_target_pairs={{0,16},{2,18},{4,20},{6,22},{8,24},{10,26},{12,28},{14,30},{16,0},... | collective-permute-start | bytes 196616 | tf_op jit(solution)/shard_map/ppermute | solution.py:47
  39.1 6.3 %copy-start.2 = (bf16[2048,256]{1,0:T(8,128)(2,1)S(1)}, bf16[2048,256]{1,0:T(8,128)(2,1)}, u32[]{:S(2)}) copy-start(bf16[2048,256]{1,0:T(8,128)(2,1)} %param.9) | copy-start | bytes 3145732
  39.2 4.9 %collective-permute-start.4 = (bf16[64,256]{1,0:T(8,128)(2,1)S(1)}, bf16[64,256]{1,0:T(8,128)(2,1)S(1)}, u32[]{:S(2)}, u32[]{:S(2)}) collective-permute-start(bf16[64,256]{1,0:T(8,128)(2,1)S(1)} %add_convert_fusion.1), channel_id=1, source_target_pairs={{0,16},{2,18},{4,20},{6,22},{8,24},{10,26},{12,28},{14,30},{16,0},... | collective-permute-start | bytes 98312 | tf_op jit(solution)/shard_map/ppermute | solution.py:57
  45.9 10.9 %collective-permute-start.8 = (bf16[1088,256]{1,0:T(8,128)(2,1)S(1)}, bf16[1088,256]{1,0:T(8,128)(2,1)S(1)}, u32[]{:S(2)}, u32[]{:S(2)}) collective-permute-start(bf16[1088,256]{1,0:T(8,128)(2,1)S(1)} %add_convert_fusion), channel_id=1, source_target_pairs={{0,1},{1,0},{2,3},{3,2},{4,5},{5,4},{6,7},{7,6},{8,9},{9,8},{10,11... | collective-permute-start | bytes 1671176 | tf_op jit(solution)/shard_map/ppermute | solution.py:57
  47.1 4.3 %collective-permute-start.6 = (bf16[128,256]{1,0:T(8,128)(2,1)S(1)}, bf16[128,256]{1,0:T(8,128)(2,1)S(1)}, u32[]{:S(2)}, u32[]{:S(2)}) collective-permute-start(bf16[128,256]{1,0:T(8,128)(2,1)S(1)} %maximum_select_fusion.3), channel_id=1, source_target_pairs={{0,8},{2,10},{4,12},{6,14},{8,0},{10,2},{12,4},{14,6},{16,24},{18,... | collective-permute-start | bytes 196616 | tf_op jit(solution)/shard_map/ppermute | solution.py:57
  51.4 5.0 %collective-permute-start.7 = (bf16[256,256]{1,0:T(8,128)(2,1)S(1)}, bf16[256,256]{1,0:T(8,128)(2,1)S(1)}, u32[]{:S(2)}, u32[]{:S(2)}) collective-permute-start(bf16[256,256]{1,0:T(8,128)(2,1)S(1)} %maximum_select_fusion.2), channel_id=1, source_target_pairs={{0,4},{2,6},{4,0},{6,2},{8,12},{10,14},{12,8},{14,10},{16,20},{18,... | collective-permute-start | bytes 393224 | tf_op jit(solution)/shard_map/ppermute | solution.py:57
  57.0 1.8 %collective-permute-start.9 = (bf16[512,256]{1,0:T(8,128)(2,1)S(1)}, bf16[512,256]{1,0:T(8,128)(2,1)S(1)}, u32[]{:S(2)}, u32[]{:S(2)}) collective-permute-start(bf16[512,256]{1,0:T(8,128)(2,1)S(1)} %maximum_select_fusion.1), channel_id=1, source_target_pairs={{0,2},{2,0},{4,6},{6,4},{8,10},{10,8},{12,14},{14,12},{16,18},{18,... | collective-permute-start | bytes 786440 | tf_op jit(solution)/shard_map/ppermute | solution.py:57

commit v20 on v19

--- a/solution.py
+++ b/solution.py
@@ -80,13 +80,16 @@
     tag_part = transposed_product(link_errors, item_factors)
     joint_part = jnp.concatenate([user_part, tag_part], 0)
 
+    joint_part, rating_errors, link_errors = lax.optimization_barrier(
+        (joint_part, rating_errors, link_errors)
+    )
+    (joint_share,), (joint_offset,) = halving_scatter(
+        [joint_part], "loop", loop_count, loop_position
+    )
     item_part = transposed_product(rating_errors, user_factors) + jnp.dot(
         link_errors, tag_factors, preferred_element_type=jnp.float32
     )
-    joint_part, item_part = lax.optimization_barrier((joint_part, item_part))
-    (joint_share,), (joint_offset,) = halving_scatter(
-        [joint_part], "loop", loop_count, loop_position
-    )
+    item_part, _ = lax.optimization_barrier((item_part, rating_errors))
     group_steps = group_count.bit_length() - 1
     first_bits = list(range(min(2, group_steps)))
     first_rows = item_part.shape[0] >> len(first_bits)

time: 60 us -> 62.5 us (1.042)
  matrix products: 6.33 us -> 8.53 us
    dot_general x2, matrix products: 1.55 us -> 3.74 us  [transposed_product(): lax.dot_general(first_operand, second_operand, (((0,), (0,)), ((), ())),...]
    unnamed x14 -> x18, local copies, waits for them, and re-layouts: 2.09 us -> 2.3 us
  transfers between devices with their start and end apart: 10 -> 10, of which waited for: 8 -> 7; matrix products, arithmetic and copies ran while one was open for 9% -> 16% of each run, Pallas kernels for 0% -> 0%
where the time goes in v20:
time: 62.5 us; the launch traced here: 62.1 us
  waiting for transfers between devices  23 us (37%)
  starting transfers between devices  16.5 us (26%)
  matrix products  8.53 us (14%)
  local copies, waits for them, and re-layouts  6.96 us (11%)
  other arithmetic  6.19 us (10%)
  between operations  0.85 us (1%)
    ppermute x5, waiting for transfers between devices, halving_scatter(): got = lax.ppermute(tuple(sent), axis, xor_pairs(count, bit))  15 us
    ppermute x5, starting transfers between devices, halving_scatter(): got = lax.ppermute(tuple(sent), axis, xor_pairs(count, bit))  8.88 us
    ppermute x5, waiting for transfers between devices, doubling_gather(): got = lax.ppermute(tuple(parts), axis, xor_pairs(count, bit))  8.07 us
    ppermute x5, starting transfers between devices, doubling_gather(): got = lax.ppermute(tuple(parts), axis, xor_pairs(count, bit))  7.61 us
    dot_general x2, matrix products, transposed_product(): lax.dot_general(first_operand, second_operand, (((0,), (0,)), ((), ())),...  3.74 us
    add x4, other arithmetic, halving_scatter(): parts = [k + g for k, g in zip(kept, got)]  3.66 us
    unnamed x18, local copies, waits for them, and re-layouts  2.3 us
    dot_general x2, matrix products, residual_of(): lax.dot_general(row_factors, column_factors, (((1,), (1,)), ((), ())), pr...  2.26 us
  transfers between devices with their start and end apart: 10, of which 7 were waited for; matrix products, arithmetic and copies ran while one was open for 16% of the time, Pallas kernels for 0%

profile of v20, /device:TPU:0, one launch (start us, length us, event | category | flops | bytes accessed | tf_op | source)
XLA Modules:
  0.0 62.1 jit_solution(9766284417581542682)
XLA Ops:
  2.8 1.3 %copy-done.4 = bf16[2048,1024]{1,0:T(8,128)(2,1)S(1)} copy-done((bf16[2048,1024]{1,0:T(8,128)(2,1)S(1)}, bf16[2048,1024]{1,0:T(8,128)(2,1)}, u32[]{:S(2)}) %copy-start.4) | copy-done | bytes 4194328
  4.1 2.0 %fusion = bf16[2048,1024]{1,0:T(8,128)(2,1)S(1)} fusion(f32[256,8,8,128]{3,2,1,0:T(8,128)S(1)} %bitcast.22, bf16[2048,1024]{1,0:T(8,128)(2,1)S(1)} %copy-done.4, bf16[2048,256]{1,0:T(8,128)(2,1)S(1)} %copy-done.1, bf16[1024,256]{1,0:T(8,128)(2,1)S(1)} %copy-done), kind=kOutput, calls=%fused_computation.5 | convolution fusion | flops 1082130432 | bytes 18350080 | tf_op jit(solution)/shard_map/dot_general | solution.py:19
  6.1 1.3 %fusion.4 = f32[2048,256]{1,0:T(8,128)S(1)} fusion(bf16[2048,1024]{1,0:T(8,128)(2,1)S(1)} %fusion, bf16[1024,256]{1,0:T(8,128)(2,1)S(1)} %copy-done), kind=kOutput, calls=%fused_computation.30 | convolution fusion | flops 1073741824 | bytes 6815744 | tf_op jit(solution)/shard_map/dot_general | solution.py:79
  8.4 1.1 %constant_dynamic-slice_fusion.2 = f32[1088,256]{1,0:T(8,128)} fusion(f32[2176,256]{1,0:T(8,128)S(1)} %pad_maximum_fusion, s32[]{:T(128)S(6)} %select_n.88), kind=kLoop, calls=%fused_computation.25 | loop fusion | bytes 2228228 | tf_op jit(solution)/shard_map/dynamic_slice | solution.py:46
  9.5 3.0 %collective-permute-start.5 = (f32[1088,256]{1,0:T(8,128)}, f32[1088,256]{1,0:T(8,128)}, u32[]{:S(2)}, u32[]{:S(2)}) collective-permute-start(f32[1088,256]{1,0:T(8,128)} %constant_dynamic-slice_fusion.2), channel_id=1, source_target_pairs={{0,1},{1,0},{2,3},{3,2},{4,5},{5,4},{6,7},{7,6},{8,9},{9,8},{10,11... | collective-permute-start | bytes 3342344 | tf_op jit(solution)/shard_map/ppermute | solution.py:47
  12.5 3.5 %fusion.6 = f32[1024,256]{1,0:T(8,128)S(1)} fusion(bf16[2048,1024]{1,0:T(8,128)(2,1)} %copy-done.5, bf16[2048,256]{1,0:T(8,128)(2,1)S(1)} %copy-done.2), kind=kOutput, calls=%fused_computation.32 | convolution fusion | flops 1073741824 | bytes 6291456 | tf_op jit(solution)/shard_map/dot_general | solution.py:26
  16.0 1.3 %convolution_add_fusion = f32[1024,256]{1,0:T(8,128)} fusion(f32[1024,256]{1,0:T(8,128)S(1)} %fusion.6, bf16[1024,128]{1,0:T(8,128)(2,1)S(1)} %fusion.2, bf16[128,256]{1,0:T(8,128)(2,1)S(1)} %copy-done.6), kind=kOutput, calls=%fused_computation.7 | convolution fusion | flops 67371008 | bytes 2424832 | tf_op jit(solution)/shard_map/dot_general | solution.py:89
  17.2 14.0 %conditional.1 = (f32[256,256]{1,0:T(8,128)S(1)}, s32[]{:T(128)}) conditional(s32[]{:T(128)} %convert_element_type.33, () %tuple.21, (s32[]{:T(128)}, f32[1024,256]{1,0:T(8,128)}) %tuple.24), branch_computations={%region_0.0_spmd, %region_1.0_spmd} | conditional | flops 196631 | bytes 7078268 | solution.py:103
  18.4 2.0 %collective-permute-done = f32[512,256]{1,0:T(8,128)} collective-permute-done((f32[512,256]{1,0:T(8,128)S(1)}, f32[512,256]{1,0:T(8,128)}, u32[]{:S(2)}, u32[]{:S(2)}) %collective-permute-start) | collective-permute-done | bytes 524320 | tf_op jit(solution)/shard_map/cond/branch_1_fun/ppermute | solution.py:47
  20.4 1.3 %dynamic-slice_add_fusion = f32[512,256]{1,0:T(8,128)S(1)} fusion(f32[512,256]{1,0:T(8,128)} %collective-permute-done, f32[1024,256]{1,0:T(8,128)} %get-tuple-element.4, s32[]{:T(128)S(6)} %select_n.56), kind=kLoop, calls=%fused_computation | loop fusion | flops 131072 | bytes 1572868 | tf_op jit(solution)/shard_map/cond/branch_1_fun/add | solution.py:48
  21.7 1.5 %collective-permute-start.1 = (f32[256,256]{1,0:T(8,128)S(1)}, f32[256,256]{1,0:T(8,128)}, u32[]{:S(2)}, u32[]{:S(2)}) collective-permute-start(f32[256,256]{1,0:T(8,128)S(1)} %constant_dynamic-slice_fusion), channel_id=1, source_target_pairs={{0,4},{2,6},{4,0},{6,2},{8,12},{10,14},{12,8},{14,10},{16,20},{18,... | collective-permute-start | bytes 786440 | tf_op jit(solution)/shard_map/cond/branch_1_fun/ppermute | solution.py:47
  23.3 7.0 %collective-permute-done.1 = f32[256,256]{1,0:T(8,128)} collective-permute-done((f32[256,256]{1,0:T(8,128)S(1)}, f32[256,256]{1,0:T(8,128)}, u32[]{:S(2)}, u32[]{:S(2)}) %collective-permute-start.1) | collective-permute-done | bytes 262176 | tf_op jit(solution)/shard_map/cond/branch_1_fun/ppermute | solution.py:47
  31.3 1.6 %collective-permute-start.2 = (f32[128,256]{1,0:T(8,128)S(1)}, f32[128,256]{1,0:T(8,128)S(1)}, u32[]{:S(2)}, u32[]{:S(2)}) collective-permute-start(f32[128,256]{1,0:T(8,128)S(1)} %constant_dynamic-slice_fusion.4), channel_id=1, source_target_pairs={{0,8},{2,10},{4,12},{6,14},{8,0},{10,2},{12,4},{14,6},{16,24},{18,... | collective-permute-start | bytes 393224 | tf_op jit(solution)/shard_map/ppermute | solution.py:47
  32.9 3.4 %collective-permute-done.2 = f32[128,256]{1,0:T(8,128)S(1)} collective-permute-done((f32[128,256]{1,0:T(8,128)S(1)}, f32[128,256]{1,0:T(8,128)S(1)}, u32[]{:S(2)}, u32[]{:S(2)}) %collective-permute-start.2) | collective-permute-done | bytes 131104 | tf_op jit(solution)/shard_map/ppermute | solution.py:47
  36.3 2.7 %collective-permute-start.3 = (f32[64,256]{1,0:T(8,128)S(1)}, f32[64,256]{1,0:T(8,128)S(1)}, u32[]{:S(2)}, u32[]{:S(2)}) collective-permute-start(f32[64,256]{1,0:T(8,128)S(1)} %constant_dynamic-slice_fusion.3), channel_id=1, source_target_pairs={{0,16},{2,18},{4,20},{6,22},{8,24},{10,26},{12,28},{14,30},{16,0},... | collective-permute-start | bytes 196616 | tf_op jit(solution)/shard_map/ppermute | solution.py:47
  39.0 2.6 %collective-permute-done.3 = f32[64,256]{1,0:T(8,128)S(1)} collective-permute-done((f32[64,256]{1,0:T(8,128)S(1)}, f32[64,256]{1,0:T(8,128)S(1)}, u32[]{:S(2)}, u32[]{:S(2)}) %collective-permute-start.3) | collective-permute-done | bytes 65568 | tf_op jit(solution)/shard_map/ppermute | solution.py:47
  41.6 2.7 %collective-permute-start.4 = (bf16[64,256]{1,0:T(8,128)(2,1)S(1)}, bf16[64,256]{1,0:T(8,128)(2,1)S(1)}, u32[]{:S(2)}, u32[]{:S(2)}) collective-permute-start(bf16[64,256]{1,0:T(8,128)(2,1)S(1)} %add_convert_fusion.1), channel_id=1, source_target_pairs={{0,16},{2,18},{4,20},{6,22},{8,24},{10,26},{12,28},{14,30},{16,0},... | collective-permute-start | bytes 98312 | tf_op jit(solution)/shard_map/ppermute | solution.py:57
  44.3 2.2 %collective-permute-done.4 = bf16[64,256]{1,0:T(8,128)(2,1)S(1)} collective-permute-done((bf16[64,256]{1,0:T(8,128)(2,1)S(1)}, bf16[64,256]{1,0:T(8,128)(2,1)S(1)}, u32[]{:S(2)}, u32[]{:S(2)}) %collective-permute-start.4) | collective-permute-done | bytes 32800 | tf_op jit(solution)/shard_map/ppermute | solution.py:57
  46.5 1.4 %dynamic-slice_add_fusion.2 = f32[1088,256]{1,0:T(8,128)S(1)} fusion(f32[1088,256]{1,0:T(8,128)} %collective-permute-done.5, f32[2176,256]{1,0:T(8,128)S(1)} %pad_maximum_fusion, s32[]{:T(128)S(6)} %select_n.87), kind=kLoop, calls=%fused_computation.15 | loop fusion | flops 278528 | bytes 3342340 | tf_op jit(solution)/shard_map/add | solution.py:48
  48.3 1.4 %collective-permute-start.8 = (bf16[1088,256]{1,0:T(8,128)(2,1)S(1)}, bf16[1088,256]{1,0:T(8,128)(2,1)S(1)}, u32[]{:S(2)}, u32[]{:S(2)}) collective-permute-start(bf16[1088,256]{1,0:T(8,128)(2,1)S(1)} %add_convert_fusion), channel_id=1, source_target_pairs={{0,1},{1,0},{2,3},{3,2},{4,5},{5,4},{6,7},{7,6},{8,9},{9,8},{10,11... | collective-permute-start | bytes 1671176 | tf_op jit(solution)/shard_map/ppermute | solution.py:57
  49.7 1.8 %collective-permute-start.6 = (bf16[128,256]{1,0:T(8,128)(2,1)S(1)}, bf16[128,256]{1,0:T(8,128)(2,1)S(1)}, u32[]{:S(2)}, u32[]{:S(2)}) collective-permute-start(bf16[128,256]{1,0:T(8,128)(2,1)S(1)} %maximum_select_fusion.3), channel_id=1, source_target_pairs={{0,8},{2,10},{4,12},{6,14},{8,0},{10,2},{12,4},{14,6},{16,24},{18,... | collective-permute-start | bytes 196616 | tf_op jit(solution)/shard_map/ppermute | solution.py:57
  51.6 2.4 %collective-permute-done.6 = bf16[128,256]{1,0:T(8,128)(2,1)S(1)} collective-permute-done((bf16[128,256]{1,0:T(8,128)(2,1)S(1)}, bf16[128,256]{1,0:T(8,128)(2,1)S(1)}, u32[]{:S(2)}, u32[]{:S(2)}) %collective-permute-start.6) | collective-permute-done | bytes 65568 | tf_op jit(solution)/shard_map/ppermute | solution.py:57
  54.0 1.6 %collective-permute-start.7 = (bf16[256,256]{1,0:T(8,128)(2,1)S(1)}, bf16[256,256]{1,0:T(8,128)(2,1)S(1)}, u32[]{:S(2)}, u32[]{:S(2)}) collective-permute-start(bf16[256,256]{1,0:T(8,128)(2,1)S(1)} %maximum_select_fusion.2), channel_id=1, source_target_pairs={{0,4},{2,6},{4,0},{6,2},{8,12},{10,14},{12,8},{14,10},{16,20},{18,... | collective-permute-start | bytes 393224 | tf_op jit(solution)/shard_map/ppermute | solution.py:57
  55.6 3.5 %collective-permute-done.7 = bf16[256,256]{1,0:T(8,128)(2,1)S(1)} collective-permute-done((bf16[256,256]{1,0:T(8,128)(2,1)S(1)}, bf16[256,256]{1,0:T(8,128)(2,1)S(1)}, u32[]{:S(2)}, u32[]{:S(2)}) %collective-permute-start.7) | collective-permute-done | bytes 131104 | tf_op jit(solution)/shard_map/ppermute | solution.py:57
  (46 shorter events, 8.8 us)
Async XLA Ops:
  1.4 1.0 %copy-start = (bf16[1024,256]{1,0:T(8,128)(2,1)S(1)}, bf16[1024,256]{1,0:T(8,128)(2,1)}, u32[]{:S(2)}) copy-start(bf16[1024,256]{1,0:T(8,128)(2,1)} %param.10) | copy-start | bytes 1572868
  1.4 1.4 %copy-start.1 = (bf16[2048,256]{1,0:T(8,128)(2,1)S(1)}, bf16[2048,256]{1,0:T(8,128)(2,1)}, u32[]{:S(2)}) copy-start(bf16[2048,256]{1,0:T(8,128)(2,1)} %param.9) | copy-start | bytes 3145732
  1.4 2.7 %copy-start.4 = (bf16[2048,1024]{1,0:T(8,128)(2,1)S(1)}, bf16[2048,1024]{1,0:T(8,128)(2,1)}, u32[]{:S(2)}) copy-start(bf16[2048,1024]{1,0:T(8,128)(2,1)} %param.12) | copy-start | bytes 12582916
  6.0 1.9 %copy-start.5 = (bf16[2048,1024]{1,0:T(8,128)(2,1)}, bf16[2048,1024]{1,0:T(8,128)(2,1)S(1)}, u32[]{:S(2)}) copy-start(bf16[2048,1024]{1,0:T(8,128)(2,1)S(1)} %fusion) | copy-start | bytes 12582916
  6.0 1.3 %copy-start.8 = (s32[8,1]{0,1:T(1,128)S(1)}, s32[8,1]{0,1:T(1,128)}, u32[]{:S(2)}) copy-start(s32[8,1]{0,1:T(1,128)} %param.15) | copy-start | bytes 100
  6.1 1.4 %copy-start.6 = (bf16[128,256]{1,0:T(8,128)(2,1)S(1)}, bf16[128,256]{1,0:T(8,128)(2,1)}, u32[]{:S(2)}) copy-start(bf16[128,256]{1,0:T(8,128)(2,1)} %param.11) | copy-start | bytes 196612
  6.1 1.4 %copy-start.7 = (bf16[1024,128]{1,0:T(8,128)(2,1)S(1)}, bf16[1024,128]{1,0:T(8,128)(2,1)}, u32[]{:S(2)}) copy-start(bf16[1024,128]{1,0:T(8,128)(2,1)} %param.14) | copy-start | bytes 786436
  8.4 4.1 %copy-start.2 = (bf16[2048,256]{1,0:T(8,128)(2,1)S(1)}, bf16[2048,256]{1,0:T(8,128)(2,1)}, u32[]{:S(2)}) copy-start(bf16[2048,256]{1,0:T(8,128)(2,1)} %param.9) | copy-start | bytes 3145732
  9.5 37.0 %collective-permute-start.5 = (f32[1088,256]{1,0:T(8,128)}, f32[1088,256]{1,0:T(8,128)}, u32[]{:S(2)}, u32[]{:S(2)}) collective-permute-start(f32[1088,256]{1,0:T(8,128)} %constant_dynamic-slice_fusion.2), channel_id=1, source_target_pairs={{0,1},{1,0},{2,3},{3,2},{4,5},{5,4},{6,7},{7,6},{8,9},{9,8},{10,11... | collective-permute-start | bytes 3342344 | tf_op jit(solution)/shard_map/ppermute | solution.py:47
  18.3 2.1 %collective-permute-start = (f32[512,256]{1,0:T(8,128)S(1)}, f32[512,256]{1,0:T(8,128)}, u32[]{:S(2)}, u32[]{:S(2)}) collective-permute-start(f32[512,256]{1,0:T(8,128)S(1)} %constant_dynamic-slice_fusion.1), channel_id=1, source_target_pairs={{0,2},{2,0},{4,6},{6,4},{8,10},{10,8},{12,14},{14,12},{16,18},{18,... | collective-permute-start | bytes 1572872 | tf_op jit(solution)/shard_map/cond/branch_1_fun/ppermute | solution.py:47
  21.7 8.5 %collective-permute-start.1 = (f32[256,256]{1,0:T(8,128)S(1)}, f32[256,256]{1,0:T(8,128)}, u32[]{:S(2)}, u32[]{:S(2)}) collective-permute-start(f32[256,256]{1,0:T(8,128)S(1)} %constant_dynamic-slice_fusion), channel_id=1, source_target_pairs={{0,4},{2,6},{4,0},{6,2},{8,12},{10,14},{12,8},{14,10},{16,20},{18,... | collective-permute-start | bytes 786440 | tf_op jit(solution)/shard_map/cond/branch_1_fun/ppermute | solution.py:47
  31.3 5.0 %collective-permute-start.2 = (f32[128,256]{1,0:T(8,128)S(1)}, f32[128,256]{1,0:T(8,128)S(1)}, u32[]{:S(2)}, u32[]{:S(2)}) collective-permute-start(f32[128,256]{1,0:T(8,128)S(1)} %constant_dynamic-slice_fusion.4), channel_id=1, source_target_pairs={{0,8},{2,10},{4,12},{6,14},{8,0},{10,2},{12,4},{14,6},{16,24},{18,... | collective-permute-start | bytes 393224 | tf_op jit(solution)/shard_map/ppermute | solution.py:47
  36.3 5.2 %collective-permute-start.3 = (f32[64,256]{1,0:T(8,128)S(1)}, f32[64,256]{1,0:T(8,128)S(1)}, u32[]{:S(2)}, u32[]{:S(2)}) collective-permute-start(f32[64,256]{1,0:T(8,128)S(1)} %constant_dynamic-slice_fusion.3), channel_id=1, source_target_pairs={{0,16},{2,18},{4,20},{6,22},{8,24},{10,26},{12,28},{14,30},{16,0},... | collective-permute-start | bytes 196616 | tf_op jit(solution)/shard_map/ppermute | solution.py:47
  41.6 6.3 %copy-start.3 = (bf16[2048,256]{1,0:T(8,128)(2,1)S(1)}, bf16[2048,256]{1,0:T(8,128)(2,1)}, u32[]{:S(2)}) copy-start(bf16[2048,256]{1,0:T(8,128)(2,1)} %param.9) | copy-start | bytes 3145732
  41.6 4.9 %collective-permute-start.4 = (bf16[64,256]{1,0:T(8,128)(2,1)S(1)}, bf16[64,256]{1,0:T(8,128)(2,1)S(1)}, u32[]{:S(2)}, u32[]{:S(2)}) collective-permute-start(bf16[64,256]{1,0:T(8,128)(2,1)S(1)} %add_convert_fusion.1), channel_id=1, source_target_pairs={{0,16},{2,18},{4,20},{6,22},{8,24},{10,26},{12,28},{14,30},{16,0},... | collective-permute-start | bytes 98312 | tf_op jit(solution)/shard_map/ppermute | solution.py:57
  48.3 10.9 %collective-permute-start.8 = (bf16[1088,256]{1,0:T(8,128)(2,1)S(1)}, bf16[1088,256]{1,0:T(8,128)(2,1)S(1)}, u32[]{:S(2)}, u32[]{:S(2)}) collective-permute-start(bf16[1088,256]{1,0:T(8,128)(2,1)S(1)} %add_convert_fusion), channel_id=1, source_target_pairs={{0,1},{1,0},{2,3},{3,2},{4,5},{5,4},{6,7},{7,6},{8,9},{9,8},{10,11... | collective-permute-start | bytes 1671176 | tf_op jit(solution)/shard_map/ppermute | solution.py:57
  49.7 4.3 %collective-permute-start.6 = (bf16[128,256]{1,0:T(8,128)(2,1)S(1)}, bf16[128,256]{1,0:T(8,128)(2,1)S(1)}, u32[]{:S(2)}, u32[]{:S(2)}) collective-permute-start(bf16[128,256]{1,0:T(8,128)(2,1)S(1)} %maximum_select_fusion.3), channel_id=1, source_target_pairs={{0,8},{2,10},{4,12},{6,14},{8,0},{10,2},{12,4},{14,6},{16,24},{18,... | collective-permute-start | bytes 196616 | tf_op jit(solution)/shard_map/ppermute | solution.py:57
  54.0 5.0 %collective-permute-start.7 = (bf16[256,256]{1,0:T(8,128)(2,1)S(1)}, bf16[256,256]{1,0:T(8,128)(2,1)S(1)}, u32[]{:S(2)}, u32[]{:S(2)}) collective-permute-start(bf16[256,256]{1,0:T(8,128)(2,1)S(1)} %maximum_select_fusion.2), channel_id=1, source_target_pairs={{0,4},{2,6},{4,0},{6,2},{8,12},{10,14},{12,8},{14,10},{16,20},{18,... | collective-permute-start | bytes 393224 | tf_op jit(solution)/shard_map/ppermute | solution.py:57
  59.5 1.8 %collective-permute-start.9 = (bf16[512,256]{1,0:T(8,128)(2,1)S(1)}, bf16[512,256]{1,0:T(8,128)(2,1)S(1)}, u32[]{:S(2)}, u32[]{:S(2)}) collective-permute-start(bf16[512,256]{1,0:T(8,128)(2,1)S(1)} %maximum_select_fusion.1), channel_id=1, source_target_pairs={{0,2},{2,0},{4,6},{6,4},{8,10},{10,8},{12,14},{14,12},{16,18},{18,... | collective-permute-start | bytes 786440 | tf_op jit(solution)/shard_map/ppermute | solution.py:57

commit v21 on v19

--- a/solution.py
+++ b/solution.py
@@ -88,7 +88,7 @@
         [joint_part], "loop", loop_count, loop_position
     )
     group_steps = group_count.bit_length() - 1
-    first_bits = list(range(min(2, group_steps)))
+    first_bits = list(range(min(3, group_steps)))
     first_rows = item_part.shape[0] >> len(first_bits)
 
     def group_first(item_part):

time: 60 us -> 62.9 us (1.048)
  other arithmetic: 6.19 us -> 8.17 us
  starting transfers between devices: 16.7 us -> 15.8 us
  waiting for transfers between devices: 22.8 us -> 23.7 us
  local copies, waits for them, and re-layouts: 6.74 us -> 7.6 us
    convert_element_type x2, other arithmetic: 0.42 us -> 1.75 us  [advance(): return (factors.astype(jnp.float32) + rate * gradient).astype(jnp.bfloat16)]
    dynamic_slice x5, local copies, waits for them, and re-layouts: 2.23 us -> 3.08 us  [halving_scatter(): lax.dynamic_slice_in_dim(p, (1 - side) * h, h, 0)]
    ppermute x5, starting transfers between devices: 7.79 us -> 6.95 us  [doubling_gather(): got = lax.ppermute(tuple(parts), axis, xor_pairs(count, bit))]
    ppermute x5, waiting for transfers between devices: 7.91 us -> 8.74 us  [doubling_gather(): got = lax.ppermute(tuple(parts), axis, xor_pairs(count, bit))]
    add x4, other arithmetic: 3.66 us -> 4.32 us  [halving_scatter(): parts = [k + g for k, g in zip(kept, got)]]
    unnamed x14 -> x16, local copies, waits for them, and re-layouts: 2.09 us -> 2.1 us
  transfers between devices with their start and end apart: 10 -> 10, of which waited for: 8 -> 8; matrix products, arithmetic and copies ran while one was open for 9% -> 12% of each run, Pallas kernels for 0% -> 0%
where the time goes in v21:
time: 62.9 us; the launch traced here: 62.4 us
  waiting for transfers between devices  23.7 us (38%)
  starting transfers between devices  15.8 us (25%)
  other arithmetic  8.17 us (13%)
  local copies, waits for them, and re-layouts  7.6 us (12%)
  matrix products  6.33 us (10%)
  between operations  0.81 us (1%)
    ppermute x5, waiting for transfers between devices, halving_scatter(): got = lax.ppermute(tuple(sent), axis, xor_pairs(count, bit))  14.9 us
    ppermute x5, starting transfers between devices, halving_scatter(): got = lax.ppermute(tuple(sent), axis, xor_pairs(count, bit))  8.84 us
    ppermute x5, waiting for transfers between devices, doubling_gather(): got = lax.ppermute(tuple(parts), axis, xor_pairs(count, bit))  8.74 us
    ppermute x5, starting transfers between devices, doubling_gather(): got = lax.ppermute(tuple(parts), axis, xor_pairs(count, bit))  6.95 us
    add x4, other arithmetic, halving_scatter(): parts = [k + g for k, g in zip(kept, got)]  4.32 us
    dynamic_slice x5, local copies, waits for them, and re-layouts, halving_scatter(): lax.dynamic_slice_in_dim(p, (1 - side) * h, h, 0)  3.08 us
    dot_general x2, matrix products, residual_of(): lax.dot_general(row_factors, column_factors, (((1,), (1,)), ((), ())), pr...  2.26 us
    unnamed x16, local copies, waits for them, and re-layouts  2.1 us
  transfers between devices with their start and end apart: 10, of which 8 were waited for; matrix products, arithmetic and copies ran while one was open for 12% of the time, Pallas kernels for 0%

profile of v21, /device:TPU:0, one launch (start us, length us, event | category | flops | bytes accessed | tf_op | source)
XLA Modules:
  0.0 62.4 jit_solution(7374185510758454934)
XLA Ops:
  2.8 1.3 %copy-done.3 = bf16[2048,1024]{1,0:T(8,128)(2,1)S(1)} copy-done((bf16[2048,1024]{1,0:T(8,128)(2,1)S(1)}, bf16[2048,1024]{1,0:T(8,128)(2,1)}, u32[]{:S(2)}) %copy-start.3) | copy-done | bytes 4194328
  4.1 2.0 %fusion = bf16[2048,1024]{1,0:T(8,128)(2,1)S(1)} fusion(f32[256,8,8,128]{3,2,1,0:T(8,128)S(1)} %bitcast.22, bf16[2048,1024]{1,0:T(8,128)(2,1)S(1)} %copy-done.3, bf16[2048,256]{1,0:T(8,128)(2,1)S(1)} %copy-done.1, bf16[1024,256]{1,0:T(8,128)(2,1)S(1)} %copy-done), kind=kOutput, calls=%fused_computation.7 | convolution fusion | flops 1082130432 | bytes 18350080 | tf_op jit(solution)/shard_map/dot_general | solution.py:19
  6.0 1.3 %fusion.4 = f32[2048,256]{1,0:T(8,128)S(1)} fusion(bf16[2048,1024]{1,0:T(8,128)(2,1)S(1)} %fusion, bf16[1024,256]{1,0:T(8,128)(2,1)S(1)} %copy-done), kind=kOutput, calls=%fused_computation.30 | convolution fusion | flops 1073741824 | bytes 6815744 | tf_op jit(solution)/shard_map/dot_general | solution.py:79
  7.4 1.3 %fusion.6 = f32[1024,256]{1,0:T(8,128)S(1)} fusion(bf16[2048,1024]{1,0:T(8,128)(2,1)S(1)} %fusion, bf16[2048,256]{1,0:T(8,128)(2,1)S(1)} %copy-done.1), kind=kOutput, calls=%fused_computation.32 | convolution fusion | flops 1073741824 | bytes 6291456 | tf_op jit(solution)/shard_map/dot_general | solution.py:26
  9.3 1.2 %convolution_add_fusion = f32[1024,256]{1,0:T(8,128)} fusion(f32[1024,256]{1,0:T(8,128)S(1)} %fusion.6, bf16[1024,128]{1,0:T(8,128)(2,1)S(1)} %fusion.2, bf16[128,256]{1,0:T(8,128)(2,1)S(1)} %copy-done.4), kind=kOutput, calls=%fused_computation.9 | convolution fusion | flops 67371008 | bytes 2424832 | tf_op jit(solution)/shard_map/dot_general | solution.py:83
  10.7 1.1 %constant_dynamic-slice_fusion.3 = f32[1088,256]{1,0:T(8,128)} fusion(f32[2176,256]{1,0:T(8,128)S(1)} %pad_maximum_fusion, s32[]{:T(128)S(6)} %select_n.86), kind=kLoop, calls=%fused_computation.27 | loop fusion | bytes 2228228 | tf_op jit(solution)/shard_map/dynamic_slice | solution.py:46
  11.8 3.0 %collective-permute-start.5 = (f32[1088,256]{1,0:T(8,128)}, f32[1088,256]{1,0:T(8,128)}, u32[]{:S(2)}, u32[]{:S(2)}) collective-permute-start(f32[1088,256]{1,0:T(8,128)} %constant_dynamic-slice_fusion.3), channel_id=1, source_target_pairs={{0,1},{1,0},{2,3},{3,2},{4,5},{5,4},{6,7},{7,6},{8,9},{9,8},{10,11... | collective-permute-start | bytes 3342344 | tf_op jit(solution)/shard_map/ppermute | solution.py:47
  14.8 19.7 %conditional.1 = (f32[128,256]{1,0:T(8,128)}, s32[]{:T(128)}) conditional(s32[]{:T(128)} %convert_element_type.33, () %tuple.20, (s32[]{:T(128)}, f32[1024,256]{1,0:T(8,128)}) %tuple.22), branch_computations={%region_0.0_spmd, %region_1.0_spmd} | conditional | flops 229411 | bytes 8258104 | solution.py:100
  14.8 1.1 %constant_dynamic-slice_fusion.2 = f32[512,256]{1,0:T(8,128)S(1)} fusion(f32[1024,256]{1,0:T(8,128)} %get-tuple-element.4, s32[]{:T(128)S(6)} %select_n.57), kind=kLoop, calls=%fused_computation.5 | loop fusion | bytes 1048580 | tf_op jit(solution)/shard_map/cond/branch_1_fun/dynamic_slice | solution.py:46
  16.0 2.0 %collective-permute-done = f32[512,256]{1,0:T(8,128)} collective-permute-done((f32[512,256]{1,0:T(8,128)S(1)}, f32[512,256]{1,0:T(8,128)}, u32[]{:S(2)}, u32[]{:S(2)}) %collective-permute-start) | collective-permute-done | bytes 524320 | tf_op jit(solution)/shard_map/cond/branch_1_fun/ppermute | solution.py:47
  18.0 1.3 %dynamic-slice_add_fusion = f32[512,256]{1,0:T(8,128)S(1)} fusion(f32[512,256]{1,0:T(8,128)} %collective-permute-done, f32[1024,256]{1,0:T(8,128)} %get-tuple-element.4, s32[]{:T(128)S(6)} %select_n.56), kind=kLoop, calls=%fused_computation | loop fusion | flops 131072 | bytes 1572868 | tf_op jit(solution)/shard_map/cond/branch_1_fun/add | solution.py:48
  19.3 1.6 %collective-permute-start.1 = (f32[256,256]{1,0:T(8,128)S(1)}, f32[256,256]{1,0:T(8,128)}, u32[]{:S(2)}, u32[]{:S(2)}) collective-permute-start(f32[256,256]{1,0:T(8,128)S(1)} %constant_dynamic-slice_fusion.1), channel_id=1, source_target_pairs={{0,4},{2,6},{4,0},{6,2},{8,12},{10,14},{12,8},{14,10},{16,20},{18,... | collective-permute-start | bytes 786440 | tf_op jit(solution)/shard_map/cond/branch_1_fun/ppermute | solution.py:47
  20.8 7.0 %collective-permute-done.1 = f32[256,256]{1,0:T(8,128)} collective-permute-done((f32[256,256]{1,0:T(8,128)S(1)}, f32[256,256]{1,0:T(8,128)}, u32[]{:S(2)}, u32[]{:S(2)}) %collective-permute-start.1) | collective-permute-done | bytes 262176 | tf_op jit(solution)/shard_map/cond/branch_1_fun/ppermute | solution.py:47
  28.8 1.6 %collective-permute-start.2 = (f32[128,256]{1,0:T(8,128)S(1)}, f32[128,256]{1,0:T(8,128)S(1)}, u32[]{:S(2)}, u32[]{:S(2)}) collective-permute-start(f32[128,256]{1,0:T(8,128)S(1)} %constant_dynamic-slice_fusion), channel_id=1, source_target_pairs={{0,8},{2,10},{4,12},{6,14},{8,0},{10,2},{12,4},{14,6},{16,24},{18,... | collective-permute-start | bytes 393224 | tf_op jit(solution)/shard_map/cond/branch_1_fun/ppermute | solution.py:47
  30.5 3.4 %collective-permute-done.2 = f32[128,256]{1,0:T(8,128)S(1)} collective-permute-done((f32[128,256]{1,0:T(8,128)S(1)}, f32[128,256]{1,0:T(8,128)S(1)}, u32[]{:S(2)}, u32[]{:S(2)}) %collective-permute-start.2) | collective-permute-done | bytes 131104 | tf_op jit(solution)/shard_map/cond/branch_1_fun/ppermute | solution.py:47
  35.4 2.6 %collective-permute-start.3 = (f32[64,256]{1,0:T(8,128)S(1)}, f32[64,256]{1,0:T(8,128)S(1)}, u32[]{:S(2)}, u32[]{:S(2)}) collective-permute-start(f32[64,256]{1,0:T(8,128)S(1)} %constant_dynamic-slice_fusion.4), channel_id=1, source_target_pairs={{0,16},{2,18},{4,20},{6,22},{8,24},{10,26},{12,28},{14,30},{16,0},... | collective-permute-start | bytes 196616 | tf_op jit(solution)/shard_map/ppermute | solution.py:47
  38.0 2.6 %collective-permute-done.3 = f32[64,256]{1,0:T(8,128)S(1)} collective-permute-done((f32[64,256]{1,0:T(8,128)S(1)}, f32[64,256]{1,0:T(8,128)S(1)}, u32[]{:S(2)}, u32[]{:S(2)}) %collective-permute-start.3) | collective-permute-done | bytes 65568 | tf_op jit(solution)/shard_map/ppermute | solution.py:47
  41.4 2.7 %collective-permute-start.4 = (bf16[64,256]{1,0:T(8,128)(2,1)S(1)}, bf16[64,256]{1,0:T(8,128)(2,1)S(1)}, u32[]{:S(2)}, u32[]{:S(2)}) collective-permute-start(bf16[64,256]{1,0:T(8,128)(2,1)S(1)} %add_convert_fusion.1), channel_id=1, source_target_pairs={{0,16},{2,18},{4,20},{6,22},{8,24},{10,26},{12,28},{14,30},{16,0},... | collective-permute-start | bytes 98312 | tf_op jit(solution)/shard_map/ppermute | solution.py:57
  44.2 2.1 %collective-permute-done.4 = bf16[64,256]{1,0:T(8,128)(2,1)S(1)} collective-permute-done((bf16[64,256]{1,0:T(8,128)(2,1)S(1)}, bf16[64,256]{1,0:T(8,128)(2,1)S(1)}, u32[]{:S(2)}, u32[]{:S(2)}) %collective-permute-start.4) | collective-permute-done | bytes 32800 | tf_op jit(solution)/shard_map/ppermute | solution.py:57
  46.3 1.4 %dynamic-slice_add_fusion.3 = f32[1088,256]{1,0:T(8,128)S(1)} fusion(f32[1088,256]{1,0:T(8,128)} %collective-permute-done.5, f32[2176,256]{1,0:T(8,128)S(1)} %pad_maximum_fusion, s32[]{:T(128)S(6)} %select_n.85), kind=kLoop, calls=%fused_computation.17 | loop fusion | flops 278528 | bytes 3342340 | tf_op jit(solution)/shard_map/add | solution.py:48
  49.1 2.0 %collective-permute-start.6 = (bf16[128,256]{1,0:T(8,128)(2,1)S(1)}, bf16[128,256]{1,0:T(8,128)(2,1)S(1)}, u32[]{:S(2)}, u32[]{:S(2)}) collective-permute-start(bf16[128,256]{1,0:T(8,128)(2,1)S(1)} %maximum_select_fusion.3), channel_id=1, source_target_pairs={{0,8},{2,10},{4,12},{6,14},{8,0},{10,2},{12,4},{14,6},{16,24},{18,... | collective-permute-start | bytes 196616 | tf_op jit(solution)/shard_map/ppermute | solution.py:57
  51.1 2.3 %collective-permute-done.6 = bf16[128,256]{1,0:T(8,128)(2,1)S(1)} collective-permute-done((bf16[128,256]{1,0:T(8,128)(2,1)S(1)}, bf16[128,256]{1,0:T(8,128)(2,1)S(1)}, u32[]{:S(2)}, u32[]{:S(2)}) %collective-permute-start.6) | collective-permute-done | bytes 65568 | tf_op jit(solution)/shard_map/ppermute | solution.py:57
  53.4 1.7 %collective-permute-start.7 = (bf16[256,256]{1,0:T(8,128)(2,1)S(1)}, bf16[256,256]{1,0:T(8,128)(2,1)S(1)}, u32[]{:S(2)}, u32[]{:S(2)}) collective-permute-start(bf16[256,256]{1,0:T(8,128)(2,1)S(1)} %maximum_select_fusion.2), channel_id=1, source_target_pairs={{0,4},{2,6},{4,0},{6,2},{8,12},{10,14},{12,8},{14,10},{16,20},{18,... | collective-permute-start | bytes 393224 | tf_op jit(solution)/shard_map/ppermute | solution.py:57
  55.1 3.3 %collective-permute-done.7 = bf16[256,256]{1,0:T(8,128)(2,1)S(1)} collective-permute-done((bf16[256,256]{1,0:T(8,128)(2,1)S(1)}, bf16[256,256]{1,0:T(8,128)(2,1)S(1)}, u32[]{:S(2)}, u32[]{:S(2)}) %collective-permute-start.7) | collective-permute-done | bytes 131104 | tf_op jit(solution)/shard_map/ppermute | solution.py:57
  (44 shorter events, 11.8 us)
Async XLA Ops:
  1.4 1.0 %copy-start = (bf16[1024,256]{1,0:T(8,128)(2,1)S(1)}, bf16[1024,256]{1,0:T(8,128)(2,1)}, u32[]{:S(2)}) copy-start(bf16[1024,256]{1,0:T(8,128)(2,1)} %param.10) | copy-start | bytes 1572868
  1.4 1.4 %copy-start.1 = (bf16[2048,256]{1,0:T(8,128)(2,1)S(1)}, bf16[2048,256]{1,0:T(8,128)(2,1)}, u32[]{:S(2)}) copy-start(bf16[2048,256]{1,0:T(8,128)(2,1)} %param.9) | copy-start | bytes 3145732
  1.4 2.7 %copy-start.3 = (bf16[2048,1024]{1,0:T(8,128)(2,1)S(1)}, bf16[2048,1024]{1,0:T(8,128)(2,1)}, u32[]{:S(2)}) copy-start(bf16[2048,1024]{1,0:T(8,128)(2,1)} %param.12) | copy-start | bytes 12582916
  7.3 1.3 %copy-start.7 = (s32[8,1]{0,1:T(1,128)S(1)}, s32[8,1]{0,1:T(1,128)}, u32[]{:S(2)}) copy-start(s32[8,1]{0,1:T(1,128)} %param.15) | copy-start | bytes 100
  7.3 1.4 %copy-start.4 = (bf16[128,256]{1,0:T(8,128)(2,1)S(1)}, bf16[128,256]{1,0:T(8,128)(2,1)}, u32[]{:S(2)}) copy-start(bf16[128,256]{1,0:T(8,128)(2,1)} %param.11) | copy-start | bytes 196612
  7.3 1.4 %copy-start.6 = (bf16[1024,128]{1,0:T(8,128)(2,1)S(1)}, bf16[1024,128]{1,0:T(8,128)(2,1)}, u32[]{:S(2)}) copy-start(bf16[1024,128]{1,0:T(8,128)(2,1)} %param.14) | copy-start | bytes 786436
  11.8 34.5 %collective-permute-start.5 = (f32[1088,256]{1,0:T(8,128)}, f32[1088,256]{1,0:T(8,128)}, u32[]{:S(2)}, u32[]{:S(2)}) collective-permute-start(f32[1088,256]{1,0:T(8,128)} %constant_dynamic-slice_fusion.3), channel_id=1, source_target_pairs={{0,1},{1,0},{2,3},{3,2},{4,5},{5,4},{6,7},{7,6},{8,9},{9,8},{10,11... | collective-permute-start | bytes 3342344 | tf_op jit(solution)/shard_map/ppermute | solution.py:47
  15.9 2.1 %collective-permute-start = (f32[512,256]{1,0:T(8,128)S(1)}, f32[512,256]{1,0:T(8,128)}, u32[]{:S(2)}, u32[]{:S(2)}) collective-permute-start(f32[512,256]{1,0:T(8,128)S(1)} %constant_dynamic-slice_fusion.2), channel_id=1, source_target_pairs={{0,2},{2,0},{4,6},{6,4},{8,10},{10,8},{12,14},{14,12},{16,18},{18,... | collective-permute-start | bytes 1572872 | tf_op jit(solution)/shard_map/cond/branch_1_fun/ppermute | solution.py:47
  19.3 8.5 %collective-permute-start.1 = (f32[256,256]{1,0:T(8,128)S(1)}, f32[256,256]{1,0:T(8,128)}, u32[]{:S(2)}, u32[]{:S(2)}) collective-permute-start(f32[256,256]{1,0:T(8,128)S(1)} %constant_dynamic-slice_fusion.1), channel_id=1, source_target_pairs={{0,4},{2,6},{4,0},{6,2},{8,12},{10,14},{12,8},{14,10},{16,20},{18,... | collective-permute-start | bytes 786440 | tf_op jit(solution)/shard_map/cond/branch_1_fun/ppermute | solution.py:47
  28.8 5.0 %collective-permute-start.2 = (f32[128,256]{1,0:T(8,128)S(1)}, f32[128,256]{1,0:T(8,128)S(1)}, u32[]{:S(2)}, u32[]{:S(2)}) collective-permute-start(f32[128,256]{1,0:T(8,128)S(1)} %constant_dynamic-slice_fusion), channel_id=1, source_target_pairs={{0,8},{2,10},{4,12},{6,14},{8,0},{10,2},{12,4},{14,6},{16,24},{18,... | collective-permute-start | bytes 393224 | tf_op jit(solution)/shard_map/cond/branch_1_fun/ppermute | solution.py:47
  34.5 13.2 %copy-start.5 = (bf16[128,256]{1,0:T(8,128)(2,1)S(1)}, bf16[128,256]{1,0:T(8,128)(2,1)}, u32[]{:S(2)}) copy-start(bf16[128,256]{1,0:T(8,128)(2,1)} %param.11) | copy-start | bytes 196612
  35.4 5.2 %collective-permute-start.3 = (f32[64,256]{1,0:T(8,128)S(1)}, f32[64,256]{1,0:T(8,128)S(1)}, u32[]{:S(2)}, u32[]{:S(2)}) collective-permute-start(f32[64,256]{1,0:T(8,128)S(1)} %constant_dynamic-slice_fusion.4), channel_id=1, source_target_pairs={{0,16},{2,18},{4,20},{6,22},{8,24},{10,26},{12,28},{14,30},{16,0},... | collective-permute-start | bytes 196616 | tf_op jit(solution)/shard_map/ppermute | solution.py:47
  41.4 6.3 %copy-start.2 = (bf16[2048,256]{1,0:T(8,128)(2,1)S(1)}, bf16[2048,256]{1,0:T(8,128)(2,1)}, u32[]{:S(2)}) copy-start(bf16[2048,256]{1,0:T(8,128)(2,1)} %param.9) | copy-start | bytes 3145732
  41.4 4.9 %collective-permute-start.4 = (bf16[64,256]{1,0:T(8,128)(2,1)S(1)}, bf16[64,256]{1,0:T(8,128)(2,1)S(1)}, u32[]{:S(2)}, u32[]{:S(2)}) collective-permute-start(bf16[64,256]{1,0:T(8,128)(2,1)S(1)} %add_convert_fusion.1), channel_id=1, source_target_pairs={{0,16},{2,18},{4,20},{6,22},{8,24},{10,26},{12,28},{14,30},{16,0},... | collective-permute-start | bytes 98312 | tf_op jit(solution)/shard_map/ppermute | solution.py:57
  48.7 10.9 %collective-permute-start.8 = (bf16[1088,256]{1,0:T(8,128)(2,1)S(1)}, bf16[1088,256]{1,0:T(8,128)(2,1)S(1)}, u32[]{:S(2)}, u32[]{:S(2)}) collective-permute-start(bf16[1088,256]{1,0:T(8,128)(2,1)S(1)} %add_convert_fusion), channel_id=1, source_target_pairs={{0,1},{1,0},{2,3},{3,2},{4,5},{5,4},{6,7},{7,6},{8,9},{9,8},{10,11... | collective-permute-start | bytes 1671176 | tf_op jit(solution)/shard_map/ppermute | solution.py:57
  49.1 4.3 %collective-permute-start.6 = (bf16[128,256]{1,0:T(8,128)(2,1)S(1)}, bf16[128,256]{1,0:T(8,128)(2,1)S(1)}, u32[]{:S(2)}, u32[]{:S(2)}) collective-permute-start(bf16[128,256]{1,0:T(8,128)(2,1)S(1)} %maximum_select_fusion.3), channel_id=1, source_target_pairs={{0,8},{2,10},{4,12},{6,14},{8,0},{10,2},{12,4},{14,6},{16,24},{18,... | collective-permute-start | bytes 196616 | tf_op jit(solution)/shard_map/ppermute | solution.py:57
  53.4 5.0 %collective-permute-start.7 = (bf16[256,256]{1,0:T(8,128)(2,1)S(1)}, bf16[256,256]{1,0:T(8,128)(2,1)S(1)}, u32[]{:S(2)}, u32[]{:S(2)}) collective-permute-start(bf16[256,256]{1,0:T(8,128)(2,1)S(1)} %maximum_select_fusion.2), channel_id=1, source_target_pairs={{0,4},{2,6},{4,0},{6,2},{8,12},{10,14},{12,8},{14,10},{16,20},{18,... | collective-permute-start | bytes 393224 | tf_op jit(solution)/shard_map/ppermute | solution.py:57
  59.8 1.8 %collective-permute-start.9 = (bf16[512,256]{1,0:T(8,128)(2,1)S(1)}, bf16[512,256]{1,0:T(8,128)(2,1)S(1)}, u32[]{:S(2)}, u32[]{:S(2)}) collective-permute-start(bf16[512,256]{1,0:T(8,128)(2,1)S(1)} %maximum_select_fusion.1), channel_id=1, source_target_pairs={{0,2},{2,0},{4,6},{6,4},{8,10},{10,8},{12,14},{14,12},{16,18},{18,... | collective-permute-start | bytes 786440 | tf_op jit(solution)/shard_map/ppermute | solution.py:57
